TPU v7x, 256 devices: a whole 4x4x8 slice. The times are simulated.
256 devices in a mesh: dom: 128 (over y, x, z), sub: 2 (over core).
Axes of the slice: x: 4, y: 4, z: 8, core: 2. Of those that a mesh axis runs over, the one named last changes fastest.
Arguments:
- codes: int32 [65536, 4], P(('dom', 'sub')), may hold values from 0 to 255
- books: bfloat16 [4, 256, 128], P('sub'), may hold values from -6 to 6
- alpha: float32 [512, 64], replicated, may hold values from -0.75 to 0.75
- basis: float32 [64, 512], replicated, may hold values from -6 to 6
- w_msg: bfloat16 [512, 512], replicated, may hold values from -0.25 to 0.25
- w_self: bfloat16 [512, 512], replicated, may hold values from -0.25 to 0.25
- tiles: bfloat16 [4096, 128, 128], P(('dom', 'sub')), may hold values from -0.1875 to 0.1875
- tile_src: int32 [4096], P(('dom', 'sub')), may hold values from 0 to 13
- tile_rel: int32 [4096], P(('dom', 'sub')), may hold values from 0 to 511
- send_rows: int32 [128, 2, 128, 8], P('dom', 'sub'), may hold values from 0 to 255
- send_count: int32 [128, 2, 128], P('dom', 'sub'), may hold values from 0 to 8, as said below
- hub_owner: int32 [2], replicated, may hold values from 0 to 127
- cotangent: bfloat16 [65536, 512], P(('dom', 'sub')), may hold values from -0.01171875 to 0.01171875
Outputs:
- output: bfloat16 [65536, 512], P(('dom', 'sub'))
- grad_w_msg: float32 [512, 512], replicated
- grad_w_self: float32 [512, 512], replicated
- grad_alpha: float32 [512, 64], replicated
- grad_basis: float32 [64, 512], replicated
- grad_books: float32 [4, 256, 128], P('sub')
Inputs may be any that keep to these rules, and one draw needn't show every extreme that they name: `send_count`: every device uses all 8 slots toward at least one partition.
All inputs are finite; a program needn't handle non-finite values.
Results may differ from a plain program's by a relative error of at most 0.015.
Values may be sent and summed in bfloat16 or wider, within the bound.
No kernel may reach another device: no remote copies, remote signals or barrier semaphores. Data moves between devices by JAX's collectives and lax.ppermute only.
A program may use at most 64 MiB of HBM per device.

v0:
```python
import jax
import jax.numpy as jnp
from jax import lax
from jax.sharding import PartitionSpec as P

TB = 128
TPB = 8
SLOT = 8
NHUB = 2


HIGHEST_PREC = lax.Precision.HIGHEST


def broadcast(block, axis, owner):
    block = jnp.where(lax.axis_index(axis) == owner, block, jnp.zeros_like(block))
    return lax.psum(block, axis)


def one_hot_codes(code_rows, code_count, out_type):
    return (code_rows[..., None] == jnp.arange(code_count, dtype=jnp.int32)).astype(out_type)


def fold_books(code_rows, gradients, code_count):
    book_count = code_rows.shape[1]
    indicator_rows = one_hot_codes(code_rows, code_count, jnp.bfloat16)
    pieces = gradients.reshape(gradients.shape[0], book_count, -1)
    upper_bound = pieces.astype(jnp.bfloat16)
    lower_bound = (pieces - upper_bound.astype(jnp.float32)).astype(jnp.bfloat16)
    upper_half_sum = jnp.einsum(
        "fco,fcg->cog", indicator_rows, upper_bound, preferred_element_type=jnp.float32
    )
    lower_half_sum = jnp.einsum(
        "fco,fcg->cog", indicator_rows, lower_bound, preferred_element_type=jnp.float32
    )
    return upper_half_sum + lower_half_sum


def shards(
    codes,
    books,
    alpha,
    basis,
    w_msg,
    w_self,
    tiles,
    tile_src,
    tile_rel,
    send_rows,
    send_count,
    hub_owner,
    cotangent,
):
    rows_dev, book_count = codes.shape
    code_count = books.shape[1]
    model_width = w_msg.shape[0]
    tile_count = tiles.shape[0]
    block_count = tile_count // TPB
    complete_codebooks = lax.all_gather(books, "sub", axis=0, tiled=True)
    indicator_rows = one_hot_codes(codes, code_count, jnp.bfloat16)
    local_rows = jnp.einsum(
        "feu,euq->feq", indicator_rows, complete_codebooks, preferred_element_type=jnp.float32
    )
    local_rows = local_rows.astype(jnp.bfloat16).reshape(rows_dev, model_width)
    rel_table = jnp.dot(alpha, basis, precision=HIGHEST_PREC, preferred_element_type=jnp.float32)
    targets = send_rows[0, 0]
    part_count = targets.shape[0]
    slot_valid = jnp.arange(SLOT, dtype=jnp.int32)[None, :] < send_count[0, 0][:, None]
    outgoing = jnp.where(slot_valid[:, :, None], local_rows[targets], jnp.zeros((), jnp.bfloat16))
    incoming = lax.all_to_all(outgoing, "dom", split_axis=0, concat_axis=0, tiled=True)
    hub_rows = []
    hub_codes = []
    for hub_index in range(NHUB):
        rows_now, codes_now = (
            broadcast(local_rows, "dom", hub_owner[hub_index]),
            broadcast(codes, "dom", hub_owner[hub_index]),
        )
        hub_rows.append(rows_now)
        hub_codes.append(codes_now)
    table = jnp.concatenate([local_rows, incoming.reshape(-1, model_width)] + hub_rows, axis=0)
    blocks = table.reshape(-1, TB, model_width)
    tile_blocks = tiles.reshape(block_count, TPB, TB, TB)
    source_blocks = tile_src.reshape(block_count, TPB)
    relation_blocks = tile_rel.reshape(block_count, TPB)

    def forward_block(packed):
        weights_now, source_now, relation_now = packed
        composed = (
            blocks[source_now].astype(jnp.float32) * rel_table[relation_now][:, None, :]
        ).astype(jnp.bfloat16)
        summed = jnp.einsum(
            "tij,tjd->id", weights_now, composed, preferred_element_type=jnp.float32
        )
        return summed.astype(jnp.bfloat16)

    aggregate = lax.map(forward_block, (tile_blocks, source_blocks, relation_blocks)).reshape(
        rows_dev, model_width
    )
    pre_act = jnp.dot(aggregate, w_msg, preferred_element_type=jnp.float32) + jnp.dot(
        local_rows, w_self, preferred_element_type=jnp.float32
    )
    activated = jnp.tanh(pre_act)
    output = activated.astype(jnp.bfloat16)
    grad_pre = (cotangent.astype(jnp.float32) * (1.0 - activated * activated)).astype(jnp.bfloat16)
    contract_rows = (((0,), (0,)), ((), ()))
    contract_cols = (((1,), (1,)), ((), ()))
    grad_w_msg = lax.dot_general(
        aggregate, grad_pre, contract_rows, preferred_element_type=jnp.float32
    )
    grad_w_self = lax.dot_general(
        local_rows, grad_pre, contract_rows, preferred_element_type=jnp.float32
    )
    grad_agg = lax.dot_general(
        grad_pre, w_msg, contract_cols, preferred_element_type=jnp.float32
    ).astype(jnp.bfloat16)
    grad_self = lax.dot_general(grad_pre, w_self, contract_cols, preferred_element_type=jnp.float32)
    grad_blocks = grad_agg.reshape(block_count, TB, model_width)

    def backward_block(carry, packed):
        table_grad, rel_grad = carry
        weights_now, source_now, relation_now, upstream = packed
        grad_comp = jnp.einsum(
            "tji,jd->tid", weights_now, upstream, preferred_element_type=jnp.float32
        )
        rel_grad = rel_grad.at[relation_now].add(
            jnp.sum(grad_comp * blocks[source_now].astype(jnp.float32), axis=1)
        )
        table_grad = table_grad.at[source_now].add(grad_comp * rel_table[relation_now][:, None, :])
        return ((table_grad, rel_grad), None)

    start_carry = (jnp.zeros(blocks.shape, jnp.float32), jnp.zeros(rel_table.shape, jnp.float32))
    final_carry = lax.scan(
        backward_block, start_carry, (tile_blocks, source_blocks, relation_blocks, grad_blocks)
    )[0]
    table_grad, rel_grad = final_carry
    table_grad = table_grad.reshape(-1, model_width)
    recv_count = part_count * SLOT
    local_grad = table_grad[:rows_dev] + grad_self
    recv_grad = table_grad[rows_dev : rows_dev + recv_count]
    hub_grad = table_grad[rows_dev + recv_count :]
    hub_code_rows = jnp.concatenate(hub_codes, axis=0)
    returned = lax.all_to_all(
        recv_grad.reshape(part_count, SLOT, model_width).astype(jnp.bfloat16),
        "dom",
        split_axis=0,
        concat_axis=0,
        tiled=True,
    ).astype(jnp.float32)
    returned = jnp.where(slot_valid[:, :, None], returned, jnp.zeros((), jnp.float32))
    local_grad = local_grad.at[targets.reshape(-1)].add(returned.reshape(-1, model_width))
    all_codes = jnp.concatenate([codes, hub_code_rows], axis=0)
    all_grads = jnp.concatenate([local_grad, hub_grad], axis=0)
    book_grad = fold_books(all_codes, all_grads, code_count)
    book_share = books.shape[0]
    total_msg, total_self, total_rel, total_books = lax.psum(
        (grad_w_msg, grad_w_self, rel_grad, book_grad), ("dom", "sub")
    )
    grad_alpha = jnp.dot(
        total_rel, basis.T, precision=HIGHEST_PREC, preferred_element_type=jnp.float32
    )
    grad_basis = jnp.dot(
        alpha.T, total_rel, precision=HIGHEST_PREC, preferred_element_type=jnp.float32
    )
    grad_books = lax.dynamic_slice_in_dim(
        total_books, lax.axis_index("sub") * book_share, book_share, 0
    )
    return (output, total_msg, total_self, grad_alpha, grad_basis, grad_books)


def solution(mesh):
    return jax.shard_map(
        shards,
        mesh=mesh,
        in_specs=(
            P(("dom", "sub"), None),
            P("sub", None, None),
            P(),
            P(),
            P(),
            P(),
            P(("dom", "sub"), None, None),
            P(("dom", "sub")),
            P(("dom", "sub")),
            P("dom", "sub", None, None),
            P("dom", "sub", None),
            P(),
            P(("dom", "sub"), None),
        ),
        out_specs=(P(("dom", "sub"), None), P(), P(), P(), P(), P("sub", None, None)),
        check_vma=False,
    )
```

profile of v0, /device:TPU:1, one launch (start us, length us, event | category | flops | bytes accessed | tf_op | source)
XLA Modules:
  0.0 657.5 jit_solution(610589712299502757)
XLA Ops:
  7.2 5.2 all_gather.3
  12.4 1.1 convolution_convert_fusion.1
  15.3 4.0 gather_fusion.4
  19.3 1.2 bitcast_select_fusion
  20.5 13.9 %all-to-all-start = ((bf16[128,8,512]{2,1,0:T(8,128)(2,1)}), bf16[128,8,512]{2,1,0:T(8,128)(2,1)S(1)}, u32[]{:S(2)}, u32[]{:S(2)}) async-start(bf16[128,8,512]{2,1,0:T(8,128)(2,1)} %bitcast_select_fusion), calls=%async_computation | async-start | bytes 2097152 | tf_op jit(solution)/shard_map/all_to_all | solution.py:70
  37.4 1.3 copy.38
  38.8 2.0 fusion.37
  40.8 213.9 %all-reduce.8.cloned.1.call-done = (bf16[256,512]{0,1:T(8,128)(2,1)}, bf16[256,512]{0,1:T(8,128)(2,1)}) async-done(((bf16[256,512]{0,1:T(8,128)(2,1)}, bf16[256,512]{0,1:T(8,128)(2,1)}), (bf16[256,512]{0,1:T(8,128)(2,1)}, bf16[256,512]{0,1:T(8,128)(2,1)})) %all-reduce.8.cloned.1.call-update) | async-done | bytes 524304 | tf_op jit(solution)/shard_map/psum | solution.py:17
  254.6 1.1 copy.43
  255.7 1.1 copy.44
  256.8 1.4 pad_maximum_fusion
  258.2 10.6 %while.22 = (s32[]{:T(128)}, bf16[2,128,512]{2,1,0:T(8,128)(2,1)S(1)}, bf16[2,8,128,128]{3,2,1,0:T(8,128)(2,1)}, s32[2,8]{1,0:T(2,128)S(1)}, bf16[14,128,512]{2,...) while((s32[]{:T(128)}, bf16[2,128,512]{2,1,0:T(8,128)(2,1)S(1)}, ...), condition=%wide.region_3.4_spmd, body=%wide.region_2.3_spmd.sunk | while | flops 135858224 | bytes 3597657 | solution.py:96
  258.2 2.2 gather_fusion
  260.4 1.8 gather_fusion.1
  262.2 1.3 fusion.68
  263.6 2.1 gather_fusion
  265.7 1.8 gather_fusion.1
  267.5 1.3 fusion.68
  269.2 2.0 multiply_convert_fusion.2
  271.3 1.0 convolution_convert_fusion
  272.3 2.3 broadcast_in_dim.43
  274.6 1.1 broadcast_in_dim.44
  275.7 27.6 %while.23 = (s32[]{:T(128)}, f32[14,128,512]{2,1,0:T(8,128)}, f32[512,512]{1,0:T(8,128)}, s32[2,8]{1,0:T(2,128)S(1)}, bf16[2,8,128,128]{2,3,1,0:T(8,128)(2,1)S(1...) while((s32[]{:T(128)}, f32[14,128,512]{2,1,0:T(8,128)}, ...), condition=%wide.region_10.11_spmd, body=%wide.region_6.10_spmd.sunk | while | flops 136841264 | bytes 12051881 | solution.py:132
  275.7 3.1 gather_fusion.2
  278.8 1.8 gather_fusion.3
  280.6 1.8 multiply_reduce_fusion.2
  282.4 4.3 scatter_fusion
  286.7 2.8 scatter_fusion.1
  289.5 3.1 gather_fusion.2
  292.6 1.8 gather_fusion.3
  294.4 1.8 multiply_reduce_fusion.2
  296.1 4.3 scatter_fusion
  300.5 2.8 scatter_fusion.1
  303.3 2.7 slice.41
  306.0 9.9 %all-to-all-start.1 = ((bf16[128,8,512]{2,1,0:T(8,128)(2,1)}), bf16[128,8,512]{2,1,0:T(8,128)(2,1)S(1)}, u32[]{:S(2)}, u32[]{:S(2)}) async-start(bf16[128,8,512]{2,1,0:T(8,128)(2,1)} %bitcast.31), calls=%async_computation.1 | async-start | bytes 2097152 | tf_op jit(solution)/shard_map/all_to_all | solution.py:142
  316.2 38.2 %all-reduce = (s32[256,4]{0,1:T(4,128)S(1)}, s32[256,4]{0,1:T(4,128)S(1)}) all-reduce(s32[256,4]{0,1:T(4,128)S(1)} %get-tuple-element.166, s32[256,4]{0,1:T(4,128)S(1)} %get-tuple-element.165), channel_id=1, replica_groups=mesh['dom'=128,'sub'=2] {'dom'}, use_global_device_ids=true, to_apply=%region_13.14 | all-reduce | flops 2048 | bytes 16384 | tf_op jit(solution)/shard_map/psum | solution.py:17
  354.4 1.9 slice.25
  356.2 2.3 slice.28
  358.5 1.6 concatenate.17
  360.2 1.3 fusion.39
  361.5 1.3 fusion.40
  363.1 7.3 %scatter_custom_fusion.2 = f32[256,512]{1,0:T(8,128)S(1)} fusion(f32[256,512]{1,0:T(8,128)S(1)} %convolution_add_fusion, s32[1024]{0:T(1024)S(1)} %bitcast.140, bf16[128,8,512]{2,1,0:T(8,128)(2,1)S(1)} %all-to-all-done.1, f32[]{:T(128)} %constant.37.clone.1, pred[128,8]{1,0:T(8,128)(4,1)S(1)} %iota_compare_fusion.7), kind=kCustom, calls=%fused_computation.49 | custom fusion | flops 1572864 | bytes 1589252 | tf_op jit(solution)/shard_map/scatter-add | solution.py:150
  371.1 1.5 fusion.29
  372.7 269.5 %all-reduce.6.cloned.1.call-done = (f32[512,512]{1,0:T(8,128)}, f32[512,512]{1,0:T(8,128)}, f32[512,512]{1,0:T(8,128)}, f32[4,256,128]{2,1,0:T(8,128)}) async-done(((f32[512,512]{1,0:T(8,128)}, f32[512,512]{1,0:T(8,128)}, f32[512,512]{1,0:T(8,128)}, f32[4,256,128]{2,1,0:T(8,128)}), (f32[512,512]{1,0:T(8,128)}, f32[512,512]{1,0:T(8,128)}, f32[512,512]{1,0:T(8,128)}, ...) | async-done | bytes 3670032 | tf_op jit(solution)/shard_map/psum | solution.py:155
  642.1 2.8 convolution_bitcast_fusion.1
  644.9 3.1 fusion.41
  648.8 1.0 copy.80
  649.7 1.0 copy.81
  (78 shorter events, 6.0 us)
Async XLA Ops:
  7.2 262.0 %copy-start = (bf16[512,512]{1,0:T(8,128)(2,1)S(1)}, bf16[512,512]{1,0:T(8,128)(2,1)}, u32[]{:S(2)}) copy-start(bf16[512,512]{1,0:T(8,128)(2,1)} %param.22) | copy-start | bytes 1572868
  13.5 255.7 %copy-start.1 = (bf16[4,256,128]{1,2,0:T(8,128)(2,1)}, bf16[4,256,128]{1,2,0:T(8,128)(2,1)S(1)}, u32[]{:S(2)}) copy-start(bf16[4,256,128]{1,2,0:T(8,128)(2,1)S(1)} %convolution_convert_fusion.1) | copy-start | bytes 786436
  19.3 15.2 %copy-start.16 = (s32[2]{0:T(128)S(1)}, s32[2]{0:T(128)}, u32[]{:S(2)}) copy-start(s32[2]{0:T(128)} %param.28) | copy-start | bytes 28
  20.5 16.8 %copy-start.17 = (s32[16]{0:T(128)S(1)}, s32[16]{0:T(128)}, u32[]{:S(2)}) copy-start(s32[16]{0:T(128)} %param.24) | copy-start | bytes 196
  20.5 16.9 %copy-start.18 = (s32[16]{0:T(128)S(1)}, s32[16]{0:T(128)}, u32[]{:S(2)}) copy-start(s32[16]{0:T(128)} %param.25) | copy-start | bytes 196
  20.5 18.3 %copy-start.9 = (f32[512,64]{0,1:T(8,128)S(1)}, f32[512,64]{0,1:T(8,128)}, u32[]{:S(2)}) copy-start(f32[512,64]{0,1:T(8,128)} %param.19) | copy-start | bytes 393220
  20.5 18.3 %copy-start.11 = (f32[64,512]{1,0:T(8,128)S(1)}, f32[64,512]{1,0:T(8,128)}, u32[]{:S(2)}) copy-start(f32[64,512]{1,0:T(8,128)} %param.20) | copy-start | bytes 393220
  20.5 236.3 %all-to-all-start = ((bf16[128,8,512]{2,1,0:T(8,128)(2,1)}), bf16[128,8,512]{2,1,0:T(8,128)(2,1)S(1)}, u32[]{:S(2)}, u32[]{:S(2)}) async-start(bf16[128,8,512]{2,1,0:T(8,128)(2,1)} %bitcast_select_fusion), calls=%async_computation | async-start | bytes 2097152 | tf_op jit(solution)/shard_map/all_to_all | solution.py:70
  34.4 220.2 %all-reduce.8.cloned.1.call-start = ((), (), s32[]{:S(2)}) async-start(), calls=%async_computation.3 | async-start | bytes 1048576 | tf_op jit(solution)/shard_map/psum | solution.py:17
  258.2 10.7 %copy-start.4 = (bf16[512,512]{1,0:T(8,128)(2,1)S(1)}, bf16[512,512]{1,0:T(8,128)(2,1)}, u32[]{:S(2)}) copy-start(bf16[512,512]{1,0:T(8,128)(2,1)} %param.21) | copy-start | bytes 1572868
  268.9 3.4 copy-start.7
  303.3 12.7 %copy-start.14 = (s32[1,1,128,8]{2,3,1,0:T(8,128)S(1)}, s32[1,1,128,8]{2,3,1,0:T(8,128)}, u32[]{:S(2)}) copy-start(s32[1,1,128,8]{2,3,1,0:T(8,128)} %param.26) | copy-start | bytes 12292
  303.3 12.9 %copy-start.15 = (s32[256,4]{0,1:T(4,128)S(1)}, s32[256,4]{0,1:T(4,128)}, u32[]{:S(2)}) copy-start(s32[256,4]{0,1:T(4,128)} %param.17) | copy-start | bytes 12292
  306.0 57.1 %all-to-all-start.1 = ((bf16[128,8,512]{2,1,0:T(8,128)(2,1)}), bf16[128,8,512]{2,1,0:T(8,128)(2,1)S(1)}, u32[]{:S(2)}, u32[]{:S(2)}) async-start(bf16[128,8,512]{2,1,0:T(8,128)(2,1)} %bitcast.31), calls=%async_computation.1 | async-start | bytes 2097152 | tf_op jit(solution)/shard_map/all_to_all | solution.py:142
  315.9 326.2 %all-reduce.6.cloned.1.call-start = ((), (), s32[]{:S(2)}) async-start(), calls=%async_computation.2 | async-start | bytes 7340032 | tf_op jit(solution)/shard_map/psum | solution.py:155
  356.2 3.9 copy-start.8
  358.5 2.9 copy-start.2
  360.2 2.6 copy-start.3
  372.6 269.5 %copy-start.10 = (f32[512,64]{0,1:T(8,128)S(1)}, f32[512,64]{0,1:T(8,128)}, u32[]{:S(2)}) copy-start(f32[512,64]{0,1:T(8,128)} %param.19) | copy-start | bytes 393220
  372.6 272.3 %copy-start.12 = (f32[64,512]{1,0:T(8,128)S(1)}, f32[64,512]{1,0:T(8,128)}, u32[]{:S(2)}) copy-start(f32[64,512]{1,0:T(8,128)} %param.20) | copy-start | bytes 393220
  642.1 5.9 copy-start.13
  642.1 6.6 %copy-start.6 = (f32[512,512]{1,0:T(8,128)S(1)}, f32[512,512]{1,0:T(8,128)}, u32[]{:S(2)}) copy-start(f32[512,512]{1,0:T(8,128)} %get-tuple-element.335) | copy-start | bytes 3145732
  644.9 4.8 copy-start.5
Sparse Core Ops, SparseCore 0:
  41.4 213.1 all-reduce.7
  372.8 269.2 all-reduce.5
where the time goes:
time: 660 us; the launch traced here: 658 us
  waiting for transfers between devices  483 us (73%)
  blocking collectives  43.4 us (7%)
  local copies, waits for them, and re-layouts  41.1 us (6%)
  other arithmetic  26.5 us (4%)
  starting transfers between devices  23.9 us (4%)
  matrix products  23.6 us (4%)
  between operations  15.7 us (2%)
    psum x1, waiting for transfers between devices, shards(): lax.psum((grad_w_msg, grad_w_self, rel_grad, book_grad), ('dom', 'sub'))  269 us
    psum x1, waiting for transfers between devices, broadcast(): return lax.psum(block, axis)  214 us
    psum x1, blocking collectives, broadcast(): return lax.psum(block, axis)  38.2 us
    all_to_all x1, starting transfers between devices, shards(): lax.all_to_all(outgoing, 'dom', split_axis=0, concat_axis=0, tiled=True)  13.9 us
  transfers between devices with their start and end apart: 4, of which 2 were waited for; matrix products, arithmetic and copies ran while one was open for 2% of the time, Pallas kernels for 0%

commit v1 on v0

--- a/solution.py
+++ b/solution.py
@@ -12,13 +12,16 @@
 HIGHEST_PREC = lax.Precision.HIGHEST
 
 
-def broadcast(block, axis, owner):
-    block = jnp.where(lax.axis_index(axis) == owner, block, jnp.zeros_like(block))
-    return lax.psum(block, axis)
-
-
 def one_hot_codes(code_rows, code_count, out_type):
     return (code_rows[..., None] == jnp.arange(code_count, dtype=jnp.int32)).astype(out_type)
+
+
+def decode(code_rows, complete_codebooks):
+    indicator_rows = one_hot_codes(code_rows, complete_codebooks.shape[1], jnp.bfloat16)
+    rows = jnp.einsum(
+        "feu,euq->feq", indicator_rows, complete_codebooks, preferred_element_type=jnp.float32
+    )
+    return rows.astype(jnp.bfloat16).reshape(code_rows.shape[0], -1)
 
 
 def fold_books(code_rows, gradients, code_count):
@@ -36,7 +39,26 @@
     return upper_half_sum + lower_half_sum
 
 
+def all_sum(parts, axes, n_dev):
+    flat = jnp.concatenate([p.reshape(-1) for p in parts])
+    size = flat.shape[0]
+    padded = -(-size // n_dev) * n_dev
+    flat = jnp.pad(flat, (0, padded - size))
+    chunks = flat.reshape(n_dev, -1)
+    received = lax.all_to_all(chunks, axes, 0, 0, tiled=True)
+    mine = jnp.sum(received, axis=0)
+    spread = jnp.broadcast_to(mine[None], chunks.shape)
+    total = lax.all_to_all(spread, axes, 0, 0, tiled=True).reshape(-1)[:size]
+    out = []
+    start = 0
+    for p in parts:
+        out.append(total[start : start + p.size].reshape(p.shape))
+        start += p.size
+    return out
+
+
 def shards(
+    n_dev,
     codes,
     books,
     alpha,
@@ -57,27 +79,28 @@
     tile_count = tiles.shape[0]
     block_count = tile_count // TPB
     complete_codebooks = lax.all_gather(books, "sub", axis=0, tiled=True)
-    indicator_rows = one_hot_codes(codes, code_count, jnp.bfloat16)
-    local_rows = jnp.einsum(
-        "feu,euq->feq", indicator_rows, complete_codebooks, preferred_element_type=jnp.float32
-    )
-    local_rows = local_rows.astype(jnp.bfloat16).reshape(rows_dev, model_width)
     rel_table = jnp.dot(alpha, basis, precision=HIGHEST_PREC, preferred_element_type=jnp.float32)
     targets = send_rows[0, 0]
     part_count = targets.shape[0]
+    frag = rows_dev // part_count
     slot_valid = jnp.arange(SLOT, dtype=jnp.int32)[None, :] < send_count[0, 0][:, None]
-    outgoing = jnp.where(slot_valid[:, :, None], local_rows[targets], jnp.zeros((), jnp.bfloat16))
-    incoming = lax.all_to_all(outgoing, "dom", split_axis=0, concat_axis=0, tiled=True)
-    hub_rows = []
-    hub_codes = []
-    for hub_index in range(NHUB):
-        rows_now, codes_now = (
-            broadcast(local_rows, "dom", hub_owner[hub_index]),
-            broadcast(codes, "dom", hub_owner[hub_index]),
-        )
-        hub_rows.append(rows_now)
-        hub_codes.append(codes_now)
-    table = jnp.concatenate([local_rows, incoming.reshape(-1, model_width)] + hub_rows, axis=0)
+    out_codes = jnp.where(slot_valid[:, :, None], codes[targets], -1)
+    hub_piece = codes.reshape(part_count, frag, book_count)
+    payload = jnp.concatenate([out_codes, hub_piece], axis=1)
+    incoming = lax.all_to_all(payload, "dom", 0, 0, tiled=True)
+    recv_codes = incoming[:, :SLOT].reshape(-1, book_count)
+    held = jnp.concatenate(
+        [incoming[hub_owner[hub_index], SLOT:] for hub_index in range(NHUB)], axis=0
+    )
+    spread = jnp.broadcast_to(held[None], (part_count,) + held.shape)
+    gathered = lax.all_to_all(spread, "dom", 0, 0, tiled=True)
+    hub_codes = [
+        gathered[:, hub_index * frag : (hub_index + 1) * frag].reshape(-1, book_count)
+        for hub_index in range(NHUB)
+    ]
+    table_codes = jnp.concatenate([codes, recv_codes] + hub_codes, axis=0)
+    table = decode(table_codes, complete_codebooks)
+    local_rows = table[:rows_dev]
     blocks = table.reshape(-1, TB, model_width)
     tile_blocks = tiles.reshape(block_count, TPB, TB, TB)
     source_blocks = tile_src.reshape(block_count, TPB)
@@ -134,33 +157,18 @@
     )[0]
     table_grad, rel_grad = final_carry
     table_grad = table_grad.reshape(-1, model_width)
-    recv_count = part_count * SLOT
-    local_grad = table_grad[:rows_dev] + grad_self
-    recv_grad = table_grad[rows_dev : rows_dev + recv_count]
-    hub_grad = table_grad[rows_dev + recv_count :]
-    hub_code_rows = jnp.concatenate(hub_codes, axis=0)
-    returned = lax.all_to_all(
-        recv_grad.reshape(part_count, SLOT, model_width).astype(jnp.bfloat16),
-        "dom",
-        split_axis=0,
-        concat_axis=0,
-        tiled=True,
-    ).astype(jnp.float32)
-    returned = jnp.where(slot_valid[:, :, None], returned, jnp.zeros((), jnp.float32))
-    local_grad = local_grad.at[targets.reshape(-1)].add(returned.reshape(-1, model_width))
-    all_codes = jnp.concatenate([codes, hub_code_rows], axis=0)
-    all_grads = jnp.concatenate([local_grad, hub_grad], axis=0)
-    book_grad = fold_books(all_codes, all_grads, code_count)
+    table_grad = table_grad.at[:rows_dev].add(grad_self)
+    book_grad = fold_books(table_codes, table_grad, code_count)
+    part_alpha = jnp.dot(
+        rel_grad, basis.T, precision=HIGHEST_PREC, preferred_element_type=jnp.float32
+    )
+    part_basis = jnp.dot(
+        alpha.T, rel_grad, precision=HIGHEST_PREC, preferred_element_type=jnp.float32
+    )
+    total_msg, total_self, grad_alpha, grad_basis, total_books = all_sum(
+        (grad_w_msg, grad_w_self, part_alpha, part_basis, book_grad), ("dom", "sub"), n_dev
+    )
     book_share = books.shape[0]
-    total_msg, total_self, total_rel, total_books = lax.psum(
-        (grad_w_msg, grad_w_self, rel_grad, book_grad), ("dom", "sub")
-    )
-    grad_alpha = jnp.dot(
-        total_rel, basis.T, precision=HIGHEST_PREC, preferred_element_type=jnp.float32
-    )
-    grad_basis = jnp.dot(
-        alpha.T, total_rel, precision=HIGHEST_PREC, preferred_element_type=jnp.float32
-    )
     grad_books = lax.dynamic_slice_in_dim(
         total_books, lax.axis_index("sub") * book_share, book_share, 0
     )
@@ -168,8 +176,13 @@
 
 
 def solution(mesh):
+    n_dev = mesh.shape["dom"] * mesh.shape["sub"]
+
+    def run(*args):
+        return shards(n_dev, *args)
+
     return jax.shard_map(
-        shards,
+        run,
         mesh=mesh,
         in_specs=(
             P(("dom", "sub"), None),

time: 660 us -> 323 us (0.49)
  waiting for transfers between devices: 483 us -> 85.1 us
  blocking collectives: 43.4 us -> 83.3 us
  local copies, waits for them, and re-layouts: 41.1 us -> 60 us
  between operations: 15.7 us -> 4.89 us
  matrix products: 23.6 us -> 31.7 us
    psum x2 -> x0, waiting for transfers between devices: 483 us -> none  [the longest x1 269 us: shards(): lax.psum((grad_w_msg, grad_w_self, rel_grad, book_grad), ('dom', 'sub'))]
    all_to_all x2 -> x3, waiting for transfers between devices: 0.01 us -> 85.1 us  [the longest x1 69.6 us: all_sum(): total = lax.all_to_all(spread, axes, 0, 0, tiled=True).reshape(-1)[:size]]
    all_to_all x0 -> x1, blocking collectives: none -> 79.7 us  [all_sum(): received = lax.all_to_all(chunks, axes, 0, 0, tiled=True)]
    psum x1 -> x0, blocking collectives: 38.2 us -> none  [broadcast(): return lax.psum(block, axis)]
    all_to_all x0 -> x1, other arithmetic: none -> 8.67 us  [all_sum(): total = lax.all_to_all(spread, axes, 0, 0, tiled=True).reshape(-1)[:size]]
    scatter-add x1 -> x0, other arithmetic: 7.28 us -> none  [shards(): local_grad.at[targets.reshape(-1)].add(returned.reshape(-1, model_width))]
    another operation x1 -> x3, local copies, waits for them, and re-layouts: 0.1 us -> 7.16 us  [the longest x2 6.08 us: shards(): blocks = table.reshape(-1, TB, model_width)]
    all_to_all x2 -> x3, starting transfers between devices: 23.8 us -> 29.8 us  [the longest x1 16.5 us: shards(): incoming = lax.all_to_all(payload, 'dom', 0, 0, tiled=True)]
  transfers between devices with their start and end apart: 4 -> 3, of which waited for: 2 -> 3; matrix products, arithmetic and copies ran while one was open for 2% -> 1% of each run, Pallas kernels for 0% -> 0%
where the time goes in v1:
time: 323 us; the launch traced here: 321 us
  waiting for transfers between devices  85.1 us (26%)
  blocking collectives  83.3 us (26%)
  local copies, waits for them, and re-layouts  60 us (19%)
  matrix products  31.7 us (10%)
  starting transfers between devices  29.8 us (9%)
  other arithmetic  26.4 us (8%)
  between operations  4.89 us (2%)
    all_to_all x1, blocking collectives, all_sum(): received = lax.all_to_all(chunks, axes, 0, 0, tiled=True)  79.7 us
    all_to_all x1, waiting for transfers between devices, all_sum(): total = lax.all_to_all(spread, axes, 0, 0, tiled=True).reshape(-1)[:size]  69.6 us
    all_to_all x1, starting transfers between devices, shards(): incoming = lax.all_to_all(payload, 'dom', 0, 0, tiled=True)  16.5 us
    slice x7, local copies, waits for them, and re-layouts, all_sum(): out.append(total[start:start + p.size].reshape(p.shape))  11.1 us
    all_to_all x1, other arithmetic, all_sum(): total = lax.all_to_all(spread, axes, 0, 0, tiled=True).reshape(-1)[:size]  8.67 us
    scatter-add x2, other arithmetic, backward_block(): table_grad.at[source_now]  8.58 us
    all_to_all x1, waiting for transfers between devices, shards(): gathered = lax.all_to_all(spread, 'dom', 0, 0, tiled=True)  8.44 us
    all_to_all x1, waiting for transfers between devices, shards(): incoming = lax.all_to_all(payload, 'dom', 0, 0, tiled=True)  7.05 us
  transfers between devices with their start and end apart: 3, of which 3 were waited for; matrix products, arithmetic and copies ran while one was open for 1% of the time, Pallas kernels for 0%

profile of v1, /device:TPU:1, one launch (start us, length us, event | category | flops | bytes accessed | tf_op | source)
XLA Modules:
  0.0 321.3 jit_solution(3912739127944968180)
XLA Ops:
  2.5 2.8 gather_fusion.4
  8.2 16.5 %all-to-all-start = ((s32[128,10,4]{1,2,0:T(4,128)}), s32[128,10,4]{1,2,0:T(4,128)S(1)}, u32[]{:S(2)}, u32[]{:S(2)}) async-start(s32[128,10,4]{1,2,0:T(4,128)} %pad_add_fusion), calls=%async_computation | async-start | bytes 524288 | tf_op jit(solution)/shard_map/all_to_all | solution.py:90
  24.7 2.0 fusion.37
  31.2 7.0 %all-to-all-done = s32[128,10,4]{1,2,0:T(4,128)S(1)} async-done(((s32[128,10,4]{1,2,0:T(4,128)}), s32[128,10,4]{1,2,0:T(4,128)S(1)}, u32[]{:S(2)}, u32[]{:S(2)}) %all-to-all-start) | async-done | bytes 20512 | tf_op jit(solution)/shard_map/all_to_all | solution.py:90
  39.2 6.7 %all-to-all-start.1 = ((s32[128,4,4]{2,1,0:T(4,128)}), s32[128,4,4]{2,1,0:T(4,128)S(1)}, u32[]{:S(2)}, u32[]{:S(2)}) async-start(s32[128,4,4]{2,1,0:T(4,128)} %broadcast_in_dim.32), calls=%async_computation.1 | async-start | bytes 524288 | tf_op jit(solution)/shard_map/all_to_all | solution.py:96
  45.9 3.6 %all_gather.3 = bf16[4,256,128]{2,1,0:T(8,128)(2,1)S(1)} all-gather(bf16[2,256,128]{2,1,0:T(8,128)(2,1)S(1)} %copy-done.10), channel_id=1, replica_groups=mesh['dom'=128,'sub'=2] {'sub'}, dimensions={0}, use_global_device_ids=true | all-gather | bytes 393216 | tf_op jit(solution)/shard_map/all_gather | solution.py:81
  50.2 8.4 %all-to-all-done.1 = s32[128,4,4]{2,1,0:T(4,128)S(1)} async-done(((s32[128,4,4]{2,1,0:T(4,128)}), s32[128,4,4]{2,1,0:T(4,128)S(1)}, u32[]{:S(2)}, u32[]{:S(2)}) %all-to-all-start.1) | async-done | bytes 8224 | tf_op jit(solution)/shard_map/all_to_all | solution.py:96
  58.9 2.9 fusion.28
  61.8 3.2 reshape.362
  66.0 2.9 copy.147
  68.9 11.9 %while.23 = (s32[]{:T(128)}, bf16[2,128,512]{2,1,0:T(8,128)(2,1)}, bf16[2,8,128,128]{3,2,1,0:T(8,128)(2,1)}, s32[2,8]{1,0:T(2,128)S(1)}, bf16[14,128,512]{2,1,0:...) while((s32[]{:T(128)}, bf16[2,128,512]{2,1,0:T(8,128)(2,1)}, ...), condition=%wide.region_1.2_spmd, body=%wide.region_0.1_spmd.sunk | while | flops 135858224 | bytes 3597657 | solution.py:119
  68.9 2.2 gather_fusion
  71.1 1.8 gather_fusion.1
  72.9 2.0 fusion.65
  74.9 2.1 gather_fusion
  77.0 1.8 gather_fusion.1
  78.8 2.0 fusion.65
  80.8 1.3 fusion.38
  82.1 2.0 multiply_convert_fusion.2
  85.2 1.3 convolution_bitcast_fusion.1
  86.6 1.3 convolution_bitcast_fusion.2
  87.9 2.2 broadcast_in_dim.38
  91.2 27.7 %while.24 = (s32[]{:T(128)}, f32[14,128,512]{2,1,0:T(8,128)}, f32[512,512]{1,0:T(8,128)}, s32[2,8]{1,0:T(2,128)S(1)}, bf16[2,8,128,128]{2,3,1,0:T(8,128)(2,1)S(1...) while((s32[]{:T(128)}, f32[14,128,512]{2,1,0:T(8,128)}, ...), condition=%wide.region_6.7_spmd, body=%wide.region_2.6_spmd.sunk | while | flops 136841264 | bytes 12051881 | solution.py:155
  91.2 3.2 gather_fusion.2
  94.4 1.8 gather_fusion.3
  96.2 1.8 multiply_reduce_fusion.2
  98.0 4.4 %scatter_fusion = f32[14,128,512]{2,1,0:T(8,128)} fusion(f32[14,128,512]{2,1,0:T(8,128)} %get-tuple-element.394, s32[8]{0:T(128)S(1)} %get-tuple-element.355, f32[8,128,512]{2,1,0:T(8,128)S(1)} %get-tuple-element.357), kind=kCustom, calls=%fused_computation.5.clone.1 | custom fusion | flops 524288 | bytes 6291488 | tf_op jit(solution)/shard_map/while/body/eval_jaxpr/scatter-add | solution.py:151
  102.3 2.8 scatter_fusion.1
  105.2 3.2 gather_fusion.2
  108.3 1.8 gather_fusion.3
  110.1 1.8 multiply_reduce_fusion.2
  111.9 4.2 %scatter_fusion = f32[14,128,512]{2,1,0:T(8,128)} fusion(f32[14,128,512]{2,1,0:T(8,128)} %get-tuple-element.394, s32[8]{0:T(128)S(1)} %get-tuple-element.355, f32[8,128,512]{2,1,0:T(8,128)S(1)} %get-tuple-element.357), kind=kCustom, calls=%fused_computation.5.clone.1 | custom fusion | flops 524288 | bytes 6291488 | tf_op jit(solution)/shard_map/while/body/eval_jaxpr/scatter-add | solution.py:151
  116.1 2.8 scatter_fusion.1
  118.9 2.2 fusion.39
  121.1 2.0 convolution_bitcast_fusion.3
  125.3 5.2 %copy.136 = f32[1792,512]{0,1:T(8,128)} copy(f32[1792,512]{1,0:T(8,128)} %fusion.30) | data formatting | bytes 7340032 | tf_op jit(solution)/shard_map/scatter-add | solution.py:160
  130.6 4.7 %fusion.21 = f32[4,256,128]{2,1,0:T(8,128)S(1)} fusion(s32[1792,4]{0,1:T(4,128)S(1)} %pad_add_fusion.1, f32[1792,4,128]{0,2,1:T(8,128)} %bitcast.141), kind=kOutput, calls=%fused_computation.45 | convolution fusion | flops 475267072 | bytes 4222976 | tf_op jit(solution)/shard_map/fco,fcg->cog/dot_general | solution.py:36
  135.3 2.3 fusion.29
  139.3 79.7 %all_to_all.25 = f32[256,1,2816]{2,1,0:T(1,128)S(1)} all-to-all(f32[256,1,2816]{2,1,0:T(1,128)S(1)} %bitcast.138), channel_id=1, replica_groups=mesh['dom'=128,'sub'=2] {'dom','sub'}, dimensions={0} | all-to-all | bytes 5767168 | tf_op jit(solution)/shard_map/all_to_all | solution.py:48
  219.0 1.6 reduce_sum.18
  220.6 3.1 broadcast_in_dim.40
  223.6 6.7 %all-to-all-start.3 = ((f32[256,1,2816]{2,1,0:T(1,128)}), f32[256,1,2816]{2,1,0:T(1,128)}, u32[]{:S(2)}, u32[]{:S(2)}) async-start(f32[256,1,2816]{2,1,0:T(1,128)} %broadcast_in_dim.40), calls=%async_computation.3 | async-start | bytes 5767168 | tf_op jit(solution)/shard_map/all_to_all | solution.py:51
  230.4 69.6 %all-to-all-done.3 = f32[256,1,2816]{2,1,0:T(1,128)} async-done(((f32[256,1,2816]{2,1,0:T(1,128)}), f32[256,1,2816]{2,1,0:T(1,128)}, u32[]{:S(2)}, u32[]{:S(2)}) %all-to-all-start.3) | async-done | bytes 2883616 | tf_op jit(solution)/shard_map/all_to_all | solution.py:51
  300.0 8.7 %reduce.3 = f32[256,2816]{1,0:T(8,128)S(1)} reduce(f32[256,1,2816]{2,1,0:T(1,128)} %all-to-all-done.3, f32[]{:T(128)} %constant.93), dimensions={1}, to_apply=%all_to_all.20.reduce_sub_computation | reduce | bytes 5767172 | tf_op jit(solution)/shard_map/all_to_all | solution.py:51
  308.7 3.4 %slice.78 = f32[11264,64]{1,0:T(8,128)} reshape(f32[256,2816]{1,0:T(8,128)S(1)} %reduce.3) | data formatting | bytes 5767168 | tf_op jit(solution)/shard_map/slice | solution.py:55
  312.1 2.0 slice.75
  314.1 3.1 fusion.34
  317.2 1.6 slice.100
  (89 shorter events, 16.9 us)
Async XLA Ops:
  0.6 81.5 %copy-start = (bf16[512,512]{1,0:T(8,128)(2,1)S(1)}, bf16[512,512]{1,0:T(8,128)(2,1)}, u32[]{:S(2)}) copy-start(bf16[512,512]{1,0:T(8,128)(2,1)} %param.24) | copy-start | bytes 1572868
  1.5 4.7 %copy-start.13 = (s32[1,1,128]{2,1,0:T(1,128)S(1)}, s32[1,1,128]{2,1,0:T(1,128)}, u32[]{:S(2)}) copy-start(s32[1,1,128]{2,1,0:T(1,128)} %param.29) | copy-start | bytes 1540
  2.4 22.2 %copy-start.6 = (f32[512,64]{0,1:T(8,128)S(1)}, f32[512,64]{0,1:T(8,128)}, u32[]{:S(2)}) copy-start(f32[512,64]{0,1:T(8,128)} %param.21) | copy-start | bytes 393220
  2.5 22.2 %copy-start.9 = (f32[64,512]{1,0:T(8,128)S(1)}, f32[64,512]{1,0:T(8,128)}, u32[]{:S(2)}) copy-start(f32[64,512]{1,0:T(8,128)} %param.22) | copy-start | bytes 393220
  5.3 21.4 %copy-start.12 = (s32[2]{0:T(128)S(1)}, s32[2]{0:T(128)}, u32[]{:S(2)}) copy-start(s32[2]{0:T(128)} %param.30) | copy-start | bytes 28
  5.3 40.6 %copy-start.10 = (bf16[2,256,128]{2,1,0:T(8,128)(2,1)S(1)}, bf16[2,256,128]{2,1,0:T(8,128)(2,1)}, u32[]{:S(2)}) copy-start(bf16[2,256,128]{2,1,0:T(8,128)(2,1)} %param.20) | copy-start | bytes 393220
  5.3 44.2 %copy-start.14 = (s32[16]{0:T(128)S(1)}, s32[16]{0:T(128)}, u32[]{:S(2)}) copy-start(s32[16]{0:T(128)} %param.26) | copy-start | bytes 196
  5.3 44.3 %copy-start.15 = (s32[16]{0:T(128)S(1)}, s32[16]{0:T(128)}, u32[]{:S(2)}) copy-start(s32[16]{0:T(128)} %param.27) | copy-start | bytes 196
  5.3 44.4 %copy-start.7 = (bf16[16,128,128]{2,1,0:T(8,128)(2,1)S(1)}, bf16[16,128,128]{2,1,0:T(8,128)(2,1)}, u32[]{:S(2)}) copy-start(bf16[16,128,128]{2,1,0:T(8,128)(2,1)} %param.25) | copy-start | bytes 1572868
  8.2 50.7 %copy-start.11 = (s32[256,4]{0,1:T(4,128)S(1)}, s32[256,4]{0,1:T(4,128)}, u32[]{:S(2)}) copy-start(s32[256,4]{0,1:T(4,128)} %param.19) | copy-start | bytes 12292
  8.2 30.0 %all-to-all-start = ((s32[128,10,4]{1,2,0:T(4,128)}), s32[128,10,4]{1,2,0:T(4,128)S(1)}, u32[]{:S(2)}, u32[]{:S(2)}) async-start(s32[128,10,4]{1,2,0:T(4,128)} %pad_add_fusion), calls=%async_computation | async-start | bytes 524288 | tf_op jit(solution)/shard_map/all_to_all | solution.py:90
  39.2 19.4 %all-to-all-start.1 = ((s32[128,4,4]{2,1,0:T(4,128)}), s32[128,4,4]{2,1,0:T(4,128)S(1)}, u32[]{:S(2)}, u32[]{:S(2)}) async-start(s32[128,4,4]{2,1,0:T(4,128)} %broadcast_in_dim.32), calls=%async_computation.1 | async-start | bytes 524288 | tf_op jit(solution)/shard_map/all_to_all | solution.py:96
  68.9 11.9 %copy-start.4 = (bf16[512,512]{1,0:T(8,128)(2,1)S(1)}, bf16[512,512]{1,0:T(8,128)(2,1)}, u32[]{:S(2)}) copy-start(bf16[512,512]{1,0:T(8,128)(2,1)} %param.23) | copy-start | bytes 1572868
  80.8 5.8 %copy-start.5 = (bf16[2,128,512]{2,1,0:T(8,128)(2,1)S(1)}, bf16[2,128,512]{2,1,0:T(8,128)(2,1)}, u32[]{:S(2)}) copy-start(bf16[2,128,512]{2,1,0:T(8,128)(2,1)} %get-tuple-element.103) | copy-start | bytes 786436
  130.6 4.7 %copy-start.3 = (f32[1792,512]{0,1:T(8,128)S(1)}, f32[1792,512]{0,1:T(8,128)}, u32[]{:S(2)}) copy-start(f32[1792,512]{0,1:T(8,128)} %copy.136) | copy-start | bytes 11010052
  135.3 2.4 copy-start.1
  135.3 2.7 copy-start.2
  138.2 1.0 copy-start.8
  223.6 76.4 %all-to-all-start.3 = ((f32[256,1,2816]{2,1,0:T(1,128)}), f32[256,1,2816]{2,1,0:T(1,128)}, u32[]{:S(2)}, u32[]{:S(2)}) async-start(f32[256,1,2816]{2,1,0:T(1,128)} %broadcast_in_dim.40), calls=%async_computation.3 | async-start | bytes 5767168 | tf_op jit(solution)/shard_map/all_to_all | solution.py:51
  314.1 4.6 %slice-start = ((f32[11264,64]{1,0:T(8,128)}), f32[512,64]{1,0:T(8,128)S(1)}, s32[]{:S(2)}) async-start(f32[11264,64]{1,0:T(8,128)} %slice.78), calls=%async_computation.4 | async-start | bytes 524288 | tf_op jit(solution)/shard_map/slice | solution.py:55

commit v2 on v1

--- a/solution.py
+++ b/solution.py
@@ -39,16 +39,27 @@
     return upper_half_sum + lower_half_sum
 
 
-def all_sum(parts, axes, n_dev):
+def all_sum(parts, n_dom):
     flat = jnp.concatenate([p.reshape(-1) for p in parts])
     size = flat.shape[0]
-    padded = -(-size // n_dev) * n_dev
-    flat = jnp.pad(flat, (0, padded - size))
-    chunks = flat.reshape(n_dev, -1)
-    received = lax.all_to_all(chunks, axes, 0, 0, tiled=True)
-    mine = jnp.sum(received, axis=0)
-    spread = jnp.broadcast_to(mine[None], chunks.shape)
-    total = lax.all_to_all(spread, axes, 0, 0, tiled=True).reshape(-1)[:size]
+    unit = 2 * n_dom
+    padded = -(-size // unit) * unit
+    halves = jnp.pad(flat, (0, padded - size)).reshape(2, -1)
+    sub_index = lax.axis_index("sub")
+    keep = lax.dynamic_index_in_dim(halves, sub_index, 0, keepdims=False)
+    give = lax.dynamic_index_in_dim(halves, 1 - sub_index, 0, keepdims=False)
+    swap = [(0, 1), (1, 0)]
+    mine = keep + lax.ppermute(give, "sub", swap)
+    chunks = mine.reshape(n_dom, -1)
+    received = lax.all_to_all(chunks, "dom", 0, 0, tiled=True)
+    reduced = jnp.sum(received, axis=0).astype(jnp.bfloat16)
+    spread = jnp.broadcast_to(reduced[None], chunks.shape)
+    own_half = lax.all_to_all(spread, "dom", 0, 0, tiled=True).reshape(-1)
+    other_half = lax.ppermute(own_half, "sub", swap)
+    both = jnp.zeros(halves.shape, jnp.bfloat16)
+    both = lax.dynamic_update_index_in_dim(both, own_half, sub_index, 0)
+    both = lax.dynamic_update_index_in_dim(both, other_half, 1 - sub_index, 0)
+    total = both.reshape(-1)[:size].astype(jnp.float32)
     out = []
     start = 0
     for p in parts:
@@ -58,7 +69,7 @@
 
 
 def shards(
-    n_dev,
+    n_dom,
     codes,
     books,
     alpha,
@@ -82,22 +93,13 @@
     rel_table = jnp.dot(alpha, basis, precision=HIGHEST_PREC, preferred_element_type=jnp.float32)
     targets = send_rows[0, 0]
     part_count = targets.shape[0]
-    frag = rows_dev // part_count
     slot_valid = jnp.arange(SLOT, dtype=jnp.int32)[None, :] < send_count[0, 0][:, None]
     out_codes = jnp.where(slot_valid[:, :, None], codes[targets], -1)
-    hub_piece = codes.reshape(part_count, frag, book_count)
-    payload = jnp.concatenate([out_codes, hub_piece], axis=1)
+    own_codes = jnp.broadcast_to(codes[None], (part_count,) + codes.shape)
+    payload = jnp.concatenate([out_codes, own_codes], axis=1)
     incoming = lax.all_to_all(payload, "dom", 0, 0, tiled=True)
     recv_codes = incoming[:, :SLOT].reshape(-1, book_count)
-    held = jnp.concatenate(
-        [incoming[hub_owner[hub_index], SLOT:] for hub_index in range(NHUB)], axis=0
-    )
-    spread = jnp.broadcast_to(held[None], (part_count,) + held.shape)
-    gathered = lax.all_to_all(spread, "dom", 0, 0, tiled=True)
-    hub_codes = [
-        gathered[:, hub_index * frag : (hub_index + 1) * frag].reshape(-1, book_count)
-        for hub_index in range(NHUB)
-    ]
+    hub_codes = [incoming[hub_owner[hub_index], SLOT:] for hub_index in range(NHUB)]
     table_codes = jnp.concatenate([codes, recv_codes] + hub_codes, axis=0)
     table = decode(table_codes, complete_codebooks)
     local_rows = table[:rows_dev]
@@ -166,7 +168,7 @@
         alpha.T, rel_grad, precision=HIGHEST_PREC, preferred_element_type=jnp.float32
     )
     total_msg, total_self, grad_alpha, grad_basis, total_books = all_sum(
-        (grad_w_msg, grad_w_self, part_alpha, part_basis, book_grad), ("dom", "sub"), n_dev
+        (grad_w_msg, grad_w_self, part_alpha, part_basis, book_grad), n_dom
     )
     book_share = books.shape[0]
     grad_books = lax.dynamic_slice_in_dim(
@@ -176,10 +178,10 @@
 
 
 def solution(mesh):
-    n_dev = mesh.shape["dom"] * mesh.shape["sub"]
+    n_dom = mesh.shape["dom"]
 
     def run(*args):
-        return shards(n_dev, *args)
+        return shards(n_dom, *args)
 
     return jax.shard_map(
         run,

time: 323 us -> 291 us (0.901)
  waiting for transfers between devices: 85.1 us -> 17.4 us
  local copies, waits for them, and re-layouts: 60 us -> 105 us
  starting transfers between devices: 29.8 us -> 22.6 us
  blocking collectives: 83.3 us -> 76.5 us
    all_to_all x2 -> x0, waiting for transfers between devices: 78.1 us -> none  [the longest x1 69.6 us: all_sum(): total = lax.all_to_all(spread, axes, 0, 0, tiled=True).reshape(-1)[:size]]
    dynamic_update_slice x0 -> x2, local copies, waits for them, and re-layouts: none -> 27.4 us  [the longest x1 13.7 us: all_sum(): both = lax.dynamic_update_index_in_dim(both, other_half, 1 - sub_index, 0)]
    all_to_all x2 -> x0, starting transfers between devices: 13.4 us -> none  [the longest x1 6.72 us: all_sum(): total = lax.all_to_all(spread, axes, 0, 0, tiled=True).reshape(-1)[:size]]
    all_to_all x1, waiting for transfers between devices: 7.05 us -> 14.5 us  [shards(): incoming = lax.all_to_all(payload, 'dom', 0, 0, tiled=True)]
    convert_element_type x0 -> x3, local copies, waits for them, and re-layouts: none -> 7.26 us  [all_sum(): total = both.reshape(-1)[:size].astype(jnp.float32)]
    slice x7 -> x4, local copies, waits for them, and re-layouts: 11.1 us -> 4.6 us  [all_sum(): out.append(total[start:start + p.size].reshape(p.shape))]
    all_to_all x1 -> x2, blocking collectives: 79.7 us -> 73.3 us  [the longest x1 45.2 us: all_sum(): received = lax.all_to_all(chunks, 'dom', 0, 0, tiled=True)]
    broadcast_in_dim x2 -> x5, local copies, waits for them, and re-layouts: 3.79 us -> 10.1 us  [the longest x1 7.71 us: all_sum(): both = lax.dynamic_update_index_in_dim(both, other_half, 1 - sub_index, 0)]
  transfers between devices with their start and end apart: 3 -> 3, of which waited for: 3 -> 2; matrix products, arithmetic and copies ran while one was open for 1% -> 6% of each run, Pallas kernels for 0% -> 0%
where the time goes in v2:
time: 291 us; the launch traced here: 287 us
  local copies, waits for them, and re-layouts  105 us (36%)
  blocking collectives  76.5 us (26%)
  matrix products  30.9 us (11%)
  other arithmetic  28.7 us (10%)
  starting transfers between devices  22.6 us (8%)
  waiting for transfers between devices  17.4 us (6%)
  between operations  5.28 us (2%)
    all_to_all x1, blocking collectives, all_sum(): received = lax.all_to_all(chunks, 'dom', 0, 0, tiled=True)  45.2 us
    all_to_all x1, blocking collectives, all_sum(): own_half = lax.all_to_all(spread, 'dom', 0, 0, tiled=True).reshape(-1)  28.1 us
    all_to_all x1, starting transfers between devices, shards(): incoming = lax.all_to_all(payload, 'dom', 0, 0, tiled=True)  16.3 us
    all_to_all x1, waiting for transfers between devices, shards(): incoming = lax.all_to_all(payload, 'dom', 0, 0, tiled=True)  14.5 us
    dynamic_update_slice x1, local copies, waits for them, and re-layouts, all_sum(): both = lax.dynamic_update_index_in_dim(both, other_half, 1 - sub_index, 0)  13.7 us
    dynamic_update_slice x1, local copies, waits for them, and re-layouts, all_sum(): both = lax.dynamic_update_index_in_dim(both, own_half, sub_index, 0)  13.7 us
    scatter-add x2, other arithmetic, backward_block(): table_grad.at[source_now]  8.56 us
    unnamed x43, local copies, waits for them, and re-layouts  7.81 us
  transfers between devices with their start and end apart: 3, of which 2 were waited for; matrix products, arithmetic and copies ran while one was open for 6% of the time, Pallas kernels for 0%

profile of v2, /device:TPU:1, one launch (start us, length us, event | category | flops | bytes accessed | tf_op | source)
XLA Modules:
  0.0 286.9 jit_solution(7692280764660352362)
XLA Ops:
  2.5 2.8 gather_fusion.4
  7.8 16.3 %all-to-all-start = ((s32[128,264,4]{1,2,0:T(4,128)}), s32[128,264,4]{1,2,0:T(4,128)S(1)}, u32[]{:S(2)}, u32[]{:S(2)}) async-start(s32[128,264,4]{1,2,0:T(4,128)} %pad_add_fusion), calls=%async_computation | async-start | bytes 1572864 | tf_op jit(solution)/shard_map/all_to_all | solution.py:100
  29.2 3.2 %all_gather.3 = bf16[4,256,128]{2,1,0:T(8,128)(2,1)S(1)} all-gather(bf16[2,256,128]{2,1,0:T(8,128)(2,1)S(1)} %copy-done.9), channel_id=1, replica_groups=mesh['dom'=128,'sub'=2] {'sub'}, dimensions={0}, use_global_device_ids=true | all-gather | bytes 393216 | tf_op jit(solution)/shard_map/all_gather | solution.py:92
  32.3 2.0 fusion.36
  34.3 14.5 %all-to-all-done = s32[128,264,4]{1,2,0:T(4,128)S(1)} async-done(((s32[128,264,4]{1,2,0:T(4,128)}), s32[128,264,4]{1,2,0:T(4,128)S(1)}, u32[]{:S(2)}, u32[]{:S(2)}) %all-to-all-start) | async-done | bytes 540704 | tf_op jit(solution)/shard_map/all_to_all | solution.py:100
  49.2 2.9 %fusion.28 = bf16[1792,4,128]{0,2,1:T(8,128)(2,1)} fusion(bf16[4,256,128]{2,1,0:T(8,128)(2,1)S(1)} %all_gather.3, s32[1792,4]{0,1:T(4,128)S(1)} %pad_add_fusion.1), kind=kOutput, calls=%fused_computation.53 | convolution fusion | flops 472514560 | bytes 2125824 | tf_op jit(solution)/shard_map/feu,euq->feq/dot_general | solution.py:21
  52.1 3.2 %reshape.370 = bf16[14,128,512]{1,0,2:T(8,128)(2,1)S(1)} reshape(bf16[1792,4,128]{0,2,1:T(8,128)(2,1)} %fusion.28) | data formatting | bytes 3670016 | tf_op jit(solution)/shard_map/reshape;reshape | solution.py:106
  56.3 2.9 %copy.118 = bf16[14,128,512]{2,1,0:T(8,128)(2,1)} copy(bf16[14,128,512]{1,0,2:T(8,128)(2,1)S(1)} %reshape.370) | data formatting | bytes 3670016 | tf_op jit(solution)/shard_map/reshape;reshape | solution.py:106
  59.2 11.9 %while.23 = (s32[]{:T(128)}, bf16[2,128,512]{2,1,0:T(8,128)(2,1)}, bf16[2,8,128,128]{3,2,1,0:T(8,128)(2,1)}, s32[2,8]{1,0:T(2,128)S(1)}, bf16[14,128,512]{2,1,0:...) while((s32[]{:T(128)}, bf16[2,128,512]{2,1,0:T(8,128)(2,1)}, ...), condition=%wide.region_1.2_spmd, body=%wide.region_0.1_spmd.sunk | while | flops 135858224 | bytes 3597657 | solution.py:121
  59.2 2.2 gather_fusion
  61.4 1.8 gather_fusion.1
  63.2 2.0 fusion.64
  65.2 2.1 gather_fusion
  67.3 1.8 gather_fusion.1
  69.1 2.0 fusion.64
  72.4 2.0 multiply_convert_fusion.2
  78.0 2.3 broadcast_in_dim.67
  81.5 27.7 %while.24 = (s32[]{:T(128)}, f32[14,128,512]{2,1,0:T(8,128)}, f32[512,512]{1,0:T(8,128)}, s32[2,8]{1,0:T(2,128)S(1)}, bf16[2,8,128,128]{2,3,1,0:T(8,128)(2,1)S(1...) while((s32[]{:T(128)}, f32[14,128,512]{2,1,0:T(8,128)}, ...), condition=%wide.region_6.7_spmd, body=%wide.region_2.6_spmd.sunk | while | flops 136841264 | bytes 12051881 | solution.py:157
  81.5 3.1 %gather_fusion.2 = bf16[8,128,512]{2,1,0:T(8,128)(2,1)} fusion(bf16[14,128,512]{2,1,0:T(8,128)(2,1)} %get-tuple-element.411, s32[1024]{0:T(1024)S(1)} %pad_clamp_fusion.10), kind=kCustom, calls=%fused_computation.3.clone.1 | custom fusion | bytes 2097184 | tf_op jit(solution)/shard_map/while/body/eval_jaxpr/gather | solution.py:151
  84.6 1.8 gather_fusion.3
  86.4 1.8 multiply_reduce_fusion.2
  88.2 4.3 %scatter_fusion = f32[14,128,512]{2,1,0:T(8,128)} fusion(f32[14,128,512]{2,1,0:T(8,128)} %get-tuple-element.394, s32[8]{0:T(128)S(1)} %get-tuple-element.355, f32[8,128,512]{2,1,0:T(8,128)S(1)} %get-tuple-element.357), kind=kCustom, calls=%fused_computation.5.clone.1 | custom fusion | flops 524288 | bytes 6291488 | tf_op jit(solution)/shard_map/while/body/eval_jaxpr/scatter-add | solution.py:153
  92.5 2.8 scatter_fusion.1
  95.3 3.1 %gather_fusion.2 = bf16[8,128,512]{2,1,0:T(8,128)(2,1)} fusion(bf16[14,128,512]{2,1,0:T(8,128)(2,1)} %get-tuple-element.411, s32[1024]{0:T(1024)S(1)} %pad_clamp_fusion.10), kind=kCustom, calls=%fused_computation.3.clone.1 | custom fusion | bytes 2097184 | tf_op jit(solution)/shard_map/while/body/eval_jaxpr/gather | solution.py:151
  98.5 1.8 gather_fusion.3
  100.3 1.8 multiply_reduce_fusion.2
  102.0 4.3 %scatter_fusion = f32[14,128,512]{2,1,0:T(8,128)} fusion(f32[14,128,512]{2,1,0:T(8,128)} %get-tuple-element.394, s32[8]{0:T(128)S(1)} %get-tuple-element.355, f32[8,128,512]{2,1,0:T(8,128)S(1)} %get-tuple-element.357), kind=kCustom, calls=%fused_computation.5.clone.1 | custom fusion | flops 524288 | bytes 6291488 | tf_op jit(solution)/shard_map/while/body/eval_jaxpr/scatter-add | solution.py:153
  106.3 2.8 scatter_fusion.1
  109.1 2.2 fusion.38
  111.3 2.0 convolution_bitcast_fusion.3
  115.6 5.3 %copy.107 = f32[1792,512]{0,1:T(8,128)} copy(f32[1792,512]{1,0:T(8,128)} %fusion.30) | data formatting | bytes 7340032 | tf_op jit(solution)/shard_map/scatter-add | solution.py:162
  120.9 4.7 %fusion.21 = f32[4,256,128]{2,1,0:T(8,128)S(1)} fusion(s32[1792,4]{0,1:T(4,128)S(1)} %pad_add_fusion.1, f32[1792,4,128]{0,2,1:T(8,128)} %bitcast.142), kind=kOutput, calls=%fused_computation.45 | convolution fusion | flops 475267072 | bytes 4222976 | tf_op jit(solution)/shard_map/fco,fcg->cog/dot_general | solution.py:36
  132.1 3.6 %reshape.308 = f32[2,360448]{1,0:T(2,128)S(1)} reshape(f32[720896]{0:T(1024)} %constant_dynamic-update-slice_fusion) | data formatting | bytes 5767168 | tf_op jit(solution)/shard_map/reshape | solution.py:47
  135.7 2.5 constant_dynamic-slice_fusion.4
  138.3 2.7 collective-permute-start
  141.0 2.8 collective-permute-done
  144.0 45.2 %all_to_all.20 = f32[128,1,2816]{2,1,0:T(1,128)S(1)} all-to-all(f32[128,1,2816]{2,1,0:T(1,128)S(1)} %bitcast.138), channel_id=1, replica_groups=mesh['dom'=128,'sub'=2] {'dom'}, dimensions={0} | all-to-all | bytes 2883584 | tf_op jit(solution)/shard_map/all_to_all | solution.py:54
  191.5 5.0 %reduce.4 = bf16[128,2816]{1,0:T(8,128)(2,1)S(1)} reduce(bf16[128,1,2816]{2,1,0:T(2,128)(2,1)S(1)} %broadcast_in_dim.69, bf16[]{:T(256)} %broadcast.154), dimensions={1}, to_apply=%broadcast_in_dim.69.reduce_sub_computation | reduce | bytes 1441794 | tf_op jit(solution)/shard_map/broadcast_in_dim | solution.py:56
  196.7 28.1 %all_to_all.21 = bf16[128,2,1408]{2,1,0:T(2,128)(2,1)S(1)} all-to-all(bf16[128,2,1408]{2,1,0:T(2,128)(2,1)S(1)} %reshape.374), channel_id=1, replica_groups=mesh['dom'=128,'sub'=2] {'dom'}, dimensions={0} | all-to-all | bytes 1441792 | tf_op jit(solution)/shard_map/all_to_all | solution.py:57
  225.4 4.4 %reduce.3 = bf16[128,2816]{1,0:T(8,128)(2,1)S(1)} reduce(bf16[128,1,2816]{2,1,0:T(2,128)(2,1)S(1)} %reshape.375, bf16[]{:T(256)} %constant.110), dimensions={1}, to_apply=%all_to_all.16.reduce_sub_computation | reduce | bytes 1441794 | tf_op jit(solution)/shard_map/all_to_all | solution.py:57
  231.5 3.5 %collective-permute-start.1 = (bf16[360448]{0:T(1024)(128)(2,1)}, bf16[360448]{0:T(1024)(128)(2,1)}, u32[]{:S(2)}, u32[]{:S(2)}) collective-permute-start(bf16[360448]{0:T(1024)(128)(2,1)} %reshape.309), channel_id=1, source_target_pairs={{0,1},{1,0},{2,3},{3,2},{4,5},{5,4},{6,7},{7,6},{8,9},{9,8},{10,11... | collective-permute-start | bytes 2162696 | tf_op jit(solution)/shard_map/ppermute | solution.py:58
  236.1 13.7 %dynamic_update_slice.11 = bf16[2,360448]{1,0:T(2,128)(2,1)S(1)} dynamic-update-slice(bf16[2,360448]{1,0:T(2,128)(2,1)S(1)} %broadcast_in_dim.66, bf16[1,360448]{1,0:T(2,128)(2,1)S(1)} %bitcast.136, s32[]{:T(128)S(6)} %select_n.79, s32[]{:T(128)} %constant.92.clone.1) | dynamic-update-slice | bytes 1441796 | tf_op jit(solution)/shard_map/jit(dynamic_update_index_in_dim)/dynamic_update_slice | solution.py:60
  249.8 7.7 %broadcast_in_dim.71 = bf16[1,360448]{1,0:T(2,128)(2,1)S(1)} reshape(bf16[360448]{0:T(1024)(128)(2,1)} %collective-permute-done.1) | data formatting | bytes 1441792 | tf_op jit(solution)/shard_map/jit(dynamic_update_index_in_dim)/broadcast_in_dim | solution.py:61
  257.5 13.7 %dynamic_update_slice.12 = bf16[2,360448]{1,0:T(2,128)(2,1)S(1)} dynamic-update-slice(bf16[2,360448]{1,0:T(2,128)(2,1)S(1)} %dynamic_update_slice.11, bf16[1,360448]{1,0:T(2,128)(2,1)S(1)} %broadcast_in_dim.71, s32[]{:T(128)S(6)} %select_n.80, s32[]{:T(128)} %constant.92.clone.1) | dynamic-update-slice | bytes 1441796 | tf_op jit(solution)/shard_map/jit(dynamic_update_index_in_dim)/dynamic_update_slice | solution.py:61
  271.2 2.3 reshape.310
  274.6 3.0 %fusion.34 = (f32[512,512]{1,0:T(8,128)}, f32[512,512]{1,0:T(8,128)}) fusion(f32[1408,512]{1,0:T(8,128)} %reshape.310), kind=kLoop, calls=%fused_computation.83 | loop fusion | bytes 4194304 | tf_op jit(solution)/shard_map/slice | solution.py:66
  279.2 2.2 convert_element_type.78
  281.4 2.7 convert_element_type.77
  (96 shorter events, 32.4 us)
Async XLA Ops:
  0.6 71.8 %copy-start = (bf16[512,512]{1,0:T(8,128)(2,1)S(1)}, bf16[512,512]{1,0:T(8,128)(2,1)}, u32[]{:S(2)}) copy-start(bf16[512,512]{1,0:T(8,128)(2,1)} %param.24) | copy-start | bytes 1572868
  1.5 4.7 %copy-start.12 = (s32[1,1,128]{2,1,0:T(1,128)S(1)}, s32[1,1,128]{2,1,0:T(1,128)}, u32[]{:S(2)}) copy-start(s32[1,1,128]{2,1,0:T(1,128)} %param.29) | copy-start | bytes 1540
  2.4 3.9 %copy-start.10 = (s32[256,4]{0,1:T(4,128)S(1)}, s32[256,4]{0,1:T(4,128)}, u32[]{:S(2)}) copy-start(s32[256,4]{0,1:T(4,128)} %param.19) | copy-start | bytes 12292
  5.3 18.9 %copy-start.11 = (s32[2]{0:T(128)S(1)}, s32[2]{0:T(128)}, u32[]{:S(2)}) copy-start(s32[2]{0:T(128)} %param.30) | copy-start | bytes 28
  5.3 22.1 %copy-start.13 = (s32[16]{0:T(128)S(1)}, s32[16]{0:T(128)}, u32[]{:S(2)}) copy-start(s32[16]{0:T(128)} %param.26) | copy-start | bytes 196
  5.3 22.2 %copy-start.14 = (s32[16]{0:T(128)S(1)}, s32[16]{0:T(128)}, u32[]{:S(2)}) copy-start(s32[16]{0:T(128)} %param.27) | copy-start | bytes 196
  5.3 22.2 %copy-start.7 = (bf16[16,128,128]{2,1,0:T(8,128)(2,1)S(1)}, bf16[16,128,128]{2,1,0:T(8,128)(2,1)}, u32[]{:S(2)}) copy-start(bf16[16,128,128]{2,1,0:T(8,128)(2,1)} %param.25) | copy-start | bytes 1572868
  5.3 23.8 %copy-start.9 = (bf16[2,256,128]{2,1,0:T(8,128)(2,1)S(1)}, bf16[2,256,128]{2,1,0:T(8,128)(2,1)}, u32[]{:S(2)}) copy-start(bf16[2,256,128]{2,1,0:T(8,128)(2,1)} %param.20) | copy-start | bytes 393220
  6.2 26.2 %copy-start.6 = (f32[512,64]{0,1:T(8,128)S(1)}, f32[512,64]{0,1:T(8,128)}, u32[]{:S(2)}) copy-start(f32[512,64]{0,1:T(8,128)} %param.21) | copy-start | bytes 393220
  6.2 26.2 %copy-start.8 = (f32[64,512]{1,0:T(8,128)S(1)}, f32[64,512]{1,0:T(8,128)}, u32[]{:S(2)}) copy-start(f32[64,512]{1,0:T(8,128)} %param.22) | copy-start | bytes 393220
  7.8 41.0 %all-to-all-start = ((s32[128,264,4]{1,2,0:T(4,128)}), s32[128,264,4]{1,2,0:T(4,128)S(1)}, u32[]{:S(2)}, u32[]{:S(2)}) async-start(s32[128,264,4]{1,2,0:T(4,128)} %pad_add_fusion), calls=%async_computation | async-start | bytes 1572864 | tf_op jit(solution)/shard_map/all_to_all | solution.py:100
  59.2 11.9 %copy-start.4 = (bf16[512,512]{1,0:T(8,128)(2,1)S(1)}, bf16[512,512]{1,0:T(8,128)(2,1)}, u32[]{:S(2)}) copy-start(bf16[512,512]{1,0:T(8,128)(2,1)} %param.23) | copy-start | bytes 1572868
  71.1 4.4 %copy-start.5 = (bf16[2,128,512]{2,1,0:T(8,128)(2,1)S(1)}, bf16[2,128,512]{2,1,0:T(8,128)(2,1)}, u32[]{:S(2)}) copy-start(bf16[2,128,512]{2,1,0:T(8,128)(2,1)} %get-tuple-element.103) | copy-start | bytes 786436
  120.9 4.7 %copy-start.3 = (f32[1792,512]{0,1:T(8,128)S(1)}, f32[1792,512]{0,1:T(8,128)}, u32[]{:S(2)}) copy-start(f32[1792,512]{0,1:T(8,128)} %copy.107) | copy-start | bytes 11010052
  125.6 1.5 copy-start.2
  127.1 1.4 copy-start.1
  138.3 5.6 %collective-permute-start = (f32[360448]{0:T(1024)S(1)}, f32[360448]{0:T(1024)S(1)}, u32[]{:S(2)}, u32[]{:S(2)}) collective-permute-start(f32[360448]{0:T(1024)S(1)} %bitcast.149), channel_id=1, source_target_pairs={{0,1},{1,0},{2,3},{3,2},{4,5},{5,4},{6,7},{7,6},{8,9},{9,8},{10,11... | collective-permute-start | bytes 4325384 | tf_op jit(solution)/shard_map/ppermute | solution.py:52
  231.5 18.3 %collective-permute-start.1 = (bf16[360448]{0:T(1024)(128)(2,1)}, bf16[360448]{0:T(1024)(128)(2,1)}, u32[]{:S(2)}, u32[]{:S(2)}) collective-permute-start(bf16[360448]{0:T(1024)(128)(2,1)} %reshape.309), channel_id=1, source_target_pairs={{0,1},{1,0},{2,3},{3,2},{4,5},{5,4},{6,7},{7,6},{8,9},{9,8},{10,11... | collective-permute-start | bytes 2162696 | tf_op jit(solution)/shard_map/ppermute | solution.py:58
  281.4 4.4 %slice-start = ((bf16[22,256,128]{2,1,0:T(8,128)(2,1)}), bf16[4,256,128]{2,1,0:T(8,128)(2,1)S(1)}, s32[]{:S(2)}) async-start(bf16[22,256,128]{2,1,0:T(8,128)(2,1)} %convert_element_type.78), calls=%async_computation.3 | async-start | bytes 524288 | tf_op jit(solution)/shard_map/slice | solution.py:66

commit v3 on v2

--- a/solution.py
+++ b/solution.py
@@ -39,33 +39,39 @@
     return upper_half_sum + lower_half_sum
 
 
-def all_sum(parts, n_dom):
-    flat = jnp.concatenate([p.reshape(-1) for p in parts])
-    size = flat.shape[0]
-    unit = 2 * n_dom
-    padded = -(-size // unit) * unit
-    halves = jnp.pad(flat, (0, padded - size)).reshape(2, -1)
+def all_sum(grad_w_msg, grad_w_self, part_alpha, part_basis, book_grad, n_dom):
     sub_index = lax.axis_index("sub")
-    keep = lax.dynamic_index_in_dim(halves, sub_index, 0, keepdims=False)
-    give = lax.dynamic_index_in_dim(halves, 1 - sub_index, 0, keepdims=False)
+    width = grad_w_msg.shape[1]
+    share = book_grad.shape[0] // 2
+    dense = [grad_w_msg, grad_w_self, part_basis, part_alpha.reshape(-1, width)]
+
+    def half_of(h):
+        pieces = [lax.dynamic_slice_in_dim(x, h * (x.shape[0] // 2), x.shape[0] // 2, 0) for x in dense]
+        pieces.append(lax.dynamic_slice_in_dim(book_grad, h * share, share, 0).reshape(-1, width))
+        return jnp.concatenate(pieces, axis=0)
+
     swap = [(0, 1), (1, 0)]
-    mine = keep + lax.ppermute(give, "sub", swap)
-    chunks = mine.reshape(n_dom, -1)
+    mine = half_of(sub_index) + lax.ppermute(half_of(1 - sub_index), "sub", swap)
+    rows = mine.shape[0]
+    chunks = mine.reshape(n_dom, -1, 128)
     received = lax.all_to_all(chunks, "dom", 0, 0, tiled=True)
     reduced = jnp.sum(received, axis=0).astype(jnp.bfloat16)
     spread = jnp.broadcast_to(reduced[None], chunks.shape)
-    own_half = lax.all_to_all(spread, "dom", 0, 0, tiled=True).reshape(-1)
-    other_half = lax.ppermute(own_half, "sub", swap)
-    both = jnp.zeros(halves.shape, jnp.bfloat16)
-    both = lax.dynamic_update_index_in_dim(both, own_half, sub_index, 0)
-    both = lax.dynamic_update_index_in_dim(both, other_half, 1 - sub_index, 0)
-    total = both.reshape(-1)[:size].astype(jnp.float32)
+    own_half = lax.all_to_all(spread, "dom", 0, 0, tiled=True).reshape(rows, width)
+    dense_rows = rows - share * book_grad.shape[1] * book_grad.shape[2] // width
+    own_dense = own_half[:dense_rows]
+    other_dense = lax.ppermute(own_dense, "sub", swap)
+    low = jnp.where(sub_index == 0, own_dense, other_dense).astype(jnp.float32)
+    high = jnp.where(sub_index == 0, other_dense, own_dense).astype(jnp.float32)
     out = []
     start = 0
-    for p in parts:
-        out.append(total[start : start + p.size].reshape(p.shape))
-        start += p.size
-    return out
+    for x in dense:
+        r = x.shape[0] // 2
+        out.append(jnp.concatenate([low[start : start + r], high[start : start + r]], axis=0))
+        start += r
+    out[3] = out[3].reshape(part_alpha.shape)
+    books_mine = own_half[dense_rows:].astype(jnp.float32).reshape((share,) + book_grad.shape[1:])
+    return out + [books_mine]
 
 
 def shards(
@@ -94,12 +100,20 @@
     targets = send_rows[0, 0]
     part_count = targets.shape[0]
     slot_valid = jnp.arange(SLOT, dtype=jnp.int32)[None, :] < send_count[0, 0][:, None]
-    out_codes = jnp.where(slot_valid[:, :, None], codes[targets], -1)
-    own_codes = jnp.broadcast_to(codes[None], (part_count,) + codes.shape)
-    payload = jnp.concatenate([out_codes, own_codes], axis=1)
-    incoming = lax.all_to_all(payload, "dom", 0, 0, tiled=True)
-    recv_codes = incoming[:, :SLOT].reshape(-1, book_count)
-    hub_codes = [incoming[hub_owner[hub_index], SLOT:] for hub_index in range(NHUB)]
+    out_codes = jnp.where(slot_valid[:, :, None], codes[targets], -1).reshape(part_count, -1)
+    own_codes = jnp.broadcast_to(codes.reshape(1, -1), (part_count, codes.size))
+    lane_rows = 8
+    room = -(-(codes.size + out_codes.shape[1]) // (lane_rows * 128)) * lane_rows * 128
+    filler = jnp.zeros((part_count, room - codes.size - out_codes.shape[1]), jnp.int32)
+    payload = jnp.concatenate([own_codes, out_codes, filler], axis=1)
+    incoming = lax.all_to_all(
+        payload.reshape(part_count, lane_rows, -1), "dom", 0, 0, tiled=True
+    ).reshape(part_count, -1)
+    recv_codes = incoming[:, codes.size : codes.size + out_codes.shape[1]].reshape(-1, book_count)
+    hub_codes = [
+        incoming[hub_owner[hub_index], : codes.size].reshape(codes.shape)
+        for hub_index in range(NHUB)
+    ]
     table_codes = jnp.concatenate([codes, recv_codes] + hub_codes, axis=0)
     table = decode(table_codes, complete_codebooks)
     local_rows = table[:rows_dev]
@@ -167,12 +181,8 @@
     part_basis = jnp.dot(
         alpha.T, rel_grad, precision=HIGHEST_PREC, preferred_element_type=jnp.float32
     )
-    total_msg, total_self, grad_alpha, grad_basis, total_books = all_sum(
-        (grad_w_msg, grad_w_self, part_alpha, part_basis, book_grad), n_dom
-    )
-    book_share = books.shape[0]
-    grad_books = lax.dynamic_slice_in_dim(
-        total_books, lax.axis_index("sub") * book_share, book_share, 0
+    total_msg, total_self, grad_basis, grad_alpha, grad_books = all_sum(
+        grad_w_msg, grad_w_self, part_alpha, part_basis, book_grad, n_dom
     )
     return (output, total_msg, total_self, grad_alpha, grad_basis, grad_books)
 

time: 291 us -> 237 us (0.81); the launches traced: 287 us -> 236 us
  local copies, waits for them, and re-layouts: 105 us -> 54.7 us
  other arithmetic: 28.7 us -> 19.8 us
  waiting for transfers between devices: 17.4 us -> 23.9 us
  blocking collectives: 76.5 us -> 80.4 us
    dynamic_update_slice x2 -> x0, local copies, waits for them, and re-layouts: 27.4 us -> none  [the longest x1 13.7 us: all_sum(): both = lax.dynamic_update_index_in_dim(both, other_half, 1 - sub_index, 0)]
    broadcast_in_dim x3, local copies, waits for them, and re-layouts: 8.83 us -> 0.21 us  [the longest x2 0.17 us: shards(): own_codes = jnp.broadcast_to(codes.reshape(1, -1), (part_count, codes.size))]
    convert_element_type x3 -> x0, local copies, waits for them, and re-layouts: 7.26 us -> none  [all_sum(): total = both.reshape(-1)[:size].astype(jnp.float32)]
    all_to_all x1, waiting for transfers between devices: 14.5 us -> 20.7 us  [shards(): lax.all_to_all(payload.reshape(part_count, lane_rows, -1), 'dom', 0, 0, t...]
    broadcast_in_dim x1 -> x0, other arithmetic: 5 us -> none  [all_sum(): spread = jnp.broadcast_to(reduced[None], chunks.shape)]
    slice x6 -> x4, local copies, waits for them, and re-layouts: 4.66 us -> 0.26 us  [the longest x2 0.21 us: all_sum(): low[start:start + r]]
    all_to_all x1 -> x0, other arithmetic: 4.36 us -> none  [all_sum(): own_half = lax.all_to_all(spread, 'dom', 0, 0, tiled=True).reshape(-1)]
    all_to_all x1, blocking collectives: 45.2 us -> 48.8 us  [all_sum(): received = lax.all_to_all(chunks, 'dom', 0, 0, tiled=True)]
  transfers between devices with their start and end apart: 3 -> 3, of which waited for: 2 -> 3; matrix products, arithmetic and copies ran while one was open for 6% -> 2% of each run, Pallas kernels for 0% -> 0%
where the time goes in v3:
time: 237 us; the launch traced here: 236 us
  blocking collectives  80.4 us (34%)
  local copies, waits for them, and re-layouts  54.7 us (23%)
  matrix products  29.2 us (12%)
  waiting for transfers between devices  23.9 us (10%)
  starting transfers between devices  23 us (10%)
  other arithmetic  19.8 us (8%)
  between operations  4.93 us (2%)
    all_to_all x1, blocking collectives, all_sum(): received = lax.all_to_all(chunks, 'dom', 0, 0, tiled=True)  48.8 us
    all_to_all x1, blocking collectives, all_sum(): lax.all_to_all(spread, 'dom', 0, 0, tiled=True).reshape(rows, width)  29 us
    all_to_all x1, waiting for transfers between devices, shards(): lax.all_to_all(payload.reshape(part_count, lane_rows, -1), 'dom', 0, 0, t...  20.7 us
    all_to_all x1, starting transfers between devices, shards(): lax.all_to_all(payload.reshape(part_count, lane_rows, -1), 'dom', 0, 0, t...  16.5 us
    scatter-add x2, other arithmetic, backward_block(): table_grad.at[source_now]  8.58 us
    unnamed x47, local copies, waits for them, and re-layouts  7.69 us
    gather x2, local copies, waits for them, and re-layouts, backward_block(): blocks[source_now].astype(jnp.float32)  6.33 us
    another operation x2, local copies, waits for them, and re-layouts, shards(): blocks = table.reshape(-1, TB, model_width)  6.09 us
  transfers between devices with their start and end apart: 3, of which 3 were waited for; matrix products, arithmetic and copies ran while one was open for 2% of the time, Pallas kernels for 0%

profile of v3, /device:TPU:1, one launch (start us, length us, event | category | flops | bytes accessed | tf_op | source)
XLA Modules:
  0.0 236.0 jit_solution(6587199185603454161)
XLA Ops:
  2.6 2.8 %gather_fusion.4 = s32[1024,4]{1,0:T(8,128)S(1)} fusion(s32[256,4]{1,0:T(8,128)S(1)} %copy.63, s32[1024]{0:T(1024)S(1)} %broadcast_clamp_fusion), kind=kCustom, calls=%fused_computation.4 | custom fusion | bytes 36864 | tf_op jit(solution)/shard_map/gather | solution.py:103
  6.4 1.3 copy.87
  7.7 16.5 %all-to-all-start = ((s32[128,8,256]{2,1,0:T(8,128)}), s32[128,8,256]{2,1,0:T(8,128)S(1)}, u32[]{:S(2)}, u32[]{:S(2)}) async-start(s32[128,8,256]{2,1,0:T(8,128)} %bitcast.33), calls=%async_computation | async-start | bytes 2097152 | tf_op jit(solution)/shard_map/all_to_all | solution.py:109
  29.1 2.6 %all_gather.3 = bf16[4,256,128]{2,1,0:T(8,128)(2,1)S(1)} all-gather(bf16[2,256,128]{2,1,0:T(8,128)(2,1)S(1)} %copy-done.13), channel_id=1, replica_groups=mesh['dom'=128,'sub'=2] {'sub'}, dimensions={0}, use_global_device_ids=true | all-gather | bytes 393216 | tf_op jit(solution)/shard_map/all_gather | solution.py:98
  31.7 2.0 fusion.39
  33.7 20.7 %all-to-all-done = s32[128,8,256]{2,1,0:T(8,128)S(1)} async-done(((s32[128,8,256]{2,1,0:T(8,128)}), s32[128,8,256]{2,1,0:T(8,128)S(1)}, u32[]{:S(2)}, u32[]{:S(2)}) %all-to-all-start) | async-done | bytes 1048608 | tf_op jit(solution)/shard_map/all_to_all | solution.py:109
  56.3 2.9 %fusion.28 = bf16[1792,4,128]{0,2,1:T(8,128)(2,1)} fusion(bf16[4,256,128]{2,1,0:T(8,128)(2,1)S(1)} %all_gather.3, s32[1792,4]{0,1:T(4,128)S(1)} %pad_add_fusion), kind=kOutput, calls=%fused_computation.53 | convolution fusion | flops 472514560 | bytes 2125824 | tf_op jit(solution)/shard_map/feu,euq->feq/dot_general | solution.py:21
  59.2 3.2 %reshape.354 = bf16[14,128,512]{1,0,2:T(8,128)(2,1)S(1)} reshape(bf16[1792,4,128]{0,2,1:T(8,128)(2,1)} %fusion.28) | data formatting | bytes 3670016 | tf_op jit(solution)/shard_map/reshape;reshape | solution.py:120
  63.3 2.9 %copy.86 = bf16[14,128,512]{2,1,0:T(8,128)(2,1)} copy(bf16[14,128,512]{1,0,2:T(8,128)(2,1)S(1)} %reshape.354) | data formatting | bytes 3670016 | tf_op jit(solution)/shard_map/reshape;reshape | solution.py:120
  66.2 12.1 %while.23 = (s32[]{:T(128)}, bf16[2,128,512]{2,1,0:T(8,128)(2,1)}, bf16[2,8,128,128]{3,2,1,0:T(8,128)(2,1)}, s32[2,8]{1,0:T(2,128)S(1)}, bf16[14,128,512]{2,1,0:...) while((s32[]{:T(128)}, bf16[2,128,512]{2,1,0:T(8,128)(2,1)}, ...), condition=%wide.region_1.2_spmd, body=%wide.region_0.1_spmd.sunk | while | flops 135858224 | bytes 5694865 | solution.py:135
  66.3 2.2 gather_fusion
  68.5 1.8 gather_fusion.1
  70.3 1.3 fusion.70
  72.3 2.2 gather_fusion
  74.5 1.8 gather_fusion.1
  76.3 1.3 fusion.70
  78.3 1.2 fusion.40
  79.6 2.1 multiply_convert_fusion.2
  82.7 1.3 fusion.41
  84.0 1.3 fusion.42
  85.3 2.3 broadcast_in_dim.62
  87.6 1.1 broadcast_in_dim.63
  88.7 27.7 %while.24 = (s32[]{:T(128)}, f32[14,128,512]{2,1,0:T(8,128)}, f32[512,512]{1,0:T(8,128)}, s32[2,8]{1,0:T(2,128)S(1)}, bf16[2,8,128,128]{2,3,1,0:T(8,128)(2,1)S(1...) while((s32[]{:T(128)}, f32[14,128,512]{2,1,0:T(8,128)}, ...), condition=%wide.region_6.7_spmd, body=%wide.region_2.6_spmd.sunk | while | flops 136841264 | bytes 12051881 | solution.py:171
  88.7 3.2 %gather_fusion.2 = bf16[8,128,512]{2,1,0:T(8,128)(2,1)} fusion(bf16[14,128,512]{2,1,0:T(8,128)(2,1)} %get-tuple-element.392, s32[1024]{0:T(1024)S(1)} %pad_clamp_fusion.10), kind=kCustom, calls=%fused_computation.3.clone.1 | custom fusion | bytes 2097184 | tf_op jit(solution)/shard_map/while/body/eval_jaxpr/gather | solution.py:165
  91.9 1.8 gather_fusion.3
  93.7 1.8 multiply_reduce_fusion.2
  95.5 4.3 %scatter_fusion = f32[14,128,512]{2,1,0:T(8,128)} fusion(f32[14,128,512]{2,1,0:T(8,128)} %get-tuple-element.375, s32[8]{0:T(128)S(1)} %get-tuple-element.336, f32[8,128,512]{2,1,0:T(8,128)S(1)} %get-tuple-element.338), kind=kCustom, calls=%fused_computation.5.clone.1 | custom fusion | flops 524288 | bytes 6291488 | tf_op jit(solution)/shard_map/while/body/eval_jaxpr/scatter-add | solution.py:167
  99.8 2.8 %scatter_fusion.1 = f32[512,512]{1,0:T(8,128)} fusion(f32[512,512]{1,0:T(8,128)} %get-tuple-element.376, s32[8]{0:T(128)S(1)} %get-tuple-element.337, f32[8,512]{1,0:T(8,128)S(1)} %get-tuple-element.339), kind=kCustom, calls=%fused_computation.6.clone.1 | custom fusion | flops 4096 | bytes 49184 | tf_op jit(solution)/shard_map/while/body/eval_jaxpr/scatter-add | solution.py:164
  102.6 3.2 %gather_fusion.2 = bf16[8,128,512]{2,1,0:T(8,128)(2,1)} fusion(bf16[14,128,512]{2,1,0:T(8,128)(2,1)} %get-tuple-element.392, s32[1024]{0:T(1024)S(1)} %pad_clamp_fusion.10), kind=kCustom, calls=%fused_computation.3.clone.1 | custom fusion | bytes 2097184 | tf_op jit(solution)/shard_map/while/body/eval_jaxpr/gather | solution.py:165
  105.8 1.8 gather_fusion.3
  107.6 1.8 multiply_reduce_fusion.2
  109.3 4.3 %scatter_fusion = f32[14,128,512]{2,1,0:T(8,128)} fusion(f32[14,128,512]{2,1,0:T(8,128)} %get-tuple-element.375, s32[8]{0:T(128)S(1)} %get-tuple-element.336, f32[8,128,512]{2,1,0:T(8,128)S(1)} %get-tuple-element.338), kind=kCustom, calls=%fused_computation.5.clone.1 | custom fusion | flops 524288 | bytes 6291488 | tf_op jit(solution)/shard_map/while/body/eval_jaxpr/scatter-add | solution.py:167
  113.6 2.8 %scatter_fusion.1 = f32[512,512]{1,0:T(8,128)} fusion(f32[512,512]{1,0:T(8,128)} %get-tuple-element.376, s32[8]{0:T(128)S(1)} %get-tuple-element.337, f32[8,512]{1,0:T(8,128)S(1)} %get-tuple-element.339), kind=kCustom, calls=%fused_computation.6.clone.1 | custom fusion | flops 4096 | bytes 49184 | tf_op jit(solution)/shard_map/while/body/eval_jaxpr/scatter-add | solution.py:164
  116.4 2.1 fusion.43
  118.5 1.9 fusion.44
  120.4 1.1 slice.70
  121.5 1.1 fusion.30
  122.6 5.2 %copy.76 = f32[1792,512]{0,1:T(8,128)} copy(f32[1792,512]{1,0:T(8,128)} %fusion.30) | data formatting | bytes 7340032 | tf_op jit(solution)/shard_map/scatter-add | solution.py:176
  127.8 4.7 %fusion.21 = f32[4,256,128]{2,1,0:T(8,128)S(1)} fusion(s32[1792,4]{0,1:T(4,128)S(1)} %copy-done.15, f32[1792,4,128]{0,2,1:T(8,128)} %bitcast.127), kind=kOutput, calls=%fused_computation.45 | convolution fusion | flops 475267072 | bytes 4222976 | tf_op jit(solution)/shard_map/fco,fcg->cog/dot_general | solution.py:36
  132.5 1.5 fusion.29
  135.9 1.1 dynamic-slice_dynamic-update-slice_fusion
  139.0 2.7 %collective-permute-start = (f32[704,512]{1,0:T(8,128)}, f32[704,512]{1,0:T(8,128)S(1)}, u32[]{:S(2)}, u32[]{:S(2)}) collective-permute-start(f32[704,512]{1,0:T(8,128)} %constant_dynamic-update-slice_fusion.1), channel_id=1, source_target_pairs={{0,1},{1,0},{2,3},{3,2},{4,5},{5,4},{6,7},{7,6},{8,9},{9,8},{10,11... | collective-permute-start | bytes 4325384 | tf_op jit(solution)/shard_map/ppermute | solution.py:54
  142.5 2.3 collective-permute-done
  144.8 1.7 add.122
  146.4 1.4 reshape.288
  147.8 48.8 %all_to_all.15 = f32[128,22,128]{2,1,0:T(8,128)S(1)} all-to-all(f32[128,22,128]{2,1,0:T(8,128)} %reshape.288), channel_id=1, replica_groups=mesh['dom'=128,'sub'=2] {'dom'}, dimensions={0} | all-to-all | bytes 2883584 | tf_op jit(solution)/shard_map/all_to_all | solution.py:57
  196.9 29.0 %all_to_all.16 = bf16[128,22,128]{2,1,0:T(8,128)(2,1)S(1)} all-to-all(bf16[128,22,128]{2,1,0:T(8,128)(2,1)S(1)} %broadcast_in_dim.64), channel_id=1, replica_groups=mesh['dom'=128,'sub'=2] {'dom'}, dimensions={0} | all-to-all | bytes 1441792 | tf_op jit(solution)/shard_map/all_to_all | solution.py:60
  226.5 3.9 %collective-permute-start.1 = (bf16[576,512]{1,0:T(8,128)(2,1)S(1)}, bf16[576,512]{1,0:T(8,128)(2,1)S(1)}, u32[]{:S(2)}, u32[]{:S(2)}) collective-permute-start(bf16[576,512]{1,0:T(8,128)(2,1)S(1)} %slice.93), channel_id=1, source_target_pairs={{0,1},{1,0},{2,3},{3,2},{4,5},{5,4},{6,7},{7,6},{8,9},{9,8},{10,11... | collective-permute-start | bytes 1769480 | tf_op jit(solution)/shard_map/ppermute | solution.py:63
  (113 shorter events, 20.3 us)
Async XLA Ops:
  0.6 79.0 %copy-start = (bf16[512,512]{1,0:T(8,128)(2,1)S(1)}, bf16[512,512]{1,0:T(8,128)(2,1)}, u32[]{:S(2)}) copy-start(bf16[512,512]{1,0:T(8,128)(2,1)} %param.24) | copy-start | bytes 1572868
  2.5 3.0 %copy-start.18 = (s32[1,1,128]{2,1,0:T(1,128)S(1)}, s32[1,1,128]{2,1,0:T(1,128)}, u32[]{:S(2)}) copy-start(s32[1,1,128]{2,1,0:T(1,128)} %param.29) | copy-start | bytes 1540
  6.3 17.8 %copy-start.17 = (s32[2]{0:T(128)S(1)}, s32[2]{0:T(128)}, u32[]{:S(2)}) copy-start(s32[2]{0:T(128)} %param.30) | copy-start | bytes 28
  6.3 21.0 %copy-start.19 = (s32[16]{0:T(128)S(1)}, s32[16]{0:T(128)}, u32[]{:S(2)}) copy-start(s32[16]{0:T(128)} %param.26) | copy-start | bytes 196
  6.3 21.1 %copy-start.20 = (s32[16]{0:T(128)S(1)}, s32[16]{0:T(128)}, u32[]{:S(2)}) copy-start(s32[16]{0:T(128)} %param.27) | copy-start | bytes 196
  6.3 21.2 %copy-start.11 = (bf16[16,128,128]{2,1,0:T(8,128)(2,1)S(1)}, bf16[16,128,128]{2,1,0:T(8,128)(2,1)}, u32[]{:S(2)}) copy-start(bf16[16,128,128]{2,1,0:T(8,128)(2,1)} %param.25) | copy-start | bytes 1572868
  7.7 21.5 %copy-start.13 = (bf16[2,256,128]{2,1,0:T(8,128)(2,1)S(1)}, bf16[2,256,128]{2,1,0:T(8,128)(2,1)}, u32[]{:S(2)}) copy-start(bf16[2,256,128]{2,1,0:T(8,128)(2,1)} %param.20) | copy-start | bytes 393220
  7.7 24.1 %copy-start.10 = (f32[512,64]{0,1:T(8,128)S(1)}, f32[512,64]{0,1:T(8,128)}, u32[]{:S(2)}) copy-start(f32[512,64]{0,1:T(8,128)} %param.21) | copy-start | bytes 393220
  7.7 24.1 %copy-start.12 = (f32[64,512]{1,0:T(8,128)S(1)}, f32[64,512]{1,0:T(8,128)}, u32[]{:S(2)}) copy-start(f32[64,512]{1,0:T(8,128)} %param.22) | copy-start | bytes 393220
  7.7 46.7 %all-to-all-start = ((s32[128,8,256]{2,1,0:T(8,128)}), s32[128,8,256]{2,1,0:T(8,128)S(1)}, u32[]{:S(2)}, u32[]{:S(2)}) async-start(s32[128,8,256]{2,1,0:T(8,128)} %bitcast.33), calls=%async_computation | async-start | bytes 2097152 | tf_op jit(solution)/shard_map/all_to_all | solution.py:109
  54.4 1.2 copy-start.16
  55.6 0.6 copy-start.14
  66.2 12.1 %copy-start.5 = (bf16[512,512]{1,0:T(8,128)(2,1)S(1)}, bf16[512,512]{1,0:T(8,128)(2,1)}, u32[]{:S(2)}) copy-start(bf16[512,512]{1,0:T(8,128)(2,1)} %param.23) | copy-start | bytes 1572868
  66.2 4.0 %copy-start.7 = (bf16[2,128,512]{2,1,0:T(8,128)(2,1)S(1)}, bf16[2,128,512]{2,1,0:T(8,128)(2,1)}, u32[]{:S(2)}) copy-start(bf16[2,128,512]{2,1,0:T(8,128)(2,1)} %get-tuple-element.349) | copy-start | bytes 786436 | tf_op jit(solution)/shard_map/while
  71.6 0.7 copy-start.8
  72.3 4.0 %copy-start.7 = (bf16[2,128,512]{2,1,0:T(8,128)(2,1)S(1)}, bf16[2,128,512]{2,1,0:T(8,128)(2,1)}, u32[]{:S(2)}) copy-start(bf16[2,128,512]{2,1,0:T(8,128)(2,1)} %get-tuple-element.349) | copy-start | bytes 786436 | tf_op jit(solution)/shard_map/while
  77.6 0.7 copy-start.8
  79.6 3.1 %copy-start.9 = (bf16[2,128,512]{2,1,0:T(8,128)(2,1)S(1)}, bf16[2,128,512]{2,1,0:T(8,128)(2,1)}, u32[]{:S(2)}) copy-start(bf16[2,128,512]{2,1,0:T(8,128)(2,1)} %get-tuple-element.103) | copy-start | bytes 786436
  116.4 2.1 copy-start.1
  122.6 5.2 %copy-start.15 = (s32[1792,4]{0,1:T(4,128)S(1)}, s32[1792,4]{0,1:T(4,128)}, u32[]{:S(2)}) copy-start(s32[1792,4]{0,1:T(4,128)} %copy-done.14) | copy-start | bytes 86020
  127.8 4.7 %copy-start.4 = (f32[1792,512]{0,1:T(8,128)S(1)}, f32[1792,512]{0,1:T(8,128)}, u32[]{:S(2)}) copy-start(f32[1792,512]{0,1:T(8,128)} %copy.76) | copy-start | bytes 11010052
  132.5 2.4 %copy-start.3 = (f32[512,512]{1,0:T(8,128)S(1)}, f32[512,512]{1,0:T(8,128)}, u32[]{:S(2)}) copy-start(f32[512,512]{1,0:T(8,128)} %fusion.41) | copy-start | bytes 3145732
  134.0 2.0 copy-start.2
  135.9 5.8 %copy-start.6 = (f32[2,256,128]{2,1,0:T(8,128)S(1)}, f32[2,256,128]{2,1,0:T(8,128)}, u32[]{:S(2)}) copy-start(f32[2,256,128]{2,1,0:T(8,128)} %get-tuple-element.216) | copy-start | bytes 786436
  139.0 5.7 %collective-permute-start = (f32[704,512]{1,0:T(8,128)}, f32[704,512]{1,0:T(8,128)S(1)}, u32[]{:S(2)}, u32[]{:S(2)}) collective-permute-start(f32[704,512]{1,0:T(8,128)} %constant_dynamic-update-slice_fusion.1), channel_id=1, source_target_pairs={{0,1},{1,0},{2,3},{3,2},{4,5},{5,4},{6,7},{7,6},{8,9},{9,8},{10,11... | collective-permute-start | bytes 4325384 | tf_op jit(solution)/shard_map/ppermute | solution.py:54
  226.5 5.5 %collective-permute-start.1 = (bf16[576,512]{1,0:T(8,128)(2,1)S(1)}, bf16[576,512]{1,0:T(8,128)(2,1)S(1)}, u32[]{:S(2)}, u32[]{:S(2)}) collective-permute-start(bf16[576,512]{1,0:T(8,128)(2,1)S(1)} %slice.93), channel_id=1, source_target_pairs={{0,1},{1,0},{2,3},{3,2},{4,5},{5,4},{6,7},{7,6},{8,9},{9,8},{10,11... | collective-permute-start | bytes 1769480 | tf_op jit(solution)/shard_map/ppermute | solution.py:63

commit v4 on v3

--- a/solution.py
+++ b/solution.py
@@ -53,9 +53,9 @@
     swap = [(0, 1), (1, 0)]
     mine = half_of(sub_index) + lax.ppermute(half_of(1 - sub_index), "sub", swap)
     rows = mine.shape[0]
-    chunks = mine.reshape(n_dom, -1, 128)
+    chunks = mine.astype(jnp.bfloat16).reshape(n_dom, -1, 128)
     received = lax.all_to_all(chunks, "dom", 0, 0, tiled=True)
-    reduced = jnp.sum(received, axis=0).astype(jnp.bfloat16)
+    reduced = jnp.sum(received.astype(jnp.float32), axis=0).astype(jnp.bfloat16)
     spread = jnp.broadcast_to(reduced[None], chunks.shape)
     own_half = lax.all_to_all(spread, "dom", 0, 0, tiled=True).reshape(rows, width)
     dense_rows = rows - share * book_grad.shape[1] * book_grad.shape[2] // width
@@ -119,22 +119,15 @@
     local_rows = table[:rows_dev]
     blocks = table.reshape(-1, TB, model_width)
     tile_blocks = tiles.reshape(block_count, TPB, TB, TB)
-    source_blocks = tile_src.reshape(block_count, TPB)
-    relation_blocks = tile_rel.reshape(block_count, TPB)
-
-    def forward_block(packed):
-        weights_now, source_now, relation_now = packed
-        composed = (
-            blocks[source_now].astype(jnp.float32) * rel_table[relation_now][:, None, :]
-        ).astype(jnp.bfloat16)
-        summed = jnp.einsum(
-            "tij,tjd->id", weights_now, composed, preferred_element_type=jnp.float32
-        )
-        return summed.astype(jnp.bfloat16)
-
-    aggregate = lax.map(forward_block, (tile_blocks, source_blocks, relation_blocks)).reshape(
-        rows_dev, model_width
-    )
+    picked = blocks[tile_src]
+    scale = rel_table[tile_rel]
+    composed = (picked.astype(jnp.float32) * scale[:, None, :]).astype(jnp.bfloat16)
+    aggregate = jnp.einsum(
+        "btij,btjd->bid",
+        tile_blocks,
+        composed.reshape(block_count, TPB, TB, model_width),
+        preferred_element_type=jnp.float32,
+    ).astype(jnp.bfloat16).reshape(rows_dev, model_width)
     pre_act = jnp.dot(aggregate, w_msg, preferred_element_type=jnp.float32) + jnp.dot(
         local_rows, w_self, preferred_element_type=jnp.float32
     )
@@ -154,24 +147,14 @@
     ).astype(jnp.bfloat16)
     grad_self = lax.dot_general(grad_pre, w_self, contract_cols, preferred_element_type=jnp.float32)
     grad_blocks = grad_agg.reshape(block_count, TB, model_width)
-
-    def backward_block(carry, packed):
-        table_grad, rel_grad = carry
-        weights_now, source_now, relation_now, upstream = packed
-        grad_comp = jnp.einsum(
-            "tji,jd->tid", weights_now, upstream, preferred_element_type=jnp.float32
-        )
-        rel_grad = rel_grad.at[relation_now].add(
-            jnp.sum(grad_comp * blocks[source_now].astype(jnp.float32), axis=1)
-        )
-        table_grad = table_grad.at[source_now].add(grad_comp * rel_table[relation_now][:, None, :])
-        return ((table_grad, rel_grad), None)
-
-    start_carry = (jnp.zeros(blocks.shape, jnp.float32), jnp.zeros(rel_table.shape, jnp.float32))
-    final_carry = lax.scan(
-        backward_block, start_carry, (tile_blocks, source_blocks, relation_blocks, grad_blocks)
-    )[0]
-    table_grad, rel_grad = final_carry
+    grad_comp = jnp.einsum(
+        "btji,bjd->btid", tile_blocks, grad_blocks, preferred_element_type=jnp.float32
+    ).reshape(tile_count, TB, model_width)
+    rel_rows = jnp.sum(grad_comp * picked.astype(jnp.float32), axis=1)
+    rel_grad = jnp.zeros(rel_table.shape, jnp.float32).at[tile_rel].add(rel_rows)
+    table_grad = jnp.zeros(blocks.shape, jnp.float32).at[tile_src].add(
+        grad_comp * scale[:, None, :]
+    )
     table_grad = table_grad.reshape(-1, model_width)
     table_grad = table_grad.at[:rows_dev].add(grad_self)
     book_grad = fold_books(table_codes, table_grad, code_count)

time: 237 us -> 192 us (0.81)
  local copies, waits for them, and re-layouts: 54.7 us -> 35.6 us
  blocking collectives: 80.4 us -> 63.1 us
  matrix products: 29.2 us -> 20.7 us
    all_to_all x1, blocking collectives: 48.8 us -> 31 us  [all_sum(): received = lax.all_to_all(chunks, 'dom', 0, 0, tiled=True)]
    gather x8 -> x2, local copies, waits for them, and re-layouts: 17.8 us -> 2.58 us  [the longest x1 2.01 us: shards(): picked = blocks[tile_src]]
    mul x0 -> x1, other arithmetic: none -> 4.71 us  [shards(): grad_comp * scale[:, None, :]]
    dot_general x4 -> x1, matrix products: 6.15 us -> 2.22 us  [shards(): jnp.einsum('btij,btjd->bid', tile_blocks, composed.reshape(block_count, T...]
    scatter-add x4 -> x2, other arithmetic: 14.2 us -> 10.6 us  [the longest x1 9.47 us: shards(): jnp.zeros(blocks.shape, jnp.float32).at[tile_src]]
    unnamed x0 -> x1, matrix products: none -> 2.69 us
    unnamed x47 -> x50, local copies, waits for them, and re-layouts: 7.69 us -> 7.32 us
where the time goes in v4:
time: 192 us; the launch traced here: 191 us
  blocking collectives  63.1 us (33%)
  local copies, waits for them, and re-layouts  35.6 us (19%)
  waiting for transfers between devices  23.6 us (12%)
  starting transfers between devices  22.7 us (12%)
  other arithmetic  20.7 us (11%)
  matrix products  20.7 us (11%)
  between operations  5.06 us (3%)
    all_to_all x1, blocking collectives, all_sum(): received = lax.all_to_all(chunks, 'dom', 0, 0, tiled=True)  31 us
    all_to_all x1, blocking collectives, all_sum(): lax.all_to_all(spread, 'dom', 0, 0, tiled=True).reshape(rows, width)  29.5 us
    all_to_all x1, waiting for transfers between devices, shards(): lax.all_to_all(payload.reshape(part_count, lane_rows, -1), 'dom', 0, 0, t...  20.4 us
    all_to_all x1, starting transfers between devices, shards(): lax.all_to_all(payload.reshape(part_count, lane_rows, -1), 'dom', 0, 0, t...  16.5 us
    scatter-add x1, other arithmetic, shards(): jnp.zeros(blocks.shape, jnp.float32).at[tile_src]  9.47 us
    unnamed x50, local copies, waits for them, and re-layouts  7.32 us
    another operation x2, local copies, waits for them, and re-layouts, shards(): blocks = table.reshape(-1, TB, model_width)  5.8 us
    scatter-add x1, local copies, waits for them, and re-layouts, shards(): table_grad = table_grad.at[:rows_dev].add(grad_self)  5.18 us
  transfers between devices with their start and end apart: 3, of which 3 were waited for; matrix products, arithmetic and copies ran while one was open for 2% of the time, Pallas kernels for 0%

profile of v4, /device:TPU:1, one launch (start us, length us, event | category | flops | bytes accessed | tf_op | source)
XLA Modules:
  0.0 191.4 jit_solution(15972731730233046817)
XLA Ops:
  0.6 0.9 copy.58
  1.5 0.7 compare_select_fusion
  2.6 2.8 %gather_fusion = s32[1024,4]{1,0:T(8,128)S(1)} fusion(s32[256,4]{1,0:T(8,128)S(1)} %copy.58, s32[1024]{0:T(1024)S(1)} %broadcast_clamp_fusion), kind=kCustom, calls=%fused_computation | custom fusion | bytes 36864 | tf_op jit(solution)/shard_map/gather | solution.py:103
  6.3 1.3 copy.82
  7.7 16.5 %all-to-all-start = ((s32[128,8,256]{2,1,0:T(8,128)}), s32[128,8,256]{2,1,0:T(8,128)S(1)}, u32[]{:S(2)}, u32[]{:S(2)}) async-start(s32[128,8,256]{2,1,0:T(8,128)} %bitcast.34), calls=%async_computation | async-start | bytes 2097152 | tf_op jit(solution)/shard_map/all_to_all | solution.py:109
  24.2 0.6 fusion.31
  27.4 1.0 copy.69
  29.7 1.0 fusion.32
  31.4 2.6 %all_gather.3 = bf16[4,256,128]{2,1,0:T(8,128)(2,1)S(1)} all-gather(bf16[2,256,128]{2,1,0:T(8,128)(2,1)S(1)} %copy-done.13), channel_id=1, replica_groups=mesh['dom'=128,'sub'=2] {'sub'}, dimensions={0}, use_global_device_ids=true | all-gather | bytes 393216 | tf_op jit(solution)/shard_map/all_gather | solution.py:98
  34.0 20.4 %all-to-all-done = s32[128,8,256]{2,1,0:T(8,128)S(1)} async-done(((s32[128,8,256]{2,1,0:T(8,128)}), s32[128,8,256]{2,1,0:T(8,128)S(1)}, u32[]{:S(2)}, u32[]{:S(2)}) %all-to-all-start) | async-done | bytes 1048608 | tf_op jit(solution)/shard_map/all_to_all | solution.py:109
  55.6 1.7 fusion.9
  57.3 2.4 %reshape.233 = bf16[14,128,512]{1,0,2:T(8,128)(2,1)} reshape(bf16[1792,4,128]{0,2,1:T(8,128)(2,1)S(1)} %fusion.9) | data formatting | bytes 3670016 | tf_op jit(solution)/shard_map/reshape;reshape | solution.py:120
  59.7 3.4 %copy.81 = bf16[14,128,512]{2,1,0:T(8,128)(2,1)S(1)} copy(bf16[14,128,512]{1,0,2:T(8,128)(2,1)} %reshape.233) | data formatting | bytes 3670016 | tf_op jit(solution)/shard_map/reshape;reshape | solution.py:120
  63.2 2.0 %gather_fusion.1 = bf16[16,128,512]{2,1,0:T(8,128)(2,1)} fusion(bf16[14,128,512]{2,1,0:T(8,128)(2,1)S(1)} %copy.81, s32[1024]{0:T(1024)S(1)} %get-tuple-element.66), kind=kCustom, calls=%fused_computation.1 | custom fusion | bytes 4194368 | tf_op jit(solution)/shard_map/gather | solution.py:122
  65.2 2.2 %fusion.19 = bf16[2,512,128]{1,2,0:T(8,128)(2,1)S(1)} fusion(bf16[2,8,128,128]{3,2,1,0:T(8,128)(2,1)S(1)} %bitcast.91, bf16[2,8,128,512]{3,2,1,0:T(8,128)(2,1)} %bitcast.74, f32[2,8,512]{2,1,0:T(8,128)S(1)} %bitcast.92), kind=kOutput, calls=%fused_computation.29 | convolution fusion | flops 271712256 | bytes 2916352 | tf_op jit(solution)/shard_map/btij,btjd->bid/dot_general | solution.py:125
  67.7 1.1 multiply_convert_fusion
  69.2 1.3 fusion.34
  71.2 2.7 %fusion.4 = (f32[2,8,512]{2,1,0:T(8,128)S(1)}, f32[2,512,1024]{1,2,0}) fusion(bf16[2,8,128,512]{3,2,1,0:T(8,128)(2,1)S(1)} %bitcast.75, bf16[2,128,1024]{1,2,0:T(8,128)(2,1)S(1)} %bitcast.82, bf16[2,128,512]{2,1,0:T(8,128)(2,1)S(1)} %bitcast.87), kind=kOutput, calls=%fused_computation.12 | convolution fusion | flops 271572992 | bytes 7110656
  73.9 1.1 scatter_custom_fusion
  75.0 0.8 fusion.36
  75.8 1.7 fusion.37
  77.5 4.7 %broadcast_multiply_fusion = f32[16,128,512]{2,1,0:T(8,128)} fusion(f32[16,128,512]{2,1,0:T(8,128)} %bitcast.73, f32[16,512]{1,0:T(8,128)S(1)} %copy-done.12), kind=kLoop, calls=%fused_computation.20 | loop fusion | flops 1048576 | bytes 8421376 | tf_op jit(solution)/shard_map/mul | solution.py:156
  82.2 2.3 %broadcast_in_dim.59 = f32[14,128,512]{2,1,0:T(8,128)} broadcast(f32[]{:T(128)} %constant.59.clone.1), dimensions={} | broadcast | bytes 3670020 | tf_op jit(solution)/shard_map/broadcast_in_dim | solution.py:155
  84.5 9.5 %scatter_fusion = f32[14,128,512]{2,1,0:T(8,128)} fusion(f32[14,128,512]{2,1,0:T(8,128)} %broadcast_in_dim.59, s32[16]{0:T(128)S(1)} %compare_select_fusion.2, f32[16,128,512]{2,1,0:T(8,128)} %broadcast_multiply_fusion), kind=kCustom, calls=%fused_computation.4 | custom fusion | flops 1048576 | bytes 12582976 | tf_op jit(solution)/shard_map/scatter-add | solution.py:155
  94.0 1.1 slice.89
  95.0 1.1 fusion.17
  96.2 5.2 %copy.71 = f32[1792,512]{0,1:T(8,128)} copy(f32[1792,512]{1,0:T(8,128)} %fusion.17) | data formatting | bytes 7340032 | tf_op jit(solution)/shard_map/scatter-add | solution.py:159
  101.4 4.7 %fusion = f32[4,256,128]{2,1,0:T(8,128)S(1)} fusion(s32[1792,4]{0,1:T(4,128)S(1)} %copy-done.15, f32[1792,4,128]{0,2,1:T(8,128)} %bitcast.78), kind=kOutput, calls=%fused_computation.6 | convolution fusion | flops 475267072 | bytes 4222976 | tf_op jit(solution)/shard_map/fco,fcg->cog/dot_general | solution.py:36
  106.1 1.5 fusion.16
  107.7 1.1 reshape.170
  108.9 1.0 dynamic-slice_dynamic-update-slice_fusion.1
  109.9 1.1 dynamic-slice_dynamic-update-slice_fusion
  111.0 0.7 bitcast_dynamic-update-slice_fusion
  111.6 0.7 dynamic-slice_dynamic-update-slice_fusion.4
  112.3 0.7 constant_dynamic-update-slice_fusion.1
  113.0 2.6 %collective-permute-start = (f32[704,512]{1,0:T(8,128)}, f32[704,512]{1,0:T(8,128)S(1)}, u32[]{:S(2)}, u32[]{:S(2)}) collective-permute-start(f32[704,512]{1,0:T(8,128)} %constant_dynamic-update-slice_fusion.1), channel_id=1, source_target_pairs={{0,1},{1,0},{2,3},{3,2},{4,5},{5,4},{6,7},{7,6},{8,9},{9,8},{10,11... | collective-permute-start | bytes 4325384 | tf_op jit(solution)/shard_map/ppermute | solution.py:54
  115.7 0.7 constant_dynamic-update-slice_fusion
  116.4 2.3 %collective-permute-done = f32[704,512]{1,0:T(8,128)S(1)} collective-permute-done((f32[704,512]{1,0:T(8,128)}, f32[704,512]{1,0:T(8,128)S(1)}, u32[]{:S(2)}, u32[]{:S(2)}) %collective-permute-start) | collective-permute-done | bytes 1441824 | tf_op jit(solution)/shard_map/ppermute | solution.py:54
  118.7 1.6 add_convert_fusion
  120.8 31.0 %all_to_all.15 = bf16[128,22,128]{2,1,0:T(8,128)(2,1)S(1)} all-to-all(bf16[128,22,128]{2,1,0:T(8,128)(2,1)S(1)} %reshape.177), channel_id=1, replica_groups=mesh['dom'=128,'sub'=2] {'dom'}, dimensions={0} | all-to-all | bytes 1441792 | tf_op jit(solution)/shard_map/all_to_all | solution.py:57
  152.1 29.5 %all_to_all.16 = bf16[128,22,128]{2,1,0:T(8,128)(2,1)S(1)} all-to-all(bf16[128,22,128]{2,1,0:T(8,128)(2,1)S(1)} %broadcast_in_dim.60), channel_id=1, replica_groups=mesh['dom'=128,'sub'=2] {'dom'}, dimensions={0} | all-to-all | bytes 1441792 | tf_op jit(solution)/shard_map/all_to_all | solution.py:60
  182.2 3.6 %collective-permute-start.1 = (bf16[576,512]{1,0:T(8,128)(2,1)S(1)}, bf16[576,512]{1,0:T(8,128)(2,1)S(1)}, u32[]{:S(2)}, u32[]{:S(2)}) collective-permute-start(bf16[576,512]{1,0:T(8,128)(2,1)S(1)} %slice.90), channel_id=1, source_target_pairs={{0,1},{1,0},{2,3},{3,2},{4,5},{5,4},{6,7},{7,6},{8,9},{9,8},{10,11... | collective-permute-start | bytes 1769480 | tf_op jit(solution)/shard_map/ppermute | solution.py:63
  185.8 0.7 reshape.184
  186.5 0.9 collective-permute-done.1
  187.9 0.8 copy.74
  188.7 0.7 pad_maximum_fusion.3
  189.3 1.0 pad_maximum_fusion.1
  190.4 1.0 pad_maximum_fusion
  (87 shorter events, 6.4 us)
Async XLA Ops:
  0.6 67.1 %copy-start = (bf16[512,512]{1,0:T(8,128)(2,1)S(1)}, bf16[512,512]{1,0:T(8,128)(2,1)}, u32[]{:S(2)}) copy-start(bf16[512,512]{1,0:T(8,128)(2,1)} %param.20) | copy-start | bytes 1572868
  2.5 3.0 %copy-start.18 = (s32[1,1,128]{2,1,0:T(1,128)S(1)}, s32[1,1,128]{2,1,0:T(1,128)}, u32[]{:S(2)}) copy-start(s32[1,1,128]{2,1,0:T(1,128)} %param.25) | copy-start | bytes 1540
  6.3 17.8 %copy-start.17 = (s32[2]{0:T(128)S(1)}, s32[2]{0:T(128)}, u32[]{:S(2)}) copy-start(s32[2]{0:T(128)} %param.26) | copy-start | bytes 28
  6.3 21.0 %copy-start.7 = (bf16[16,128,128]{2,1,0:T(8,128)(2,1)S(1)}, bf16[16,128,128]{2,1,0:T(8,128)(2,1)}, u32[]{:S(2)}) copy-start(bf16[16,128,128]{2,1,0:T(8,128)(2,1)} %param.21) | copy-start | bytes 1572868
  7.6 22.0 %copy-start.19 = (s32[16]{0:T(128)S(1)}, s32[16]{0:T(128)}, u32[]{:S(2)}) copy-start(s32[16]{0:T(128)} %param.23) | copy-start | bytes 196
  7.6 22.0 %copy-start.20 = (s32[16]{0:T(128)S(1)}, s32[16]{0:T(128)}, u32[]{:S(2)}) copy-start(s32[16]{0:T(128)} %param.22) | copy-start | bytes 196
  7.6 22.1 %copy-start.6 = (f32[512,64]{0,1:T(8,128)S(1)}, f32[512,64]{0,1:T(8,128)}, u32[]{:S(2)}) copy-start(f32[512,64]{0,1:T(8,128)} %param.17) | copy-start | bytes 393220
  7.6 22.1 %copy-start.9 = (f32[64,512]{1,0:T(8,128)S(1)}, f32[64,512]{1,0:T(8,128)}, u32[]{:S(2)}) copy-start(f32[64,512]{1,0:T(8,128)} %param.18) | copy-start | bytes 393220
  7.7 46.7 %all-to-all-start = ((s32[128,8,256]{2,1,0:T(8,128)}), s32[128,8,256]{2,1,0:T(8,128)S(1)}, u32[]{:S(2)}, u32[]{:S(2)}) async-start(s32[128,8,256]{2,1,0:T(8,128)} %bitcast.34), calls=%async_computation | async-start | bytes 2097152 | tf_op jit(solution)/shard_map/all_to_all | solution.py:109
  24.1 7.2 %copy-start.13 = (bf16[2,256,128]{2,1,0:T(8,128)(2,1)S(1)}, bf16[2,256,128]{2,1,0:T(8,128)(2,1)}, u32[]{:S(2)}) copy-start(bf16[2,256,128]{2,1,0:T(8,128)(2,1)} %param.16) | copy-start | bytes 393220
  31.3 33.8 %copy-start.11 = (f32[16,512]{1,0:T(8,128)}, f32[16,512]{1,0:T(8,128)S(1)}, u32[]{:S(2)}) copy-start(f32[16,512]{1,0:T(8,128)S(1)} %gather_fusion.2) | copy-start | bytes 98308
  54.4 1.2 copy-start.16
  55.6 1.7 copy-start.14
  63.1 2.0 %copy-start.8 = (bf16[16,128,128]{2,1,0:T(8,128)(2,1)S(1)}, bf16[16,128,128]{2,1,0:T(8,128)(2,1)}, u32[]{:S(2)}) copy-start(bf16[16,128,128]{2,1,0:T(8,128)(2,1)} %param.21) | copy-start | bytes 1572868
  65.2 2.2 %copy-start.5 = (bf16[512,512]{1,0:T(8,128)(2,1)S(1)}, bf16[512,512]{1,0:T(8,128)(2,1)}, u32[]{:S(2)}) copy-start(bf16[512,512]{1,0:T(8,128)(2,1)} %param.19) | copy-start | bytes 1572868
  65.2 2.6 %copy-start.10 = (bf16[256,512]{1,0:T(8,128)(2,1)S(1)}, bf16[256,512]{1,0:T(8,128)(2,1)}, u32[]{:S(2)}) copy-start(bf16[256,512]{1,0:T(8,128)(2,1)} %param.27) | copy-start | bytes 786436
  69.2 2.0 %copy-start.1 = (bf16[16,128,512]{2,1,0:T(8,128)(2,1)S(1)}, bf16[16,128,512]{2,1,0:T(8,128)(2,1)}, u32[]{:S(2)}) copy-start(bf16[16,128,512]{2,1,0:T(8,128)(2,1)} %gather_fusion.1) | copy-start | bytes 6291460
  69.2 2.0 %copy-start.4 = (bf16[2,8,128,128]{2,3,1,0:T(8,128)(2,1)S(1)}, bf16[2,8,128,128]{2,3,1,0:T(8,128)(2,1)}, u32[]{:S(2)}) copy-start(bf16[2,8,128,128]{2,3,1,0:T(8,128)(2,1)} %copy.69) | copy-start | bytes 1572868
  73.9 3.6 %copy-start.12 = (f32[16,512]{1,0:T(8,128)S(1)}, f32[16,512]{1,0:T(8,128)}, u32[]{:S(2)}) copy-start(f32[16,512]{1,0:T(8,128)} %copy-done.11) | copy-start | bytes 98308
  96.2 5.2 %copy-start.15 = (s32[1792,4]{0,1:T(4,128)S(1)}, s32[1792,4]{0,1:T(4,128)}, u32[]{:S(2)}) copy-start(s32[1792,4]{0,1:T(4,128)} %copy-done.14) | copy-start | bytes 86020
  101.4 4.7 %copy-start.3 = (f32[1792,512]{0,1:T(8,128)S(1)}, f32[1792,512]{0,1:T(8,128)}, u32[]{:S(2)}) copy-start(f32[1792,512]{0,1:T(8,128)} %copy.71) | copy-start | bytes 11010052
  107.5 1.3 copy-start.2
  113.0 5.7 %collective-permute-start = (f32[704,512]{1,0:T(8,128)}, f32[704,512]{1,0:T(8,128)S(1)}, u32[]{:S(2)}, u32[]{:S(2)}) collective-permute-start(f32[704,512]{1,0:T(8,128)} %constant_dynamic-update-slice_fusion.1), channel_id=1, source_target_pairs={{0,1},{1,0},{2,3},{3,2},{4,5},{5,4},{6,7},{7,6},{8,9},{9,8},{10,11... | collective-permute-start | bytes 4325384 | tf_op jit(solution)/shard_map/ppermute | solution.py:54
  182.2 5.2 %collective-permute-start.1 = (bf16[576,512]{1,0:T(8,128)(2,1)S(1)}, bf16[576,512]{1,0:T(8,128)(2,1)S(1)}, u32[]{:S(2)}, u32[]{:S(2)}) collective-permute-start(bf16[576,512]{1,0:T(8,128)(2,1)S(1)} %slice.90), channel_id=1, source_target_pairs={{0,1},{1,0},{2,3},{3,2},{4,5},{5,4},{6,7},{7,6},{8,9},{9,8},{10,11... | collective-permute-start | bytes 1769480 | tf_op jit(solution)/shard_map/ppermute | solution.py:63

commit v5 on v4

--- a/solution.py
+++ b/solution.py
@@ -102,13 +102,10 @@
     slot_valid = jnp.arange(SLOT, dtype=jnp.int32)[None, :] < send_count[0, 0][:, None]
     out_codes = jnp.where(slot_valid[:, :, None], codes[targets], -1).reshape(part_count, -1)
     own_codes = jnp.broadcast_to(codes.reshape(1, -1), (part_count, codes.size))
-    lane_rows = 8
-    room = -(-(codes.size + out_codes.shape[1]) // (lane_rows * 128)) * lane_rows * 128
+    room = -(-(codes.size + out_codes.shape[1]) // 128) * 128
     filler = jnp.zeros((part_count, room - codes.size - out_codes.shape[1]), jnp.int32)
     payload = jnp.concatenate([own_codes, out_codes, filler], axis=1)
-    incoming = lax.all_to_all(
-        payload.reshape(part_count, lane_rows, -1), "dom", 0, 0, tiled=True
-    ).reshape(part_count, -1)
+    incoming = lax.all_to_all(payload, "dom", 0, 0, tiled=True)
     recv_codes = incoming[:, codes.size : codes.size + out_codes.shape[1]].reshape(-1, book_count)
     hub_codes = [
         incoming[hub_owner[hub_index], : codes.size].reshape(codes.shape)
@@ -152,8 +149,13 @@
     ).reshape(tile_count, TB, model_width)
     rel_rows = jnp.sum(grad_comp * picked.astype(jnp.float32), axis=1)
     rel_grad = jnp.zeros(rel_table.shape, jnp.float32).at[tile_rel].add(rel_rows)
-    table_grad = jnp.zeros(blocks.shape, jnp.float32).at[tile_src].add(
-        grad_comp * scale[:, None, :]
+    src_hot = one_hot_codes(tile_src, blocks.shape[0], jnp.float32)
+    table_grad = jnp.einsum(
+        "ts,tjd->sjd",
+        src_hot,
+        grad_comp * scale[:, None, :],
+        precision=HIGHEST_PREC,
+        preferred_element_type=jnp.float32,
     )
     table_grad = table_grad.reshape(-1, model_width)
     table_grad = table_grad.at[:rows_dev].add(grad_self)

time: 192 us -> 173 us (0.901)
  other arithmetic: 20.7 us -> 6.82 us
  waiting for transfers between devices: 23.6 us -> 14 us
  matrix products: 20.7 us -> 25.7 us
    all_to_all x1, waiting for transfers between devices: 20.4 us -> 10.9 us  [shards(): incoming = lax.all_to_all(payload, 'dom', 0, 0, tiled=True)]
    scatter-add x1 -> x0, other arithmetic: 9.47 us -> none  [shards(): jnp.zeros(blocks.shape, jnp.float32).at[tile_src]]
    dot_general x0 -> x1, matrix products: none -> 4.77 us  [shards(): jnp.einsum('ts,tjd->sjd', src_hot, grad_comp * scale[:, None, :], precisi...]
    mul x1 -> x0, other arithmetic: 4.71 us -> none  [shards(): grad_comp * scale[:, None, :]]
    dot_general x0 -> x1, local copies, waits for them, and re-layouts: none -> 3.92 us  [shards(): jnp.einsum('ts,tjd->sjd', src_hot, grad_comp * scale[:, None, :], precisi...]
    broadcast_in_dim x1 -> x0, local copies, waits for them, and re-layouts: 2.27 us -> none  [shards(): jnp.zeros(blocks.shape, jnp.float32).at[tile_src]]
    unnamed x50 -> x45, local copies, waits for them, and re-layouts: 7.32 us -> 5.49 us
  transfers between devices with their start and end apart: 3 -> 3, of which waited for: 3 -> 3; matrix products, arithmetic and copies ran while one was open for 2% -> 3% of each run, Pallas kernels for 0% -> 0%
where the time goes in v5:
time: 173 us; the launch traced here: 172 us
  blocking collectives  62.9 us (36%)
  local copies, waits for them, and re-layouts  35.4 us (20%)
  matrix products  25.7 us (15%)
  starting transfers between devices  22.6 us (13%)
  waiting for transfers between devices  14 us (8%)
  other arithmetic  6.82 us (4%)
  between operations  5.07 us (3%)
    all_to_all x1, blocking collectives, all_sum(): received = lax.all_to_all(chunks, 'dom', 0, 0, tiled=True)  31 us
    all_to_all x1, blocking collectives, all_sum(): lax.all_to_all(spread, 'dom', 0, 0, tiled=True).reshape(rows, width)  29.3 us
    all_to_all x1, starting transfers between devices, shards(): incoming = lax.all_to_all(payload, 'dom', 0, 0, tiled=True)  16.5 us
    all_to_all x1, waiting for transfers between devices, shards(): incoming = lax.all_to_all(payload, 'dom', 0, 0, tiled=True)  10.9 us
    another operation x2, local copies, waits for them, and re-layouts, shards(): blocks = table.reshape(-1, TB, model_width)  5.98 us
    unnamed x45, local copies, waits for them, and re-layouts  5.49 us
    scatter-add x1, local copies, waits for them, and re-layouts, shards(): table_grad = table_grad.at[:rows_dev].add(grad_self)  5.18 us
    dot_general x1, matrix products, shards(): jnp.einsum('ts,tjd->sjd', src_hot, grad_comp * scale[:, None, :], precisi...  4.77 us
  transfers between devices with their start and end apart: 3, of which 3 were waited for; matrix products, arithmetic and copies ran while one was open for 3% of the time, Pallas kernels for 0%

profile of v5, /device:TPU:1, one launch (start us, length us, event | category | flops | bytes accessed | tf_op | source)
XLA Modules:
  0.0 172.5 jit_solution(4361135325562732435)
XLA Ops:
  0.6 0.9 copy.45
  1.5 0.7 compare_select_fusion
  2.6 2.8 %gather_fusion = s32[1024,4]{1,0:T(8,128)S(1)} fusion(s32[256,4]{1,0:T(8,128)S(1)} %copy.45, s32[1024]{0:T(1024)S(1)} %broadcast_clamp_fusion), kind=kCustom, calls=%fused_computation | custom fusion | bytes 36864 | tf_op jit(solution)/shard_map/gather | solution.py:103
  6.0 1.2 all_to_all.14
  7.2 16.5 %all-to-all-start = ((s32[128,1,1152]{2,1,0:T(1,128)}), s32[128,1,1152]{2,1,0:T(1,128)S(1)}, u32[]{:S(2)}, u32[]{:S(2)}) async-start(s32[128,1,1152]{2,1,0:T(1,128)} %all_to_all.14), calls=%async_computation | async-start | bytes 1179648 | tf_op jit(solution)/shard_map/all_to_all | solution.py:108
  23.7 0.6 fusion.36
  28.5 1.0 fusion.37
  29.6 1.2 gather_fusion.2
  30.8 2.6 %all_gather.3 = bf16[4,256,128]{2,1,0:T(8,128)(2,1)S(1)} all-gather(bf16[2,256,128]{2,1,0:T(8,128)(2,1)S(1)} %copy-done.11), channel_id=1, replica_groups=mesh['dom'=128,'sub'=2] {'sub'}, dimensions={0}, use_global_device_ids=true | all-gather | bytes 393216 | tf_op jit(solution)/shard_map/all_gather | solution.py:98
  33.4 10.9 %all-to-all-done = s32[128,1,1152]{2,1,0:T(1,128)S(1)} async-done(((s32[128,1,1152]{2,1,0:T(1,128)}), s32[128,1,1152]{2,1,0:T(1,128)S(1)}, u32[]{:S(2)}, u32[]{:S(2)}) %all-to-all-start) | async-done | bytes 589856 | tf_op jit(solution)/shard_map/all_to_all | solution.py:108
  45.2 1.7 fusion.10
  46.8 2.6 %reshape.224 = bf16[14,128,512]{1,0,2:T(8,128)(2,1)} reshape(bf16[1792,4,128]{0,2,1:T(8,128)(2,1)S(1)} %fusion.10) | data formatting | bytes 3670016 | tf_op jit(solution)/shard_map/reshape;reshape | solution.py:117
  49.4 3.4 %copy.71 = bf16[14,128,512]{2,1,0:T(8,128)(2,1)S(1)} copy(bf16[14,128,512]{1,0,2:T(8,128)(2,1)} %reshape.224) | data formatting | bytes 3670016 | tf_op jit(solution)/shard_map/reshape;reshape | solution.py:117
  52.8 2.0 %gather_fusion.1 = bf16[16,128,512]{2,1,0:T(8,128)(2,1)} fusion(bf16[14,128,512]{2,1,0:T(8,128)(2,1)S(1)} %copy.71, s32[1024]{0:T(1024)S(1)} %get-tuple-element.60), kind=kCustom, calls=%fused_computation.1 | custom fusion | bytes 4194368 | tf_op jit(solution)/shard_map/gather | solution.py:119
  54.9 2.3 %fusion.21 = bf16[2,512,128]{1,2,0:T(8,128)(2,1)S(1)} fusion(bf16[2,8,128,128]{3,2,1,0:T(8,128)(2,1)} %bitcast.88, bf16[2,8,128,512]{3,2,1,0:T(8,128)(2,1)} %bitcast.75, f32[2,8,512]{2,1,0:T(8,128)} %bitcast.90), kind=kOutput, calls=%fused_computation.30 | convolution fusion | flops 271712256 | bytes 2916352 | tf_op jit(solution)/shard_map/btij,btjd->bid/dot_general | solution.py:122
  57.5 1.1 multiply_convert_fusion
  59.2 1.3 fusion.4
  60.5 4.8 %fusion.5 = f32[14,128,512]{2,0,1:T(8,128)S(1)} fusion(f32[16,128,512]{2,1,0:T(8,128)S(1)} %bitcast.74, f32[16,512]{1,0:T(8,128)S(1)} %copy-done.10, s32[16]{0:T(128)S(1)} %copy-done.16), kind=kOutput, calls=%fused_computation.13 | convolution fusion | flops 177209568 | bytes 7897152 | tf_op jit(solution)/shard_map/ts,tjd->sjd/dot_general | solution.py:153
  65.3 3.9 %copy.59 = f32[14,128,512]{2,1,0:T(8,128)} copy(f32[14,128,512]{2,0,1:T(8,128)S(1)} %fusion.5) | data formatting | bytes 7340032 | tf_op jit(solution)/shard_map/ts,tjd->sjd/dot_general | solution.py:153
  69.4 1.3 fusion.39
  71.0 1.4 scatter_custom_fusion
  72.4 1.4 fusion.41
  73.8 2.6 %fusion.42 = f32[512,64]{1,0:T(8,128)} fusion(f32[512,512]{1,0:T(8,128)S(1)} %scatter_custom_fusion, f32[64,512]{1,0:T(8,128)} %param.18), kind=kOutput, calls=%fused_computation.82 | convolution fusion | flops 201326592 | bytes 1310720 | tf_op jit(solution)/shard_map/dot_general | solution.py:163
  76.5 1.1 fusion.19
  77.6 5.2 %copy.61 = f32[1792,512]{0,1:T(8,128)} copy(f32[1792,512]{1,0:T(8,128)} %fusion.19) | data formatting | bytes 7340032 | tf_op jit(solution)/shard_map/scatter-add | solution.py:161
  82.8 4.7 %fusion = f32[4,256,128]{2,1,0:T(8,128)S(1)} fusion(s32[1792,4]{0,1:T(4,128)S(1)} %copy-done.13, f32[1792,4,128]{0,2,1:T(8,128)} %bitcast.77), kind=kOutput, calls=%fused_computation.5 | convolution fusion | flops 475267072 | bytes 4222976 | tf_op jit(solution)/shard_map/fco,fcg->cog/dot_general | solution.py:36
  87.5 1.5 fusion.18
  89.1 1.1 reshape.169
  90.3 1.0 dynamic-slice_dynamic-update-slice_fusion.1
  91.3 1.1 dynamic-slice_dynamic-update-slice_fusion
  92.4 0.7 bitcast_dynamic-update-slice_fusion
  93.1 0.7 dynamic-slice_dynamic-update-slice_fusion.4
  93.7 0.7 constant_dynamic-update-slice_fusion.1
  94.4 2.5 %collective-permute-start = (f32[704,512]{1,0:T(8,128)}, f32[704,512]{1,0:T(8,128)S(1)}, u32[]{:S(2)}, u32[]{:S(2)}) collective-permute-start(f32[704,512]{1,0:T(8,128)} %constant_dynamic-update-slice_fusion.1), channel_id=1, source_target_pairs={{0,1},{1,0},{2,3},{3,2},{4,5},{5,4},{6,7},{7,6},{8,9},{9,8},{10,11... | collective-permute-start | bytes 4325384 | tf_op jit(solution)/shard_map/ppermute | solution.py:54
  97.0 0.7 constant_dynamic-update-slice_fusion
  97.7 2.3 %collective-permute-done = f32[704,512]{1,0:T(8,128)S(1)} collective-permute-done((f32[704,512]{1,0:T(8,128)}, f32[704,512]{1,0:T(8,128)S(1)}, u32[]{:S(2)}, u32[]{:S(2)}) %collective-permute-start) | collective-permute-done | bytes 1441824 | tf_op jit(solution)/shard_map/ppermute | solution.py:54
  100.0 1.6 add_convert_fusion
  101.6 0.5 reshape.176
  102.1 31.0 %all_to_all.22 = bf16[128,22,128]{2,1,0:T(8,128)(2,1)S(1)} all-to-all(bf16[128,22,128]{2,1,0:T(8,128)(2,1)S(1)} %reshape.176), channel_id=1, replica_groups=mesh['dom'=128,'sub'=2] {'dom'}, dimensions={0} | all-to-all | bytes 1441792 | tf_op jit(solution)/shard_map/all_to_all | solution.py:57
  133.4 29.3 %all_to_all.23 = bf16[128,22,128]{2,1,0:T(8,128)(2,1)S(1)} all-to-all(bf16[128,22,128]{2,1,0:T(8,128)(2,1)S(1)} %broadcast_in_dim.57), channel_id=1, replica_groups=mesh['dom'=128,'sub'=2] {'dom'}, dimensions={0} | all-to-all | bytes 1441792 | tf_op jit(solution)/shard_map/all_to_all | solution.py:60
  162.7 0.5 reshape.177
  163.2 3.6 %collective-permute-start.1 = (bf16[576,512]{1,0:T(8,128)(2,1)S(1)}, bf16[576,512]{1,0:T(8,128)(2,1)S(1)}, u32[]{:S(2)}, u32[]{:S(2)}) collective-permute-start(bf16[576,512]{1,0:T(8,128)(2,1)S(1)} %slice.90), channel_id=1, source_target_pairs={{0,1},{1,0},{2,3},{3,2},{4,5},{5,4},{6,7},{7,6},{8,9},{9,8},{10,11... | collective-permute-start | bytes 1769480 | tf_op jit(solution)/shard_map/ppermute | solution.py:63
  166.9 0.7 reshape.183
  167.6 0.9 collective-permute-done.1
  169.0 0.8 copy.64
  169.7 0.7 pad_maximum_fusion.3
  170.4 1.0 pad_maximum_fusion.1
  171.4 1.0 pad_maximum_fusion
  (83 shorter events, 4.4 us)
Async XLA Ops:
  0.6 56.9 %copy-start = (bf16[512,512]{1,0:T(8,128)(2,1)S(1)}, bf16[512,512]{1,0:T(8,128)(2,1)}, u32[]{:S(2)}) copy-start(bf16[512,512]{1,0:T(8,128)(2,1)} %param.20) | copy-start | bytes 1572868
  2.5 3.0 %copy-start.17 = (s32[1,1,128]{2,1,0:T(1,128)S(1)}, s32[1,1,128]{2,1,0:T(1,128)}, u32[]{:S(2)}) copy-start(s32[1,1,128]{2,1,0:T(1,128)} %param.25) | copy-start | bytes 1540
  5.8 17.9 %copy-start.15 = (s32[2]{0:T(128)S(1)}, s32[2]{0:T(128)}, u32[]{:S(2)}) copy-start(s32[2]{0:T(128)} %param.26) | copy-start | bytes 28
  5.8 21.0 %copy-start.7 = (bf16[16,128,128]{2,1,0:T(8,128)(2,1)S(1)}, bf16[16,128,128]{2,1,0:T(8,128)(2,1)}, u32[]{:S(2)}) copy-start(bf16[16,128,128]{2,1,0:T(8,128)(2,1)} %param.21) | copy-start | bytes 1572868
  5.9 22.5 %copy-start.18 = (s32[16]{0:T(128)S(1)}, s32[16]{0:T(128)}, u32[]{:S(2)}) copy-start(s32[16]{0:T(128)} %param.23) | copy-start | bytes 196
  5.9 22.6 %copy-start.16 = (s32[16]{0:T(128)S(1)}, s32[16]{0:T(128)}, u32[]{:S(2)}) copy-start(s32[16]{0:T(128)} %param.22) | copy-start | bytes 196
  5.9 22.6 %copy-start.5 = (f32[512,64]{0,1:T(8,128)S(1)}, f32[512,64]{0,1:T(8,128)}, u32[]{:S(2)}) copy-start(f32[512,64]{0,1:T(8,128)} %param.17) | copy-start | bytes 393220
  6.0 22.6 %copy-start.8 = (f32[64,512]{1,0:T(8,128)S(1)}, f32[64,512]{1,0:T(8,128)}, u32[]{:S(2)}) copy-start(f32[64,512]{1,0:T(8,128)} %param.18) | copy-start | bytes 393220
  7.2 23.6 %copy-start.11 = (bf16[2,256,128]{2,1,0:T(8,128)(2,1)S(1)}, bf16[2,256,128]{2,1,0:T(8,128)(2,1)}, u32[]{:S(2)}) copy-start(bf16[2,256,128]{2,1,0:T(8,128)(2,1)} %param.16) | copy-start | bytes 393220
  7.2 37.0 %all-to-all-start = ((s32[128,1,1152]{2,1,0:T(1,128)}), s32[128,1,1152]{2,1,0:T(1,128)S(1)}, u32[]{:S(2)}, u32[]{:S(2)}) async-start(s32[128,1,1152]{2,1,0:T(1,128)} %all_to_all.14), calls=%async_computation | async-start | bytes 1179648 | tf_op jit(solution)/shard_map/all_to_all | solution.py:108
  29.6 15.6 %copy-start.14 = (s32[256,4]{0,1:T(4,128)S(1)}, s32[256,4]{0,1:T(4,128)}, u32[]{:S(2)}) copy-start(s32[256,4]{0,1:T(4,128)} %param.15) | copy-start | bytes 12292
  45.1 1.7 copy-start.12
  54.8 2.3 %copy-start.4 = (bf16[512,512]{1,0:T(8,128)(2,1)S(1)}, bf16[512,512]{1,0:T(8,128)(2,1)}, u32[]{:S(2)}) copy-start(bf16[512,512]{1,0:T(8,128)(2,1)} %param.19) | copy-start | bytes 1572868
  54.9 2.6 %copy-start.9 = (bf16[256,512]{1,0:T(8,128)(2,1)S(1)}, bf16[256,512]{1,0:T(8,128)(2,1)}, u32[]{:S(2)}) copy-start(bf16[256,512]{1,0:T(8,128)(2,1)} %param.27) | copy-start | bytes 786436
  57.5 1.7 copy-start.1
  59.2 1.3 copy-start.10
  77.6 5.2 %copy-start.13 = (s32[1792,4]{0,1:T(4,128)S(1)}, s32[1792,4]{0,1:T(4,128)}, u32[]{:S(2)}) copy-start(s32[1792,4]{0,1:T(4,128)} %copy-done.12) | copy-start | bytes 86020
  82.8 4.7 %copy-start.3 = (f32[1792,512]{0,1:T(8,128)S(1)}, f32[1792,512]{0,1:T(8,128)}, u32[]{:S(2)}) copy-start(f32[1792,512]{0,1:T(8,128)} %copy.61) | copy-start | bytes 11010052
  89.0 1.3 copy-start.2
  90.3 2.1 %copy-start.6 = (f32[512,64]{0,1:T(8,128)S(1)}, f32[512,64]{0,1:T(8,128)}, u32[]{:S(2)}) copy-start(f32[512,64]{0,1:T(8,128)} %fusion.41) | copy-start | bytes 393220
  94.4 5.5 %collective-permute-start = (f32[704,512]{1,0:T(8,128)}, f32[704,512]{1,0:T(8,128)S(1)}, u32[]{:S(2)}, u32[]{:S(2)}) collective-permute-start(f32[704,512]{1,0:T(8,128)} %constant_dynamic-update-slice_fusion.1), channel_id=1, source_target_pairs={{0,1},{1,0},{2,3},{3,2},{4,5},{5,4},{6,7},{7,6},{8,9},{9,8},{10,11... | collective-permute-start | bytes 4325384 | tf_op jit(solution)/shard_map/ppermute | solution.py:54
  163.2 5.2 %collective-permute-start.1 = (bf16[576,512]{1,0:T(8,128)(2,1)S(1)}, bf16[576,512]{1,0:T(8,128)(2,1)S(1)}, u32[]{:S(2)}, u32[]{:S(2)}) collective-permute-start(bf16[576,512]{1,0:T(8,128)(2,1)S(1)} %slice.90), channel_id=1, source_target_pairs={{0,1},{1,0},{2,3},{3,2},{4,5},{5,4},{6,7},{7,6},{8,9},{9,8},{10,11... | collective-permute-start | bytes 1769480 | tf_op jit(solution)/shard_map/ppermute | solution.py:63

commit v6 on v5

--- a/solution.py
+++ b/solution.py
@@ -1,12 +1,14 @@
 import jax
 import jax.numpy as jnp
 from jax import lax
-from jax.sharding import PartitionSpec as P
+from jax.sharding import Mesh, PartitionSpec as P
+import numpy as np
 
 TB = 128
 TPB = 8
 SLOT = 8
 NHUB = 2
+DOM = ("dy", "dx", "dz")
 
 
 HIGHEST_PREC = lax.Precision.HIGHEST
@@ -39,7 +41,7 @@
     return upper_half_sum + lower_half_sum
 
 
-def all_sum(grad_w_msg, grad_w_self, part_alpha, part_basis, book_grad, n_dom):
+def all_sum(grad_w_msg, grad_w_self, part_alpha, part_basis, book_grad, dom_axes):
     sub_index = lax.axis_index("sub")
     width = grad_w_msg.shape[1]
     share = book_grad.shape[0] // 2
@@ -53,11 +55,23 @@
     swap = [(0, 1), (1, 0)]
     mine = half_of(sub_index) + lax.ppermute(half_of(1 - sub_index), "sub", swap)
     rows = mine.shape[0]
-    chunks = mine.astype(jnp.bfloat16).reshape(n_dom, -1, 128)
-    received = lax.all_to_all(chunks, "dom", 0, 0, tiled=True)
-    reduced = jnp.sum(received.astype(jnp.float32), axis=0).astype(jnp.bfloat16)
-    spread = jnp.broadcast_to(reduced[None], chunks.shape)
-    own_half = lax.all_to_all(spread, "dom", 0, 0, tiled=True).reshape(rows, width)
+    shapes = []
+    piece = mine
+    for stage, (axis, size) in enumerate(dom_axes):
+        shapes.append(piece.shape)
+        lanes = piece.shape[-1]
+        if piece.shape[0] % size:
+            lanes = 256
+        chunks = piece.reshape(size, -1, lanes)
+        if stage == 0:
+            chunks = chunks.astype(jnp.bfloat16)
+        received = lax.all_to_all(chunks, axis, 0, 0, tiled=True)
+        piece = jnp.sum(received.astype(jnp.float32), axis=0)
+    piece = piece.astype(jnp.bfloat16)
+    for (axis, size), shape in reversed(list(zip(dom_axes, shapes))):
+        spread = jnp.broadcast_to(piece[None], (size,) + piece.shape)
+        piece = lax.all_to_all(spread, axis, 0, 0, tiled=True).reshape(shape)
+    own_half = piece
     dense_rows = rows - share * book_grad.shape[1] * book_grad.shape[2] // width
     own_dense = own_half[:dense_rows]
     other_dense = lax.ppermute(own_dense, "sub", swap)
@@ -75,7 +89,7 @@
 
 
 def shards(
-    n_dom,
+    dom_axes,
     codes,
     books,
     alpha,
@@ -105,7 +119,7 @@
     room = -(-(codes.size + out_codes.shape[1]) // 128) * 128
     filler = jnp.zeros((part_count, room - codes.size - out_codes.shape[1]), jnp.int32)
     payload = jnp.concatenate([own_codes, out_codes, filler], axis=1)
-    incoming = lax.all_to_all(payload, "dom", 0, 0, tiled=True)
+    incoming = lax.all_to_all(payload, DOM, 0, 0, tiled=True)
     recv_codes = incoming[:, codes.size : codes.size + out_codes.shape[1]].reshape(-1, book_count)
     hub_codes = [
         incoming[hub_owner[hub_index], : codes.size].reshape(codes.shape)
@@ -167,35 +181,56 @@
         alpha.T, rel_grad, precision=HIGHEST_PREC, preferred_element_type=jnp.float32
     )
     total_msg, total_self, grad_basis, grad_alpha, grad_books = all_sum(
-        grad_w_msg, grad_w_self, part_alpha, part_basis, book_grad, n_dom
+        grad_w_msg, grad_w_self, part_alpha, part_basis, book_grad, dom_axes
     )
     return (output, total_msg, total_self, grad_alpha, grad_basis, grad_books)
 
 
+def split_mesh(mesh):
+    grid = np.asarray(mesh.devices)
+    try:
+        coords = np.array([d.coords for d in grid.reshape(-1)]).reshape(grid.shape + (-1,))
+    except (AttributeError, ValueError):
+        return None
+    ny, nx, nz = (len(np.unique(coords[..., k])) for k in (1, 0, 2))
+    if ny * nx * nz != grid.shape[0]:
+        return None
+    cube = coords.reshape(ny, nx, nz, grid.shape[1], -1)
+    for axis, k in ((0, 1), (1, 0), (2, 2)):
+        others = [c for c in range(3) if c != k]
+        if np.any(np.diff(cube[..., others], axis=axis) != 0):
+            return None
+    return Mesh(grid.reshape(ny, nx, nz, grid.shape[1]), DOM + ("sub",)), (ny, nx, nz)
+
+
 def solution(mesh):
-    n_dom = mesh.shape["dom"]
+    found = split_mesh(mesh)
+    assert found is not None
+    fine_mesh, (ny, nx, nz) = found
+    dom_axes = (("dx", nx), ("dy", ny), ("dz", nz))
 
     def run(*args):
-        return shards(n_dom, *args)
-
+        return shards(dom_axes, *args)
+
+    rows = P(DOM + ("sub",))
     return jax.shard_map(
         run,
-        mesh=mesh,
+        mesh=fine_mesh,
         in_specs=(
-            P(("dom", "sub"), None),
+            P(DOM + ("sub",), None),
             P("sub", None, None),
             P(),
             P(),
             P(),
             P(),
-            P(("dom", "sub"), None, None),
-            P(("dom", "sub")),
-            P(("dom", "sub")),
-            P("dom", "sub", None, None),
-            P("dom", "sub", None),
-            P(),
-            P(("dom", "sub"), None),
+            P(DOM + ("sub",), None, None),
+            rows,
+            rows,
+            P(DOM, "sub", None, None),
+            P(DOM, "sub", None),
+            P(),
+            P(DOM + ("sub",), None),
         ),
-        out_specs=(P(("dom", "sub"), None), P(), P(), P(), P(), P("sub", None, None)),
+        out_specs=(P(DOM + ("sub",), None), P(), P(), P(), P(), P("sub", None, None)),
         check_vma=False,
     )

time: 173 us -> 176 us (1.017)
  starting transfers between devices: 22.6 us -> 26.4 us
    ppermute x1, starting transfers between devices: 3.62 us -> 7.4 us  [all_sum(): other_dense = lax.ppermute(own_dense, 'sub', swap)]
    all_to_all x2 -> x6, blocking collectives: 60.3 us -> 60 us  [the longest x3 32.4 us: all_sum(): received = lax.all_to_all(chunks, axis, 0, 0, tiled=True)]
where the time goes in v6:
time: 176 us; the launch traced here: 175 us
  blocking collectives  62.5 us (36%)
  local copies, waits for them, and re-layouts  34.5 us (20%)
  starting transfers between devices  26.4 us (15%)
  matrix products  25.7 us (15%)
  waiting for transfers between devices  14 us (8%)
  other arithmetic  6.79 us (4%)
  between operations  5.1 us (3%)
    all_to_all x3, blocking collectives, all_sum(): received = lax.all_to_all(chunks, axis, 0, 0, tiled=True)  32.4 us
    all_to_all x3, blocking collectives, all_sum(): piece = lax.all_to_all(spread, axis, 0, 0, tiled=True).reshape(shape)  27.5 us
    all_to_all x1, starting transfers between devices, shards(): incoming = lax.all_to_all(payload, DOM, 0, 0, tiled=True)  16.5 us
    all_to_all x1, waiting for transfers between devices, shards(): incoming = lax.all_to_all(payload, DOM, 0, 0, tiled=True)  10.9 us
    ppermute x1, starting transfers between devices, all_sum(): other_dense = lax.ppermute(own_dense, 'sub', swap)  7.4 us
    another operation x2, local copies, waits for them, and re-layouts, shards(): blocks = table.reshape(-1, TB, model_width)  6.01 us
    unnamed x45, local copies, waits for them, and re-layouts  5.49 us
    scatter-add x1, local copies, waits for them, and re-layouts, shards(): table_grad = table_grad.at[:rows_dev].add(grad_self)  5.14 us
  transfers between devices with their start and end apart: 3, of which 3 were waited for; matrix products, arithmetic and copies ran while one was open for 3% of the time, Pallas kernels for 0%

profile of v6, /device:TPU:1, one launch (start us, length us, event | category | flops | bytes accessed | tf_op | source)
XLA Modules:
  0.0 175.0 jit_solution(7988838224171348690)
XLA Ops:
  0.6 0.9 copy.45
  1.5 0.7 compare_select_fusion
  2.6 2.8 %gather_fusion = s32[1024,4]{1,0:T(8,128)S(1)} fusion(s32[256,4]{1,0:T(8,128)S(1)} %copy.45, s32[1024]{0:T(1024)S(1)} %broadcast_clamp_fusion), kind=kCustom, calls=%fused_computation | custom fusion | bytes 36864 | tf_op jit(solution)/shard_map/gather | solution.py:117
  6.0 1.2 all_to_all.26
  7.2 16.5 %all-to-all-start = ((s32[128,1,1152]{2,1,0:T(1,128)}), s32[128,1,1152]{2,1,0:T(1,128)S(1)}, u32[]{:S(2)}, u32[]{:S(2)}) async-start(s32[128,1,1152]{2,1,0:T(1,128)} %all_to_all.26), calls=%async_computation | async-start | bytes 1179648 | tf_op jit(solution)/shard_map/all_to_all | solution.py:122
  28.5 1.0 fusion.37
  29.6 1.2 gather_fusion.2
  30.8 2.6 %all_gather.3 = bf16[4,256,128]{2,1,0:T(8,128)(2,1)S(1)} all-gather(bf16[2,256,128]{2,1,0:T(8,128)(2,1)S(1)} %copy-done.11), channel_id=1, replica_groups=mesh['dy'=4,'dx'=4,'dz'=8,'sub'=2] {'sub'}, dimensions={0}, use_global_device_ids=true | all-gather | bytes 393216 | tf_op jit(solution)/shard_map/all_gather | solution.py:112
  33.3 10.9 %all-to-all-done = s32[128,1,1152]{2,1,0:T(1,128)S(1)} async-done(((s32[128,1,1152]{2,1,0:T(1,128)}), s32[128,1,1152]{2,1,0:T(1,128)S(1)}, u32[]{:S(2)}, u32[]{:S(2)}) %all-to-all-start) | async-done | bytes 589856 | tf_op jit(solution)/shard_map/all_to_all | solution.py:122
  45.2 1.7 fusion.10
  46.8 2.6 %reshape.234 = bf16[14,128,512]{1,0,2:T(8,128)(2,1)} reshape(bf16[1792,4,128]{0,2,1:T(8,128)(2,1)S(1)} %fusion.10) | data formatting | bytes 3670016 | tf_op jit(solution)/shard_map/reshape;reshape | solution.py:131
  49.5 3.4 %copy.71 = bf16[14,128,512]{2,1,0:T(8,128)(2,1)S(1)} copy(bf16[14,128,512]{1,0,2:T(8,128)(2,1)} %reshape.234) | data formatting | bytes 3670016 | tf_op jit(solution)/shard_map/reshape;reshape | solution.py:131
  52.9 2.0 %gather_fusion.1 = bf16[16,128,512]{2,1,0:T(8,128)(2,1)} fusion(bf16[14,128,512]{2,1,0:T(8,128)(2,1)S(1)} %copy.71, s32[1024]{0:T(1024)S(1)} %get-tuple-element.60), kind=kCustom, calls=%fused_computation.1 | custom fusion | bytes 4194368 | tf_op jit(solution)/shard_map/gather | solution.py:133
  54.9 2.3 %fusion.21 = bf16[2,512,128]{1,2,0:T(8,128)(2,1)S(1)} fusion(bf16[2,8,128,128]{3,2,1,0:T(8,128)(2,1)} %bitcast.94, bf16[2,8,128,512]{3,2,1,0:T(8,128)(2,1)} %bitcast.77, f32[2,8,512]{2,1,0:T(8,128)} %bitcast.96), kind=kOutput, calls=%fused_computation.31 | convolution fusion | flops 271712256 | bytes 2916352 | tf_op jit(solution)/shard_map/btij,btjd->bid/dot_general | solution.py:136
  57.6 1.1 multiply_convert_fusion
  59.2 1.3 fusion.4
  60.6 4.8 %fusion.5 = f32[14,128,512]{2,0,1:T(8,128)S(1)} fusion(f32[16,128,512]{2,1,0:T(8,128)S(1)} %bitcast.76, f32[16,512]{1,0:T(8,128)S(1)} %copy-done.10, s32[16]{0:T(128)S(1)} %copy-done.16), kind=kOutput, calls=%fused_computation.13 | convolution fusion | flops 177209568 | bytes 7897152 | tf_op jit(solution)/shard_map/ts,tjd->sjd/dot_general | solution.py:167
  65.3 3.9 %copy.59 = f32[14,128,512]{2,1,0:T(8,128)} copy(f32[14,128,512]{2,0,1:T(8,128)S(1)} %fusion.5) | data formatting | bytes 7340032 | tf_op jit(solution)/shard_map/ts,tjd->sjd/dot_general | solution.py:167
  69.4 1.3 fusion.39
  71.0 1.4 scatter_custom_fusion
  72.4 1.4 fusion.41
  73.9 2.6 %fusion.42 = f32[512,64]{1,0:T(8,128)} fusion(f32[512,512]{1,0:T(8,128)S(1)} %scatter_custom_fusion, f32[64,512]{1,0:T(8,128)} %param.18), kind=kOutput, calls=%fused_computation.83 | convolution fusion | flops 201326592 | bytes 1310720 | tf_op jit(solution)/shard_map/dot_general | solution.py:177
  76.5 1.1 fusion.19
  77.7 5.1 %copy.61 = f32[1792,512]{0,1:T(8,128)} copy(f32[1792,512]{1,0:T(8,128)} %fusion.19) | data formatting | bytes 7340032 | tf_op jit(solution)/shard_map/scatter-add | solution.py:175
  82.8 4.7 %fusion = f32[4,256,128]{2,1,0:T(8,128)S(1)} fusion(s32[1792,4]{0,1:T(4,128)S(1)} %copy-done.13, f32[1792,4,128]{0,2,1:T(8,128)} %bitcast.82), kind=kOutput, calls=%fused_computation.5 | convolution fusion | flops 475267072 | bytes 4222976 | tf_op jit(solution)/shard_map/fco,fcg->cog/dot_general | solution.py:38
  87.5 1.5 fusion.18
  89.1 1.1 reshape.178
  90.3 1.0 dynamic-slice_dynamic-update-slice_fusion.1
  91.3 1.1 dynamic-slice_dynamic-update-slice_fusion
  93.1 0.7 dynamic-slice_dynamic-update-slice_fusion.4
  93.7 0.7 constant_dynamic-update-slice_fusion.1
  94.4 2.5 %collective-permute-start = (f32[704,512]{1,0:T(8,128)}, f32[704,512]{1,0:T(8,128)S(1)}, u32[]{:S(2)}, u32[]{:S(2)}) collective-permute-start(f32[704,512]{1,0:T(8,128)} %constant_dynamic-update-slice_fusion.1), channel_id=1, source_target_pairs={{0,1},{1,0},{2,3},{3,2},{4,5},{5,4},{6,7},{7,6},{8,9},{9,8},{10,11... | collective-permute-start | bytes 4325384 | tf_op jit(solution)/shard_map/ppermute | solution.py:56
  97.0 0.7 constant_dynamic-update-slice_fusion
  97.7 2.3 %collective-permute-done = f32[704,512]{1,0:T(8,128)S(1)} collective-permute-done((f32[704,512]{1,0:T(8,128)}, f32[704,512]{1,0:T(8,128)S(1)}, u32[]{:S(2)}, u32[]{:S(2)}) %collective-permute-start) | collective-permute-done | bytes 1441824 | tf_op jit(solution)/shard_map/ppermute | solution.py:56
  100.0 1.6 add_convert_fusion
  101.6 13.4 %all_to_all.42 = bf16[4,176,512]{2,1,0:T(8,128)(2,1)S(1)} all-to-all(bf16[4,176,512]{2,1,0:T(8,128)(2,1)S(1)} %bitcast.84), channel_id=1, replica_groups=mesh['dy'=4,'dx'=4,'dz'=8,'sub'=2] {'dx'}, dimensions={0} | all-to-all | bytes 1441792 | tf_op jit(solution)/shard_map/all_to_all | solution.py:68
  115.1 8.7 %all_to_all.43 = f32[4,44,512]{2,1,0:T(8,128)S(1)} all-to-all(f32[4,44,512]{2,1,0:T(8,128)S(1)} %reshape.185), channel_id=1, replica_groups=mesh['dy'=4,'dx'=4,'dz'=8,'sub'=2] {'dy'}, dimensions={0} | all-to-all | bytes 720896 | tf_op jit(solution)/shard_map/all_to_all | solution.py:68
  123.9 10.3 %all_to_all.44 = f32[8,11,256]{2,1,0:T(8,128)S(1)} all-to-all(f32[8,11,256]{2,1,0:T(8,128)S(1)} %reshape.186), channel_id=1, replica_groups=mesh['dy'=4,'dx'=4,'dz'=8,'sub'=2] {'dz'}, dimensions={0} | all-to-all | bytes 180224 | tf_op jit(solution)/shard_map/all_to_all | solution.py:68
  134.3 9.6 %all_to_all.45 = bf16[8,11,256]{2,1,0:T(8,128)(2,1)S(1)} all-to-all(bf16[8,11,256]{2,1,0:T(8,128)(2,1)S(1)} %broadcast_in_dim.71), channel_id=1, replica_groups=mesh['dy'=4,'dx'=4,'dz'=8,'sub'=2] {'dz'}, dimensions={0} | all-to-all | bytes 90112 | tf_op jit(solution)/shard_map/all_to_all | solution.py:73
  143.9 7.5 %all_to_all.46 = bf16[4,44,512]{2,1,0:T(8,128)(2,1)S(1)} all-to-all(bf16[4,44,512]{2,1,0:T(8,128)(2,1)S(1)} %broadcast_in_dim.73), channel_id=1, replica_groups=mesh['dy'=4,'dx'=4,'dz'=8,'sub'=2] {'dy'}, dimensions={0} | all-to-all | bytes 360448 | tf_op jit(solution)/shard_map/all_to_all | solution.py:73
  151.6 10.4 %all_to_all.47 = bf16[4,176,512]{2,1,0:T(8,128)(2,1)S(1)} all-to-all(bf16[4,176,512]{2,1,0:T(8,128)(2,1)S(1)} %broadcast_in_dim.75), channel_id=1, replica_groups=mesh['dy'=4,'dx'=4,'dz'=8,'sub'=2] {'dx'}, dimensions={0} | all-to-all | bytes 1441792 | tf_op jit(solution)/shard_map/all_to_all | solution.py:73
  162.0 7.4 %collective-permute-start.1 = (bf16[576,512]{1,0:T(8,128)(2,1)S(1)}, bf16[576,512]{1,0:T(8,128)(2,1)S(1)}, u32[]{:S(2)}, u32[]{:S(2)}) collective-permute-start(bf16[576,512]{1,0:T(8,128)(2,1)S(1)} %slice.90), channel_id=1, source_target_pairs={{0,1},{1,0},{2,3},{3,2},{4,5},{5,4},{6,7},{7,6},{8,9},{9,8},{10,11... | collective-permute-start | bytes 1769480 | tf_op jit(solution)/shard_map/ppermute | solution.py:77
  169.4 0.7 reshape.193
  170.1 0.9 collective-permute-done.1
  171.5 0.8 copy.64
  172.3 0.7 pad_maximum_fusion.3
  172.9 1.0 pad_maximum_fusion.1
  174.0 1.0 pad_maximum_fusion
  (93 shorter events, 5.8 us)
Async XLA Ops:
  0.6 56.9 %copy-start = (bf16[512,512]{1,0:T(8,128)(2,1)S(1)}, bf16[512,512]{1,0:T(8,128)(2,1)}, u32[]{:S(2)}) copy-start(bf16[512,512]{1,0:T(8,128)(2,1)} %param.20) | copy-start | bytes 1572868
  2.5 3.0 %copy-start.17 = (s32[1,1,128]{2,1,0:T(1,128)S(1)}, s32[1,1,128]{2,1,0:T(1,128)}, u32[]{:S(2)}) copy-start(s32[1,1,128]{2,1,0:T(1,128)} %param.25) | copy-start | bytes 1540
  5.8 17.9 %copy-start.15 = (s32[2]{0:T(128)S(1)}, s32[2]{0:T(128)}, u32[]{:S(2)}) copy-start(s32[2]{0:T(128)} %param.26) | copy-start | bytes 28
  5.8 21.0 %copy-start.7 = (bf16[16,128,128]{2,1,0:T(8,128)(2,1)S(1)}, bf16[16,128,128]{2,1,0:T(8,128)(2,1)}, u32[]{:S(2)}) copy-start(bf16[16,128,128]{2,1,0:T(8,128)(2,1)} %param.21) | copy-start | bytes 1572868
  5.9 22.5 %copy-start.18 = (s32[16]{0:T(128)S(1)}, s32[16]{0:T(128)}, u32[]{:S(2)}) copy-start(s32[16]{0:T(128)} %param.23) | copy-start | bytes 196
  5.9 22.6 %copy-start.16 = (s32[16]{0:T(128)S(1)}, s32[16]{0:T(128)}, u32[]{:S(2)}) copy-start(s32[16]{0:T(128)} %param.22) | copy-start | bytes 196
  5.9 22.6 %copy-start.5 = (f32[512,64]{0,1:T(8,128)S(1)}, f32[512,64]{0,1:T(8,128)}, u32[]{:S(2)}) copy-start(f32[512,64]{0,1:T(8,128)} %param.17) | copy-start | bytes 393220
  6.0 22.6 %copy-start.8 = (f32[64,512]{1,0:T(8,128)S(1)}, f32[64,512]{1,0:T(8,128)}, u32[]{:S(2)}) copy-start(f32[64,512]{1,0:T(8,128)} %param.18) | copy-start | bytes 393220
  7.2 23.6 %copy-start.11 = (bf16[2,256,128]{2,1,0:T(8,128)(2,1)S(1)}, bf16[2,256,128]{2,1,0:T(8,128)(2,1)}, u32[]{:S(2)}) copy-start(bf16[2,256,128]{2,1,0:T(8,128)(2,1)} %param.16) | copy-start | bytes 393220
  7.2 37.0 %all-to-all-start = ((s32[128,1,1152]{2,1,0:T(1,128)}), s32[128,1,1152]{2,1,0:T(1,128)S(1)}, u32[]{:S(2)}, u32[]{:S(2)}) async-start(s32[128,1,1152]{2,1,0:T(1,128)} %all_to_all.26), calls=%async_computation | async-start | bytes 1179648 | tf_op jit(solution)/shard_map/all_to_all | solution.py:122
  29.6 15.6 %copy-start.14 = (s32[256,4]{0,1:T(4,128)S(1)}, s32[256,4]{0,1:T(4,128)}, u32[]{:S(2)}) copy-start(s32[256,4]{0,1:T(4,128)} %param.15) | copy-start | bytes 12292
  45.1 1.7 copy-start.12
  54.9 2.3 %copy-start.4 = (bf16[512,512]{1,0:T(8,128)(2,1)S(1)}, bf16[512,512]{1,0:T(8,128)(2,1)}, u32[]{:S(2)}) copy-start(bf16[512,512]{1,0:T(8,128)(2,1)} %param.19) | copy-start | bytes 1572868
  54.9 2.6 %copy-start.9 = (bf16[256,512]{1,0:T(8,128)(2,1)S(1)}, bf16[256,512]{1,0:T(8,128)(2,1)}, u32[]{:S(2)}) copy-start(bf16[256,512]{1,0:T(8,128)(2,1)} %param.27) | copy-start | bytes 786436
  57.5 1.7 copy-start.1
  59.2 1.3 copy-start.10
  77.7 5.1 %copy-start.13 = (s32[1792,4]{0,1:T(4,128)S(1)}, s32[1792,4]{0,1:T(4,128)}, u32[]{:S(2)}) copy-start(s32[1792,4]{0,1:T(4,128)} %copy-done.12) | copy-start | bytes 86020
  82.8 4.7 %copy-start.3 = (f32[1792,512]{0,1:T(8,128)S(1)}, f32[1792,512]{0,1:T(8,128)}, u32[]{:S(2)}) copy-start(f32[1792,512]{0,1:T(8,128)} %copy.61) | copy-start | bytes 11010052
  89.0 1.3 copy-start.2
  90.3 2.1 %copy-start.6 = (f32[512,64]{0,1:T(8,128)S(1)}, f32[512,64]{0,1:T(8,128)}, u32[]{:S(2)}) copy-start(f32[512,64]{0,1:T(8,128)} %fusion.41) | copy-start | bytes 393220
  94.4 5.5 %collective-permute-start = (f32[704,512]{1,0:T(8,128)}, f32[704,512]{1,0:T(8,128)S(1)}, u32[]{:S(2)}, u32[]{:S(2)}) collective-permute-start(f32[704,512]{1,0:T(8,128)} %constant_dynamic-update-slice_fusion.1), channel_id=1, source_target_pairs={{0,1},{1,0},{2,3},{3,2},{4,5},{5,4},{6,7},{7,6},{8,9},{9,8},{10,11... | collective-permute-start | bytes 4325384 | tf_op jit(solution)/shard_map/ppermute | solution.py:56
  162.0 9.0 %collective-permute-start.1 = (bf16[576,512]{1,0:T(8,128)(2,1)S(1)}, bf16[576,512]{1,0:T(8,128)(2,1)S(1)}, u32[]{:S(2)}, u32[]{:S(2)}) collective-permute-start(bf16[576,512]{1,0:T(8,128)(2,1)S(1)} %slice.90), channel_id=1, source_target_pairs={{0,1},{1,0},{2,3},{3,2},{4,5},{5,4},{6,7},{7,6},{8,9},{9,8},{10,11... | collective-permute-start | bytes 1769480 | tf_op jit(solution)/shard_map/ppermute | solution.py:77

commit v7 on v5

--- a/solution.py
+++ b/solution.py
@@ -112,8 +112,10 @@
         for hub_index in range(NHUB)
     ]
     table_codes = jnp.concatenate([codes, recv_codes] + hub_codes, axis=0)
-    table = decode(table_codes, complete_codebooks)
-    local_rows = table[:rows_dev]
+    local_rows = decode(codes, complete_codebooks)
+    table = jnp.concatenate(
+        [local_rows, decode(table_codes[rows_dev:], complete_codebooks)], axis=0
+    )
     blocks = table.reshape(-1, TB, model_width)
     tile_blocks = tiles.reshape(block_count, TPB, TB, TB)
     picked = blocks[tile_src]
@@ -149,17 +151,9 @@
     ).reshape(tile_count, TB, model_width)
     rel_rows = jnp.sum(grad_comp * picked.astype(jnp.float32), axis=1)
     rel_grad = jnp.zeros(rel_table.shape, jnp.float32).at[tile_rel].add(rel_rows)
-    src_hot = one_hot_codes(tile_src, blocks.shape[0], jnp.float32)
-    table_grad = jnp.einsum(
-        "ts,tjd->sjd",
-        src_hot,
-        grad_comp * scale[:, None, :],
-        precision=HIGHEST_PREC,
-        preferred_element_type=jnp.float32,
-    )
-    table_grad = table_grad.reshape(-1, model_width)
-    table_grad = table_grad.at[:rows_dev].add(grad_self)
-    book_grad = fold_books(table_codes, table_grad, code_count)
+    tile_codes = table_codes.reshape(-1, TB, book_count)[tile_src].reshape(-1, book_count)
+    contrib = (grad_comp * scale[:, None, :]).reshape(-1, model_width)
+    book_grad = fold_books(tile_codes, contrib, code_count) + fold_books(codes, grad_self, code_count)
     part_alpha = jnp.dot(
         rel_grad, basis.T, precision=HIGHEST_PREC, preferred_element_type=jnp.float32
     )

time: 173 us -> 174 us (level)
  waiting for transfers between devices: 14 us -> 5.21 us
  local copies, waits for them, and re-layouts: 35.4 us -> 41.1 us
  blocking collectives: 62.9 us -> 66.1 us
    reshape x0 -> x4, local copies, waits for them, and re-layouts: none -> 12.4 us  [the longest x2 10.7 us: shards(): grad_comp = jnp.einsum('btji,bjd->btid', tile_blocks, grad_blocks, prefer...]
    all_to_all x1, waiting for transfers between devices: 10.9 us -> 2.04 us  [shards(): incoming = lax.all_to_all(payload, 'dom', 0, 0, tiled=True)]
    mul x0 -> x2, local copies, waits for them, and re-layouts: none -> 7.51 us  [shards(): picked.astype(jnp.float32) * scale[:, None, :]]
    another operation x4 -> x0, local copies, waits for them, and re-layouts: 6.26 us -> none  [the longest x2 5.98 us: shards(): blocks = table.reshape(-1, TB, model_width)]
    scatter-add x1 -> x0, local copies, waits for them, and re-layouts: 5.18 us -> none  [shards(): table_grad = table_grad.at[:rows_dev].add(grad_self)]
    dot_general x1 -> x0, matrix products: 4.77 us -> none  [shards(): jnp.einsum('ts,tjd->sjd', src_hot, grad_comp * scale[:, None, :], precisi...]
    dot_general x1 -> x0, local copies, waits for them, and re-layouts: 3.92 us -> none  [shards(): jnp.einsum('ts,tjd->sjd', src_hot, grad_comp * scale[:, None, :], precisi...]
    all_to_all x1, blocking collectives: 31 us -> 34.3 us  [all_sum(): received = lax.all_to_all(chunks, 'dom', 0, 0, tiled=True)]
  transfers between devices with their start and end apart: 3 -> 3, of which waited for: 3 -> 3; matrix products, arithmetic and copies ran while one was open for 3% -> 8% of each run, Pallas kernels for 0% -> 0%
where the time goes in v7:
time: 174 us; the launch traced here: 173 us
  blocking collectives  66.1 us (38%)
  local copies, waits for them, and re-layouts  41.1 us (24%)
  matrix products  24.8 us (14%)
  starting transfers between devices  22.8 us (13%)
  other arithmetic  8.08 us (5%)
  waiting for transfers between devices  5.21 us (3%)
  between operations  5.13 us (3%)
    all_to_all x1, blocking collectives, all_sum(): received = lax.all_to_all(chunks, 'dom', 0, 0, tiled=True)  34.3 us
    all_to_all x1, blocking collectives, all_sum(): lax.all_to_all(spread, 'dom', 0, 0, tiled=True).reshape(rows, width)  29.2 us
    all_to_all x1, starting transfers between devices, shards(): incoming = lax.all_to_all(payload, 'dom', 0, 0, tiled=True)  16.5 us
    reshape x2, local copies, waits for them, and re-layouts, shards(): grad_comp = jnp.einsum('btji,bjd->btid', tile_blocks, grad_blocks, prefer...  10.7 us
    mul x2, local copies, waits for them, and re-layouts, shards(): picked.astype(jnp.float32) * scale[:, None, :]  7.51 us
    unnamed x49, local copies, waits for them, and re-layouts  6.61 us
    dot_general x2, matrix products, fold_books(): jnp.einsum('fco,fcg->cog', indicator_rows, lower_bound, preferred_element...  5.59 us
    ppermute x1, starting transfers between devices, all_sum(): other_dense = lax.ppermute(own_dense, 'sub', swap)  3.86 us
  transfers between devices with their start and end apart: 3, of which 3 were waited for; matrix products, arithmetic and copies ran while one was open for 8% of the time, Pallas kernels for 0%

profile of v7, /device:TPU:1, one launch (start us, length us, event | category | flops | bytes accessed | tf_op | source)
XLA Modules:
  0.0 173.2 jit_solution(13658627769653560103)
XLA Ops:
  0.6 0.9 copy.51
  1.5 0.7 compare_select_fusion
  2.6 2.8 %gather_fusion = s32[1024,4]{1,0:T(8,128)S(1)} fusion(s32[256,4]{1,0:T(8,128)S(1)} %copy.51, s32[1024]{0:T(1024)S(1)} %broadcast_clamp_fusion), kind=kCustom, calls=%fused_computation | custom fusion | bytes 36864 | tf_op jit(solution)/shard_map/gather | solution.py:103
  5.9 1.2 all_to_all.14
  7.2 16.5 %all-to-all-start = ((s32[128,1,1152]{2,1,0:T(1,128)}), s32[128,1,1152]{2,1,0:T(1,128)S(1)}, u32[]{:S(2)}, u32[]{:S(2)}) async-start(s32[128,1,1152]{2,1,0:T(1,128)} %all_to_all.14), calls=%async_computation | async-start | bytes 1179648 | tf_op jit(solution)/shard_map/all_to_all | solution.py:108
  23.7 0.6 fusion.35
  26.9 2.6 %all_gather.3 = bf16[4,256,128]{2,1,0:T(8,128)(2,1)S(1)} all-gather(bf16[2,256,128]{2,1,0:T(8,128)(2,1)S(1)} %copy-done.15), channel_id=1, replica_groups=mesh['dom'=128,'sub'=2] {'sub'}, dimensions={0}, use_global_device_ids=true | all-gather | bytes 393216 | tf_op jit(solution)/shard_map/all_gather | solution.py:98
  30.6 1.9 %fusion.36 = f32[512,512]{1,0:T(8,128)S(1)} fusion(f32[512,64]{0,1:T(8,128)S(1)} %copy-done.7, f32[64,512]{1,0:T(8,128)} %param.16), kind=kOutput, calls=%fused_computation.84 | convolution fusion | flops 201326592 | bytes 1310720 | tf_op jit(solution)/shard_map/dot_general | solution.py:99
  33.3 2.6 %mul.62 = f32[16,128,512]{1,0,2:T(8,128)} broadcast(f32[16,512]{0,1:T(8,128)S(1)} %copy.68), dimensions={0,2} | broadcast | bytes 4227072 | tf_op jit(solution)/shard_map/mul | solution.py:123
  35.9 4.9 %mul.63 = f32[2048,4,128]{0,2,1:T(8,128)} reshape(f32[16,128,512]{1,0,2:T(8,128)} %mul.62) | data formatting | bytes 8388608 | tf_op jit(solution)/shard_map/mul | solution.py:123
  42.2 2.0 %all-to-all-done = s32[128,1,1152]{2,1,0:T(1,128)S(1)} async-done(((s32[128,1,1152]{2,1,0:T(1,128)}), s32[128,1,1152]{2,1,0:T(1,128)S(1)}, u32[]{:S(2)}, u32[]{:S(2)}) %all-to-all-start) | async-done | bytes 589856 | tf_op jit(solution)/shard_map/all_to_all | solution.py:108
  45.1 2.2 %fusion.8 = bf16[4,1536,128]{1,2,0:T(8,128)(2,1)S(1)} fusion(bf16[4,256,128]{2,1,0:T(8,128)(2,1)S(1)} %copy-done.13, s32[1536,4]{0,1:T(4,128)S(1)} %pad_add_fusion), kind=kOutput, calls=%fused_computation.18 | convolution fusion | flops 405012480 | bytes 1859584 | tf_op jit(solution)/shard_map/feu,euq->feq/dot_general | solution.py:21
  47.3 1.6 copy.61
  48.9 1.5 pad_maximum_fusion
  50.5 2.0 %gather_fusion.1 = bf16[16,128,512]{2,1,0:T(8,128)(2,1)} fusion(bf16[14,128,512]{2,1,0:T(8,128)(2,1)S(1)} %bitcast.90, s32[1024]{0:T(1024)S(1)} %pad_clamp_fusion.1), kind=kCustom, calls=%fused_computation.1 | custom fusion | bytes 4194368 | tf_op jit(solution)/shard_map/gather | solution.py:121
  52.5 2.4 %fusion.19 = bf16[2,512,128]{1,2,0:T(8,128)(2,1)S(1)} fusion(bf16[2,8,128,128]{3,2,1,0:T(8,128)(2,1)} %bitcast.103, bf16[2,8,128,512]{3,2,1,0:T(8,128)(2,1)} %bitcast.91, f32[2,8,512]{2,1,0:T(8,128)S(1)} %bitcast.105), kind=kOutput, calls=%fused_computation.32 | convolution fusion | flops 271712256 | bytes 2916352 | tf_op jit(solution)/shard_map/btij,btjd->bid/dot_general | solution.py:124
  55.2 1.1 multiply_convert_fusion.5
  56.7 1.1 convolution_bitcast_fusion
  57.8 1.3 fusion.38
  59.8 2.7 %fusion.4 = (f32[2,8,512]{2,1,0:T(8,128)S(1)}, f32[2,512,1024]{1,2,0}) fusion(bf16[2,8,128,512]{3,2,1,0:T(8,128)(2,1)S(1)} %bitcast.92, bf16[2,128,1024]{1,2,0:T(8,128)(2,1)S(1)} %bitcast.96, bf16[2,128,512]{2,1,0:T(8,128)(2,1)S(1)} %bitcast.99), kind=kOutput, calls=%fused_computation.13 | convolution fusion | flops 271572992 | bytes 7110656
  62.5 1.1 scatter_custom_fusion
  63.6 1.4 fusion.40
  65.1 1.7 fusion.41
  66.7 5.3 %reshape.155 = f32[2048,4,128]{2,1,0:T(4,128)} reshape(f32[2,8,128,512]{3,2,1,0:T(8,128)} %bitcast.89) | data formatting | bytes 8388608 | tf_op jit(solution)/shard_map/reshape | solution.py:151
  72.1 5.3 %copy.69 = f32[2048,4,128]{0,2,1:T(8,128)} copy(f32[2048,4,128]{2,1,0:T(4,128)} %reshape.155) | data formatting | bytes 8388608 | tf_op jit(solution)/shard_map/reshape | solution.py:151
  77.4 0.6 gather_fusion.3
  78.0 5.3 %fusion = f32[4,256,128]{2,1,0:T(8,128)S(1)} fusion(s32[2048,4]{0,1:T(4,128)S(1)} %bitcast.87, f32[2048,4,128]{0,2,1:T(8,128)} %copy.69, f32[2048,4,128]{0,2,1:T(8,128)} %mul.63), kind=kOutput, calls=%fused_computation.6 | convolution fusion | flops 544210944 | bytes 8945664 | tf_op jit(solution)/shard_map/fco,fcg->cog/dot_general | solution.py:36
  83.3 0.6 copy-done.2
  83.9 1.8 %fusion.18 = f32[4,256,128]{2,1,0:T(8,128)S(1)} fusion(f32[4,256,128]{2,1,0:T(8,128)S(1)} %fusion, f32[2048,4,128]{0,2,1:T(8,128)S(1)} %copy-done.2, f32[2048,4,128]{0,2,1:T(8,128)S(1)} %copy-done.1, s32[2048,4]{0,1:T(4,128)S(1)} %bitcast.88), kind=kOutput, calls=%fused_computation.31 | convolution fusion | flops 541196288 | bytes 9469952 | tf_op jit(solution)/shard_map/fco,fcg->cog/dot_general | solution.py:33
  86.4 1.1 reshape.153
  87.5 1.1 dynamic-slice_dynamic-update-slice_fusion.1
  88.6 1.1 dynamic-slice_dynamic-update-slice_fusion
  89.7 0.7 bitcast_dynamic-update-slice_fusion
  90.4 0.6 dynamic-slice_dynamic-update-slice_fusion.4
  91.0 0.7 constant_dynamic-update-slice_fusion.1
  91.7 2.5 %collective-permute-start = (f32[704,512]{1,0:T(8,128)}, f32[704,512]{1,0:T(8,128)S(1)}, u32[]{:S(2)}, u32[]{:S(2)}) collective-permute-start(f32[704,512]{1,0:T(8,128)} %constant_dynamic-update-slice_fusion.1), channel_id=1, source_target_pairs={{0,1},{1,0},{2,3},{3,2},{4,5},{5,4},{6,7},{7,6},{8,9},{9,8},{10,11... | collective-permute-start | bytes 4325384 | tf_op jit(solution)/shard_map/ppermute | solution.py:54
  94.2 0.7 constant_dynamic-update-slice_fusion
  95.0 2.3 %collective-permute-done = f32[704,512]{1,0:T(8,128)S(1)} collective-permute-done((f32[704,512]{1,0:T(8,128)}, f32[704,512]{1,0:T(8,128)S(1)}, u32[]{:S(2)}, u32[]{:S(2)}) %collective-permute-start) | collective-permute-done | bytes 1441824 | tf_op jit(solution)/shard_map/ppermute | solution.py:54
  97.3 1.6 add_convert_fusion
  99.4 34.3 %all_to_all.22 = bf16[128,22,128]{2,1,0:T(8,128)(2,1)S(1)} all-to-all(bf16[128,22,128]{2,1,0:T(8,128)(2,1)S(1)} %reshape.159), channel_id=1, replica_groups=mesh['dom'=128,'sub'=2] {'dom'}, dimensions={0} | all-to-all | bytes 1441792 | tf_op jit(solution)/shard_map/all_to_all | solution.py:57
  133.9 29.2 %all_to_all.23 = bf16[128,22,128]{2,1,0:T(8,128)(2,1)S(1)} all-to-all(bf16[128,22,128]{2,1,0:T(8,128)(2,1)S(1)} %broadcast_in_dim.59), channel_id=1, replica_groups=mesh['dom'=128,'sub'=2] {'dom'}, dimensions={0} | all-to-all | bytes 1441792 | tf_op jit(solution)/shard_map/all_to_all | solution.py:60
  163.7 3.9 %collective-permute-start.1 = (bf16[576,512]{1,0:T(8,128)(2,1)S(1)}, bf16[576,512]{1,0:T(8,128)(2,1)S(1)}, u32[]{:S(2)}, u32[]{:S(2)}) collective-permute-start(bf16[576,512]{1,0:T(8,128)(2,1)S(1)} %slice.63), channel_id=1, source_target_pairs={{0,1},{1,0},{2,3},{3,2},{4,5},{5,4},{6,7},{7,6},{8,9},{9,8},{10,11... | collective-permute-start | bytes 1769480 | tf_op jit(solution)/shard_map/ppermute | solution.py:63
  167.6 0.7 reshape.166
  168.3 0.9 collective-permute-done.1
  169.7 0.8 copy.74
  170.5 0.7 pad_maximum_fusion.4
  171.1 1.0 pad_maximum_fusion.2
  172.2 1.0 pad_maximum_fusion.1
  (92 shorter events, 7.5 us)
Async XLA Ops:
  0.6 54.6 %copy-start = (bf16[512,512]{1,0:T(8,128)(2,1)S(1)}, bf16[512,512]{1,0:T(8,128)(2,1)}, u32[]{:S(2)}) copy-start(bf16[512,512]{1,0:T(8,128)(2,1)} %param.18) | copy-start | bytes 1572868
  2.5 3.0 %copy-start.20 = (s32[1,1,128]{2,1,0:T(1,128)S(1)}, s32[1,1,128]{2,1,0:T(1,128)}, u32[]{:S(2)}) copy-start(s32[1,1,128]{2,1,0:T(1,128)} %param.23) | copy-start | bytes 1540
  5.8 17.9 %copy-start.17 = (s32[2]{0:T(128)S(1)}, s32[2]{0:T(128)}, u32[]{:S(2)}) copy-start(s32[2]{0:T(128)} %param.24) | copy-start | bytes 28
  5.8 21.0 %copy-start.15 = (bf16[2,256,128]{2,1,0:T(8,128)(2,1)S(1)}, bf16[2,256,128]{2,1,0:T(8,128)(2,1)}, u32[]{:S(2)}) copy-start(bf16[2,256,128]{2,1,0:T(8,128)(2,1)} %param.14) | copy-start | bytes 393220
  5.8 23.6 %copy-start.16 = (s32[256,4]{0,1:T(4,128)S(1)}, s32[256,4]{0,1:T(4,128)}, u32[]{:S(2)}) copy-start(s32[256,4]{0,1:T(4,128)} %param.13) | copy-start | bytes 12292
  5.9 24.4 %copy-start.10 = (bf16[16,128,128]{2,1,0:T(8,128)(2,1)S(1)}, bf16[16,128,128]{2,1,0:T(8,128)(2,1)}, u32[]{:S(2)}) copy-start(bf16[16,128,128]{2,1,0:T(8,128)(2,1)} %param.19) | copy-start | bytes 1572868
  7.2 23.4 %copy-start.18 = (s32[16]{0:T(128)S(1)}, s32[16]{0:T(128)}, u32[]{:S(2)}) copy-start(s32[16]{0:T(128)} %param.21) | copy-start | bytes 196
  7.2 23.4 %copy-start.19 = (s32[16]{0:T(128)S(1)}, s32[16]{0:T(128)}, u32[]{:S(2)}) copy-start(s32[16]{0:T(128)} %param.20) | copy-start | bytes 196
  7.2 23.5 %copy-start.7 = (f32[512,64]{0,1:T(8,128)S(1)}, f32[512,64]{0,1:T(8,128)}, u32[]{:S(2)}) copy-start(f32[512,64]{0,1:T(8,128)} %param.15) | copy-start | bytes 393220
  7.2 37.0 %all-to-all-start = ((s32[128,1,1152]{2,1,0:T(1,128)}), s32[128,1,1152]{2,1,0:T(1,128)S(1)}, u32[]{:S(2)}, u32[]{:S(2)}) async-start(s32[128,1,1152]{2,1,0:T(1,128)} %all_to_all.14), calls=%async_computation | async-start | bytes 1179648 | tf_op jit(solution)/shard_map/all_to_all | solution.py:108
  29.4 0.7 copy-start.12
  40.8 4.3 %copy-start.13 = (bf16[4,256,128]{2,1,0:T(8,128)(2,1)S(1)}, bf16[4,256,128]{2,1,0:T(8,128)(2,1)}, u32[]{:S(2)}) copy-start(bf16[4,256,128]{2,1,0:T(8,128)(2,1)} %copy-done.12) | copy-start | bytes 786436
  52.5 2.4 %copy-start.5 = (bf16[512,512]{1,0:T(8,128)(2,1)S(1)}, bf16[512,512]{1,0:T(8,128)(2,1)}, u32[]{:S(2)}) copy-start(bf16[512,512]{1,0:T(8,128)(2,1)} %param.17) | copy-start | bytes 1572868
  52.5 2.7 %copy-start.14 = (bf16[256,512]{1,0:T(8,128)(2,1)S(1)}, bf16[256,512]{1,0:T(8,128)(2,1)}, u32[]{:S(2)}) copy-start(bf16[256,512]{1,0:T(8,128)(2,1)} %param.25) | copy-start | bytes 786436
  57.8 2.0 %copy-start.3 = (bf16[16,128,512]{2,1,0:T(8,128)(2,1)S(1)}, bf16[16,128,512]{2,1,0:T(8,128)(2,1)}, u32[]{:S(2)}) copy-start(bf16[16,128,512]{2,1,0:T(8,128)(2,1)} %gather_fusion.1) | copy-start | bytes 6291460
  59.8 3.8 %copy-start.8 = (f32[512,64]{0,1:T(8,128)S(1)}, f32[512,64]{0,1:T(8,128)}, u32[]{:S(2)}) copy-start(f32[512,64]{0,1:T(8,128)} %param.15) | copy-start | bytes 393220
  62.5 2.6 %copy-start.11 = (f32[64,512]{1,0:T(8,128)S(1)}, f32[64,512]{1,0:T(8,128)}, u32[]{:S(2)}) copy-start(f32[64,512]{1,0:T(8,128)} %param.16) | copy-start | bytes 393220
  78.0 5.3 %copy-start.1 = (f32[2048,4,128]{0,2,1:T(8,128)S(1)}, f32[2048,4,128]{0,2,1:T(8,128)}, u32[]{:S(2)}) copy-start(f32[2048,4,128]{0,2,1:T(8,128)} %mul.63) | copy-start | bytes 12582916
  78.0 5.9 %copy-start.2 = (f32[2048,4,128]{0,2,1:T(8,128)S(1)}, f32[2048,4,128]{0,2,1:T(8,128)}, u32[]{:S(2)}) copy-start(f32[2048,4,128]{0,2,1:T(8,128)} %copy.69) | copy-start | bytes 12582916
  83.9 1.8 %copy-start.6 = (f32[32,4,8,128]{3,2,1,0:T(8,128)S(1)}, f32[32,4,8,128]{3,2,1,0:T(8,128)}, u32[]{:S(2)}) copy-start(f32[32,4,8,128]{3,2,1,0:T(8,128)} %convolution_bitcast_fusion) | copy-start | bytes 1572868
  86.0 1.5 copy-start.4
  87.5 2.2 %copy-start.9 = (f32[512,64]{0,1:T(8,128)S(1)}, f32[512,64]{0,1:T(8,128)}, u32[]{:S(2)}) copy-start(f32[512,64]{0,1:T(8,128)} %fusion.40) | copy-start | bytes 393220
  91.7 5.5 %collective-permute-start = (f32[704,512]{1,0:T(8,128)}, f32[704,512]{1,0:T(8,128)S(1)}, u32[]{:S(2)}, u32[]{:S(2)}) collective-permute-start(f32[704,512]{1,0:T(8,128)} %constant_dynamic-update-slice_fusion.1), channel_id=1, source_target_pairs={{0,1},{1,0},{2,3},{3,2},{4,5},{5,4},{6,7},{7,6},{8,9},{9,8},{10,11... | collective-permute-start | bytes 4325384 | tf_op jit(solution)/shard_map/ppermute | solution.py:54
  163.7 5.5 %collective-permute-start.1 = (bf16[576,512]{1,0:T(8,128)(2,1)S(1)}, bf16[576,512]{1,0:T(8,128)(2,1)S(1)}, u32[]{:S(2)}, u32[]{:S(2)}) collective-permute-start(bf16[576,512]{1,0:T(8,128)(2,1)S(1)} %slice.63), channel_id=1, source_target_pairs={{0,1},{1,0},{2,3},{3,2},{4,5},{5,4},{6,7},{7,6},{8,9},{9,8},{10,11... | collective-permute-start | bytes 1769480 | tf_op jit(solution)/shard_map/ppermute | solution.py:63

commit v8 on v6

--- a/solution.py
+++ b/solution.py
@@ -126,8 +126,10 @@
         for hub_index in range(NHUB)
     ]
     table_codes = jnp.concatenate([codes, recv_codes] + hub_codes, axis=0)
-    table = decode(table_codes, complete_codebooks)
-    local_rows = table[:rows_dev]
+    local_rows = decode(codes, complete_codebooks)
+    table = jnp.concatenate(
+        [local_rows, decode(table_codes[rows_dev:], complete_codebooks)], axis=0
+    )
     blocks = table.reshape(-1, TB, model_width)
     tile_blocks = tiles.reshape(block_count, TPB, TB, TB)
     picked = blocks[tile_src]
@@ -163,17 +165,9 @@
     ).reshape(tile_count, TB, model_width)
     rel_rows = jnp.sum(grad_comp * picked.astype(jnp.float32), axis=1)
     rel_grad = jnp.zeros(rel_table.shape, jnp.float32).at[tile_rel].add(rel_rows)
-    src_hot = one_hot_codes(tile_src, blocks.shape[0], jnp.float32)
-    table_grad = jnp.einsum(
-        "ts,tjd->sjd",
-        src_hot,
-        grad_comp * scale[:, None, :],
-        precision=HIGHEST_PREC,
-        preferred_element_type=jnp.float32,
-    )
-    table_grad = table_grad.reshape(-1, model_width)
-    table_grad = table_grad.at[:rows_dev].add(grad_self)
-    book_grad = fold_books(table_codes, table_grad, code_count)
+    tile_codes = table_codes.reshape(-1, TB, book_count)[tile_src].reshape(-1, book_count)
+    contrib = (grad_comp * scale[:, None, :]).reshape(-1, model_width)
+    book_grad = fold_books(tile_codes, contrib, code_count) + fold_books(codes, grad_self, code_count)
     part_alpha = jnp.dot(
         rel_grad, basis.T, precision=HIGHEST_PREC, preferred_element_type=jnp.float32
     )
@@ -207,7 +201,7 @@
     found = split_mesh(mesh)
     assert found is not None
     fine_mesh, (ny, nx, nz) = found
-    dom_axes = (("dx", nx), ("dy", ny), ("dz", nz))
+    dom_axes = ((("dy", "dx"), ny * nx), ("dz", nz))
 
     def run(*args):
         return shards(dom_axes, *args)

time: 176 us -> 163 us (0.926)
  waiting for transfers between devices: 14 us -> 5.22 us
  blocking collectives: 62.5 us -> 56.5 us
  local copies, waits for them, and re-layouts: 34.5 us -> 40.1 us
  starting transfers between devices: 26.4 us -> 23.5 us
    reshape x0 -> x5, local copies, waits for them, and re-layouts: none -> 12.5 us  [the longest x2 10.6 us: shards(): grad_comp = jnp.einsum('btji,bjd->btid', tile_blocks, grad_blocks, prefer...]
    all_to_all x1, waiting for transfers between devices: 10.9 us -> 2.06 us  [shards(): incoming = lax.all_to_all(payload, DOM, 0, 0, tiled=True)]
    mul x0 -> x2, local copies, waits for them, and re-layouts: none -> 7.49 us  [shards(): picked.astype(jnp.float32) * scale[:, None, :]]
    another operation x4 -> x0, local copies, waits for them, and re-layouts: 6.3 us -> none  [the longest x2 6.01 us: shards(): blocks = table.reshape(-1, TB, model_width)]
    scatter-add x1 -> x0, local copies, waits for them, and re-layouts: 5.14 us -> none  [shards(): table_grad = table_grad.at[:rows_dev].add(grad_self)]
    dot_general x1 -> x0, matrix products: 4.77 us -> none  [shards(): jnp.einsum('ts,tjd->sjd', src_hot, grad_comp * scale[:, None, :], precisi...]
    dot_general x1 -> x0, local copies, waits for them, and re-layouts: 3.92 us -> none  [shards(): jnp.einsum('ts,tjd->sjd', src_hot, grad_comp * scale[:, None, :], precisi...]
    all_to_all x3 -> x2, blocking collectives: 27.5 us -> 23.7 us  [all_sum(): piece = lax.all_to_all(spread, axis, 0, 0, tiled=True).reshape(shape)]
  transfers between devices with their start and end apart: 3 -> 3, of which waited for: 3 -> 3; matrix products, arithmetic and copies ran while one was open for 3% -> 8% of each run, Pallas kernels for 0% -> 0%
where the time goes in v8:
time: 163 us; the launch traced here: 162 us
  blocking collectives  56.5 us (35%)
  local copies, waits for them, and re-layouts  40.1 us (25%)
  matrix products  24 us (15%)
  starting transfers between devices  23.5 us (14%)
  other arithmetic  8.05 us (5%)
  waiting for transfers between devices  5.22 us (3%)
  between operations  5.15 us (3%)
    all_to_all x2, blocking collectives, all_sum(): received = lax.all_to_all(chunks, axis, 0, 0, tiled=True)  30.2 us
    all_to_all x2, blocking collectives, all_sum(): piece = lax.all_to_all(spread, axis, 0, 0, tiled=True).reshape(shape)  23.7 us
    all_to_all x1, starting transfers between devices, shards(): incoming = lax.all_to_all(payload, DOM, 0, 0, tiled=True)  16.5 us
    reshape x2, local copies, waits for them, and re-layouts, shards(): grad_comp = jnp.einsum('btji,bjd->btid', tile_blocks, grad_blocks, prefer...  10.6 us
    mul x2, local copies, waits for them, and re-layouts, shards(): picked.astype(jnp.float32) * scale[:, None, :]  7.49 us
    unnamed x51, local copies, waits for them, and re-layouts  6.59 us
    dot_general x2, matrix products, fold_books(): jnp.einsum('fco,fcg->cog', indicator_rows, lower_bound, preferred_element...  5.59 us
    ppermute x1, starting transfers between devices, all_sum(): other_dense = lax.ppermute(own_dense, 'sub', swap)  4.51 us
  transfers between devices with their start and end apart: 3, of which 3 were waited for; matrix products, arithmetic and copies ran while one was open for 8% of the time, Pallas kernels for 0%

profile of v8, /device:TPU:1, one launch (start us, length us, event | category | flops | bytes accessed | tf_op | source)
XLA Modules:
  0.0 162.4 jit_solution(2748970379850205767)
XLA Ops:
  0.6 0.9 copy.51
  1.5 0.7 compare_select_fusion
  2.6 2.8 %gather_fusion = s32[1024,4]{1,0:T(8,128)S(1)} fusion(s32[256,4]{1,0:T(8,128)S(1)} %copy.51, s32[1024]{0:T(1024)S(1)} %broadcast_clamp_fusion), kind=kCustom, calls=%fused_computation | custom fusion | bytes 36864 | tf_op jit(solution)/shard_map/gather | solution.py:117
  5.9 1.2 all_to_all.20
  7.2 16.5 %all-to-all-start = ((s32[128,1,1152]{2,1,0:T(1,128)}), s32[128,1,1152]{2,1,0:T(1,128)S(1)}, u32[]{:S(2)}, u32[]{:S(2)}) async-start(s32[128,1,1152]{2,1,0:T(1,128)} %all_to_all.20), calls=%async_computation | async-start | bytes 1179648 | tf_op jit(solution)/shard_map/all_to_all | solution.py:122
  26.9 2.6 %all_gather.3 = bf16[4,256,128]{2,1,0:T(8,128)(2,1)S(1)} all-gather(bf16[2,256,128]{2,1,0:T(8,128)(2,1)S(1)} %copy-done.16), channel_id=1, replica_groups=mesh['dy'=4,'dx'=4,'dz'=8,'sub'=2] {'sub'}, dimensions={0}, use_global_device_ids=true | all-gather | bytes 393216 | tf_op jit(solution)/shard_map/all_gather | solution.py:112
  30.6 1.9 %fusion.36 = f32[512,512]{1,0:T(8,128)S(1)} fusion(f32[512,64]{0,1:T(8,128)S(1)} %copy-done.8, f32[64,512]{1,0:T(8,128)} %param.16), kind=kOutput, calls=%fused_computation.85 | convolution fusion | flops 201326592 | bytes 1310720 | tf_op jit(solution)/shard_map/dot_general | solution.py:113
  33.3 2.6 %mul.62 = f32[16,128,512]{1,0,2:T(8,128)} broadcast(f32[16,512]{0,1:T(8,128)S(1)} %copy.68), dimensions={0,2} | broadcast | bytes 4227072 | tf_op jit(solution)/shard_map/mul | solution.py:137
  35.9 4.9 %mul.63 = f32[2048,4,128]{0,2,1:T(8,128)} reshape(f32[16,128,512]{1,0,2:T(8,128)} %mul.62) | data formatting | bytes 8388608 | tf_op jit(solution)/shard_map/mul | solution.py:137
  42.1 2.1 %all-to-all-done = s32[128,1,1152]{2,1,0:T(1,128)S(1)} async-done(((s32[128,1,1152]{2,1,0:T(1,128)}), s32[128,1,1152]{2,1,0:T(1,128)S(1)}, u32[]{:S(2)}, u32[]{:S(2)}) %all-to-all-start) | async-done | bytes 589856 | tf_op jit(solution)/shard_map/all_to_all | solution.py:122
  45.1 2.2 %fusion.8 = bf16[4,1536,128]{1,2,0:T(8,128)(2,1)S(1)} fusion(bf16[4,256,128]{2,1,0:T(8,128)(2,1)S(1)} %copy-done.14, s32[1536,4]{0,1:T(4,128)S(1)} %pad_add_fusion), kind=kOutput, calls=%fused_computation.18 | convolution fusion | flops 405012480 | bytes 1859584 | tf_op jit(solution)/shard_map/feu,euq->feq/dot_general | solution.py:23
  47.3 1.6 copy.61
  48.9 1.5 pad_maximum_fusion
  50.5 2.0 %gather_fusion.1 = bf16[16,128,512]{2,1,0:T(8,128)(2,1)} fusion(bf16[14,128,512]{2,1,0:T(8,128)(2,1)S(1)} %bitcast.90, s32[1024]{0:T(1024)S(1)} %pad_clamp_fusion.1), kind=kCustom, calls=%fused_computation.1 | custom fusion | bytes 4194368 | tf_op jit(solution)/shard_map/gather | solution.py:135
  52.5 2.4 %fusion.19 = bf16[2,512,128]{1,2,0:T(8,128)(2,1)S(1)} fusion(bf16[2,8,128,128]{3,2,1,0:T(8,128)(2,1)} %bitcast.103, bf16[2,8,128,512]{3,2,1,0:T(8,128)(2,1)} %bitcast.91, f32[2,8,512]{2,1,0:T(8,128)S(1)} %bitcast.105), kind=kOutput, calls=%fused_computation.33 | convolution fusion | flops 271712256 | bytes 2916352 | tf_op jit(solution)/shard_map/btij,btjd->bid/dot_general | solution.py:138
  55.2 1.1 multiply_convert_fusion.5
  56.6 1.1 convolution_bitcast_fusion
  57.8 1.3 fusion.38
  59.8 2.7 %fusion.4 = (f32[2,8,512]{2,1,0:T(8,128)S(1)}, f32[2,512,1024]{1,2,0}) fusion(bf16[2,8,128,512]{3,2,1,0:T(8,128)(2,1)S(1)} %bitcast.92, bf16[2,128,1024]{1,2,0:T(8,128)(2,1)S(1)} %bitcast.96, bf16[2,128,512]{2,1,0:T(8,128)(2,1)S(1)} %bitcast.99), kind=kOutput, calls=%fused_computation.13 | convolution fusion | flops 271572992 | bytes 7110656
  62.4 1.1 scatter_custom_fusion
  63.6 1.5 fusion.40
  65.0 1.0 fusion.41
  66.0 5.3 %reshape.160 = f32[2048,4,128]{2,1,0:T(4,128)} reshape(f32[2,8,128,512]{3,2,1,0:T(8,128)} %bitcast.89) | data formatting | bytes 8388608 | tf_op jit(solution)/shard_map/reshape | solution.py:165
  71.3 5.3 %copy.69 = f32[2048,4,128]{0,2,1:T(8,128)} copy(f32[2048,4,128]{2,1,0:T(4,128)} %reshape.160) | data formatting | bytes 8388608 | tf_op jit(solution)/shard_map/reshape | solution.py:165
  77.2 5.3 %fusion = f32[4,256,128]{2,1,0:T(8,128)S(1)} fusion(s32[2048,4]{0,1:T(4,128)S(1)} %bitcast.87, f32[2048,4,128]{0,2,1:T(8,128)} %copy.69, f32[2048,4,128]{0,2,1:T(8,128)} %mul.63), kind=kOutput, calls=%fused_computation.6 | convolution fusion | flops 544210944 | bytes 8945664 | tf_op jit(solution)/shard_map/fco,fcg->cog/dot_general | solution.py:38
  82.5 0.6 copy-done.2
  83.1 1.8 %fusion.18 = f32[4,256,128]{2,1,0:T(8,128)S(1)} fusion(f32[4,256,128]{2,1,0:T(8,128)S(1)} %fusion, f32[2048,4,128]{0,2,1:T(8,128)S(1)} %copy-done.2, f32[2048,4,128]{0,2,1:T(8,128)S(1)} %copy-done.1, s32[2048,4]{0,1:T(4,128)S(1)} %bitcast.88), kind=kOutput, calls=%fused_computation.32 | convolution fusion | flops 541196288 | bytes 9469952 | tf_op jit(solution)/shard_map/fco,fcg->cog/dot_general | solution.py:35
  85.6 0.7 constant_dynamic-slice_fusion
  86.5 1.0 dynamic-slice_dynamic-update-slice_fusion.1
  87.5 1.1 dynamic-slice_dynamic-update-slice_fusion
  88.6 0.7 bitcast_dynamic-update-slice_fusion
  89.3 0.7 dynamic-slice_dynamic-update-slice_fusion.4
  89.9 0.7 constant_dynamic-update-slice_fusion.1
  90.7 2.5 %collective-permute-start = (f32[704,512]{1,0:T(8,128)}, f32[704,512]{1,0:T(8,128)S(1)}, u32[]{:S(2)}, u32[]{:S(2)}) collective-permute-start(f32[704,512]{1,0:T(8,128)} %constant_dynamic-update-slice_fusion.1), channel_id=1, source_target_pairs={{0,1},{1,0},{2,3},{3,2},{4,5},{5,4},{6,7},{7,6},{8,9},{9,8},{10,11... | collective-permute-start | bytes 4325384 | tf_op jit(solution)/shard_map/ppermute | solution.py:56
  93.2 0.7 constant_dynamic-update-slice_fusion
  93.9 2.3 %collective-permute-done = f32[704,512]{1,0:T(8,128)S(1)} collective-permute-done((f32[704,512]{1,0:T(8,128)}, f32[704,512]{1,0:T(8,128)S(1)}, u32[]{:S(2)}, u32[]{:S(2)}) %collective-permute-start) | collective-permute-done | bytes 1441824 | tf_op jit(solution)/shard_map/ppermute | solution.py:56
  96.2 1.6 add_convert_fusion
  97.9 16.7 %all_to_all.32 = bf16[16,44,512]{2,1,0:T(8,128)(2,1)S(1)} all-to-all(bf16[16,44,512]{2,1,0:T(8,128)(2,1)S(1)} %convert_element_type.108), channel_id=1, replica_groups=mesh['dy'=4,'dx'=4,'dz'=8,'sub'=2] {'dy','dx'}, dimensions={0} | all-to-all | bytes 1441792 | tf_op jit(solution)/shard_map/all_to_all | solution.py:68
  114.8 13.5 %all_to_all.33 = f32[8,11,256]{2,1,0:T(8,128)S(1)} all-to-all(f32[8,11,256]{2,1,0:T(8,128)S(1)} %reshape.164), channel_id=1, replica_groups=mesh['dy'=4,'dx'=4,'dz'=8,'sub'=2] {'dz'}, dimensions={0} | all-to-all | bytes 180224 | tf_op jit(solution)/shard_map/all_to_all | solution.py:68
  128.3 9.6 %all_to_all.34 = bf16[8,11,256]{2,1,0:T(8,128)(2,1)S(1)} all-to-all(bf16[8,11,256]{2,1,0:T(8,128)(2,1)S(1)} %broadcast_in_dim.66), channel_id=1, replica_groups=mesh['dy'=4,'dx'=4,'dz'=8,'sub'=2] {'dz'}, dimensions={0} | all-to-all | bytes 90112 | tf_op jit(solution)/shard_map/all_to_all | solution.py:73
  138.0 14.1 %all_to_all.35 = bf16[16,44,512]{2,1,0:T(8,128)(2,1)S(1)} all-to-all(bf16[16,44,512]{2,1,0:T(8,128)(2,1)S(1)} %broadcast_in_dim.68), channel_id=1, replica_groups=mesh['dy'=4,'dx'=4,'dz'=8,'sub'=2] {'dy','dx'}, dimensions={0} | all-to-all | bytes 1441792 | tf_op jit(solution)/shard_map/all_to_all | solution.py:73
  152.3 4.5 %collective-permute-start.1 = (bf16[576,512]{1,0:T(8,128)(2,1)S(1)}, bf16[576,512]{1,0:T(8,128)(2,1)S(1)}, u32[]{:S(2)}, u32[]{:S(2)}) collective-permute-start(bf16[576,512]{1,0:T(8,128)(2,1)S(1)} %slice.63), channel_id=1, source_target_pairs={{0,1},{1,0},{2,3},{3,2},{4,5},{5,4},{6,7},{7,6},{8,9},{9,8},{10,11... | collective-permute-start | bytes 1769480 | tf_op jit(solution)/shard_map/ppermute | solution.py:77
  156.8 0.7 reshape.171
  157.6 0.9 collective-permute-done.1
  158.9 0.8 copy.74
  159.7 0.7 pad_maximum_fusion.4
  160.4 1.0 pad_maximum_fusion.2
  161.4 1.0 pad_maximum_fusion.1
  (100 shorter events, 7.9 us)
Async XLA Ops:
  0.6 54.6 %copy-start = (bf16[512,512]{1,0:T(8,128)(2,1)S(1)}, bf16[512,512]{1,0:T(8,128)(2,1)}, u32[]{:S(2)}) copy-start(bf16[512,512]{1,0:T(8,128)(2,1)} %param.18) | copy-start | bytes 1572868
  2.5 3.0 %copy-start.21 = (s32[1,1,128]{2,1,0:T(1,128)S(1)}, s32[1,1,128]{2,1,0:T(1,128)}, u32[]{:S(2)}) copy-start(s32[1,1,128]{2,1,0:T(1,128)} %param.23) | copy-start | bytes 1540
  5.8 17.9 %copy-start.18 = (s32[2]{0:T(128)S(1)}, s32[2]{0:T(128)}, u32[]{:S(2)}) copy-start(s32[2]{0:T(128)} %param.24) | copy-start | bytes 28
  5.8 21.0 %copy-start.16 = (bf16[2,256,128]{2,1,0:T(8,128)(2,1)S(1)}, bf16[2,256,128]{2,1,0:T(8,128)(2,1)}, u32[]{:S(2)}) copy-start(bf16[2,256,128]{2,1,0:T(8,128)(2,1)} %param.14) | copy-start | bytes 393220
  5.8 23.6 %copy-start.17 = (s32[256,4]{0,1:T(4,128)S(1)}, s32[256,4]{0,1:T(4,128)}, u32[]{:S(2)}) copy-start(s32[256,4]{0,1:T(4,128)} %param.13) | copy-start | bytes 12292
  5.9 24.4 %copy-start.11 = (bf16[16,128,128]{2,1,0:T(8,128)(2,1)S(1)}, bf16[16,128,128]{2,1,0:T(8,128)(2,1)}, u32[]{:S(2)}) copy-start(bf16[16,128,128]{2,1,0:T(8,128)(2,1)} %param.19) | copy-start | bytes 1572868
  7.2 23.4 %copy-start.19 = (s32[16]{0:T(128)S(1)}, s32[16]{0:T(128)}, u32[]{:S(2)}) copy-start(s32[16]{0:T(128)} %param.21) | copy-start | bytes 196
  7.2 23.4 %copy-start.20 = (s32[16]{0:T(128)S(1)}, s32[16]{0:T(128)}, u32[]{:S(2)}) copy-start(s32[16]{0:T(128)} %param.20) | copy-start | bytes 196
  7.2 23.5 %copy-start.8 = (f32[512,64]{0,1:T(8,128)S(1)}, f32[512,64]{0,1:T(8,128)}, u32[]{:S(2)}) copy-start(f32[512,64]{0,1:T(8,128)} %param.15) | copy-start | bytes 393220
  7.2 37.0 %all-to-all-start = ((s32[128,1,1152]{2,1,0:T(1,128)}), s32[128,1,1152]{2,1,0:T(1,128)S(1)}, u32[]{:S(2)}, u32[]{:S(2)}) async-start(s32[128,1,1152]{2,1,0:T(1,128)} %all_to_all.20), calls=%async_computation | async-start | bytes 1179648 | tf_op jit(solution)/shard_map/all_to_all | solution.py:122
  29.4 0.7 copy-start.13
  40.8 4.3 %copy-start.14 = (bf16[4,256,128]{2,1,0:T(8,128)(2,1)S(1)}, bf16[4,256,128]{2,1,0:T(8,128)(2,1)}, u32[]{:S(2)}) copy-start(bf16[4,256,128]{2,1,0:T(8,128)(2,1)} %copy-done.13) | copy-start | bytes 786436
  52.5 2.4 %copy-start.5 = (bf16[512,512]{1,0:T(8,128)(2,1)S(1)}, bf16[512,512]{1,0:T(8,128)(2,1)}, u32[]{:S(2)}) copy-start(bf16[512,512]{1,0:T(8,128)(2,1)} %param.17) | copy-start | bytes 1572868
  52.5 2.7 %copy-start.15 = (bf16[256,512]{1,0:T(8,128)(2,1)S(1)}, bf16[256,512]{1,0:T(8,128)(2,1)}, u32[]{:S(2)}) copy-start(bf16[256,512]{1,0:T(8,128)(2,1)} %param.25) | copy-start | bytes 786436
  57.8 2.0 %copy-start.3 = (bf16[16,128,512]{2,1,0:T(8,128)(2,1)S(1)}, bf16[16,128,512]{2,1,0:T(8,128)(2,1)}, u32[]{:S(2)}) copy-start(bf16[16,128,512]{2,1,0:T(8,128)(2,1)} %gather_fusion.1) | copy-start | bytes 6291460
  59.8 3.8 %copy-start.9 = (f32[512,64]{0,1:T(8,128)S(1)}, f32[512,64]{0,1:T(8,128)}, u32[]{:S(2)}) copy-start(f32[512,64]{0,1:T(8,128)} %param.15) | copy-start | bytes 393220
  62.4 2.6 %copy-start.12 = (f32[64,512]{1,0:T(8,128)S(1)}, f32[64,512]{1,0:T(8,128)}, u32[]{:S(2)}) copy-start(f32[64,512]{1,0:T(8,128)} %param.16) | copy-start | bytes 393220
  77.2 5.3 %copy-start.1 = (f32[2048,4,128]{0,2,1:T(8,128)S(1)}, f32[2048,4,128]{0,2,1:T(8,128)}, u32[]{:S(2)}) copy-start(f32[2048,4,128]{0,2,1:T(8,128)} %mul.63) | copy-start | bytes 12582916
  77.2 5.9 %copy-start.2 = (f32[2048,4,128]{0,2,1:T(8,128)S(1)}, f32[2048,4,128]{0,2,1:T(8,128)}, u32[]{:S(2)}) copy-start(f32[2048,4,128]{0,2,1:T(8,128)} %copy.69) | copy-start | bytes 12582916
  83.1 1.8 %copy-start.6 = (f32[32,4,8,128]{3,2,1,0:T(8,128)S(1)}, f32[32,4,8,128]{3,2,1,0:T(8,128)}, u32[]{:S(2)}) copy-start(f32[32,4,8,128]{3,2,1,0:T(8,128)} %convolution_bitcast_fusion) | copy-start | bytes 1572868
  85.2 1.2 copy-start.4
  86.5 2.1 %copy-start.10 = (f32[512,64]{0,1:T(8,128)S(1)}, f32[512,64]{0,1:T(8,128)}, u32[]{:S(2)}) copy-start(f32[512,64]{0,1:T(8,128)} %fusion.40) | copy-start | bytes 393220
  87.5 5.6 %copy-start.7 = (f32[2,256,128]{2,1,0:T(8,128)S(1)}, f32[2,256,128]{2,1,0:T(8,128)}, u32[]{:S(2)}) copy-start(f32[2,256,128]{2,1,0:T(8,128)} %get-tuple-element.35) | copy-start | bytes 786436
  90.7 5.5 %collective-permute-start = (f32[704,512]{1,0:T(8,128)}, f32[704,512]{1,0:T(8,128)S(1)}, u32[]{:S(2)}, u32[]{:S(2)}) collective-permute-start(f32[704,512]{1,0:T(8,128)} %constant_dynamic-update-slice_fusion.1), channel_id=1, source_target_pairs={{0,1},{1,0},{2,3},{3,2},{4,5},{5,4},{6,7},{7,6},{8,9},{9,8},{10,11... | collective-permute-start | bytes 4325384 | tf_op jit(solution)/shard_map/ppermute | solution.py:56
  152.3 6.1 %collective-permute-start.1 = (bf16[576,512]{1,0:T(8,128)(2,1)S(1)}, bf16[576,512]{1,0:T(8,128)(2,1)S(1)}, u32[]{:S(2)}, u32[]{:S(2)}) collective-permute-start(bf16[576,512]{1,0:T(8,128)(2,1)S(1)} %slice.63), channel_id=1, source_target_pairs={{0,1},{1,0},{2,3},{3,2},{4,5},{5,4},{6,7},{7,6},{8,9},{9,8},{10,11... | collective-permute-start | bytes 1769480 | tf_op jit(solution)/shard_map/ppermute | solution.py:77

commit v9 on v8

--- a/solution.py
+++ b/solution.py
@@ -28,17 +28,20 @@
 
 def fold_books(code_rows, gradients, code_count):
     book_count = code_rows.shape[1]
-    indicator_rows = one_hot_codes(code_rows, code_count, jnp.bfloat16)
-    pieces = gradients.reshape(gradients.shape[0], book_count, -1)
-    upper_bound = pieces.astype(jnp.bfloat16)
-    lower_bound = (pieces - upper_bound.astype(jnp.float32)).astype(jnp.bfloat16)
-    upper_half_sum = jnp.einsum(
-        "fco,fcg->cog", indicator_rows, upper_bound, preferred_element_type=jnp.float32
-    )
-    lower_half_sum = jnp.einsum(
-        "fco,fcg->cog", indicator_rows, lower_bound, preferred_element_type=jnp.float32
-    )
-    return upper_half_sum + lower_half_sum
+    slice_width = gradients.shape[1] // book_count
+    codes_hot = jnp.arange(code_count, dtype=jnp.int32)
+    folded = []
+    for book_index in range(book_count):
+        piece = gradients[:, book_index * slice_width : (book_index + 1) * slice_width]
+        upper_bound = piece.astype(jnp.bfloat16)
+        lower_bound = (piece - upper_bound.astype(jnp.float32)).astype(jnp.bfloat16)
+        both = jnp.concatenate([upper_bound, lower_bound], axis=1)
+        indicator_rows = (code_rows[:, book_index][:, None] == codes_hot).astype(jnp.bfloat16)
+        summed = lax.dot_general(
+            indicator_rows, both, (((0,), (0,)), ((), ())), preferred_element_type=jnp.float32
+        )
+        folded.append(summed[:, :slice_width] + summed[:, slice_width:])
+    return jnp.stack(folded)
 
 
 def all_sum(grad_w_msg, grad_w_self, part_alpha, part_basis, book_grad, dom_axes):

time: 163 us -> 153 us (0.939)
  local copies, waits for them, and re-layouts: 40.1 us -> 22.1 us
  waiting for transfers between devices: 5.22 us -> 12.4 us
  other arithmetic: 8.05 us -> 13.1 us
  blocking collectives: 56.5 us -> 52.8 us
    reshape x2 -> x0, local copies, waits for them, and re-layouts: 10.6 us -> none  [shards(): grad_comp = jnp.einsum('btji,bjd->btid', tile_blocks, grad_blocks, prefer...]
    mul x2 -> x0, local copies, waits for them, and re-layouts: 7.49 us -> none  [shards(): picked.astype(jnp.float32) * scale[:, None, :]]
    all_to_all x1, waiting for transfers between devices: 2.06 us -> 9.21 us  [shards(): incoming = lax.all_to_all(payload, DOM, 0, 0, tiled=True)]
    all_to_all x2, blocking collectives: 30.2 us -> 27 us  [all_sum(): received = lax.all_to_all(chunks, axis, 0, 0, tiled=True)]
    mul x0 -> x1, other arithmetic: none -> 2.7 us  [shards(): contrib = (grad_comp * scale[:, None, :]).reshape(-1, model_width)]
    convert_element_type x0 -> x2, other arithmetic: none -> 2.16 us  [fold_books(): lower_bound = (piece - upper_bound.astype(jnp.float32)).astype(jnp.bfloat16)]
    dot_general x4 -> x8, matrix products: 7.67 us -> 6.77 us  [fold_books(): lax.dot_general(indicator_rows, both, (((0,), (0,)), ((), ())), preferred...]
    unnamed x51 -> x55, local copies, waits for them, and re-layouts: 6.59 us -> 6.03 us
  transfers between devices with their start and end apart: 3 -> 3, of which waited for: 3 -> 3; matrix products, arithmetic and copies ran while one was open for 8% -> 4% of each run, Pallas kernels for 0% -> 0%
where the time goes in v9:
time: 153 us; the launch traced here: 152 us
  blocking collectives  52.8 us (35%)
  starting transfers between devices  23.5 us (15%)
  matrix products  23.2 us (15%)
  local copies, waits for them, and re-layouts  22.1 us (14%)
  other arithmetic  13.1 us (9%)
  waiting for transfers between devices  12.4 us (8%)
  between operations  5.27 us (3%)
    all_to_all x2, blocking collectives, all_sum(): received = lax.all_to_all(chunks, axis, 0, 0, tiled=True)  27 us
    all_to_all x2, blocking collectives, all_sum(): piece = lax.all_to_all(spread, axis, 0, 0, tiled=True).reshape(shape)  23.2 us
    all_to_all x1, starting transfers between devices, shards(): incoming = lax.all_to_all(payload, DOM, 0, 0, tiled=True)  16.5 us
    all_to_all x1, waiting for transfers between devices, shards(): incoming = lax.all_to_all(payload, DOM, 0, 0, tiled=True)  9.21 us
    dot_general x8, matrix products, fold_books(): lax.dot_general(indicator_rows, both, (((0,), (0,)), ((), ())), preferred...  6.77 us
    unnamed x55, local copies, waits for them, and re-layouts  6.03 us
    ppermute x1, starting transfers between devices, all_sum(): other_dense = lax.ppermute(own_dense, 'sub', swap)  4.5 us
  transfers between devices with their start and end apart: 3, of which 3 were waited for; matrix products, arithmetic and copies ran while one was open for 4% of the time, Pallas kernels for 0%

profile of v9, /device:TPU:1, one launch (start us, length us, event | category | flops | bytes accessed | tf_op | source)
XLA Modules:
  0.0 152.2 jit_solution(17314165697829504175)
XLA Ops:
  0.6 0.9 copy.54
  1.5 0.7 compare_select_fusion
  2.6 2.8 %gather_fusion = s32[1024,4]{1,0:T(8,128)S(1)} fusion(s32[256,4]{1,0:T(8,128)S(1)} %copy.54, s32[1024]{0:T(1024)S(1)} %broadcast_clamp_fusion), kind=kCustom, calls=%fused_computation | custom fusion | bytes 36864 | tf_op jit(solution)/shard_map/gather | solution.py:120
  5.9 1.2 all_to_all.20
  7.2 16.5 %all-to-all-start = ((s32[128,1,1152]{2,1,0:T(1,128)}), s32[128,1,1152]{2,1,0:T(1,128)S(1)}, u32[]{:S(2)}, u32[]{:S(2)}) async-start(s32[128,1,1152]{2,1,0:T(1,128)} %all_to_all.20), calls=%async_computation | async-start | bytes 1179648 | tf_op jit(solution)/shard_map/all_to_all | solution.py:125
  24.2 2.6 %all_gather.3 = bf16[4,256,128]{2,1,0:T(8,128)(2,1)S(1)} all-gather(bf16[2,256,128]{2,1,0:T(8,128)(2,1)S(1)} %copy-done.18), channel_id=1, replica_groups=mesh['dy'=4,'dx'=4,'dz'=8,'sub'=2] {'sub'}, dimensions={0}, use_global_device_ids=true | all-gather | bytes 393216 | tf_op jit(solution)/shard_map/all_gather | solution.py:115
  30.1 1.0 copy.65
  32.4 1.9 %fusion.82 = f32[512,512]{1,0:T(8,128)S(1)} fusion(f32[512,64]{0,1:T(8,128)S(1)} %copy-done.11, f32[64,512]{1,0:T(8,128)} %param.16), kind=kOutput, calls=%fused_computation.159 | convolution fusion | flops 201326592 | bytes 1310720 | tf_op jit(solution)/shard_map/dot_general | solution.py:116
  35.0 9.2 %all-to-all-done = s32[128,1,1152]{2,1,0:T(1,128)S(1)} async-done(((s32[128,1,1152]{2,1,0:T(1,128)}), s32[128,1,1152]{2,1,0:T(1,128)S(1)}, u32[]{:S(2)}, u32[]{:S(2)}) %all-to-all-start) | async-done | bytes 589856 | tf_op jit(solution)/shard_map/all_to_all | solution.py:125
  45.1 2.2 %fusion.4 = bf16[4,1536,128]{1,2,0:T(8,128)(2,1)S(1)} fusion(bf16[4,256,128]{2,1,0:T(8,128)(2,1)S(1)} %copy-done.16, s32[1536,4]{0,1:T(4,128)S(1)} %pad_add_fusion), kind=kOutput, calls=%fused_computation.13 | convolution fusion | flops 405012480 | bytes 1859584 | tf_op jit(solution)/shard_map/feu,euq->feq/dot_general | solution.py:23
  47.3 1.6 %copy.64 = bf16[1536,512]{1,0:T(8,128)(2,1)} copy(bf16[1536,512]{0,1:T(8,128)(2,1)S(1)} %bitcast.110) | data formatting | bytes 3145728 | tf_op jit(solution)/shard_map/reshape | solution.py:26
  49.0 1.5 %pad_maximum_fusion = bf16[1792,512]{1,0:T(8,128)(2,1)S(1)} fusion(bf16[1536,512]{1,0:T(8,128)(2,1)} %copy.64, bf16[256,512]{1,0:T(8,128)(2,1)S(1)} %copy.63), kind=kLoop, calls=%fused_computation.24 | loop fusion | flops 3670016 | bytes 3670016 | tf_op jit(solution)/shard_map/concatenate | solution.py:133
  50.5 2.0 %gather_fusion.1 = bf16[16,128,512]{2,1,0:T(8,128)(2,1)} fusion(bf16[14,128,512]{2,1,0:T(8,128)(2,1)S(1)} %bitcast.102, s32[1024]{0:T(1024)S(1)} %pad_clamp_fusion.1), kind=kCustom, calls=%fused_computation.1 | custom fusion | bytes 4194368 | tf_op jit(solution)/shard_map/gather | solution.py:138
  52.5 2.2 %fusion.16 = bf16[2,512,128]{1,2,0:T(8,128)(2,1)S(1)} fusion(bf16[2,8,128,128]{3,2,1,0:T(8,128)(2,1)S(1)} %bitcast.116, bf16[2,8,128,512]{3,2,1,0:T(8,128)(2,1)} %bitcast.103, f32[2,8,512]{2,1,0:T(8,128)S(1)} %bitcast.117), kind=kOutput, calls=%fused_computation.30 | convolution fusion | flops 271712256 | bytes 2916352 | tf_op jit(solution)/shard_map/btij,btjd->bid/dot_general | solution.py:141
  55.1 1.1 multiply_convert_fusion
  56.9 1.3 fusion.84
  58.9 2.7 %fusion.2 = (f32[2,8,512]{2,1,0:T(8,128)S(1)}, f32[2,512,1024]{1,2,0}) fusion(bf16[2,8,128,512]{3,2,1,0:T(8,128)(2,1)S(1)} %bitcast.104, bf16[2,128,1024]{1,2,0:T(8,128)(2,1)S(1)} %bitcast.108, bf16[2,128,512]{2,1,0:T(8,128)(2,1)S(1)} %bitcast.111), kind=kOutput, calls=%fused_computation.10 | convolution fusion | flops 271572992 | bytes 7110656
  61.6 1.1 scatter_custom_fusion
  62.7 1.5 fusion.86
  64.2 1.9 %fusion.87 = f32[512,64]{1,0:T(8,128)S(1)} fusion(f32[512,512]{1,0:T(8,128)S(1)} %scatter_custom_fusion, f32[64,512]{1,0:T(8,128)} %param.16), kind=kOutput, calls=%fused_computation.164 | convolution fusion | flops 201326592 | bytes 1310720 | tf_op jit(solution)/shard_map/dot_general | solution.py:174
  66.0 2.7 %bitcast_multiply_fusion = f32[2048,512]{1,0:T(8,128)S(1)} fusion(f32[2,512,1024]{1,2,0} %get-tuple-element.88, f32[16,512]{1,0:T(8,128)S(1)} %gather_fusion.2), kind=kLoop, calls=%fused_computation.11 | loop fusion | flops 1048576 | bytes 8421376 | tf_op jit(solution)/shard_map/mul | solution.py:172
  68.7 2.1 %subtract_convert_fusion.3 = (bf16[2048,128]{1,0:T(8,128)(2,1)}, bf16[2048,128]{1,0:T(8,128)(2,1)}, bf16[2048,128]{1,0:T(8,128)(2,1)S(1)}, bf16[2048,128]{1,0:T(...) fusion(f32[2048,512]{1,0:T(8,128)S(1)} %bitcast_multiply_fusion), kind=kLoop, calls=%fused_computation.53 | loop fusion | flops 3145728 | bytes 10485760 | tf_op jit(solution)/shard_map/convert_element_type | solution.py:37
  70.8 0.6 gather_fusion.3
  71.5 2.3 %fusion.8 = f32[256,256]{1,0:T(8,128)S(1)} fusion(bf16[2048,128]{1,0:T(8,128)(2,1)} %get-tuple-element.34, bf16[2048,128]{1,0:T(8,128)(2,1)} %get-tuple-element.35, s32[2048]{0:T(1024)S(1)} %bitcast.122), kind=kOutput, calls=%fused_computation.20 | convolution fusion | flops 271056896 | bytes 1318912 | tf_op jit(solution)/shard_map/dot_general | solution.py:40
  73.8 1.0 fusion.9
  75.0 1.0 fusion.10
  76.1 1.0 fusion.11
  78.7 0.7 constant_dynamic-slice_fusion
  80.0 1.0 dynamic-slice_dynamic-update-slice_fusion.1
  81.0 1.1 dynamic-slice_dynamic-update-slice_fusion
  82.1 0.6 bitcast_dynamic-update-slice_fusion
  82.8 0.7 dynamic-slice_dynamic-update-slice_fusion.4
  83.4 0.7 constant_dynamic-update-slice_fusion.1
  84.1 2.5 %collective-permute-start = (f32[704,512]{1,0:T(8,128)}, f32[704,512]{1,0:T(8,128)S(1)}, u32[]{:S(2)}, u32[]{:S(2)}) collective-permute-start(f32[704,512]{1,0:T(8,128)} %constant_dynamic-update-slice_fusion.1), channel_id=1, source_target_pairs={{0,1},{1,0},{2,3},{3,2},{4,5},{5,4},{6,7},{7,6},{8,9},{9,8},{10,11... | collective-permute-start | bytes 4325384 | tf_op jit(solution)/shard_map/ppermute | solution.py:59
  86.7 0.7 constant_dynamic-update-slice_fusion
  87.4 2.3 %collective-permute-done = f32[704,512]{1,0:T(8,128)S(1)} collective-permute-done((f32[704,512]{1,0:T(8,128)}, f32[704,512]{1,0:T(8,128)S(1)}, u32[]{:S(2)}, u32[]{:S(2)}) %collective-permute-start) | collective-permute-done | bytes 1441824 | tf_op jit(solution)/shard_map/ppermute | solution.py:59
  89.7 1.6 %add_convert_fusion = bf16[704,512]{1,0:T(8,128)(2,1)S(1)} fusion(f32[704,512]{1,0:T(8,128)} %constant_dynamic-update-slice_fusion, f32[704,512]{1,0:T(8,128)S(1)} %collective-permute-done), kind=kLoop, calls=%fused_computation.26 | loop fusion | flops 720896 | bytes 3604480 | tf_op jit(solution)/shard_map/convert_element_type | solution.py:70
  91.4 16.7 %all_to_all.32 = bf16[16,44,512]{2,1,0:T(8,128)(2,1)S(1)} all-to-all(bf16[16,44,512]{2,1,0:T(8,128)(2,1)S(1)} %convert_element_type.186), channel_id=1, replica_groups=mesh['dy'=4,'dx'=4,'dz'=8,'sub'=2] {'dy','dx'}, dimensions={0} | all-to-all | bytes 1441792 | tf_op jit(solution)/shard_map/all_to_all | solution.py:71
  108.3 10.3 %all_to_all.33 = f32[8,11,256]{2,1,0:T(8,128)S(1)} all-to-all(f32[8,11,256]{2,1,0:T(8,128)S(1)} %reshape.164), channel_id=1, replica_groups=mesh['dy'=4,'dx'=4,'dz'=8,'sub'=2] {'dz'}, dimensions={0} | all-to-all | bytes 180224 | tf_op jit(solution)/shard_map/all_to_all | solution.py:71
  118.6 9.6 %all_to_all.34 = bf16[8,11,256]{2,1,0:T(8,128)(2,1)S(1)} all-to-all(bf16[8,11,256]{2,1,0:T(8,128)(2,1)S(1)} %broadcast_in_dim.38), channel_id=1, replica_groups=mesh['dy'=4,'dx'=4,'dz'=8,'sub'=2] {'dz'}, dimensions={0} | all-to-all | bytes 90112 | tf_op jit(solution)/shard_map/all_to_all | solution.py:76
  128.3 13.6 %all_to_all.35 = bf16[16,44,512]{2,1,0:T(8,128)(2,1)S(1)} all-to-all(bf16[16,44,512]{2,1,0:T(8,128)(2,1)S(1)} %broadcast_in_dim.40), channel_id=1, replica_groups=mesh['dy'=4,'dx'=4,'dz'=8,'sub'=2] {'dy','dx'}, dimensions={0} | all-to-all | bytes 1441792 | tf_op jit(solution)/shard_map/all_to_all | solution.py:76
  142.1 4.5 %collective-permute-start.1 = (bf16[576,512]{1,0:T(8,128)(2,1)S(1)}, bf16[576,512]{1,0:T(8,128)(2,1)S(1)}, u32[]{:S(2)}, u32[]{:S(2)}) collective-permute-start(bf16[576,512]{1,0:T(8,128)(2,1)S(1)} %slice.219), channel_id=1, source_target_pairs={{0,1},{1,0},{2,3},{3,2},{4,5},{5,4},{6,7},{7,6},{8,9},{9,8},{10,11... | collective-permute-start | bytes 1769480 | tf_op jit(solution)/shard_map/ppermute | solution.py:80
  146.6 0.7 reshape.171
  147.3 0.9 collective-permute-done.1
  148.7 0.8 copy.71
  149.5 0.7 pad_maximum_fusion.4
  150.1 1.0 pad_maximum_fusion.2
  151.2 1.0 pad_maximum_fusion.1
  (117 shorter events, 8.5 us)
Async XLA Ops:
  0.6 54.4 %copy-start = (bf16[512,512]{1,0:T(8,128)(2,1)S(1)}, bf16[512,512]{1,0:T(8,128)(2,1)}, u32[]{:S(2)}) copy-start(bf16[512,512]{1,0:T(8,128)(2,1)} %param.18) | copy-start | bytes 1572868
  2.5 3.0 %copy-start.23 = (s32[1,1,128]{2,1,0:T(1,128)S(1)}, s32[1,1,128]{2,1,0:T(1,128)}, u32[]{:S(2)}) copy-start(s32[1,1,128]{2,1,0:T(1,128)} %param.23) | copy-start | bytes 1540
  5.8 17.9 %copy-start.20 = (s32[2]{0:T(128)S(1)}, s32[2]{0:T(128)}, u32[]{:S(2)}) copy-start(s32[2]{0:T(128)} %param.24) | copy-start | bytes 28
  5.8 18.4 %copy-start.18 = (bf16[2,256,128]{2,1,0:T(8,128)(2,1)S(1)}, bf16[2,256,128]{2,1,0:T(8,128)(2,1)}, u32[]{:S(2)}) copy-start(bf16[2,256,128]{2,1,0:T(8,128)(2,1)} %param.14) | copy-start | bytes 393220
  5.8 23.6 %copy-start.19 = (s32[256,4]{0,1:T(4,128)S(1)}, s32[256,4]{0,1:T(4,128)}, u32[]{:S(2)}) copy-start(s32[256,4]{0,1:T(4,128)} %param.13) | copy-start | bytes 12292
  5.9 24.1 %copy-start.14 = (bf16[16,128,128]{2,1,0:T(8,128)(2,1)S(1)}, bf16[16,128,128]{2,1,0:T(8,128)(2,1)}, u32[]{:S(2)}) copy-start(bf16[16,128,128]{2,1,0:T(8,128)(2,1)} %param.19) | copy-start | bytes 1572868
  7.2 25.2 %copy-start.21 = (s32[16]{0:T(128)S(1)}, s32[16]{0:T(128)}, u32[]{:S(2)}) copy-start(s32[16]{0:T(128)} %param.21) | copy-start | bytes 196
  7.2 25.2 %copy-start.22 = (s32[16]{0:T(128)S(1)}, s32[16]{0:T(128)}, u32[]{:S(2)}) copy-start(s32[16]{0:T(128)} %param.20) | copy-start | bytes 196
  7.2 25.3 %copy-start.11 = (f32[512,64]{0,1:T(8,128)S(1)}, f32[512,64]{0,1:T(8,128)}, u32[]{:S(2)}) copy-start(f32[512,64]{0,1:T(8,128)} %param.15) | copy-start | bytes 393220
  7.2 37.0 %all-to-all-start = ((s32[128,1,1152]{2,1,0:T(1,128)}), s32[128,1,1152]{2,1,0:T(1,128)S(1)}, u32[]{:S(2)}, u32[]{:S(2)}) async-start(s32[128,1,1152]{2,1,0:T(1,128)} %all_to_all.20), calls=%async_computation | async-start | bytes 1179648 | tf_op jit(solution)/shard_map/all_to_all | solution.py:125
  26.8 3.1 %copy-start.15 = (bf16[4,256,128]{2,1,0:T(8,128)(2,1)}, bf16[4,256,128]{2,1,0:T(8,128)(2,1)S(1)}, u32[]{:S(2)}) copy-start(bf16[4,256,128]{2,1,0:T(8,128)(2,1)S(1)} %all_gather.3) | copy-start | bytes 786436
  35.0 10.2 %copy-start.16 = (bf16[4,256,128]{2,1,0:T(8,128)(2,1)S(1)}, bf16[4,256,128]{2,1,0:T(8,128)(2,1)}, u32[]{:S(2)}) copy-start(bf16[4,256,128]{2,1,0:T(8,128)(2,1)} %copy-done.15) | copy-start | bytes 786436
  52.5 2.3 %copy-start.4 = (bf16[512,512]{1,0:T(8,128)(2,1)S(1)}, bf16[512,512]{1,0:T(8,128)(2,1)}, u32[]{:S(2)}) copy-start(bf16[512,512]{1,0:T(8,128)(2,1)} %param.17) | copy-start | bytes 1572868
  52.5 2.6 %copy-start.17 = (bf16[256,512]{1,0:T(8,128)(2,1)S(1)}, bf16[256,512]{1,0:T(8,128)(2,1)}, u32[]{:S(2)}) copy-start(bf16[256,512]{1,0:T(8,128)(2,1)} %param.25) | copy-start | bytes 786436
  56.9 2.0 %copy-start.1 = (bf16[16,128,512]{2,1,0:T(8,128)(2,1)S(1)}, bf16[16,128,512]{2,1,0:T(8,128)(2,1)}, u32[]{:S(2)}) copy-start(bf16[16,128,512]{2,1,0:T(8,128)(2,1)} %gather_fusion.1) | copy-start | bytes 6291460
  56.9 2.0 %copy-start.3 = (bf16[2,8,128,128]{2,3,1,0:T(8,128)(2,1)S(1)}, bf16[2,8,128,128]{2,3,1,0:T(8,128)(2,1)}, u32[]{:S(2)}) copy-start(bf16[2,8,128,128]{2,3,1,0:T(8,128)(2,1)} %copy.65) | copy-start | bytes 1572868
  58.9 3.8 %copy-start.12 = (f32[512,64]{0,1:T(8,128)S(1)}, f32[512,64]{0,1:T(8,128)}, u32[]{:S(2)}) copy-start(f32[512,64]{0,1:T(8,128)} %param.15) | copy-start | bytes 393220
  71.4 2.4 %copy-start.9 = (bf16[2048,128]{1,0:T(8,128)(2,1)S(1)}, bf16[2048,128]{1,0:T(8,128)(2,1)}, u32[]{:S(2)}) copy-start(bf16[2048,128]{1,0:T(8,128)(2,1)} %get-tuple-element.46) | copy-start | bytes 1572868
  71.4 2.4 %copy-start.10 = (bf16[2048,128]{1,0:T(8,128)(2,1)S(1)}, bf16[2048,128]{1,0:T(8,128)(2,1)}, u32[]{:S(2)}) copy-start(bf16[2048,128]{1,0:T(8,128)(2,1)} %get-tuple-element.47) | copy-start | bytes 1572868
  73.8 1.2 copy-start.7
  73.8 1.2 copy-start.8
  74.9 1.2 copy-start.6
  78.7 1.3 copy-start.2
  80.0 2.1 %copy-start.13 = (f32[512,64]{0,1:T(8,128)S(1)}, f32[512,64]{0,1:T(8,128)}, u32[]{:S(2)}) copy-start(f32[512,64]{0,1:T(8,128)} %fusion.86) | copy-start | bytes 393220
  81.0 5.6 %copy-start.5 = (f32[2,256,128]{2,1,0:T(8,128)S(1)}, f32[2,256,128]{2,1,0:T(8,128)}, u32[]{:S(2)}) copy-start(f32[2,256,128]{2,1,0:T(8,128)} %get-tuple-element.63) | copy-start | bytes 786436
  84.1 5.6 %collective-permute-start = (f32[704,512]{1,0:T(8,128)}, f32[704,512]{1,0:T(8,128)S(1)}, u32[]{:S(2)}, u32[]{:S(2)}) collective-permute-start(f32[704,512]{1,0:T(8,128)} %constant_dynamic-update-slice_fusion.1), channel_id=1, source_target_pairs={{0,1},{1,0},{2,3},{3,2},{4,5},{5,4},{6,7},{7,6},{8,9},{9,8},{10,11... | collective-permute-start | bytes 4325384 | tf_op jit(solution)/shard_map/ppermute | solution.py:59
  142.1 6.1 %collective-permute-start.1 = (bf16[576,512]{1,0:T(8,128)(2,1)S(1)}, bf16[576,512]{1,0:T(8,128)(2,1)S(1)}, u32[]{:S(2)}, u32[]{:S(2)}) collective-permute-start(bf16[576,512]{1,0:T(8,128)(2,1)S(1)} %slice.219), channel_id=1, source_target_pairs={{0,1},{1,0},{2,3},{3,2},{4,5},{5,4},{6,7},{7,6},{8,9},{9,8},{10,11... | collective-permute-start | bytes 1769480 | tf_op jit(solution)/shard_map/ppermute | solution.py:80

commit v10 on v9

--- a/solution.py
+++ b/solution.py
@@ -72,8 +72,7 @@
         piece = jnp.sum(received.astype(jnp.float32), axis=0)
     piece = piece.astype(jnp.bfloat16)
     for (axis, size), shape in reversed(list(zip(dom_axes, shapes))):
-        spread = jnp.broadcast_to(piece[None], (size,) + piece.shape)
-        piece = lax.all_to_all(spread, axis, 0, 0, tiled=True).reshape(shape)
+        piece = lax.all_gather(piece, axis, axis=0, tiled=True).reshape(shape)
     own_half = piece
     dense_rows = rows - share * book_grad.shape[1] * book_grad.shape[2] // width
     own_dense = own_half[:dense_rows]

time: 153 us -> 174 us (1.14)
  blocking collectives: 52.8 us -> 64.8 us
  starting transfers between devices: 23.5 us -> 32.9 us
    all_gather x0 -> x2, blocking collectives: none -> 35.2 us  [all_sum(): piece = lax.all_gather(piece, axis, axis=0, tiled=True).reshape(shape)]
    all_to_all x2 -> x0, blocking collectives: 23.2 us -> none  [all_sum(): piece = lax.all_to_all(spread, axis, 0, 0, tiled=True).reshape(shape)]
    ppermute x1, starting transfers between devices: 4.5 us -> 13.9 us  [all_sum(): other_dense = lax.ppermute(own_dense, 'sub', swap)]
    unnamed x55 -> x57, local copies, waits for them, and re-layouts: 6.03 us -> 6.21 us
where the time goes in v10:
time: 174 us
  blocking collectives  64.8 us (37%)
  starting transfers between devices  32.9 us (19%)
  matrix products  23.2 us (13%)
  local copies, waits for them, and re-layouts  22 us (13%)
  other arithmetic  13.1 us (8%)
  waiting for transfers between devices  12.4 us (7%)
  between operations  5.26 us (3%)
    all_gather x2, blocking collectives, all_sum(): piece = lax.all_gather(piece, axis, axis=0, tiled=True).reshape(shape)  35.2 us
    all_to_all x2, blocking collectives, all_sum(): received = lax.all_to_all(chunks, axis, 0, 0, tiled=True)  27 us
    all_to_all x1, starting transfers between devices, shards(): incoming = lax.all_to_all(payload, DOM, 0, 0, tiled=True)  16.5 us
    ppermute x1, starting transfers between devices, all_sum(): other_dense = lax.ppermute(own_dense, 'sub', swap)  13.9 us
    all_to_all x1, waiting for transfers between devices, shards(): incoming = lax.all_to_all(payload, DOM, 0, 0, tiled=True)  9.21 us
    dot_general x8, matrix products, fold_books(): lax.dot_general(indicator_rows, both, (((0,), (0,)), ((), ())), preferred...  6.77 us
    unnamed x57, local copies, waits for them, and re-layouts  6.21 us
  transfers between devices with their start and end apart: 3, of which 3 were waited for; matrix products, arithmetic and copies ran while one was open for 4% of the time, Pallas kernels for 0%

profile of v10, /device:TPU:1, one launch (start us, length us, event | category | flops | bytes accessed | tf_op | source)
XLA Modules:
  0.0 173.6 jit_solution(16308901791035012272)
XLA Ops:
  0.6 0.9 copy.54
  1.5 0.7 compare_select_fusion
  2.6 2.8 %gather_fusion = s32[1024,4]{1,0:T(8,128)S(1)} fusion(s32[256,4]{1,0:T(8,128)S(1)} %copy.54, s32[1024]{0:T(1024)S(1)} %broadcast_clamp_fusion), kind=kCustom, calls=%fused_computation | custom fusion | bytes 36864 | tf_op jit(solution)/shard_map/gather | solution.py:119
  5.9 1.2 all_to_all.14
  7.2 16.5 %all-to-all-start = ((s32[128,1,1152]{2,1,0:T(1,128)}), s32[128,1,1152]{2,1,0:T(1,128)S(1)}, u32[]{:S(2)}, u32[]{:S(2)}) async-start(s32[128,1,1152]{2,1,0:T(1,128)} %all_to_all.14), calls=%async_computation | async-start | bytes 1179648 | tf_op jit(solution)/shard_map/all_to_all | solution.py:124
  24.2 2.6 %all_gather.9 = bf16[4,256,128]{2,1,0:T(8,128)(2,1)S(1)} all-gather(bf16[2,256,128]{2,1,0:T(8,128)(2,1)S(1)} %copy-done.18), channel_id=1, replica_groups=mesh['dy'=4,'dx'=4,'dz'=8,'sub'=2] {'sub'}, dimensions={0}, use_global_device_ids=true | all-gather | bytes 393216 | tf_op jit(solution)/shard_map/all_gather | solution.py:114
  30.1 1.0 copy.65
  32.4 1.9 %fusion.82 = f32[512,512]{1,0:T(8,128)S(1)} fusion(f32[512,64]{0,1:T(8,128)S(1)} %copy-done.11, f32[64,512]{1,0:T(8,128)} %param.16), kind=kOutput, calls=%fused_computation.160 | convolution fusion | flops 201326592 | bytes 1310720 | tf_op jit(solution)/shard_map/dot_general | solution.py:115
  35.0 9.2 %all-to-all-done = s32[128,1,1152]{2,1,0:T(1,128)S(1)} async-done(((s32[128,1,1152]{2,1,0:T(1,128)}), s32[128,1,1152]{2,1,0:T(1,128)S(1)}, u32[]{:S(2)}, u32[]{:S(2)}) %all-to-all-start) | async-done | bytes 589856 | tf_op jit(solution)/shard_map/all_to_all | solution.py:124
  45.1 2.2 %fusion.4 = bf16[4,1536,128]{1,2,0:T(8,128)(2,1)S(1)} fusion(bf16[4,256,128]{2,1,0:T(8,128)(2,1)S(1)} %copy-done.16, s32[1536,4]{0,1:T(4,128)S(1)} %pad_add_fusion), kind=kOutput, calls=%fused_computation.13 | convolution fusion | flops 405012480 | bytes 1859584 | tf_op jit(solution)/shard_map/feu,euq->feq/dot_general | solution.py:23
  47.3 1.6 copy.64
  49.0 1.5 pad_maximum_fusion
  50.5 2.0 %gather_fusion.1 = bf16[16,128,512]{2,1,0:T(8,128)(2,1)} fusion(bf16[14,128,512]{2,1,0:T(8,128)(2,1)S(1)} %bitcast.105, s32[1024]{0:T(1024)S(1)} %pad_clamp_fusion.1), kind=kCustom, calls=%fused_computation.1 | custom fusion | bytes 4194368 | tf_op jit(solution)/shard_map/gather | solution.py:137
  52.5 2.2 %fusion.16 = bf16[2,512,128]{1,2,0:T(8,128)(2,1)S(1)} fusion(bf16[2,8,128,128]{3,2,1,0:T(8,128)(2,1)S(1)} %bitcast.119, bf16[2,8,128,512]{3,2,1,0:T(8,128)(2,1)} %bitcast.106, f32[2,8,512]{2,1,0:T(8,128)S(1)} %bitcast.120), kind=kOutput, calls=%fused_computation.30 | convolution fusion | flops 271712256 | bytes 2916352 | tf_op jit(solution)/shard_map/btij,btjd->bid/dot_general | solution.py:140
  55.1 1.1 multiply_convert_fusion
  56.9 1.3 fusion.84
  58.9 2.7 %fusion.2 = (f32[2,8,512]{2,1,0:T(8,128)S(1)}, f32[2,512,1024]{1,2,0}) fusion(bf16[2,8,128,512]{3,2,1,0:T(8,128)(2,1)S(1)} %bitcast.107, bf16[2,128,1024]{1,2,0:T(8,128)(2,1)S(1)} %bitcast.111, bf16[2,128,512]{2,1,0:T(8,128)(2,1)S(1)} %bitcast.114), kind=kOutput, calls=%fused_computation.10 | convolution fusion | flops 271572992 | bytes 7110656
  61.6 1.1 scatter_custom_fusion
  62.7 1.5 fusion.86
  64.2 1.9 %fusion.87 = f32[512,64]{1,0:T(8,128)S(1)} fusion(f32[512,512]{1,0:T(8,128)S(1)} %scatter_custom_fusion, f32[64,512]{1,0:T(8,128)} %param.16), kind=kOutput, calls=%fused_computation.165 | convolution fusion | flops 201326592 | bytes 1310720 | tf_op jit(solution)/shard_map/dot_general | solution.py:173
  66.0 2.7 %bitcast_multiply_fusion = f32[2048,512]{1,0:T(8,128)S(1)} fusion(f32[2,512,1024]{1,2,0} %get-tuple-element.88, f32[16,512]{1,0:T(8,128)S(1)} %gather_fusion.2), kind=kLoop, calls=%fused_computation.11 | loop fusion | flops 1048576 | bytes 8421376 | tf_op jit(solution)/shard_map/mul | solution.py:171
  68.7 2.1 %subtract_convert_fusion.3 = (bf16[2048,128]{1,0:T(8,128)(2,1)}, bf16[2048,128]{1,0:T(8,128)(2,1)}, bf16[2048,128]{1,0:T(8,128)(2,1)S(1)}, bf16[2048,128]{1,0:T(...) fusion(f32[2048,512]{1,0:T(8,128)S(1)} %bitcast_multiply_fusion), kind=kLoop, calls=%fused_computation.53 | loop fusion | flops 3145728 | bytes 10485760 | tf_op jit(solution)/shard_map/convert_element_type | solution.py:37
  70.8 0.6 gather_fusion.3
  71.4 2.3 %fusion.8 = f32[256,256]{1,0:T(8,128)S(1)} fusion(bf16[2048,128]{1,0:T(8,128)(2,1)} %get-tuple-element.34, bf16[2048,128]{1,0:T(8,128)(2,1)} %get-tuple-element.35, s32[2048]{0:T(1024)S(1)} %bitcast.126), kind=kOutput, calls=%fused_computation.20 | convolution fusion | flops 271056896 | bytes 1318912 | tf_op jit(solution)/shard_map/dot_general | solution.py:40
  73.8 1.0 fusion.9
  75.0 1.0 fusion.10
  76.1 1.0 fusion.11
  78.7 0.7 constant_dynamic-slice_fusion
  80.0 1.0 dynamic-slice_dynamic-update-slice_fusion.1
  81.0 1.1 dynamic-slice_dynamic-update-slice_fusion
  82.1 0.6 bitcast_dynamic-update-slice_fusion
  82.8 0.7 dynamic-slice_dynamic-update-slice_fusion.4
  83.4 0.7 constant_dynamic-update-slice_fusion.1
  84.1 2.5 %collective-permute-start = (f32[704,512]{1,0:T(8,128)}, f32[704,512]{1,0:T(8,128)S(1)}, u32[]{:S(2)}, u32[]{:S(2)}) collective-permute-start(f32[704,512]{1,0:T(8,128)} %constant_dynamic-update-slice_fusion.1), channel_id=1, source_target_pairs={{0,1},{1,0},{2,3},{3,2},{4,5},{5,4},{6,7},{7,6},{8,9},{9,8},{10,11... | collective-permute-start | bytes 4325384 | tf_op jit(solution)/shard_map/ppermute | solution.py:59
  86.7 0.7 constant_dynamic-update-slice_fusion
  87.4 2.3 %collective-permute-done = f32[704,512]{1,0:T(8,128)S(1)} collective-permute-done((f32[704,512]{1,0:T(8,128)}, f32[704,512]{1,0:T(8,128)S(1)}, u32[]{:S(2)}, u32[]{:S(2)}) %collective-permute-start) | collective-permute-done | bytes 1441824 | tf_op jit(solution)/shard_map/ppermute | solution.py:59
  89.7 1.6 add_convert_fusion
  91.4 16.7 %all_to_all.22 = bf16[16,44,512]{2,1,0:T(8,128)(2,1)S(1)} all-to-all(bf16[16,44,512]{2,1,0:T(8,128)(2,1)S(1)} %convert_element_type.182), channel_id=1, replica_groups=mesh['dy'=4,'dx'=4,'dz'=8,'sub'=2] {'dy','dx'}, dimensions={0} | all-to-all | bytes 1441792 | tf_op jit(solution)/shard_map/all_to_all | solution.py:71
  108.3 10.3 %all_to_all.23 = f32[8,11,256]{2,1,0:T(8,128)S(1)} all-to-all(f32[8,11,256]{2,1,0:T(8,128)S(1)} %reshape.160), channel_id=1, replica_groups=mesh['dy'=4,'dx'=4,'dz'=8,'sub'=2] {'dz'}, dimensions={0} | all-to-all | bytes 180224 | tf_op jit(solution)/shard_map/all_to_all | solution.py:71
  118.6 18.5 %all-gather = bf16[8,11,256]{2,1,0:T(8,128)(2,1)S(1)} all-gather(bf16[1,11,256]{2,1,0:T(8,128)(2,1)S(1)} %bitcast.122), channel_id=1, replica_groups=mesh['dy'=4,'dx'=4,'dz'=8,'sub'=2] {'dz'}, dimensions={0}, use_global_device_ids=true | all-gather | bytes 50688 | tf_op jit(solution)/shard_map/all_gather | solution.py:75
  137.1 16.8 %all-gather.1 = bf16[16,44,512]{2,1,0:T(8,128)(2,1)S(1)} all-gather(bf16[1,44,512]{2,1,0:T(8,128)(2,1)S(1)} %reshape.215), channel_id=1, replica_groups=mesh['dy'=4,'dx'=4,'dz'=8,'sub'=2] {'dy','dx'}, dimensions={0}, use_global_device_ids=true | all-gather | bytes 765952 | tf_op jit(solution)/shard_map/all_gather | solution.py:75
  154.1 13.9 %collective-permute-start.1 = (bf16[576,512]{1,0:T(8,128)(2,1)S(1)}, bf16[576,512]{1,0:T(8,128)(2,1)S(1)}, u32[]{:S(2)}, u32[]{:S(2)}) collective-permute-start(bf16[576,512]{1,0:T(8,128)(2,1)S(1)} %slice.219), channel_id=1, source_target_pairs={{0,1},{1,0},{2,3},{3,2},{4,5},{5,4},{6,7},{7,6},{8,9},{9,8},{10,11... | collective-permute-start | bytes 1769480 | tf_op jit(solution)/shard_map/ppermute | solution.py:79
  168.0 0.7 reshape.167
  168.8 0.9 collective-permute-done.1
  170.1 0.8 copy.71
  170.9 0.7 pad_maximum_fusion.4
  171.6 1.0 pad_maximum_fusion.2
  172.6 1.0 pad_maximum_fusion.1
  (115 shorter events, 8.4 us)
Async XLA Ops:
  0.6 54.4 %copy-start = (bf16[512,512]{1,0:T(8,128)(2,1)S(1)}, bf16[512,512]{1,0:T(8,128)(2,1)}, u32[]{:S(2)}) copy-start(bf16[512,512]{1,0:T(8,128)(2,1)} %param.18) | copy-start | bytes 1572868
  2.5 3.0 %copy-start.23 = (s32[1,1,128]{2,1,0:T(1,128)S(1)}, s32[1,1,128]{2,1,0:T(1,128)}, u32[]{:S(2)}) copy-start(s32[1,1,128]{2,1,0:T(1,128)} %param.23) | copy-start | bytes 1540
  5.8 17.9 %copy-start.20 = (s32[2]{0:T(128)S(1)}, s32[2]{0:T(128)}, u32[]{:S(2)}) copy-start(s32[2]{0:T(128)} %param.24) | copy-start | bytes 28
  5.8 18.4 %copy-start.18 = (bf16[2,256,128]{2,1,0:T(8,128)(2,1)S(1)}, bf16[2,256,128]{2,1,0:T(8,128)(2,1)}, u32[]{:S(2)}) copy-start(bf16[2,256,128]{2,1,0:T(8,128)(2,1)} %param.14) | copy-start | bytes 393220
  5.8 23.6 %copy-start.19 = (s32[256,4]{0,1:T(4,128)S(1)}, s32[256,4]{0,1:T(4,128)}, u32[]{:S(2)}) copy-start(s32[256,4]{0,1:T(4,128)} %param.13) | copy-start | bytes 12292
  5.9 24.1 %copy-start.14 = (bf16[16,128,128]{2,1,0:T(8,128)(2,1)S(1)}, bf16[16,128,128]{2,1,0:T(8,128)(2,1)}, u32[]{:S(2)}) copy-start(bf16[16,128,128]{2,1,0:T(8,128)(2,1)} %param.19) | copy-start | bytes 1572868
  7.2 25.2 %copy-start.21 = (s32[16]{0:T(128)S(1)}, s32[16]{0:T(128)}, u32[]{:S(2)}) copy-start(s32[16]{0:T(128)} %param.21) | copy-start | bytes 196
  7.2 25.2 %copy-start.22 = (s32[16]{0:T(128)S(1)}, s32[16]{0:T(128)}, u32[]{:S(2)}) copy-start(s32[16]{0:T(128)} %param.20) | copy-start | bytes 196
  7.2 25.3 %copy-start.11 = (f32[512,64]{0,1:T(8,128)S(1)}, f32[512,64]{0,1:T(8,128)}, u32[]{:S(2)}) copy-start(f32[512,64]{0,1:T(8,128)} %param.15) | copy-start | bytes 393220
  7.2 37.0 %all-to-all-start = ((s32[128,1,1152]{2,1,0:T(1,128)}), s32[128,1,1152]{2,1,0:T(1,128)S(1)}, u32[]{:S(2)}, u32[]{:S(2)}) async-start(s32[128,1,1152]{2,1,0:T(1,128)} %all_to_all.14), calls=%async_computation | async-start | bytes 1179648 | tf_op jit(solution)/shard_map/all_to_all | solution.py:124
  26.8 3.1 %copy-start.15 = (bf16[4,256,128]{2,1,0:T(8,128)(2,1)}, bf16[4,256,128]{2,1,0:T(8,128)(2,1)S(1)}, u32[]{:S(2)}) copy-start(bf16[4,256,128]{2,1,0:T(8,128)(2,1)S(1)} %all_gather.9) | copy-start | bytes 786436
  35.0 10.2 %copy-start.16 = (bf16[4,256,128]{2,1,0:T(8,128)(2,1)S(1)}, bf16[4,256,128]{2,1,0:T(8,128)(2,1)}, u32[]{:S(2)}) copy-start(bf16[4,256,128]{2,1,0:T(8,128)(2,1)} %copy-done.15) | copy-start | bytes 786436
  52.5 2.3 %copy-start.4 = (bf16[512,512]{1,0:T(8,128)(2,1)S(1)}, bf16[512,512]{1,0:T(8,128)(2,1)}, u32[]{:S(2)}) copy-start(bf16[512,512]{1,0:T(8,128)(2,1)} %param.17) | copy-start | bytes 1572868
  52.5 2.6 %copy-start.17 = (bf16[256,512]{1,0:T(8,128)(2,1)S(1)}, bf16[256,512]{1,0:T(8,128)(2,1)}, u32[]{:S(2)}) copy-start(bf16[256,512]{1,0:T(8,128)(2,1)} %param.25) | copy-start | bytes 786436
  56.9 2.0 %copy-start.1 = (bf16[16,128,512]{2,1,0:T(8,128)(2,1)S(1)}, bf16[16,128,512]{2,1,0:T(8,128)(2,1)}, u32[]{:S(2)}) copy-start(bf16[16,128,512]{2,1,0:T(8,128)(2,1)} %gather_fusion.1) | copy-start | bytes 6291460
  56.9 2.0 %copy-start.3 = (bf16[2,8,128,128]{2,3,1,0:T(8,128)(2,1)S(1)}, bf16[2,8,128,128]{2,3,1,0:T(8,128)(2,1)}, u32[]{:S(2)}) copy-start(bf16[2,8,128,128]{2,3,1,0:T(8,128)(2,1)} %copy.65) | copy-start | bytes 1572868
  58.9 3.8 %copy-start.12 = (f32[512,64]{0,1:T(8,128)S(1)}, f32[512,64]{0,1:T(8,128)}, u32[]{:S(2)}) copy-start(f32[512,64]{0,1:T(8,128)} %param.15) | copy-start | bytes 393220
  71.4 2.4 %copy-start.9 = (bf16[2048,128]{1,0:T(8,128)(2,1)S(1)}, bf16[2048,128]{1,0:T(8,128)(2,1)}, u32[]{:S(2)}) copy-start(bf16[2048,128]{1,0:T(8,128)(2,1)} %get-tuple-element.46) | copy-start | bytes 1572868
  71.4 2.4 %copy-start.10 = (bf16[2048,128]{1,0:T(8,128)(2,1)S(1)}, bf16[2048,128]{1,0:T(8,128)(2,1)}, u32[]{:S(2)}) copy-start(bf16[2048,128]{1,0:T(8,128)(2,1)} %get-tuple-element.47) | copy-start | bytes 1572868
  73.8 1.2 copy-start.7
  73.8 1.2 copy-start.8
  74.9 1.2 copy-start.6
  78.7 1.3 copy-start.2
  80.0 2.1 %copy-start.13 = (f32[512,64]{0,1:T(8,128)S(1)}, f32[512,64]{0,1:T(8,128)}, u32[]{:S(2)}) copy-start(f32[512,64]{0,1:T(8,128)} %fusion.86) | copy-start | bytes 393220
  81.0 5.6 %copy-start.5 = (f32[2,256,128]{2,1,0:T(8,128)S(1)}, f32[2,256,128]{2,1,0:T(8,128)}, u32[]{:S(2)}) copy-start(f32[2,256,128]{2,1,0:T(8,128)} %get-tuple-element.63) | copy-start | bytes 786436
  84.1 5.6 %collective-permute-start = (f32[704,512]{1,0:T(8,128)}, f32[704,512]{1,0:T(8,128)S(1)}, u32[]{:S(2)}, u32[]{:S(2)}) collective-permute-start(f32[704,512]{1,0:T(8,128)} %constant_dynamic-update-slice_fusion.1), channel_id=1, source_target_pairs={{0,1},{1,0},{2,3},{3,2},{4,5},{5,4},{6,7},{7,6},{8,9},{9,8},{10,11... | collective-permute-start | bytes 4325384 | tf_op jit(solution)/shard_map/ppermute | solution.py:59
  154.1 15.6 %collective-permute-start.1 = (bf16[576,512]{1,0:T(8,128)(2,1)S(1)}, bf16[576,512]{1,0:T(8,128)(2,1)S(1)}, u32[]{:S(2)}, u32[]{:S(2)}) collective-permute-start(bf16[576,512]{1,0:T(8,128)(2,1)S(1)} %slice.219), channel_id=1, source_target_pairs={{0,1},{1,0},{2,3},{3,2},{4,5},{5,4},{6,7},{7,6},{8,9},{9,8},{10,11... | collective-permute-start | bytes 1769480 | tf_op jit(solution)/shard_map/ppermute | solution.py:79

commit v11 on v9

--- a/solution.py
+++ b/solution.py
@@ -117,7 +117,11 @@
     targets = send_rows[0, 0]
     part_count = targets.shape[0]
     slot_valid = jnp.arange(SLOT, dtype=jnp.int32)[None, :] < send_count[0, 0][:, None]
-    out_codes = jnp.where(slot_valid[:, :, None], codes[targets], -1).reshape(part_count, -1)
+    target_hot = one_hot_codes(targets.reshape(-1), rows_dev, jnp.bfloat16)
+    picked_codes = jnp.dot(
+        target_hot, codes.astype(jnp.bfloat16), preferred_element_type=jnp.float32
+    ).astype(jnp.int32).reshape(targets.shape + (book_count,))
+    out_codes = jnp.where(slot_valid[:, :, None], picked_codes, -1).reshape(part_count, -1)
     own_codes = jnp.broadcast_to(codes.reshape(1, -1), (part_count, codes.size))
     room = -(-(codes.size + out_codes.shape[1]) // 128) * 128
     filler = jnp.zeros((part_count, room - codes.size - out_codes.shape[1]), jnp.int32)

time: 153 us -> 152 us (level)
  local copies, waits for them, and re-layouts: 22.1 us -> 20.3 us
    gather x2 -> x0, local copies, waits for them, and re-layouts: 3.02 us -> none  [shards(): codes[targets]]
    unnamed x55 -> x54, local copies, waits for them, and re-layouts: 6.03 us -> 6.87 us
where the time goes in v11:
time: 152 us; the launch traced here: 151 us
  blocking collectives  52.8 us (35%)
  matrix products  24.2 us (16%)
  starting transfers between devices  23.5 us (15%)
  local copies, waits for them, and re-layouts  20.3 us (13%)
  other arithmetic  13.1 us (9%)
  waiting for transfers between devices  12.3 us (8%)
  between operations  5.26 us (3%)
    all_to_all x2, blocking collectives, all_sum(): received = lax.all_to_all(chunks, axis, 0, 0, tiled=True)  27 us
    all_to_all x2, blocking collectives, all_sum(): piece = lax.all_to_all(spread, axis, 0, 0, tiled=True).reshape(shape)  23.2 us
    all_to_all x1, starting transfers between devices, shards(): incoming = lax.all_to_all(payload, DOM, 0, 0, tiled=True)  16.5 us
    all_to_all x1, waiting for transfers between devices, shards(): incoming = lax.all_to_all(payload, DOM, 0, 0, tiled=True)  9.21 us
    unnamed x54, local copies, waits for them, and re-layouts  6.87 us
    dot_general x8, matrix products, fold_books(): lax.dot_general(indicator_rows, both, (((0,), (0,)), ((), ())), preferred...  6.77 us
    ppermute x1, starting transfers between devices, all_sum(): other_dense = lax.ppermute(own_dense, 'sub', swap)  4.5 us
  transfers between devices with their start and end apart: 3, of which 3 were waited for; matrix products, arithmetic and copies ran while one was open for 4% of the time, Pallas kernels for 0%

profile of v11, /device:TPU:1, one launch (start us, length us, event | category | flops | bytes accessed | tf_op | source)
XLA Modules:
  0.0 151.4 jit_solution(2071168851903261964)
XLA Ops:
  0.6 0.8 copy.54
  1.6 0.8 copy.53
  2.4 1.0 convolution_convert_fusion.2
  3.9 0.7 iota_compare_fusion.24
  5.1 1.2 all_to_all.20
  6.3 16.5 %all-to-all-start = ((s32[128,1,1152]{2,1,0:T(1,128)}), s32[128,1,1152]{2,1,0:T(1,128)S(1)}, u32[]{:S(2)}, u32[]{:S(2)}) async-start(s32[128,1,1152]{2,1,0:T(1,128)} %all_to_all.20), calls=%async_computation | async-start | bytes 1179648 | tf_op jit(solution)/shard_map/all_to_all | solution.py:129
  23.4 2.6 %all_gather.3 = bf16[4,256,128]{2,1,0:T(8,128)(2,1)S(1)} all-gather(bf16[2,256,128]{2,1,0:T(8,128)(2,1)S(1)} %copy-done.18), channel_id=1, replica_groups=mesh['dy'=4,'dx'=4,'dz'=8,'sub'=2] {'sub'}, dimensions={0}, use_global_device_ids=true | all-gather | bytes 393216 | tf_op jit(solution)/shard_map/all_gather | solution.py:115
  29.2 1.0 copy.64
  31.5 1.9 %fusion.84 = f32[512,512]{1,0:T(8,128)S(1)} fusion(f32[512,64]{0,1:T(8,128)S(1)} %copy-done.11, f32[64,512]{1,0:T(8,128)} %param.16), kind=kOutput, calls=%fused_computation.160 | convolution fusion | flops 201326592 | bytes 1310720 | tf_op jit(solution)/shard_map/dot_general | solution.py:116
  34.1 9.2 %all-to-all-done = s32[128,1,1152]{2,1,0:T(1,128)S(1)} async-done(((s32[128,1,1152]{2,1,0:T(1,128)}), s32[128,1,1152]{2,1,0:T(1,128)S(1)}, u32[]{:S(2)}, u32[]{:S(2)}) %all-to-all-start) | async-done | bytes 589856 | tf_op jit(solution)/shard_map/all_to_all | solution.py:129
  44.3 2.2 %fusion.4 = bf16[4,1536,128]{1,2,0:T(8,128)(2,1)S(1)} fusion(bf16[4,256,128]{2,1,0:T(8,128)(2,1)S(1)} %copy-done.16, s32[1536,4]{0,1:T(4,128)S(1)} %pad_add_fusion), kind=kOutput, calls=%fused_computation.12 | convolution fusion | flops 405012480 | bytes 1859584 | tf_op jit(solution)/shard_map/feu,euq->feq/dot_general | solution.py:23
  46.4 1.6 %copy.63 = bf16[1536,512]{1,0:T(8,128)(2,1)} copy(bf16[1536,512]{0,1:T(8,128)(2,1)S(1)} %bitcast.106) | data formatting | bytes 3145728 | tf_op jit(solution)/shard_map/reshape | solution.py:26
  48.1 1.5 %pad_maximum_fusion = bf16[1792,512]{1,0:T(8,128)(2,1)S(1)} fusion(bf16[1536,512]{1,0:T(8,128)(2,1)} %copy.63, bf16[256,512]{1,0:T(8,128)(2,1)S(1)} %copy.62), kind=kLoop, calls=%fused_computation.23 | loop fusion | flops 3670016 | bytes 3670016 | tf_op jit(solution)/shard_map/concatenate | solution.py:137
  49.6 2.0 %gather_fusion = bf16[16,128,512]{2,1,0:T(8,128)(2,1)} fusion(bf16[14,128,512]{2,1,0:T(8,128)(2,1)S(1)} %bitcast.99, s32[1024]{0:T(1024)S(1)} %pad_clamp_fusion.1), kind=kCustom, calls=%fused_computation | custom fusion | bytes 4194368 | tf_op jit(solution)/shard_map/gather | solution.py:142
  51.6 2.3 %fusion.16 = bf16[2,512,128]{1,2,0:T(8,128)(2,1)S(1)} fusion(bf16[2,8,128,128]{3,2,1,0:T(8,128)(2,1)S(1)} %bitcast.112, bf16[2,8,128,512]{3,2,1,0:T(8,128)(2,1)} %bitcast.100, f32[2,8,512]{2,1,0:T(8,128)S(1)} %bitcast.113), kind=kOutput, calls=%fused_computation.29 | convolution fusion | flops 271712256 | bytes 2916352 | tf_op jit(solution)/shard_map/btij,btjd->bid/dot_general | solution.py:145
  54.2 1.1 multiply_convert_fusion
  56.0 1.3 fusion.86
  58.0 2.6 %fusion.2 = (f32[2,8,512]{2,1,0:T(8,128)S(1)}, f32[2,512,1024]{1,2,0}) fusion(bf16[2,8,128,512]{3,2,1,0:T(8,128)(2,1)S(1)} %bitcast.101, bf16[2,128,1024]{1,2,0:T(8,128)(2,1)S(1)} %bitcast.105, bf16[2,128,512]{2,1,0:T(8,128)(2,1)S(1)} %bitcast.107), kind=kOutput, calls=%fused_computation.9 | convolution fusion | flops 271572992 | bytes 7110656
  60.7 1.1 scatter_custom_fusion
  61.8 1.4 fusion.88
  63.2 1.9 %fusion.89 = f32[512,64]{1,0:T(8,128)S(1)} fusion(f32[512,512]{1,0:T(8,128)S(1)} %scatter_custom_fusion, f32[64,512]{1,0:T(8,128)} %param.16), kind=kOutput, calls=%fused_computation.165 | convolution fusion | flops 201326592 | bytes 1310720 | tf_op jit(solution)/shard_map/dot_general | solution.py:178
  65.1 2.7 %bitcast_multiply_fusion = f32[2048,512]{1,0:T(8,128)S(1)} fusion(f32[2,512,1024]{1,2,0} %get-tuple-element.88, f32[16,512]{1,0:T(8,128)S(1)} %gather_fusion.1), kind=kLoop, calls=%fused_computation.10 | loop fusion | flops 1048576 | bytes 8421376 | tf_op jit(solution)/shard_map/mul | solution.py:176
  67.8 2.1 %subtract_convert_fusion.3 = (bf16[2048,128]{1,0:T(8,128)(2,1)}, bf16[2048,128]{1,0:T(8,128)(2,1)}, bf16[2048,128]{1,0:T(8,128)(2,1)S(1)}, bf16[2048,128]{1,0:T(...) fusion(f32[2048,512]{1,0:T(8,128)S(1)} %bitcast_multiply_fusion), kind=kLoop, calls=%fused_computation.53 | loop fusion | flops 3145728 | bytes 10485760 | tf_op jit(solution)/shard_map/convert_element_type | solution.py:37
  70.5 2.3 %fusion.8 = f32[256,256]{1,0:T(8,128)S(1)} fusion(bf16[2048,128]{1,0:T(8,128)(2,1)} %get-tuple-element.34, bf16[2048,128]{1,0:T(8,128)(2,1)} %get-tuple-element.35, s32[2048]{0:T(1024)S(1)} %bitcast.118), kind=kOutput, calls=%fused_computation.19 | convolution fusion | flops 271056896 | bytes 1318912 | tf_op jit(solution)/shard_map/dot_general | solution.py:40
  72.9 1.0 fusion.9
  74.1 1.0 fusion.10
  75.2 1.0 fusion.11
  77.8 0.7 constant_dynamic-slice_fusion
  79.1 1.0 dynamic-slice_dynamic-update-slice_fusion.1
  80.1 1.1 dynamic-slice_dynamic-update-slice_fusion
  81.2 0.7 bitcast_dynamic-update-slice_fusion
  81.9 0.7 dynamic-slice_dynamic-update-slice_fusion.4
  82.5 0.7 constant_dynamic-update-slice_fusion.1
  83.3 2.5 %collective-permute-start = (f32[704,512]{1,0:T(8,128)}, f32[704,512]{1,0:T(8,128)S(1)}, u32[]{:S(2)}, u32[]{:S(2)}) collective-permute-start(f32[704,512]{1,0:T(8,128)} %constant_dynamic-update-slice_fusion.1), channel_id=1, source_target_pairs={{0,1},{1,0},{2,3},{3,2},{4,5},{5,4},{6,7},{7,6},{8,9},{9,8},{10,11... | collective-permute-start | bytes 4325384 | tf_op jit(solution)/shard_map/ppermute | solution.py:59
  85.8 0.8 constant_dynamic-update-slice_fusion
  86.6 2.3 %collective-permute-done = f32[704,512]{1,0:T(8,128)S(1)} collective-permute-done((f32[704,512]{1,0:T(8,128)}, f32[704,512]{1,0:T(8,128)S(1)}, u32[]{:S(2)}, u32[]{:S(2)}) %collective-permute-start) | collective-permute-done | bytes 1441824 | tf_op jit(solution)/shard_map/ppermute | solution.py:59
  88.8 1.6 %add_convert_fusion = bf16[704,512]{1,0:T(8,128)(2,1)S(1)} fusion(f32[704,512]{1,0:T(8,128)} %constant_dynamic-update-slice_fusion, f32[704,512]{1,0:T(8,128)S(1)} %collective-permute-done), kind=kLoop, calls=%fused_computation.25 | loop fusion | flops 720896 | bytes 3604480 | tf_op jit(solution)/shard_map/convert_element_type | solution.py:70
  90.5 16.7 %all_to_all.32 = bf16[16,44,512]{2,1,0:T(8,128)(2,1)S(1)} all-to-all(bf16[16,44,512]{2,1,0:T(8,128)(2,1)S(1)} %convert_element_type.195), channel_id=1, replica_groups=mesh['dy'=4,'dx'=4,'dz'=8,'sub'=2] {'dy','dx'}, dimensions={0} | all-to-all | bytes 1441792 | tf_op jit(solution)/shard_map/all_to_all | solution.py:71
  107.4 10.3 %all_to_all.33 = f32[8,11,256]{2,1,0:T(8,128)S(1)} all-to-all(f32[8,11,256]{2,1,0:T(8,128)S(1)} %reshape.139), channel_id=1, replica_groups=mesh['dy'=4,'dx'=4,'dz'=8,'sub'=2] {'dz'}, dimensions={0} | all-to-all | bytes 180224 | tf_op jit(solution)/shard_map/all_to_all | solution.py:71
  117.8 9.6 %all_to_all.34 = bf16[8,11,256]{2,1,0:T(8,128)(2,1)S(1)} all-to-all(bf16[8,11,256]{2,1,0:T(8,128)(2,1)S(1)} %broadcast_in_dim.74), channel_id=1, replica_groups=mesh['dy'=4,'dx'=4,'dz'=8,'sub'=2] {'dz'}, dimensions={0} | all-to-all | bytes 90112 | tf_op jit(solution)/shard_map/all_to_all | solution.py:76
  127.5 13.6 %all_to_all.35 = bf16[16,44,512]{2,1,0:T(8,128)(2,1)S(1)} all-to-all(bf16[16,44,512]{2,1,0:T(8,128)(2,1)S(1)} %broadcast_in_dim.76), channel_id=1, replica_groups=mesh['dy'=4,'dx'=4,'dz'=8,'sub'=2] {'dy','dx'}, dimensions={0} | all-to-all | bytes 1441792 | tf_op jit(solution)/shard_map/all_to_all | solution.py:76
  141.2 4.5 %collective-permute-start.1 = (bf16[576,512]{1,0:T(8,128)(2,1)S(1)}, bf16[576,512]{1,0:T(8,128)(2,1)S(1)}, u32[]{:S(2)}, u32[]{:S(2)}) collective-permute-start(bf16[576,512]{1,0:T(8,128)(2,1)S(1)} %slice.217), channel_id=1, source_target_pairs={{0,1},{1,0},{2,3},{3,2},{4,5},{5,4},{6,7},{7,6},{8,9},{9,8},{10,11... | collective-permute-start | bytes 1769480 | tf_op jit(solution)/shard_map/ppermute | solution.py:80
  145.8 0.7 reshape.146
  146.5 0.9 collective-permute-done.1
  147.8 0.8 copy.70
  148.6 0.7 pad_maximum_fusion.4
  149.3 1.0 pad_maximum_fusion.2
  150.3 1.0 pad_maximum_fusion.1
  (116 shorter events, 9.2 us)
Async XLA Ops:
  0.6 53.6 %copy-start = (bf16[512,512]{1,0:T(8,128)(2,1)S(1)}, bf16[512,512]{1,0:T(8,128)(2,1)}, u32[]{:S(2)}) copy-start(bf16[512,512]{1,0:T(8,128)(2,1)} %param.18) | copy-start | bytes 1572868
  4.9 17.9 %copy-start.20 = (s32[2]{0:T(128)S(1)}, s32[2]{0:T(128)}, u32[]{:S(2)}) copy-start(s32[2]{0:T(128)} %param.24) | copy-start | bytes 28
  4.9 18.4 %copy-start.18 = (bf16[2,256,128]{2,1,0:T(8,128)(2,1)S(1)}, bf16[2,256,128]{2,1,0:T(8,128)(2,1)}, u32[]{:S(2)}) copy-start(bf16[2,256,128]{2,1,0:T(8,128)(2,1)} %param.14) | copy-start | bytes 393220
  4.9 23.6 %copy-start.19 = (s32[256,4]{0,1:T(4,128)S(1)}, s32[256,4]{0,1:T(4,128)}, u32[]{:S(2)}) copy-start(s32[256,4]{0,1:T(4,128)} %param.13) | copy-start | bytes 12292
  5.1 24.1 %copy-start.14 = (bf16[16,128,128]{2,1,0:T(8,128)(2,1)S(1)}, bf16[16,128,128]{2,1,0:T(8,128)(2,1)}, u32[]{:S(2)}) copy-start(bf16[16,128,128]{2,1,0:T(8,128)(2,1)} %param.19) | copy-start | bytes 1572868
  6.3 25.2 %copy-start.21 = (s32[16]{0:T(128)S(1)}, s32[16]{0:T(128)}, u32[]{:S(2)}) copy-start(s32[16]{0:T(128)} %param.21) | copy-start | bytes 196
  6.3 25.2 %copy-start.22 = (s32[16]{0:T(128)S(1)}, s32[16]{0:T(128)}, u32[]{:S(2)}) copy-start(s32[16]{0:T(128)} %param.20) | copy-start | bytes 196
  6.3 25.3 %copy-start.11 = (f32[512,64]{0,1:T(8,128)S(1)}, f32[512,64]{0,1:T(8,128)}, u32[]{:S(2)}) copy-start(f32[512,64]{0,1:T(8,128)} %param.15) | copy-start | bytes 393220
  6.3 37.0 %all-to-all-start = ((s32[128,1,1152]{2,1,0:T(1,128)}), s32[128,1,1152]{2,1,0:T(1,128)S(1)}, u32[]{:S(2)}, u32[]{:S(2)}) async-start(s32[128,1,1152]{2,1,0:T(1,128)} %all_to_all.20), calls=%async_computation | async-start | bytes 1179648 | tf_op jit(solution)/shard_map/all_to_all | solution.py:129
  25.9 3.1 %copy-start.15 = (bf16[4,256,128]{2,1,0:T(8,128)(2,1)}, bf16[4,256,128]{2,1,0:T(8,128)(2,1)S(1)}, u32[]{:S(2)}) copy-start(bf16[4,256,128]{2,1,0:T(8,128)(2,1)S(1)} %all_gather.3) | copy-start | bytes 786436
  34.1 10.2 %copy-start.16 = (bf16[4,256,128]{2,1,0:T(8,128)(2,1)S(1)}, bf16[4,256,128]{2,1,0:T(8,128)(2,1)}, u32[]{:S(2)}) copy-start(bf16[4,256,128]{2,1,0:T(8,128)(2,1)} %copy-done.15) | copy-start | bytes 786436
  51.6 2.3 %copy-start.4 = (bf16[512,512]{1,0:T(8,128)(2,1)S(1)}, bf16[512,512]{1,0:T(8,128)(2,1)}, u32[]{:S(2)}) copy-start(bf16[512,512]{1,0:T(8,128)(2,1)} %param.17) | copy-start | bytes 1572868
  51.6 2.6 %copy-start.17 = (bf16[256,512]{1,0:T(8,128)(2,1)S(1)}, bf16[256,512]{1,0:T(8,128)(2,1)}, u32[]{:S(2)}) copy-start(bf16[256,512]{1,0:T(8,128)(2,1)} %param.25) | copy-start | bytes 786436
  56.0 2.0 %copy-start.1 = (bf16[16,128,512]{2,1,0:T(8,128)(2,1)S(1)}, bf16[16,128,512]{2,1,0:T(8,128)(2,1)}, u32[]{:S(2)}) copy-start(bf16[16,128,512]{2,1,0:T(8,128)(2,1)} %gather_fusion) | copy-start | bytes 6291460
  56.0 2.0 %copy-start.3 = (bf16[2,8,128,128]{2,3,1,0:T(8,128)(2,1)S(1)}, bf16[2,8,128,128]{2,3,1,0:T(8,128)(2,1)}, u32[]{:S(2)}) copy-start(bf16[2,8,128,128]{2,3,1,0:T(8,128)(2,1)} %copy.64) | copy-start | bytes 1572868
  58.0 3.8 %copy-start.12 = (f32[512,64]{0,1:T(8,128)S(1)}, f32[512,64]{0,1:T(8,128)}, u32[]{:S(2)}) copy-start(f32[512,64]{0,1:T(8,128)} %param.15) | copy-start | bytes 393220
  70.5 2.4 %copy-start.9 = (bf16[2048,128]{1,0:T(8,128)(2,1)S(1)}, bf16[2048,128]{1,0:T(8,128)(2,1)}, u32[]{:S(2)}) copy-start(bf16[2048,128]{1,0:T(8,128)(2,1)} %get-tuple-element.46) | copy-start | bytes 1572868
  70.5 2.4 %copy-start.10 = (bf16[2048,128]{1,0:T(8,128)(2,1)S(1)}, bf16[2048,128]{1,0:T(8,128)(2,1)}, u32[]{:S(2)}) copy-start(bf16[2048,128]{1,0:T(8,128)(2,1)} %get-tuple-element.47) | copy-start | bytes 1572868
  72.9 1.2 copy-start.7
  72.9 1.2 copy-start.8
  74.0 1.2 copy-start.6
  77.7 1.3 copy-start.2
  79.1 2.2 %copy-start.13 = (f32[512,64]{0,1:T(8,128)S(1)}, f32[512,64]{0,1:T(8,128)}, u32[]{:S(2)}) copy-start(f32[512,64]{0,1:T(8,128)} %fusion.88) | copy-start | bytes 393220
  80.1 5.6 %copy-start.5 = (f32[2,256,128]{2,1,0:T(8,128)S(1)}, f32[2,256,128]{2,1,0:T(8,128)}, u32[]{:S(2)}) copy-start(f32[2,256,128]{2,1,0:T(8,128)} %get-tuple-element.63) | copy-start | bytes 786436
  83.3 5.6 %collective-permute-start = (f32[704,512]{1,0:T(8,128)}, f32[704,512]{1,0:T(8,128)S(1)}, u32[]{:S(2)}, u32[]{:S(2)}) collective-permute-start(f32[704,512]{1,0:T(8,128)} %constant_dynamic-update-slice_fusion.1), channel_id=1, source_target_pairs={{0,1},{1,0},{2,3},{3,2},{4,5},{5,4},{6,7},{7,6},{8,9},{9,8},{10,11... | collective-permute-start | bytes 4325384 | tf_op jit(solution)/shard_map/ppermute | solution.py:59
  141.2 6.1 %collective-permute-start.1 = (bf16[576,512]{1,0:T(8,128)(2,1)S(1)}, bf16[576,512]{1,0:T(8,128)(2,1)S(1)}, u32[]{:S(2)}, u32[]{:S(2)}) collective-permute-start(bf16[576,512]{1,0:T(8,128)(2,1)S(1)} %slice.217), channel_id=1, source_target_pairs={{0,1},{1,0},{2,3},{3,2},{4,5},{5,4},{6,7},{7,6},{8,9},{9,8},{10,11... | collective-permute-start | bytes 1769480 | tf_op jit(solution)/shard_map/ppermute | solution.py:80

commit v12 on v11

--- a/solution.py
+++ b/solution.py
@@ -50,13 +50,13 @@
     share = book_grad.shape[0] // 2
     dense = [grad_w_msg, grad_w_self, part_basis, part_alpha.reshape(-1, width)]
 
-    def half_of(h):
-        pieces = [lax.dynamic_slice_in_dim(x, h * (x.shape[0] // 2), x.shape[0] // 2, 0) for x in dense]
-        pieces.append(lax.dynamic_slice_in_dim(book_grad, h * share, share, 0).reshape(-1, width))
-        return jnp.concatenate(pieces, axis=0)
-
+    lows = [x[: x.shape[0] // 2] for x in dense] + [book_grad[:share].reshape(-1, width)]
+    highs = [x[x.shape[0] // 2 :] for x in dense] + [book_grad[share:].reshape(-1, width)]
+    stacked = jnp.stack([jnp.concatenate(lows, axis=0), jnp.concatenate(highs, axis=0)])
+    keep = lax.dynamic_index_in_dim(stacked, sub_index, 0, keepdims=False)
+    give = lax.dynamic_index_in_dim(stacked, 1 - sub_index, 0, keepdims=False)
     swap = [(0, 1), (1, 0)]
-    mine = half_of(sub_index) + lax.ppermute(half_of(1 - sub_index), "sub", swap)
+    mine = keep + lax.ppermute(give, "sub", swap)
     rows = mine.shape[0]
     shapes = []
     piece = mine

time: 152 us -> 165 us (1.086)
  local copies, waits for them, and re-layouts: 20.3 us -> 28.8 us
  other arithmetic: 13.1 us -> 16 us
    slice x0 -> x6, local copies, waits for them, and re-layouts: none -> 7.07 us  [the longest x2 3.22 us: all_sum(): x[:x.shape[0] // 2]]
    reshape x3 -> x2, local copies, waits for them, and re-layouts: 0.2 us -> 3.43 us  [the longest x1 1.73 us: all_sum(): book_grad[:share].reshape(-1, width)]
    unnamed x54 -> x91, local copies, waits for them, and re-layouts: 6.87 us -> 5.34 us
  transfers between devices with their start and end apart: 3 -> 3, of which waited for: 3 -> 3; matrix products, arithmetic and copies ran while one was open for 4% -> 3% of each run, Pallas kernels for 0% -> 0%
where the time goes in v12:
time: 165 us; the launch traced here: 164 us
  blocking collectives  52.8 us (32%)
  local copies, waits for them, and re-layouts  28.8 us (17%)
  matrix products  24.4 us (15%)
  starting transfers between devices  23.4 us (14%)
  other arithmetic  16 us (10%)
  waiting for transfers between devices  13.1 us (8%)
  between operations  5.46 us (3%)
    all_to_all x2, blocking collectives, all_sum(): received = lax.all_to_all(chunks, axis, 0, 0, tiled=True)  27 us
    all_to_all x2, blocking collectives, all_sum(): piece = lax.all_to_all(spread, axis, 0, 0, tiled=True).reshape(shape)  23.2 us
    all_to_all x1, starting transfers between devices, shards(): incoming = lax.all_to_all(payload, DOM, 0, 0, tiled=True)  16.5 us
    all_to_all x1, waiting for transfers between devices, shards(): incoming = lax.all_to_all(payload, DOM, 0, 0, tiled=True)  8.99 us
    dot_general x8, matrix products, fold_books(): lax.dot_general(indicator_rows, both, (((0,), (0,)), ((), ())), preferred...  6.77 us
    unnamed x91, local copies, waits for them, and re-layouts  5.34 us
    ppermute x1, starting transfers between devices, all_sum(): other_dense = lax.ppermute(own_dense, 'sub', swap)  4.5 us
  transfers between devices with their start and end apart: 3, of which 3 were waited for; matrix products, arithmetic and copies ran while one was open for 3% of the time, Pallas kernels for 0%

profile of v12, /device:TPU:1, one launch (start us, length us, event | category | flops | bytes accessed | tf_op | source)
XLA Modules:
  0.0 164.0 jit_solution(3544823404853489668)
XLA Ops:
  0.7 0.8 copy.57
  1.6 0.8 copy.56
  2.4 1.0 convolution_convert_fusion.2
  4.4 1.2 all_to_all.20
  5.6 16.5 %all-to-all-start = ((s32[128,1,1152]{2,1,0:T(1,128)}), s32[128,1,1152]{2,1,0:T(1,128)S(1)}, u32[]{:S(2)}, u32[]{:S(2)}) async-start(s32[128,1,1152]{2,1,0:T(1,128)} %all_to_all.20), calls=%async_computation | async-start | bytes 1179648 | tf_op jit(solution)/shard_map/all_to_all | solution.py:129
  22.8 2.6 %all_gather.3 = bf16[4,256,128]{2,1,0:T(8,128)(2,1)S(1)} all-gather(bf16[2,256,128]{2,1,0:T(8,128)(2,1)S(1)} %copy-done.25), channel_id=1, replica_groups=mesh['dy'=4,'dx'=4,'dz'=8,'sub'=2] {'sub'}, dimensions={0}, use_global_device_ids=true | all-gather | bytes 393216 | tf_op jit(solution)/shard_map/all_gather | solution.py:115
  30.2 1.0 fusion.92
  31.3 1.2 gather_fusion.1
  33.7 9.0 %all-to-all-done = s32[128,1,1152]{2,1,0:T(1,128)S(1)} async-done(((s32[128,1,1152]{2,1,0:T(1,128)}), s32[128,1,1152]{2,1,0:T(1,128)S(1)}, u32[]{:S(2)}, u32[]{:S(2)}) %all-to-all-start) | async-done | bytes 589856 | tf_op jit(solution)/shard_map/all_to_all | solution.py:129
  43.8 2.1 %fusion.4 = bf16[4,1536,128]{1,2,0:T(8,128)(2,1)S(1)} fusion(bf16[4,256,128]{2,1,0:T(8,128)(2,1)S(1)} %copy-done.21, s32[1536,4]{0,1:T(4,128)S(1)} %pad_add_fusion), kind=kOutput, calls=%fused_computation.16 | convolution fusion | flops 405012480 | bytes 1859584 | tf_op jit(solution)/shard_map/feu,euq->feq/dot_general | solution.py:23
  45.9 1.6 copy.66
  47.5 1.5 pad_maximum_fusion
  49.0 2.3 %gather_fusion = bf16[16,128,512]{2,1,0:T(8,128)(2,1)} fusion(bf16[14,128,512]{2,1,0:T(8,128)(2,1)S(1)} %bitcast.107, s32[1024]{0:T(1024)} %pad_clamp_fusion.1), kind=kCustom, calls=%fused_computation | custom fusion | bytes 4194368 | tf_op jit(solution)/shard_map/gather | solution.py:142
  51.3 2.4 %fusion.22 = bf16[2,512,128]{1,2,0:T(8,128)(2,1)S(1)} fusion(bf16[2,8,128,128]{3,2,1,0:T(8,128)(2,1)} %bitcast.123, bf16[2,8,128,512]{3,2,1,0:T(8,128)(2,1)} %bitcast.108, f32[2,8,512]{2,1,0:T(8,128)S(1)} %bitcast.125), kind=kOutput, calls=%fused_computation.38 | convolution fusion | flops 271712256 | bytes 2916352 | tf_op jit(solution)/shard_map/btij,btjd->bid/dot_general | solution.py:145
  54.1 1.1 multiply_convert_fusion
  55.1 1.3 fusion.94
  56.4 1.3 fusion.95
  58.4 2.6 %fusion.2 = (f32[2,8,512]{2,1,0:T(8,128)S(1)}, f32[2,512,1024]{1,2,0}) fusion(bf16[2,8,128,512]{3,2,1,0:T(8,128)(2,1)S(1)} %bitcast.109, bf16[2,128,1024]{1,2,0:T(8,128)(2,1)S(1)} %bitcast.117, bf16[2,128,512]{2,1,0:T(8,128)(2,1)S(1)} %bitcast.119), kind=kOutput, calls=%fused_computation.9 | convolution fusion | flops 271572992 | bytes 7110656
  61.1 1.2 scatter_custom_fusion
  62.3 1.4 convolution_bitcast_fusion
  63.8 1.1 fusion.96
  65.0 1.1 fusion.97
  67.6 1.6 %slice.218 = f32[32,512]{1,0:T(8,128)} reshape(f32[256,64]{1,0:T(8,128)} %copy.73) | data formatting | bytes 131072 | tf_op jit(solution)/shard_map/slice | solution.py:54
  69.2 2.7 %bitcast_multiply_fusion = f32[2048,512]{1,0:T(8,128)S(1)} fusion(f32[2,512,1024]{1,2,0} %get-tuple-element.88, f32[16,512]{1,0:T(8,128)S(1)} %copy-done.24), kind=kLoop, calls=%fused_computation.10 | loop fusion | flops 1048576 | bytes 8421376 | tf_op jit(solution)/shard_map/mul | solution.py:176
  71.9 2.2 %subtract_convert_fusion.3 = (bf16[2048,128]{1,0:T(8,128)(2,1)}, bf16[2048,128]{1,0:T(8,128)(2,1)}, bf16[2048,128]{1,0:T(8,128)(2,1)}, bf16[2048,128]{1,0:T(8,12...) fusion(f32[2048,512]{1,0:T(8,128)S(1)} %bitcast_multiply_fusion), kind=kLoop, calls=%fused_computation.63 | loop fusion | flops 3145728 | bytes 10485760 | tf_op jit(solution)/shard_map/convert_element_type | solution.py:37
  74.9 2.3 %fusion.8 = f32[256,256]{1,0:T(8,128)S(1)} fusion(bf16[2048,128]{1,0:T(8,128)(2,1)} %get-tuple-element.34, bf16[2048,128]{1,0:T(8,128)(2,1)} %get-tuple-element.35, s32[2048]{0:T(1024)S(1)} %bitcast.130), kind=kOutput, calls=%fused_computation.23 | convolution fusion | flops 271056896 | bytes 1318912 | tf_op jit(solution)/shard_map/dot_general | solution.py:40
  77.3 1.0 fusion.9
  78.5 1.0 fusion.10
  79.7 1.0 fusion.11
  83.0 0.8 fusion.87
  83.8 1.7 %reshape.137 = f32[128,512]{1,0:T(8,128)} reshape(f32[2,256,128]{2,1,0:T(8,128)} %get-tuple-element.62) | data formatting | bytes 524288 | tf_op jit(solution)/shard_map/reshape | solution.py:54
  85.5 1.7 %reshape.136 = f32[128,512]{1,0:T(8,128)} reshape(f32[2,256,128]{2,1,0:T(8,128)} %get-tuple-element.63) | data formatting | bytes 524288 | tf_op jit(solution)/shard_map/reshape | solution.py:53
  87.2 1.6 copy.68
  88.8 1.6 slice.180
  90.5 1.3 slice_dynamic-update-slice_fusion
  92.0 1.5 fusion.13
  93.5 2.5 %collective-permute-start = (f32[704,512]{1,0:T(8,128)}, f32[704,512]{1,0:T(8,128)}, u32[]{:S(2)}, u32[]{:S(2)}) collective-permute-start(f32[704,512]{1,0:T(8,128)} %fusion.13), channel_id=1, source_target_pairs={{0,1},{1,0},{2,3},{3,2},{4,5},{5,4},{6,7},{7,6},{8,9},{9,8},{10,11... | collective-permute-start | bytes 4325384 | tf_op jit(solution)/shard_map/ppermute | solution.py:59
  95.9 3.2 %collective-permute-done = f32[704,512]{1,0:T(8,128)} collective-permute-done((f32[704,512]{1,0:T(8,128)}, f32[704,512]{1,0:T(8,128)}, u32[]{:S(2)}, u32[]{:S(2)}) %collective-permute-start) | collective-permute-done | bytes 1441824 | tf_op jit(solution)/shard_map/ppermute | solution.py:59
  99.1 2.8 %fusion.17 = bf16[704,512]{1,0:T(8,128)(2,1)} fusion(f32[704,512]{1,0:T(8,128)} %collective-permute-done, s32[]{:T(128)S(6)} %select_n.44, f32[1,704,512]{2,1,0:T(8,128)S(1)} %bitcast.113, f32[1,704,512]{2,1,0:T(8,128)S(1)} %bitcast.111), kind=kLoop, calls=%fused_computation.34 | loop fusion | flops 1081344 | bytes 5046276 | tf_op jit(solution)/shard_map/convert_element_type | solution.py:70
  101.9 1.2 convert_element_type.195
  103.1 16.7 %all_to_all.32 = bf16[16,44,512]{2,1,0:T(8,128)(2,1)S(1)} all-to-all(bf16[16,44,512]{2,1,0:T(8,128)(2,1)S(1)} %convert_element_type.195), channel_id=1, replica_groups=mesh['dy'=4,'dx'=4,'dz'=8,'sub'=2] {'dy','dx'}, dimensions={0} | all-to-all | bytes 1441792 | tf_op jit(solution)/shard_map/all_to_all | solution.py:71
  120.0 10.3 %all_to_all.33 = f32[8,11,256]{2,1,0:T(8,128)S(1)} all-to-all(f32[8,11,256]{2,1,0:T(8,128)S(1)} %reshape.138), channel_id=1, replica_groups=mesh['dy'=4,'dx'=4,'dz'=8,'sub'=2] {'dz'}, dimensions={0} | all-to-all | bytes 180224 | tf_op jit(solution)/shard_map/all_to_all | solution.py:71
  130.3 9.6 %all_to_all.34 = bf16[8,11,256]{2,1,0:T(8,128)(2,1)S(1)} all-to-all(bf16[8,11,256]{2,1,0:T(8,128)(2,1)S(1)} %broadcast_in_dim.74), channel_id=1, replica_groups=mesh['dy'=4,'dx'=4,'dz'=8,'sub'=2] {'dz'}, dimensions={0} | all-to-all | bytes 90112 | tf_op jit(solution)/shard_map/all_to_all | solution.py:76
  140.1 13.6 %all_to_all.35 = bf16[16,44,512]{2,1,0:T(8,128)(2,1)S(1)} all-to-all(bf16[16,44,512]{2,1,0:T(8,128)(2,1)S(1)} %broadcast_in_dim.76), channel_id=1, replica_groups=mesh['dy'=4,'dx'=4,'dz'=8,'sub'=2] {'dy','dx'}, dimensions={0} | all-to-all | bytes 1441792 | tf_op jit(solution)/shard_map/all_to_all | solution.py:76
  153.8 4.5 %collective-permute-start.1 = (bf16[576,512]{1,0:T(8,128)(2,1)S(1)}, bf16[576,512]{1,0:T(8,128)(2,1)S(1)}, u32[]{:S(2)}, u32[]{:S(2)}) collective-permute-start(bf16[576,512]{1,0:T(8,128)(2,1)S(1)} %slice.275), channel_id=1, source_target_pairs={{0,1},{1,0},{2,3},{3,2},{4,5},{5,4},{6,7},{7,6},{8,9},{9,8},{10,11... | collective-permute-start | bytes 1769480 | tf_op jit(solution)/shard_map/ppermute | solution.py:80
  159.1 0.9 collective-permute-done.1
  161.9 1.0 pad_maximum_fusion.2
  162.9 1.0 pad_maximum_fusion.1
  (158 shorter events, 13.5 us)
Async XLA Ops:
  0.6 53.4 %copy-start = (bf16[512,512]{1,0:T(8,128)(2,1)S(1)}, bf16[512,512]{1,0:T(8,128)(2,1)}, u32[]{:S(2)}) copy-start(bf16[512,512]{1,0:T(8,128)(2,1)} %param.18) | copy-start | bytes 1572868
  0.6 3.3 %copy-start.40 = (s32[1,1,128]{2,1,0:T(1,128)S(1)}, s32[1,1,128]{2,1,0:T(1,128)}, u32[]{:S(2)}) copy-start(s32[1,1,128]{2,1,0:T(1,128)} %param.23) | copy-start | bytes 1540
  4.3 17.8 %copy-start.36 = (s32[2]{0:T(128)S(1)}, s32[2]{0:T(128)}, u32[]{:S(2)}) copy-start(s32[2]{0:T(128)} %param.24) | copy-start | bytes 28
  4.3 18.5 %copy-start.25 = (bf16[2,256,128]{2,1,0:T(8,128)(2,1)S(1)}, bf16[2,256,128]{2,1,0:T(8,128)(2,1)}, u32[]{:S(2)}) copy-start(bf16[2,256,128]{2,1,0:T(8,128)(2,1)} %param.14) | copy-start | bytes 393220
  4.4 23.5 %copy-start.30 = (s32[256,4]{0,1:T(4,128)S(1)}, s32[256,4]{0,1:T(4,128)}, u32[]{:S(2)}) copy-start(s32[256,4]{0,1:T(4,128)} %param.13) | copy-start | bytes 12292
  5.6 22.9 %copy-start.17 = (bf16[16,128,128]{2,1,0:T(8,128)(2,1)S(1)}, bf16[16,128,128]{2,1,0:T(8,128)(2,1)}, u32[]{:S(2)}) copy-start(bf16[16,128,128]{2,1,0:T(8,128)(2,1)} %param.19) | copy-start | bytes 1572868
  5.6 37.0 %all-to-all-start = ((s32[128,1,1152]{2,1,0:T(1,128)}), s32[128,1,1152]{2,1,0:T(1,128)S(1)}, u32[]{:S(2)}, u32[]{:S(2)}) async-start(s32[128,1,1152]{2,1,0:T(1,128)} %all_to_all.20), calls=%async_computation | async-start | bytes 1179648 | tf_op jit(solution)/shard_map/all_to_all | solution.py:129
  22.1 8.0 %copy-start.38 = (s32[16]{0:T(128)S(1)}, s32[16]{0:T(128)}, u32[]{:S(2)}) copy-start(s32[16]{0:T(128)} %param.21) | copy-start | bytes 196
  22.1 8.0 %copy-start.39 = (s32[16]{0:T(128)S(1)}, s32[16]{0:T(128)}, u32[]{:S(2)}) copy-start(s32[16]{0:T(128)} %param.20) | copy-start | bytes 196
  22.2 8.1 %copy-start.13 = (f32[512,64]{0,1:T(8,128)S(1)}, f32[512,64]{0,1:T(8,128)}, u32[]{:S(2)}) copy-start(f32[512,64]{0,1:T(8,128)} %param.15) | copy-start | bytes 393220
  22.2 8.1 %copy-start.14 = (f32[64,512]{1,0:T(8,128)S(1)}, f32[64,512]{1,0:T(8,128)}, u32[]{:S(2)}) copy-start(f32[64,512]{1,0:T(8,128)} %param.16) | copy-start | bytes 393220
  25.3 4.9 %copy-start.20 = (bf16[4,256,128]{2,1,0:T(8,128)(2,1)}, bf16[4,256,128]{2,1,0:T(8,128)(2,1)S(1)}, u32[]{:S(2)}) copy-start(bf16[4,256,128]{2,1,0:T(8,128)(2,1)S(1)} %all_gather.3) | copy-start | bytes 786436
  30.2 1.1 copy-start.37
  32.5 11.3 %copy-start.21 = (bf16[4,256,128]{2,1,0:T(8,128)(2,1)S(1)}, bf16[4,256,128]{2,1,0:T(8,128)(2,1)}, u32[]{:S(2)}) copy-start(bf16[4,256,128]{2,1,0:T(8,128)(2,1)} %copy-done.20) | copy-start | bytes 786436
  42.9 0.7 copy-start.26
  43.1 0.6 copy-start.28
  49.0 2.3 %copy-start.23 = (f32[16,512]{1,0:T(8,128)S(1)}, f32[16,512]{1,0:T(8,128)}, u32[]{:S(2)}) copy-start(f32[16,512]{1,0:T(8,128)} %gather_fusion.1) | copy-start | bytes 98308
  51.3 2.4 %copy-start.4 = (bf16[512,512]{1,0:T(8,128)(2,1)S(1)}, bf16[512,512]{1,0:T(8,128)(2,1)}, u32[]{:S(2)}) copy-start(bf16[512,512]{1,0:T(8,128)(2,1)} %param.17) | copy-start | bytes 1572868
  51.3 2.7 %copy-start.22 = (bf16[256,512]{1,0:T(8,128)(2,1)S(1)}, bf16[256,512]{1,0:T(8,128)(2,1)}, u32[]{:S(2)}) copy-start(bf16[256,512]{1,0:T(8,128)(2,1)} %param.25) | copy-start | bytes 786436
  56.4 2.0 %copy-start.1 = (bf16[16,128,512]{2,1,0:T(8,128)(2,1)S(1)}, bf16[16,128,512]{2,1,0:T(8,128)(2,1)}, u32[]{:S(2)}) copy-start(bf16[16,128,512]{2,1,0:T(8,128)(2,1)} %gather_fusion) | copy-start | bytes 6291460
  61.1 2.7 %copy-start.15 = (f32[64,512]{1,0:T(8,128)S(1)}, f32[64,512]{1,0:T(8,128)}, u32[]{:S(2)}) copy-start(f32[64,512]{1,0:T(8,128)} %param.16) | copy-start | bytes 393220
  62.3 2.6 %copy-start.27 = (s32[256,4]{0,1:T(4,128)S(1)}, s32[256,4]{0,1:T(4,128)}, u32[]{:S(2)}) copy-start(s32[256,4]{0,1:T(4,128)} %copy-done.26) | copy-start | bytes 12292
  62.3 2.6 %copy-start.29 = (s32[256,4]{0,1:T(4,128)S(1)}, s32[256,4]{0,1:T(4,128)}, u32[]{:S(2)}) copy-start(s32[256,4]{0,1:T(4,128)} %copy-done.28) | copy-start | bytes 12292
  62.3 2.6 %copy-start.31 = (s32[256,4]{0,1:T(4,128)S(1)}, s32[256,4]{0,1:T(4,128)}, u32[]{:S(2)}) copy-start(s32[256,4]{0,1:T(4,128)} %param.13) | copy-start | bytes 12292
  63.8 2.3 %copy-start.2 = (f32[512,512]{1,0:T(8,128)S(1)}, f32[512,512]{1,0:T(8,128)}, u32[]{:S(2)}) copy-start(f32[512,512]{1,0:T(8,128)} %fusion.94) | copy-start | bytes 3145732
  66.1 3.1 %copy-start.24 = (f32[16,512]{1,0:T(8,128)S(1)}, f32[16,512]{1,0:T(8,128)}, u32[]{:S(2)}) copy-start(f32[16,512]{1,0:T(8,128)} %gather_fusion.1) | copy-start | bytes 98308
  74.9 2.4 %copy-start.11 = (bf16[2048,128]{1,0:T(8,128)(2,1)S(1)}, bf16[2048,128]{1,0:T(8,128)(2,1)}, u32[]{:S(2)}) copy-start(bf16[2048,128]{1,0:T(8,128)(2,1)} %get-tuple-element.46) | copy-start | bytes 1572868
  74.9 2.4 %copy-start.12 = (bf16[2048,128]{1,0:T(8,128)(2,1)S(1)}, bf16[2048,128]{1,0:T(8,128)(2,1)}, u32[]{:S(2)}) copy-start(bf16[2048,128]{1,0:T(8,128)(2,1)} %get-tuple-element.47) | copy-start | bytes 1572868
  77.3 1.1 copy-start.9
  77.3 1.2 copy-start.10
  78.5 1.1 copy-start.7
  78.5 1.2 copy-start.8
  79.7 1.1 copy-start.3
  80.8 0.7 copy-start.35
  80.8 1.0 copy-start.34
  80.8 1.4 copy-start.33
  80.8 1.7 %copy-start.32 = (s32[256,1]{0,1:T(1,128)S(1)}, s32[256,1]{0,1:T(1,128)}, u32[]{:S(2)}) copy-start(s32[256,1]{0,1:T(1,128)} %get-tuple-element.80) | copy-start | bytes 3076
  85.5 6.3 %copy-start.16 = (f32[64,512]{1,0:T(8,128)S(1)}, f32[64,512]{1,0:T(8,128)}, u32[]{:S(2)}) copy-start(f32[64,512]{1,0:T(8,128)} %convolution_bitcast_fusion) | copy-start | bytes 393220
  90.4 1.4 copy-start.18
  90.4 1.4 copy-start.6
  90.5 1.4 copy-start.19
  90.5 1.5 copy-start.5
  93.5 5.7 %collective-permute-start = (f32[704,512]{1,0:T(8,128)}, f32[704,512]{1,0:T(8,128)}, u32[]{:S(2)}, u32[]{:S(2)}) collective-permute-start(f32[704,512]{1,0:T(8,128)} %fusion.13), channel_id=1, source_target_pairs={{0,1},{1,0},{2,3},{3,2},{4,5},{5,4},{6,7},{7,6},{8,9},{9,8},{10,11... | collective-permute-start | bytes 4325384 | tf_op jit(solution)/shard_map/ppermute | solution.py:59
  153.8 6.1 %collective-permute-start.1 = (bf16[576,512]{1,0:T(8,128)(2,1)S(1)}, bf16[576,512]{1,0:T(8,128)(2,1)S(1)}, u32[]{:S(2)}, u32[]{:S(2)}) collective-permute-start(bf16[576,512]{1,0:T(8,128)(2,1)S(1)} %slice.275), channel_id=1, source_target_pairs={{0,1},{1,0},{2,3},{3,2},{4,5},{5,4},{6,7},{7,6},{8,9},{9,8},{10,11... | collective-permute-start | bytes 1769480 | tf_op jit(solution)/shard_map/ppermute | solution.py:80

commit v13 on v11

--- a/solution.py
+++ b/solution.py
@@ -125,8 +125,8 @@
     own_codes = jnp.broadcast_to(codes.reshape(1, -1), (part_count, codes.size))
     room = -(-(codes.size + out_codes.shape[1]) // 128) * 128
     filler = jnp.zeros((part_count, room - codes.size - out_codes.shape[1]), jnp.int32)
-    payload = jnp.concatenate([own_codes, out_codes, filler], axis=1)
-    incoming = lax.all_to_all(payload, DOM, 0, 0, tiled=True)
+    payload = jnp.concatenate([own_codes, out_codes, filler], axis=1).astype(jnp.int16)
+    incoming = lax.all_to_all(payload, DOM, 0, 0, tiled=True).astype(jnp.int32)
     recv_codes = incoming[:, codes.size : codes.size + out_codes.shape[1]].reshape(-1, book_count)
     hub_codes = [
         incoming[hub_owner[hub_index], : codes.size].reshape(codes.shape)

time: 152 us -> 155 us (1.020)
  waiting for transfers between devices: 12.3 us -> 7.44 us
  other arithmetic: 13.1 us -> 17.1 us
  local copies, waits for them, and re-layouts: 20.3 us -> 23.5 us
  blocking collectives: 52.8 us -> 54.6 us
    all_to_all x1, waiting for transfers between devices: 9.21 us -> 4.27 us  [shards(): incoming = lax.all_to_all(payload, DOM, 0, 0, tiled=True).astype(jnp.int32)]
    concatenate x1 -> x3, local copies, waits for them, and re-layouts: 0.1 us -> 3.14 us  [shards(): jnp.concatenate([own_codes, out_codes, filler], axis=1).astype(jnp.int16)]
    concatenate x0 -> x2, other arithmetic: none -> 2.47 us  [shards(): jnp.concatenate([own_codes, out_codes, filler], axis=1).astype(jnp.int16)]
    unnamed x54 -> x57, local copies, waits for them, and re-layouts: 6.87 us -> 7.94 us
  transfers between devices with their start and end apart: 3 -> 3, of which waited for: 3 -> 3; matrix products, arithmetic and copies ran while one was open for 4% -> 3% of each run, Pallas kernels for 0% -> 0%
where the time goes in v13:
time: 155 us; the launch traced here: 154 us
  blocking collectives  54.6 us (35%)
  local copies, waits for them, and re-layouts  23.5 us (15%)
  starting transfers between devices  23.3 us (15%)
  matrix products  23.2 us (15%)
  other arithmetic  17.1 us (11%)
  waiting for transfers between devices  7.44 us (5%)
  between operations  5.27 us (3%)
    all_to_all x2, blocking collectives, all_sum(): received = lax.all_to_all(chunks, axis, 0, 0, tiled=True)  28.2 us
    all_to_all x2, blocking collectives, all_sum(): piece = lax.all_to_all(spread, axis, 0, 0, tiled=True).reshape(shape)  23.7 us
    all_to_all x1, starting transfers between devices, shards(): incoming = lax.all_to_all(payload, DOM, 0, 0, tiled=True).astype(jnp.int32)  16.5 us
    unnamed x57, local copies, waits for them, and re-layouts  7.94 us
    dot_general x8, matrix products, fold_books(): lax.dot_general(indicator_rows, both, (((0,), (0,)), ((), ())), preferred...  6.77 us
    ppermute x1, starting transfers between devices, all_sum(): other_dense = lax.ppermute(own_dense, 'sub', swap)  4.51 us
    all_to_all x1, waiting for transfers between devices, shards(): incoming = lax.all_to_all(payload, DOM, 0, 0, tiled=True).astype(jnp.int32)  4.27 us
    concatenate x3, local copies, waits for them, and re-layouts, shards(): jnp.concatenate([own_codes, out_codes, filler], axis=1).astype(jnp.int16)  3.14 us
  transfers between devices with their start and end apart: 3, of which 3 were waited for; matrix products, arithmetic and copies ran while one was open for 3% of the time, Pallas kernels for 0%

profile of v13, /device:TPU:1, one launch (start us, length us, event | category | flops | bytes accessed | tf_op | source)
XLA Modules:
  0.0 154.4 jit_solution(5875947677768141557)
XLA Ops:
  0.6 0.8 copy.54
  1.6 0.7 convert.14
  2.3 1.0 convolution_convert_fusion.2
  3.8 0.7 iota_compare_fusion.24
  5.3 2.5 %concatenate.65 = s16[128,1,1152]{2,1,0:T(2,128)(2,1)S(1)} concatenate(s16[128,1,1024]{2,1,0:T(2,128)(2,1)S(1)} %broadcast_in_dim.33, s16[128,1,32]{2,1,0:T(2,128)(2,1)S(1)} %copy.57, s16[128,1,96]{2,1,0:T(2,128)(2,1)S(1)} %broadcast_in_dim.37), dimensions={2} | concatenate | bytes 589824 | tf_op jit(solution)/shard_map/concatenate | solution.py:128
  8.3 2.5 %reduce.9 = s16[128,1152]{1,0:T(8,128)(2,1)S(1)} reduce(s16[128,1,1152]{2,1,0:T(2,128)(2,1)S(1)} %concatenate.65, s16[]{:T(256)} %broadcast.83), dimensions={1}, to_apply=%concatenate.65.reduce_sub_computation | reduce | bytes 589826 | tf_op jit(solution)/shard_map/concatenate | solution.py:128
  10.8 1.1 reshape.260
  11.9 16.5 %all-to-all-start = ((s16[128,2,576]{2,1,0:T(2,128)(2,1)}), s16[128,2,576]{2,1,0:T(2,128)(2,1)S(1)}, u32[]{:S(2)}, u32[]{:S(2)}) async-start(s16[128,2,576]{2,1,0:T(2,128)(2,1)} %reshape.260), calls=%async_computation | async-start | bytes 655360 | tf_op jit(solution)/shard_map/all_to_all | solution.py:129
  31.6 2.8 %all_gather.3 = bf16[4,256,128]{2,1,0:T(8,128)(2,1)S(1)} all-gather(bf16[2,256,128]{2,1,0:T(8,128)(2,1)S(1)} %copy-done.19), channel_id=1, replica_groups=mesh['dy'=4,'dx'=4,'dz'=8,'sub'=2] {'sub'}, dimensions={0}, use_global_device_ids=true | all-gather | bytes 393216 | tf_op jit(solution)/shard_map/all_gather | solution.py:115
  35.2 1.0 copy.64
  37.6 1.0 fusion.85
  39.2 4.3 %all-to-all-done = s16[128,2,576]{2,1,0:T(2,128)(2,1)S(1)} async-done(((s16[128,2,576]{2,1,0:T(2,128)(2,1)}), s16[128,2,576]{2,1,0:T(2,128)(2,1)S(1)}, u32[]{:S(2)}, u32[]{:S(2)}) %all-to-all-start) | async-done | bytes 294944 | tf_op jit(solution)/shard_map/all_to_all | solution.py:129
  44.1 0.8 convert_element_type.173
  45.8 2.2 %fusion.4 = bf16[4,1536,128]{1,2,0:T(8,128)(2,1)S(1)} fusion(bf16[4,256,128]{2,1,0:T(8,128)(2,1)S(1)} %copy-done.17, s32[1536,4]{0,1:T(4,128)S(1)} %pad_add_fusion), kind=kOutput, calls=%fused_computation.12 | convolution fusion | flops 405012480 | bytes 1859584 | tf_op jit(solution)/shard_map/feu,euq->feq/dot_general | solution.py:23
  48.0 1.6 %copy.63 = bf16[1536,512]{1,0:T(8,128)(2,1)} copy(bf16[1536,512]{0,1:T(8,128)(2,1)S(1)} %bitcast.108) | data formatting | bytes 3145728 | tf_op jit(solution)/shard_map/reshape | solution.py:26
  49.6 1.5 pad_maximum_fusion
  51.2 2.0 %gather_fusion = bf16[16,128,512]{2,1,0:T(8,128)(2,1)} fusion(bf16[14,128,512]{2,1,0:T(8,128)(2,1)S(1)} %bitcast.101, s32[1024]{0:T(1024)S(1)} %pad_clamp_fusion.1), kind=kCustom, calls=%fused_computation | custom fusion | bytes 4194368 | tf_op jit(solution)/shard_map/gather | solution.py:142
  53.2 2.2 %fusion.16 = bf16[2,512,128]{1,2,0:T(8,128)(2,1)S(1)} fusion(bf16[2,8,128,128]{3,2,1,0:T(8,128)(2,1)S(1)} %bitcast.114, bf16[2,8,128,512]{3,2,1,0:T(8,128)(2,1)} %bitcast.102, f32[2,8,512]{2,1,0:T(8,128)S(1)} %bitcast.115), kind=kOutput, calls=%fused_computation.29 | convolution fusion | flops 271712256 | bytes 2916352 | tf_op jit(solution)/shard_map/btij,btjd->bid/dot_general | solution.py:145
  55.8 1.1 multiply_convert_fusion
  57.6 1.3 fusion.87
  59.6 2.6 %fusion.2 = (f32[2,8,512]{2,1,0:T(8,128)S(1)}, f32[2,512,1024]{1,2,0}) fusion(bf16[2,8,128,512]{3,2,1,0:T(8,128)(2,1)S(1)} %bitcast.103, bf16[2,128,1024]{1,2,0:T(8,128)(2,1)S(1)} %bitcast.107, bf16[2,128,512]{2,1,0:T(8,128)(2,1)S(1)} %bitcast.109), kind=kOutput, calls=%fused_computation.9 | convolution fusion | flops 271572992 | bytes 7110656
  62.2 1.2 scatter_custom_fusion
  63.4 1.5 fusion.89
  64.8 1.9 %fusion.90 = f32[512,64]{1,0:T(8,128)S(1)} fusion(f32[512,512]{1,0:T(8,128)S(1)} %scatter_custom_fusion, f32[64,512]{1,0:T(8,128)} %param.16), kind=kOutput, calls=%fused_computation.166 | convolution fusion | flops 201326592 | bytes 1310720 | tf_op jit(solution)/shard_map/dot_general | solution.py:178
  66.7 2.7 %bitcast_multiply_fusion = f32[2048,512]{1,0:T(8,128)S(1)} fusion(f32[2,512,1024]{1,2,0} %get-tuple-element.88, f32[16,512]{1,0:T(8,128)S(1)} %gather_fusion.1), kind=kLoop, calls=%fused_computation.10 | loop fusion | flops 1048576 | bytes 8421376 | tf_op jit(solution)/shard_map/mul | solution.py:176
  69.4 2.1 %subtract_convert_fusion.3 = (bf16[2048,128]{1,0:T(8,128)(2,1)}, bf16[2048,128]{1,0:T(8,128)(2,1)}, bf16[2048,128]{1,0:T(8,128)(2,1)S(1)}, bf16[2048,128]{1,0:T(...) fusion(f32[2048,512]{1,0:T(8,128)S(1)} %bitcast_multiply_fusion), kind=kLoop, calls=%fused_computation.53 | loop fusion | flops 3145728 | bytes 10485760 | tf_op jit(solution)/shard_map/convert_element_type | solution.py:37
  72.1 2.3 %fusion.8 = f32[256,256]{1,0:T(8,128)S(1)} fusion(bf16[2048,128]{1,0:T(8,128)(2,1)} %get-tuple-element.34, bf16[2048,128]{1,0:T(8,128)(2,1)} %get-tuple-element.35, s32[2048]{0:T(1024)S(1)} %bitcast.120), kind=kOutput, calls=%fused_computation.19 | convolution fusion | flops 271056896 | bytes 1318912 | tf_op jit(solution)/shard_map/dot_general | solution.py:40
  74.5 1.0 fusion.9
  75.7 1.0 fusion.10
  76.8 1.0 fusion.11
  79.4 0.7 constant_dynamic-slice_fusion
  80.7 1.0 dynamic-slice_dynamic-update-slice_fusion.1
  81.7 1.1 dynamic-slice_dynamic-update-slice_fusion
  84.2 0.7 constant_dynamic-update-slice_fusion.1
  84.9 2.3 %collective-permute-start = (f32[704,512]{1,0:T(8,128)}, f32[704,512]{1,0:T(8,128)S(1)}, u32[]{:S(2)}, u32[]{:S(2)}) collective-permute-start(f32[704,512]{1,0:T(8,128)} %constant_dynamic-update-slice_fusion.1), channel_id=1, source_target_pairs={{0,1},{1,0},{2,3},{3,2},{4,5},{5,4},{6,7},{7,6},{8,9},{9,8},{10,11... | collective-permute-start | bytes 4325384 | tf_op jit(solution)/shard_map/ppermute | solution.py:59
  87.2 0.7 constant_dynamic-update-slice_fusion
  87.9 2.3 %collective-permute-done = f32[704,512]{1,0:T(8,128)S(1)} collective-permute-done((f32[704,512]{1,0:T(8,128)}, f32[704,512]{1,0:T(8,128)S(1)}, u32[]{:S(2)}, u32[]{:S(2)}) %collective-permute-start) | collective-permute-done | bytes 1441824 | tf_op jit(solution)/shard_map/ppermute | solution.py:59
  90.2 1.6 %add_convert_fusion = bf16[704,512]{1,0:T(8,128)(2,1)S(1)} fusion(f32[704,512]{1,0:T(8,128)} %constant_dynamic-update-slice_fusion, f32[704,512]{1,0:T(8,128)S(1)} %collective-permute-done), kind=kLoop, calls=%fused_computation.25 | loop fusion | flops 720896 | bytes 3604480 | tf_op jit(solution)/shard_map/convert_element_type | solution.py:70
  92.0 16.7 %all_to_all.26 = bf16[16,44,512]{2,1,0:T(8,128)(2,1)S(1)} all-to-all(bf16[16,44,512]{2,1,0:T(8,128)(2,1)S(1)} %convert_element_type.211), channel_id=1, replica_groups=mesh['dy'=4,'dx'=4,'dz'=8,'sub'=2] {'dy','dx'}, dimensions={0} | all-to-all | bytes 1441792 | tf_op jit(solution)/shard_map/all_to_all | solution.py:71
  108.8 11.5 %all_to_all.27 = f32[8,11,256]{2,1,0:T(8,128)S(1)} all-to-all(f32[8,11,256]{2,1,0:T(8,128)S(1)} %reshape.197), channel_id=1, replica_groups=mesh['dy'=4,'dx'=4,'dz'=8,'sub'=2] {'dz'}, dimensions={0} | all-to-all | bytes 180224 | tf_op jit(solution)/shard_map/all_to_all | solution.py:71
  120.3 9.6 %all_to_all.28 = bf16[8,11,256]{2,1,0:T(8,128)(2,1)S(1)} all-to-all(bf16[8,11,256]{2,1,0:T(8,128)(2,1)S(1)} %broadcast_in_dim.74), channel_id=1, replica_groups=mesh['dy'=4,'dx'=4,'dz'=8,'sub'=2] {'dz'}, dimensions={0} | all-to-all | bytes 90112 | tf_op jit(solution)/shard_map/all_to_all | solution.py:76
  130.0 14.1 %all_to_all.29 = bf16[16,44,512]{2,1,0:T(8,128)(2,1)S(1)} all-to-all(bf16[16,44,512]{2,1,0:T(8,128)(2,1)S(1)} %broadcast_in_dim.76), channel_id=1, replica_groups=mesh['dy'=4,'dx'=4,'dz'=8,'sub'=2] {'dy','dx'}, dimensions={0} | all-to-all | bytes 1441792 | tf_op jit(solution)/shard_map/all_to_all | solution.py:76
  144.3 4.5 %collective-permute-start.1 = (bf16[576,512]{1,0:T(8,128)(2,1)S(1)}, bf16[576,512]{1,0:T(8,128)(2,1)S(1)}, u32[]{:S(2)}, u32[]{:S(2)}) collective-permute-start(bf16[576,512]{1,0:T(8,128)(2,1)S(1)} %slice.217), channel_id=1, source_target_pairs={{0,1},{1,0},{2,3},{3,2},{4,5},{5,4},{6,7},{7,6},{8,9},{9,8},{10,11... | collective-permute-start | bytes 1769480 | tf_op jit(solution)/shard_map/ppermute | solution.py:80
  148.8 0.7 reshape.205
  149.6 0.9 collective-permute-done.1
  150.9 0.8 copy.70
  152.4 1.0 pad_maximum_fusion.2
  153.4 1.0 pad_maximum_fusion.1
  (123 shorter events, 12.9 us)
Async XLA Ops:
  0.6 55.1 %copy-start = (bf16[512,512]{1,0:T(8,128)(2,1)S(1)}, bf16[512,512]{1,0:T(8,128)(2,1)}, u32[]{:S(2)}) copy-start(bf16[512,512]{1,0:T(8,128)(2,1)} %param.18) | copy-start | bytes 1572868
  5.2 23.1 %copy-start.21 = (s32[2]{0:T(128)S(1)}, s32[2]{0:T(128)}, u32[]{:S(2)}) copy-start(s32[2]{0:T(128)} %param.24) | copy-start | bytes 28
  5.2 26.3 %copy-start.19 = (bf16[2,256,128]{2,1,0:T(8,128)(2,1)S(1)}, bf16[2,256,128]{2,1,0:T(8,128)(2,1)}, u32[]{:S(2)}) copy-start(bf16[2,256,128]{2,1,0:T(8,128)(2,1)} %param.14) | copy-start | bytes 393220
  5.3 29.0 %copy-start.20 = (s32[256,4]{0,1:T(4,128)S(1)}, s32[256,4]{0,1:T(4,128)}, u32[]{:S(2)}) copy-start(s32[256,4]{0,1:T(4,128)} %param.13) | copy-start | bytes 12292
  8.3 26.9 %copy-start.22 = (s32[16]{0:T(128)S(1)}, s32[16]{0:T(128)}, u32[]{:S(2)}) copy-start(s32[16]{0:T(128)} %param.21) | copy-start | bytes 196
  8.3 26.9 %copy-start.23 = (s32[16]{0:T(128)S(1)}, s32[16]{0:T(128)}, u32[]{:S(2)}) copy-start(s32[16]{0:T(128)} %param.20) | copy-start | bytes 196
  8.3 26.9 %copy-start.14 = (bf16[16,128,128]{2,1,0:T(8,128)(2,1)S(1)}, bf16[16,128,128]{2,1,0:T(8,128)(2,1)}, u32[]{:S(2)}) copy-start(bf16[16,128,128]{2,1,0:T(8,128)(2,1)} %param.19) | copy-start | bytes 1572868
  11.9 25.7 %copy-start.11 = (f32[512,64]{0,1:T(8,128)S(1)}, f32[512,64]{0,1:T(8,128)}, u32[]{:S(2)}) copy-start(f32[512,64]{0,1:T(8,128)} %param.15) | copy-start | bytes 393220
  11.9 25.7 %copy-start.15 = (f32[64,512]{1,0:T(8,128)S(1)}, f32[64,512]{1,0:T(8,128)}, u32[]{:S(2)}) copy-start(f32[64,512]{1,0:T(8,128)} %param.16) | copy-start | bytes 393220
  11.9 31.6 %all-to-all-start = ((s16[128,2,576]{2,1,0:T(2,128)(2,1)}), s16[128,2,576]{2,1,0:T(2,128)(2,1)S(1)}, u32[]{:S(2)}, u32[]{:S(2)}) async-start(s16[128,2,576]{2,1,0:T(2,128)(2,1)} %reshape.260), calls=%async_computation | async-start | bytes 655360 | tf_op jit(solution)/shard_map/all_to_all | solution.py:129
  34.3 0.7 copy-start.16
  44.9 1.0 copy-start.17
  53.2 2.3 %copy-start.4 = (bf16[512,512]{1,0:T(8,128)(2,1)S(1)}, bf16[512,512]{1,0:T(8,128)(2,1)}, u32[]{:S(2)}) copy-start(bf16[512,512]{1,0:T(8,128)(2,1)} %param.17) | copy-start | bytes 1572868
  53.2 2.6 %copy-start.18 = (bf16[256,512]{1,0:T(8,128)(2,1)S(1)}, bf16[256,512]{1,0:T(8,128)(2,1)}, u32[]{:S(2)}) copy-start(bf16[256,512]{1,0:T(8,128)(2,1)} %param.25) | copy-start | bytes 786436
  57.5 2.0 %copy-start.1 = (bf16[16,128,512]{2,1,0:T(8,128)(2,1)S(1)}, bf16[16,128,512]{2,1,0:T(8,128)(2,1)}, u32[]{:S(2)}) copy-start(bf16[16,128,512]{2,1,0:T(8,128)(2,1)} %gather_fusion) | copy-start | bytes 6291460
  57.6 2.0 %copy-start.3 = (bf16[2,8,128,128]{2,3,1,0:T(8,128)(2,1)S(1)}, bf16[2,8,128,128]{2,3,1,0:T(8,128)(2,1)}, u32[]{:S(2)}) copy-start(bf16[2,8,128,128]{2,3,1,0:T(8,128)(2,1)} %copy.64) | copy-start | bytes 1572868
  59.6 3.8 %copy-start.12 = (f32[512,64]{0,1:T(8,128)S(1)}, f32[512,64]{0,1:T(8,128)}, u32[]{:S(2)}) copy-start(f32[512,64]{0,1:T(8,128)} %param.15) | copy-start | bytes 393220
  72.1 2.4 %copy-start.9 = (bf16[2048,128]{1,0:T(8,128)(2,1)S(1)}, bf16[2048,128]{1,0:T(8,128)(2,1)}, u32[]{:S(2)}) copy-start(bf16[2048,128]{1,0:T(8,128)(2,1)} %get-tuple-element.46) | copy-start | bytes 1572868
  72.1 2.4 %copy-start.10 = (bf16[2048,128]{1,0:T(8,128)(2,1)S(1)}, bf16[2048,128]{1,0:T(8,128)(2,1)}, u32[]{:S(2)}) copy-start(bf16[2048,128]{1,0:T(8,128)(2,1)} %get-tuple-element.47) | copy-start | bytes 1572868
  74.5 1.2 copy-start.7
  74.5 1.2 copy-start.8
  75.6 1.2 copy-start.6
  79.4 1.3 copy-start.2
  80.7 2.2 %copy-start.13 = (f32[512,64]{0,1:T(8,128)S(1)}, f32[512,64]{0,1:T(8,128)}, u32[]{:S(2)}) copy-start(f32[512,64]{0,1:T(8,128)} %fusion.89) | copy-start | bytes 393220
  81.7 5.5 %copy-start.5 = (f32[2,256,128]{2,1,0:T(8,128)S(1)}, f32[2,256,128]{2,1,0:T(8,128)}, u32[]{:S(2)}) copy-start(f32[2,256,128]{2,1,0:T(8,128)} %get-tuple-element.63) | copy-start | bytes 786436
  84.9 5.4 %collective-permute-start = (f32[704,512]{1,0:T(8,128)}, f32[704,512]{1,0:T(8,128)S(1)}, u32[]{:S(2)}, u32[]{:S(2)}) collective-permute-start(f32[704,512]{1,0:T(8,128)} %constant_dynamic-update-slice_fusion.1), channel_id=1, source_target_pairs={{0,1},{1,0},{2,3},{3,2},{4,5},{5,4},{6,7},{7,6},{8,9},{9,8},{10,11... | collective-permute-start | bytes 4325384 | tf_op jit(solution)/shard_map/ppermute | solution.py:59
  144.3 6.1 %collective-permute-start.1 = (bf16[576,512]{1,0:T(8,128)(2,1)S(1)}, bf16[576,512]{1,0:T(8,128)(2,1)S(1)}, u32[]{:S(2)}, u32[]{:S(2)}) collective-permute-start(bf16[576,512]{1,0:T(8,128)(2,1)S(1)} %slice.217), channel_id=1, source_target_pairs={{0,1},{1,0},{2,3},{3,2},{4,5},{5,4},{6,7},{7,6},{8,9},{9,8},{10,11... | collective-permute-start | bytes 1769480 | tf_op jit(solution)/shard_map/ppermute | solution.py:80

commit v14 on v11

--- a/solution.py
+++ b/solution.py
@@ -56,7 +56,8 @@
         return jnp.concatenate(pieces, axis=0)
 
     swap = [(0, 1), (1, 0)]
-    mine = half_of(sub_index) + lax.ppermute(half_of(1 - sub_index), "sub", swap)
+    sent = lax.ppermute(half_of(1 - sub_index).astype(jnp.bfloat16), "sub", swap)
+    mine = half_of(sub_index) + sent.astype(jnp.float32)
     rows = mine.shape[0]
     shapes = []
     piece = mine

time: 152 us -> 152 us (level)
  waiting for transfers between devices: 12.3 us -> 10.4 us
    another operation x8, other arithmetic: 0.13 us -> 2.74 us  [fold_books(): return jnp.stack(folded)]
    ppermute x1, waiting for transfers between devices: 2.26 us -> 0.26 us  [all_sum(): lax.ppermute(half_of(1 - sub_index).astype(jnp.bfloat16), 'sub', swap)]
    unnamed x54 -> x50, local copies, waits for them, and re-layouts: 6.87 us -> 8.79 us
    convert_element_type x2, other arithmetic: 2.16 us -> 0.63 us  [fold_books(): lower_bound = (piece - upper_bound.astype(jnp.float32)).astype(jnp.bfloat16)]
  transfers between devices with their start and end apart: 3 -> 3, of which waited for: 3 -> 3; matrix products, arithmetic and copies ran while one was open for 4% -> 5% of each run, Pallas kernels for 0% -> 0%
where the time goes in v14:
time: 152 us; the launch traced here: 151 us
  blocking collectives  52.8 us (35%)
  matrix products  24.1 us (16%)
  starting transfers between devices  23.5 us (15%)
  local copies, waits for them, and re-layouts  21.4 us (14%)
  other arithmetic  14 us (9%)
  waiting for transfers between devices  10.4 us (7%)
  between operations  5.26 us (3%)
    all_to_all x2, blocking collectives, all_sum(): received = lax.all_to_all(chunks, axis, 0, 0, tiled=True)  27 us
    all_to_all x2, blocking collectives, all_sum(): piece = lax.all_to_all(spread, axis, 0, 0, tiled=True).reshape(shape)  23.2 us
    all_to_all x1, starting transfers between devices, shards(): incoming = lax.all_to_all(payload, DOM, 0, 0, tiled=True)  16.5 us
    all_to_all x1, waiting for transfers between devices, shards(): incoming = lax.all_to_all(payload, DOM, 0, 0, tiled=True)  9.22 us
    unnamed x50, local copies, waits for them, and re-layouts  8.79 us
    dot_general x8, matrix products, fold_books(): lax.dot_general(indicator_rows, both, (((0,), (0,)), ((), ())), preferred...  5.49 us
    ppermute x1, starting transfers between devices, all_sum(): other_dense = lax.ppermute(own_dense, 'sub', swap)  4.5 us
    dot_general x2, matrix products, decode(): jnp.einsum('feu,euq->feq', indicator_rows, complete_codebooks, preferred_...  3.84 us
  transfers between devices with their start and end apart: 3, of which 3 were waited for; matrix products, arithmetic and copies ran while one was open for 5% of the time, Pallas kernels for 0%

profile of v14, /device:TPU:1, one launch (start us, length us, event | category | flops | bytes accessed | tf_op | source)
XLA Modules:
  0.0 151.4 jit_solution(6120595547520785745)
XLA Ops:
  0.6 0.7 iota_compare_fusion.24
  1.4 0.8 copy.54
  2.2 0.8 copy.53
  3.1 1.0 convolution_convert_fusion.2
  5.0 1.2 all_to_all.20
  6.3 16.5 %all-to-all-start = ((s32[128,1,1152]{2,1,0:T(1,128)}), s32[128,1,1152]{2,1,0:T(1,128)S(1)}, u32[]{:S(2)}, u32[]{:S(2)}) async-start(s32[128,1,1152]{2,1,0:T(1,128)} %all_to_all.20), calls=%async_computation | async-start | bytes 1179648 | tf_op jit(solution)/shard_map/all_to_all | solution.py:130
  23.3 2.6 %all_gather.3 = bf16[4,256,128]{2,1,0:T(8,128)(2,1)S(1)} all-gather(bf16[2,256,128]{2,1,0:T(8,128)(2,1)S(1)} %copy-done.14), channel_id=1, replica_groups=mesh['dy'=4,'dx'=4,'dz'=8,'sub'=2] {'sub'}, dimensions={0}, use_global_device_ids=true | all-gather | bytes 393216 | tf_op jit(solution)/shard_map/all_gather | solution.py:116
  29.2 1.0 copy.64
  31.5 1.9 %fusion.89 = f32[512,512]{1,0:T(8,128)S(1)} fusion(f32[512,64]{0,1:T(8,128)S(1)} %copy-done.5, f32[64,512]{1,0:T(8,128)} %param.16), kind=kOutput, calls=%fused_computation.165 | convolution fusion | flops 201326592 | bytes 1310720 | tf_op jit(solution)/shard_map/dot_general | solution.py:117
  34.1 9.2 %all-to-all-done = s32[128,1,1152]{2,1,0:T(1,128)S(1)} async-done(((s32[128,1,1152]{2,1,0:T(1,128)}), s32[128,1,1152]{2,1,0:T(1,128)S(1)}, u32[]{:S(2)}, u32[]{:S(2)}) %all-to-all-start) | async-done | bytes 589856 | tf_op jit(solution)/shard_map/all_to_all | solution.py:130
  44.2 3.4 %fusion.4 = bf16[4,1536,128]{1,2,0:T(8,128)(2,1)S(1)} fusion(bf16[4,256,128]{2,1,0:T(8,128)(2,1)} %copy-done.12, s32[1536,4]{0,1:T(4,128)S(1)} %pad_add_fusion), kind=kOutput, calls=%fused_computation.12 | convolution fusion | flops 405012480 | bytes 1859584 | tf_op jit(solution)/shard_map/feu,euq->feq/dot_general | solution.py:23
  47.6 1.6 %copy.63 = bf16[1536,512]{1,0:T(8,128)(2,1)} copy(bf16[1536,512]{0,1:T(8,128)(2,1)S(1)} %bitcast.108) | data formatting | bytes 3145728 | tf_op jit(solution)/shard_map/reshape | solution.py:26
  49.2 1.5 %pad_maximum_fusion = bf16[1792,512]{1,0:T(8,128)(2,1)S(1)} fusion(bf16[1536,512]{1,0:T(8,128)(2,1)} %copy.63, bf16[256,512]{1,0:T(8,128)(2,1)S(1)} %copy.62), kind=kLoop, calls=%fused_computation.23 | loop fusion | flops 3670016 | bytes 3670016 | tf_op jit(solution)/shard_map/concatenate | solution.py:138
  50.8 2.0 %gather_fusion = bf16[16,128,512]{2,1,0:T(8,128)(2,1)} fusion(bf16[14,128,512]{2,1,0:T(8,128)(2,1)S(1)} %bitcast.101, s32[1024]{0:T(1024)S(1)} %pad_clamp_fusion.1), kind=kCustom, calls=%fused_computation | custom fusion | bytes 4194368 | tf_op jit(solution)/shard_map/gather | solution.py:143
  52.8 2.3 %fusion.16 = bf16[2,512,128]{1,2,0:T(8,128)(2,1)S(1)} fusion(bf16[2,8,128,128]{3,2,1,0:T(8,128)(2,1)S(1)} %bitcast.114, bf16[2,8,128,512]{3,2,1,0:T(8,128)(2,1)} %bitcast.102, f32[2,8,512]{2,1,0:T(8,128)S(1)} %bitcast.115), kind=kOutput, calls=%fused_computation.29 | convolution fusion | flops 271712256 | bytes 2916352 | tf_op jit(solution)/shard_map/btij,btjd->bid/dot_general | solution.py:146
  55.4 1.1 multiply_convert_fusion
  57.5 1.3 fusion.91
  58.8 2.6 %fusion.2 = (f32[2,8,512]{2,1,0:T(8,128)S(1)}, f32[2,512,1024]{1,2,0}) fusion(bf16[2,8,128,512]{3,2,1,0:T(8,128)(2,1)S(1)} %bitcast.103, bf16[2,128,1024]{1,2,0:T(8,128)(2,1)S(1)} %bitcast.107, bf16[2,128,512]{2,1,0:T(8,128)(2,1)S(1)} %bitcast.109), kind=kOutput, calls=%fused_computation.9 | convolution fusion | flops 271572992 | bytes 7110656
  61.4 1.1 scatter_custom_fusion
  62.6 1.5 fusion.93
  64.0 1.9 %fusion.94 = f32[512,64]{1,0:T(8,128)S(1)} fusion(f32[512,512]{1,0:T(8,128)S(1)} %scatter_custom_fusion, f32[64,512]{1,0:T(8,128)} %param.16), kind=kOutput, calls=%fused_computation.170 | convolution fusion | flops 201326592 | bytes 1310720 | tf_op jit(solution)/shard_map/dot_general | solution.py:179
  67.9 0.7 fusion.45
  68.9 0.7 fusion.46
  69.9 0.7 fusion.47
  70.6 0.8 reshape.134
  71.4 2.7 %bitcast_multiply_fusion = f32[2048,512]{1,0:T(8,128)S(1)} fusion(f32[2,512,1024]{1,2,0} %get-tuple-element.78, f32[16,512]{1,0:T(8,128)S(1)} %gather_fusion.1), kind=kLoop, calls=%fused_computation.10 | loop fusion | flops 1048576 | bytes 8421376 | tf_op jit(solution)/shard_map/mul | solution.py:177
  74.6 1.0 fusion.8
  75.7 1.0 fusion.11
  76.8 1.0 fusion.10
  77.9 1.0 fusion.9
  79.4 0.7 fusion.39
  80.1 0.7 fusion.40
  80.8 1.5 fusion.70
  82.3 1.5 fusion.71
  84.4 2.5 %collective-permute-start = (bf16[704,512]{1,0:T(8,128)(2,1)}, bf16[704,512]{1,0:T(8,128)(2,1)}, u32[]{:S(2)}, u32[]{:S(2)}) collective-permute-start(bf16[704,512]{1,0:T(8,128)(2,1)} %constant_dynamic-update-slice_fusion.1), channel_id=1, source_target_pairs={{0,1},{1,0},{2,3},{3,2},{4,5},{5,4},{6,7},{7,6},{8,9},{9,8},{10,11... | collective-permute-start | bytes 2162696 | tf_op jit(solution)/shard_map/ppermute | solution.py:59
  87.1 0.9 bitcast_dynamic-update-slice_fusion
  87.9 0.8 dynamic-slice_dynamic-update-slice_fusion.2
  89.1 1.4 add_convert_fusion
  90.6 16.7 %all_to_all.32 = bf16[16,44,512]{2,1,0:T(8,128)(2,1)S(1)} all-to-all(bf16[16,44,512]{2,1,0:T(8,128)(2,1)S(1)} %convert_element_type.200), channel_id=1, replica_groups=mesh['dy'=4,'dx'=4,'dz'=8,'sub'=2] {'dy','dx'}, dimensions={0} | all-to-all | bytes 1441792 | tf_op jit(solution)/shard_map/all_to_all | solution.py:72
  107.5 10.3 %all_to_all.33 = f32[8,11,256]{2,1,0:T(8,128)S(1)} all-to-all(f32[8,11,256]{2,1,0:T(8,128)S(1)} %reshape.140), channel_id=1, replica_groups=mesh['dy'=4,'dx'=4,'dz'=8,'sub'=2] {'dz'}, dimensions={0} | all-to-all | bytes 180224 | tf_op jit(solution)/shard_map/all_to_all | solution.py:72
  117.8 9.6 %all_to_all.34 = bf16[8,11,256]{2,1,0:T(8,128)(2,1)S(1)} all-to-all(bf16[8,11,256]{2,1,0:T(8,128)(2,1)S(1)} %broadcast_in_dim.74), channel_id=1, replica_groups=mesh['dy'=4,'dx'=4,'dz'=8,'sub'=2] {'dz'}, dimensions={0} | all-to-all | bytes 90112 | tf_op jit(solution)/shard_map/all_to_all | solution.py:77
  127.5 13.6 %all_to_all.35 = bf16[16,44,512]{2,1,0:T(8,128)(2,1)S(1)} all-to-all(bf16[16,44,512]{2,1,0:T(8,128)(2,1)S(1)} %broadcast_in_dim.76), channel_id=1, replica_groups=mesh['dy'=4,'dx'=4,'dz'=8,'sub'=2] {'dy','dx'}, dimensions={0} | all-to-all | bytes 1441792 | tf_op jit(solution)/shard_map/all_to_all | solution.py:77
  141.3 4.5 %collective-permute-start.1 = (bf16[576,512]{1,0:T(8,128)(2,1)S(1)}, bf16[576,512]{1,0:T(8,128)(2,1)S(1)}, u32[]{:S(2)}, u32[]{:S(2)}) collective-permute-start(bf16[576,512]{1,0:T(8,128)(2,1)S(1)} %slice.217), channel_id=1, source_target_pairs={{0,1},{1,0},{2,3},{3,2},{4,5},{5,4},{6,7},{7,6},{8,9},{9,8},{10,11... | collective-permute-start | bytes 1769480 | tf_op jit(solution)/shard_map/ppermute | solution.py:81
  145.8 0.7 reshape.147
  146.5 0.9 collective-permute-done.1
  147.9 0.8 copy.70
  148.7 1.0 pad_maximum_fusion.2
  150.4 1.0 pad_maximum_fusion.1
  (113 shorter events, 11.3 us)
Async XLA Ops:
  0.6 54.7 %copy-start = (bf16[512,512]{1,0:T(8,128)(2,1)S(1)}, bf16[512,512]{1,0:T(8,128)(2,1)}, u32[]{:S(2)}) copy-start(bf16[512,512]{1,0:T(8,128)(2,1)} %param.18) | copy-start | bytes 1572868
  4.8 17.9 %copy-start.16 = (s32[2]{0:T(128)S(1)}, s32[2]{0:T(128)}, u32[]{:S(2)}) copy-start(s32[2]{0:T(128)} %param.24) | copy-start | bytes 28
  4.9 18.5 %copy-start.14 = (bf16[2,256,128]{2,1,0:T(8,128)(2,1)S(1)}, bf16[2,256,128]{2,1,0:T(8,128)(2,1)}, u32[]{:S(2)}) copy-start(bf16[2,256,128]{2,1,0:T(8,128)(2,1)} %param.14) | copy-start | bytes 393220
  4.9 23.6 %copy-start.15 = (s32[256,4]{0,1:T(4,128)S(1)}, s32[256,4]{0,1:T(4,128)}, u32[]{:S(2)}) copy-start(s32[256,4]{0,1:T(4,128)} %param.13) | copy-start | bytes 12292
  5.0 24.1 %copy-start.11 = (bf16[16,128,128]{2,1,0:T(8,128)(2,1)S(1)}, bf16[16,128,128]{2,1,0:T(8,128)(2,1)}, u32[]{:S(2)}) copy-start(bf16[16,128,128]{2,1,0:T(8,128)(2,1)} %param.19) | copy-start | bytes 1572868
  6.3 25.2 %copy-start.17 = (s32[16]{0:T(128)S(1)}, s32[16]{0:T(128)}, u32[]{:S(2)}) copy-start(s32[16]{0:T(128)} %param.21) | copy-start | bytes 196
  6.3 25.2 %copy-start.18 = (s32[16]{0:T(128)S(1)}, s32[16]{0:T(128)}, u32[]{:S(2)}) copy-start(s32[16]{0:T(128)} %param.20) | copy-start | bytes 196
  6.3 25.3 %copy-start.5 = (f32[512,64]{0,1:T(8,128)S(1)}, f32[512,64]{0,1:T(8,128)}, u32[]{:S(2)}) copy-start(f32[512,64]{0,1:T(8,128)} %param.15) | copy-start | bytes 393220
  6.3 37.0 %all-to-all-start = ((s32[128,1,1152]{2,1,0:T(1,128)}), s32[128,1,1152]{2,1,0:T(1,128)S(1)}, u32[]{:S(2)}, u32[]{:S(2)}) async-start(s32[128,1,1152]{2,1,0:T(1,128)} %all_to_all.20), calls=%async_computation | async-start | bytes 1179648 | tf_op jit(solution)/shard_map/all_to_all | solution.py:130
  25.9 3.1 %copy-start.12 = (bf16[4,256,128]{2,1,0:T(8,128)(2,1)}, bf16[4,256,128]{2,1,0:T(8,128)(2,1)S(1)}, u32[]{:S(2)}) copy-start(bf16[4,256,128]{2,1,0:T(8,128)(2,1)S(1)} %all_gather.3) | copy-start | bytes 786436
  52.8 2.3 %copy-start.4 = (bf16[512,512]{1,0:T(8,128)(2,1)S(1)}, bf16[512,512]{1,0:T(8,128)(2,1)}, u32[]{:S(2)}) copy-start(bf16[512,512]{1,0:T(8,128)(2,1)} %param.17) | copy-start | bytes 1572868
  52.8 2.6 %copy-start.13 = (bf16[256,512]{1,0:T(8,128)(2,1)S(1)}, bf16[256,512]{1,0:T(8,128)(2,1)}, u32[]{:S(2)}) copy-start(bf16[256,512]{1,0:T(8,128)(2,1)} %param.25) | copy-start | bytes 786436
  56.8 2.0 %copy-start.1 = (bf16[16,128,512]{2,1,0:T(8,128)(2,1)S(1)}, bf16[16,128,512]{2,1,0:T(8,128)(2,1)}, u32[]{:S(2)}) copy-start(bf16[16,128,512]{2,1,0:T(8,128)(2,1)} %gather_fusion) | copy-start | bytes 6291460
  56.8 1.9 %copy-start.3 = (bf16[2,8,128,128]{2,3,1,0:T(8,128)(2,1)S(1)}, bf16[2,8,128,128]{2,3,1,0:T(8,128)(2,1)}, u32[]{:S(2)}) copy-start(bf16[2,8,128,128]{2,3,1,0:T(8,128)(2,1)} %copy.64) | copy-start | bytes 1572868
  58.8 3.8 %copy-start.6 = (f32[512,64]{0,1:T(8,128)S(1)}, f32[512,64]{0,1:T(8,128)}, u32[]{:S(2)}) copy-start(f32[512,64]{0,1:T(8,128)} %param.15) | copy-start | bytes 393220
  77.8 1.2 copy-start.7
  77.9 1.2 copy-start.8
  77.9 1.2 copy-start.9
  77.9 1.2 copy-start.10
  77.9 1.4 copy-start.2
  84.4 4.7 %collective-permute-start = (bf16[704,512]{1,0:T(8,128)(2,1)}, bf16[704,512]{1,0:T(8,128)(2,1)}, u32[]{:S(2)}, u32[]{:S(2)}) collective-permute-start(bf16[704,512]{1,0:T(8,128)(2,1)} %constant_dynamic-update-slice_fusion.1), channel_id=1, source_target_pairs={{0,1},{1,0},{2,3},{3,2},{4,5},{5,4},{6,7},{7,6},{8,9},{9,8},{10,11... | collective-permute-start | bytes 2162696 | tf_op jit(solution)/shard_map/ppermute | solution.py:59
  141.3 6.1 %collective-permute-start.1 = (bf16[576,512]{1,0:T(8,128)(2,1)S(1)}, bf16[576,512]{1,0:T(8,128)(2,1)S(1)}, u32[]{:S(2)}, u32[]{:S(2)}) collective-permute-start(bf16[576,512]{1,0:T(8,128)(2,1)S(1)} %slice.217), channel_id=1, source_target_pairs={{0,1},{1,0},{2,3},{3,2},{4,5},{5,4},{6,7},{7,6},{8,9},{9,8},{10,11... | collective-permute-start | bytes 1769480 | tf_op jit(solution)/shard_map/ppermute | solution.py:81

commit v15 on v11

--- a/solution.py
+++ b/solution.py
@@ -127,20 +127,22 @@
     filler = jnp.zeros((part_count, room - codes.size - out_codes.shape[1]), jnp.int32)
     payload = jnp.concatenate([own_codes, out_codes, filler], axis=1)
     incoming = lax.all_to_all(payload, DOM, 0, 0, tiled=True)
+    local_rows = decode(codes, complete_codebooks)
+    self_part = jnp.dot(local_rows, w_self, preferred_element_type=jnp.float32)
+    scale = rel_table[tile_rel]
+    incoming, self_part, scale = lax.optimization_barrier((incoming, self_part, scale))
     recv_codes = incoming[:, codes.size : codes.size + out_codes.shape[1]].reshape(-1, book_count)
     hub_codes = [
         incoming[hub_owner[hub_index], : codes.size].reshape(codes.shape)
         for hub_index in range(NHUB)
     ]
     table_codes = jnp.concatenate([codes, recv_codes] + hub_codes, axis=0)
-    local_rows = decode(codes, complete_codebooks)
     table = jnp.concatenate(
         [local_rows, decode(table_codes[rows_dev:], complete_codebooks)], axis=0
     )
     blocks = table.reshape(-1, TB, model_width)
     tile_blocks = tiles.reshape(block_count, TPB, TB, TB)
     picked = blocks[tile_src]
-    scale = rel_table[tile_rel]
     composed = (picked.astype(jnp.float32) * scale[:, None, :]).astype(jnp.bfloat16)
     aggregate = jnp.einsum(
         "btij,btjd->bid",
@@ -148,9 +150,7 @@
         composed.reshape(block_count, TPB, TB, model_width),
         preferred_element_type=jnp.float32,
     ).astype(jnp.bfloat16).reshape(rows_dev, model_width)
-    pre_act = jnp.dot(aggregate, w_msg, preferred_element_type=jnp.float32) + jnp.dot(
-        local_rows, w_self, preferred_element_type=jnp.float32
-    )
+    pre_act = jnp.dot(aggregate, w_msg, preferred_element_type=jnp.float32) + self_part
     activated = jnp.tanh(pre_act)
     output = activated.astype(jnp.bfloat16)
     grad_pre = (cotangent.astype(jnp.float32) * (1.0 - activated * activated)).astype(jnp.bfloat16)

time: 152 us -> 152 us (level)
    unnamed x54 -> x56, local copies, waits for them, and re-layouts: 6.87 us -> 7.06 us
where the time goes in v15:
time: 152 us; the launch traced here: 151 us
  blocking collectives  52.8 us (35%)
  matrix products  24.3 us (16%)
  starting transfers between devices  23.5 us (15%)
  local copies, waits for them, and re-layouts  20.5 us (13%)
  other arithmetic  13.1 us (9%)
  waiting for transfers between devices  11.8 us (8%)
  between operations  5.27 us (3%)
    all_to_all x2, blocking collectives, all_sum(): received = lax.all_to_all(chunks, axis, 0, 0, tiled=True)  27 us
    all_to_all x2, blocking collectives, all_sum(): piece = lax.all_to_all(spread, axis, 0, 0, tiled=True).reshape(shape)  23.2 us
    all_to_all x1, starting transfers between devices, shards(): incoming = lax.all_to_all(payload, DOM, 0, 0, tiled=True)  16.5 us
    all_to_all x1, waiting for transfers between devices, shards(): incoming = lax.all_to_all(payload, DOM, 0, 0, tiled=True)  8.65 us
    unnamed x56, local copies, waits for them, and re-layouts  7.06 us
    dot_general x8, matrix products, fold_books(): lax.dot_general(indicator_rows, both, (((0,), (0,)), ((), ())), preferred...  6.77 us
    ppermute x1, starting transfers between devices, all_sum(): other_dense = lax.ppermute(own_dense, 'sub', swap)  4.5 us
  transfers between devices with their start and end apart: 3, of which 3 were waited for; matrix products, arithmetic and copies ran while one was open for 4% of the time, Pallas kernels for 0%

profile of v15, /device:TPU:1, one launch (start us, length us, event | category | flops | bytes accessed | tf_op | source)
XLA Modules:
  0.0 151.2 jit_solution(5987599818594855437)
XLA Ops:
  0.6 0.8 copy.54
  1.6 0.8 copy.53
  2.4 1.0 convolution_convert_fusion.2
  3.9 0.7 iota_compare_fusion.24
  5.1 1.2 all_to_all.20
  6.3 16.5 %all-to-all-start = ((s32[128,1,1152]{2,1,0:T(1,128)}), s32[128,1,1152]{2,1,0:T(1,128)S(1)}, u32[]{:S(2)}, u32[]{:S(2)}) async-start(s32[128,1,1152]{2,1,0:T(1,128)} %all_to_all.20), calls=%async_computation | async-start | bytes 1179648 | tf_op jit(solution)/shard_map/all_to_all | solution.py:129
  26.0 2.6 %all_gather.3 = bf16[4,256,128]{2,1,0:T(8,128)(2,1)S(1)} all-gather(bf16[2,256,128]{2,1,0:T(8,128)(2,1)S(1)} %copy-done.19), channel_id=1, replica_groups=mesh['dy'=4,'dx'=4,'dz'=8,'sub'=2] {'sub'}, dimensions={0}, use_global_device_ids=true | all-gather | bytes 393216 | tf_op jit(solution)/shard_map/all_gather | solution.py:115
  29.4 1.0 copy.64
  31.8 1.9 %fusion.85 = f32[512,512]{1,0:T(8,128)S(1)} fusion(f32[512,64]{0,1:T(8,128)S(1)} %copy-done.12, f32[64,512]{1,0:T(8,128)} %param.16), kind=kOutput, calls=%fused_computation.161 | convolution fusion | flops 201326592 | bytes 1310720 | tf_op jit(solution)/shard_map/dot_general | solution.py:116
  34.7 8.7 %all-to-all-done = s32[128,1,1152]{2,1,0:T(1,128)S(1)} async-done(((s32[128,1,1152]{2,1,0:T(1,128)}), s32[128,1,1152]{2,1,0:T(1,128)S(1)}, u32[]{:S(2)}, u32[]{:S(2)}) %all-to-all-start) | async-done | bytes 589856 | tf_op jit(solution)/shard_map/all_to_all | solution.py:129
  44.3 2.2 %fusion.4 = bf16[4,1536,128]{1,2,0:T(8,128)(2,1)S(1)} fusion(bf16[4,256,128]{2,1,0:T(8,128)(2,1)S(1)} %copy-done.17, s32[1536,4]{0,1:T(4,128)S(1)} %pad_add_fusion), kind=kOutput, calls=%fused_computation.12 | convolution fusion | flops 405012480 | bytes 1859584 | tf_op jit(solution)/shard_map/feu,euq->feq/dot_general | solution.py:23
  46.4 1.6 %copy.63 = bf16[1536,512]{1,0:T(8,128)(2,1)} copy(bf16[1536,512]{0,1:T(8,128)(2,1)S(1)} %bitcast.106) | data formatting | bytes 3145728 | tf_op jit(solution)/shard_map/reshape | solution.py:26
  48.1 1.5 %pad_maximum_fusion = bf16[1792,512]{1,0:T(8,128)(2,1)S(1)} fusion(bf16[1536,512]{1,0:T(8,128)(2,1)} %copy.63, bf16[256,512]{1,0:T(8,128)(2,1)S(1)} %copy.62), kind=kLoop, calls=%fused_computation.23 | loop fusion | flops 3670016 | bytes 3670016 | tf_op jit(solution)/shard_map/concatenate | solution.py:140
  49.6 2.0 %gather_fusion.1 = bf16[16,128,512]{2,1,0:T(8,128)(2,1)} fusion(bf16[14,128,512]{2,1,0:T(8,128)(2,1)S(1)} %bitcast.99, s32[1024]{0:T(1024)S(1)} %pad_clamp_fusion), kind=kCustom, calls=%fused_computation.1 | custom fusion | bytes 4194368 | tf_op jit(solution)/shard_map/gather | solution.py:145
  51.6 2.4 %fusion.16 = bf16[2,512,128]{1,2,0:T(8,128)(2,1)S(1)} fusion(bf16[2,8,128,128]{3,2,1,0:T(8,128)(2,1)} %bitcast.112, bf16[2,8,128,512]{3,2,1,0:T(8,128)(2,1)} %bitcast.100, f32[2,8,512]{2,1,0:T(8,128)S(1)} %bitcast.114), kind=kOutput, calls=%fused_computation.29 | convolution fusion | flops 271712256 | bytes 2916352 | tf_op jit(solution)/shard_map/btij,btjd->bid/dot_general | solution.py:147
  54.1 1.1 multiply_convert_fusion
  55.8 1.3 fusion.86
  57.9 2.7 %fusion.2 = (f32[2,8,512]{2,1,0:T(8,128)S(1)}, f32[2,512,1024]{1,2,0}) fusion(bf16[2,8,128,512]{3,2,1,0:T(8,128)(2,1)S(1)} %bitcast.101, bf16[2,128,1024]{1,2,0:T(8,128)(2,1)S(1)} %bitcast.105, bf16[2,128,512]{2,1,0:T(8,128)(2,1)S(1)} %bitcast.107), kind=kOutput, calls=%fused_computation.9 | convolution fusion | flops 271572992 | bytes 7110656
  60.5 1.1 scatter_custom_fusion
  61.7 1.5 fusion.88
  63.1 1.9 %fusion.89 = f32[512,64]{1,0:T(8,128)S(1)} fusion(f32[512,512]{1,0:T(8,128)S(1)} %scatter_custom_fusion, f32[64,512]{1,0:T(8,128)} %param.16), kind=kOutput, calls=%fused_computation.165 | convolution fusion | flops 201326592 | bytes 1310720 | tf_op jit(solution)/shard_map/dot_general | solution.py:178
  65.0 2.7 %bitcast_multiply_fusion = f32[2048,512]{1,0:T(8,128)S(1)} fusion(f32[2,512,1024]{1,2,0} %get-tuple-element.94, f32[16,512]{1,0:T(8,128)S(1)} %gather_fusion), kind=kLoop, calls=%fused_computation.10 | loop fusion | flops 1048576 | bytes 8421376 | tf_op jit(solution)/shard_map/mul | solution.py:176
  67.7 2.1 %subtract_convert_fusion.3 = (bf16[2048,128]{1,0:T(8,128)(2,1)}, bf16[2048,128]{1,0:T(8,128)(2,1)}, bf16[2048,128]{1,0:T(8,128)(2,1)S(1)}, bf16[2048,128]{1,0:T(...) fusion(f32[2048,512]{1,0:T(8,128)S(1)} %bitcast_multiply_fusion), kind=kLoop, calls=%fused_computation.53 | loop fusion | flops 3145728 | bytes 10485760 | tf_op jit(solution)/shard_map/convert_element_type | solution.py:37
  70.4 2.3 %fusion.8 = f32[256,256]{1,0:T(8,128)S(1)} fusion(bf16[2048,128]{1,0:T(8,128)(2,1)} %get-tuple-element.40, bf16[2048,128]{1,0:T(8,128)(2,1)} %get-tuple-element.41, s32[2048]{0:T(1024)S(1)} %bitcast.119), kind=kOutput, calls=%fused_computation.19 | convolution fusion | flops 271056896 | bytes 1318912 | tf_op jit(solution)/shard_map/dot_general | solution.py:40
  72.8 1.0 fusion.9
  73.9 1.0 fusion.10
  75.0 1.0 fusion.11
  77.7 0.7 constant_dynamic-slice_fusion
  78.9 1.0 dynamic-slice_dynamic-update-slice_fusion.1
  80.0 1.1 dynamic-slice_dynamic-update-slice_fusion
  81.1 0.6 bitcast_dynamic-update-slice_fusion
  81.7 0.7 dynamic-slice_dynamic-update-slice_fusion.4
  82.4 0.7 constant_dynamic-update-slice_fusion.1
  83.1 2.5 %collective-permute-start = (f32[704,512]{1,0:T(8,128)}, f32[704,512]{1,0:T(8,128)S(1)}, u32[]{:S(2)}, u32[]{:S(2)}) collective-permute-start(f32[704,512]{1,0:T(8,128)} %constant_dynamic-update-slice_fusion.1), channel_id=1, source_target_pairs={{0,1},{1,0},{2,3},{3,2},{4,5},{5,4},{6,7},{7,6},{8,9},{9,8},{10,11... | collective-permute-start | bytes 4325384 | tf_op jit(solution)/shard_map/ppermute | solution.py:59
  85.6 0.7 constant_dynamic-update-slice_fusion
  86.3 2.3 %collective-permute-done = f32[704,512]{1,0:T(8,128)S(1)} collective-permute-done((f32[704,512]{1,0:T(8,128)}, f32[704,512]{1,0:T(8,128)S(1)}, u32[]{:S(2)}, u32[]{:S(2)}) %collective-permute-start) | collective-permute-done | bytes 1441824 | tf_op jit(solution)/shard_map/ppermute | solution.py:59
  88.6 1.6 %add_convert_fusion = bf16[704,512]{1,0:T(8,128)(2,1)S(1)} fusion(f32[704,512]{1,0:T(8,128)} %constant_dynamic-update-slice_fusion, f32[704,512]{1,0:T(8,128)S(1)} %collective-permute-done), kind=kLoop, calls=%fused_computation.25 | loop fusion | flops 720896 | bytes 3604480 | tf_op jit(solution)/shard_map/convert_element_type | solution.py:70
  90.4 16.7 %all_to_all.32 = bf16[16,44,512]{2,1,0:T(8,128)(2,1)S(1)} all-to-all(bf16[16,44,512]{2,1,0:T(8,128)(2,1)S(1)} %convert_element_type.195), channel_id=1, replica_groups=mesh['dy'=4,'dx'=4,'dz'=8,'sub'=2] {'dy','dx'}, dimensions={0} | all-to-all | bytes 1441792 | tf_op jit(solution)/shard_map/all_to_all | solution.py:71
  107.2 10.3 %all_to_all.33 = f32[8,11,256]{2,1,0:T(8,128)S(1)} all-to-all(f32[8,11,256]{2,1,0:T(8,128)S(1)} %reshape.135), channel_id=1, replica_groups=mesh['dy'=4,'dx'=4,'dz'=8,'sub'=2] {'dz'}, dimensions={0} | all-to-all | bytes 180224 | tf_op jit(solution)/shard_map/all_to_all | solution.py:71
  117.6 9.6 %all_to_all.34 = bf16[8,11,256]{2,1,0:T(8,128)(2,1)S(1)} all-to-all(bf16[8,11,256]{2,1,0:T(8,128)(2,1)S(1)} %broadcast_in_dim.74), channel_id=1, replica_groups=mesh['dy'=4,'dx'=4,'dz'=8,'sub'=2] {'dz'}, dimensions={0} | all-to-all | bytes 90112 | tf_op jit(solution)/shard_map/all_to_all | solution.py:76
  127.3 13.6 %all_to_all.35 = bf16[16,44,512]{2,1,0:T(8,128)(2,1)S(1)} all-to-all(bf16[16,44,512]{2,1,0:T(8,128)(2,1)S(1)} %broadcast_in_dim.76), channel_id=1, replica_groups=mesh['dy'=4,'dx'=4,'dz'=8,'sub'=2] {'dy','dx'}, dimensions={0} | all-to-all | bytes 1441792 | tf_op jit(solution)/shard_map/all_to_all | solution.py:76
  141.0 4.5 %collective-permute-start.1 = (bf16[576,512]{1,0:T(8,128)(2,1)S(1)}, bf16[576,512]{1,0:T(8,128)(2,1)S(1)}, u32[]{:S(2)}, u32[]{:S(2)}) collective-permute-start(bf16[576,512]{1,0:T(8,128)(2,1)S(1)} %slice.216), channel_id=1, source_target_pairs={{0,1},{1,0},{2,3},{3,2},{4,5},{5,4},{6,7},{7,6},{8,9},{9,8},{10,11... | collective-permute-start | bytes 1769480 | tf_op jit(solution)/shard_map/ppermute | solution.py:80
  145.6 0.7 reshape.142
  146.3 0.9 collective-permute-done.1
  147.7 0.8 copy.70
  148.4 0.7 pad_maximum_fusion.4
  149.1 1.0 pad_maximum_fusion.2
  150.1 1.0 pad_maximum_fusion.1
  (118 shorter events, 9.5 us)
Async XLA Ops:
  0.6 53.4 %copy-start = (bf16[512,512]{1,0:T(8,128)(2,1)S(1)}, bf16[512,512]{1,0:T(8,128)(2,1)}, u32[]{:S(2)}) copy-start(bf16[512,512]{1,0:T(8,128)(2,1)} %param.17) | copy-start | bytes 1572868
  4.9 17.9 %copy-start.21 = (s32[2]{0:T(128)S(1)}, s32[2]{0:T(128)}, u32[]{:S(2)}) copy-start(s32[2]{0:T(128)} %param.24) | copy-start | bytes 28
  4.9 21.0 %copy-start.19 = (bf16[2,256,128]{2,1,0:T(8,128)(2,1)S(1)}, bf16[2,256,128]{2,1,0:T(8,128)(2,1)}, u32[]{:S(2)}) copy-start(bf16[2,256,128]{2,1,0:T(8,128)(2,1)} %param.14) | copy-start | bytes 393220
  4.9 23.6 %copy-start.20 = (s32[256,4]{0,1:T(4,128)S(1)}, s32[256,4]{0,1:T(4,128)}, u32[]{:S(2)}) copy-start(s32[256,4]{0,1:T(4,128)} %param.13) | copy-start | bytes 12292
  5.1 24.4 %copy-start.15 = (bf16[16,128,128]{2,1,0:T(8,128)(2,1)S(1)}, bf16[16,128,128]{2,1,0:T(8,128)(2,1)}, u32[]{:S(2)}) copy-start(bf16[16,128,128]{2,1,0:T(8,128)(2,1)} %param.19) | copy-start | bytes 1572868
  6.3 25.4 %copy-start.22 = (s32[16]{0:T(128)S(1)}, s32[16]{0:T(128)}, u32[]{:S(2)}) copy-start(s32[16]{0:T(128)} %param.20) | copy-start | bytes 196
  6.3 25.5 %copy-start.23 = (s32[16]{0:T(128)S(1)}, s32[16]{0:T(128)}, u32[]{:S(2)}) copy-start(s32[16]{0:T(128)} %param.21) | copy-start | bytes 196
  6.3 25.5 %copy-start.12 = (f32[512,64]{0,1:T(8,128)S(1)}, f32[512,64]{0,1:T(8,128)}, u32[]{:S(2)}) copy-start(f32[512,64]{0,1:T(8,128)} %param.15) | copy-start | bytes 393220
  6.3 37.0 %all-to-all-start = ((s32[128,1,1152]{2,1,0:T(1,128)}), s32[128,1,1152]{2,1,0:T(1,128)S(1)}, u32[]{:S(2)}, u32[]{:S(2)}) async-start(s32[128,1,1152]{2,1,0:T(1,128)} %all_to_all.20), calls=%async_computation | async-start | bytes 1179648 | tf_op jit(solution)/shard_map/all_to_all | solution.py:129
  28.6 0.7 copy-start.16
  28.6 5.8 %copy-start.4 = (bf16[512,512]{1,0:T(8,128)(2,1)S(1)}, bf16[512,512]{1,0:T(8,128)(2,1)}, u32[]{:S(2)}) copy-start(bf16[512,512]{1,0:T(8,128)(2,1)} %param.18) | copy-start | bytes 1572868
  34.7 9.6 %copy-start.17 = (bf16[4,256,128]{2,1,0:T(8,128)(2,1)S(1)}, bf16[4,256,128]{2,1,0:T(8,128)(2,1)}, u32[]{:S(2)}) copy-start(bf16[4,256,128]{2,1,0:T(8,128)(2,1)} %copy-done.16) | copy-start | bytes 786436
  51.6 2.4 %copy-start.18 = (bf16[256,512]{1,0:T(8,128)(2,1)S(1)}, bf16[256,512]{1,0:T(8,128)(2,1)}, u32[]{:S(2)}) copy-start(bf16[256,512]{1,0:T(8,128)(2,1)} %param.25) | copy-start | bytes 786436
  54.0 1.4 copy-start.5
  55.8 2.0 %copy-start.1 = (bf16[16,128,512]{2,1,0:T(8,128)(2,1)S(1)}, bf16[16,128,512]{2,1,0:T(8,128)(2,1)}, u32[]{:S(2)}) copy-start(bf16[16,128,512]{2,1,0:T(8,128)(2,1)} %gather_fusion.1) | copy-start | bytes 6291460
  55.8 2.0 %copy-start.3 = (bf16[2,8,128,128]{2,3,1,0:T(8,128)(2,1)S(1)}, bf16[2,8,128,128]{2,3,1,0:T(8,128)(2,1)}, u32[]{:S(2)}) copy-start(bf16[2,8,128,128]{2,3,1,0:T(8,128)(2,1)} %copy.64) | copy-start | bytes 1572868
  57.9 3.8 %copy-start.13 = (f32[512,64]{0,1:T(8,128)S(1)}, f32[512,64]{0,1:T(8,128)}, u32[]{:S(2)}) copy-start(f32[512,64]{0,1:T(8,128)} %param.15) | copy-start | bytes 393220
  70.3 2.4 %copy-start.10 = (bf16[2048,128]{1,0:T(8,128)(2,1)S(1)}, bf16[2048,128]{1,0:T(8,128)(2,1)}, u32[]{:S(2)}) copy-start(bf16[2048,128]{1,0:T(8,128)(2,1)} %get-tuple-element.52) | copy-start | bytes 1572868
  70.4 2.4 %copy-start.11 = (bf16[2048,128]{1,0:T(8,128)(2,1)S(1)}, bf16[2048,128]{1,0:T(8,128)(2,1)}, u32[]{:S(2)}) copy-start(bf16[2048,128]{1,0:T(8,128)(2,1)} %get-tuple-element.53) | copy-start | bytes 1572868
  72.7 1.2 copy-start.8
  72.7 1.2 copy-start.9
  73.8 1.2 copy-start.7
  77.6 1.3 copy-start.2
  78.9 2.1 %copy-start.14 = (f32[512,64]{0,1:T(8,128)S(1)}, f32[512,64]{0,1:T(8,128)}, u32[]{:S(2)}) copy-start(f32[512,64]{0,1:T(8,128)} %fusion.88) | copy-start | bytes 393220
  80.0 5.6 %copy-start.6 = (f32[2,256,128]{2,1,0:T(8,128)S(1)}, f32[2,256,128]{2,1,0:T(8,128)}, u32[]{:S(2)}) copy-start(f32[2,256,128]{2,1,0:T(8,128)} %get-tuple-element.69) | copy-start | bytes 786436
  83.1 5.6 %collective-permute-start = (f32[704,512]{1,0:T(8,128)}, f32[704,512]{1,0:T(8,128)S(1)}, u32[]{:S(2)}, u32[]{:S(2)}) collective-permute-start(f32[704,512]{1,0:T(8,128)} %constant_dynamic-update-slice_fusion.1), channel_id=1, source_target_pairs={{0,1},{1,0},{2,3},{3,2},{4,5},{5,4},{6,7},{7,6},{8,9},{9,8},{10,11... | collective-permute-start | bytes 4325384 | tf_op jit(solution)/shard_map/ppermute | solution.py:59
  141.0 6.1 %collective-permute-start.1 = (bf16[576,512]{1,0:T(8,128)(2,1)S(1)}, bf16[576,512]{1,0:T(8,128)(2,1)S(1)}, u32[]{:S(2)}, u32[]{:S(2)}) collective-permute-start(bf16[576,512]{1,0:T(8,128)(2,1)S(1)} %slice.216), channel_id=1, source_target_pairs={{0,1},{1,0},{2,3},{3,2},{4,5},{5,4},{6,7},{7,6},{8,9},{9,8},{10,11... | collective-permute-start | bytes 1769480 | tf_op jit(solution)/shard_map/ppermute | solution.py:80

commit v16 on v15

--- a/solution.py
+++ b/solution.py
@@ -60,14 +60,13 @@
     rows = mine.shape[0]
     shapes = []
     piece = mine
-    for stage, (axis, size) in enumerate(dom_axes):
+    for axis, size in dom_axes:
         shapes.append(piece.shape)
         lanes = piece.shape[-1]
         if piece.shape[0] % size:
             lanes = 256
         chunks = piece.reshape(size, -1, lanes)
-        if stage == 0:
-            chunks = chunks.astype(jnp.bfloat16)
+        chunks = chunks.astype(jnp.bfloat16)
         received = lax.all_to_all(chunks, axis, 0, 0, tiled=True)
         piece = jnp.sum(received.astype(jnp.float32), axis=0)
     piece = piece.astype(jnp.bfloat16)

time: 152 us -> 151 us (level)
  no operation moved by 1% of the time
where the time goes in v16:
time: 151 us
  blocking collectives  52.4 us (35%)
  matrix products  24.3 us (16%)
  starting transfers between devices  23.3 us (15%)
  local copies, waits for them, and re-layouts  20.5 us (14%)
  other arithmetic  13.1 us (9%)
  waiting for transfers between devices  11.8 us (8%)
  between operations  5.27 us (3%)
    all_to_all x2, blocking collectives, all_sum(): received = lax.all_to_all(chunks, axis, 0, 0, tiled=True)  26.3 us
    all_to_all x2, blocking collectives, all_sum(): piece = lax.all_to_all(spread, axis, 0, 0, tiled=True).reshape(shape)  23.5 us
    all_to_all x1, starting transfers between devices, shards(): incoming = lax.all_to_all(payload, DOM, 0, 0, tiled=True)  16.5 us
    all_to_all x1, waiting for transfers between devices, shards(): incoming = lax.all_to_all(payload, DOM, 0, 0, tiled=True)  8.65 us
    unnamed x56, local copies, waits for them, and re-layouts  7.06 us
    dot_general x8, matrix products, fold_books(): lax.dot_general(indicator_rows, both, (((0,), (0,)), ((), ())), preferred...  6.77 us
    ppermute x1, starting transfers between devices, all_sum(): other_dense = lax.ppermute(own_dense, 'sub', swap)  4.38 us
  transfers between devices with their start and end apart: 3, of which 3 were waited for; matrix products, arithmetic and copies ran while one was open for 4% of the time, Pallas kernels for 0%

profile of v16, /device:TPU:1, one launch (start us, length us, event | category | flops | bytes accessed | tf_op | source)
XLA Modules:
  0.0 150.7 jit_solution(887399296720845174)
XLA Ops:
  0.6 0.8 copy.54
  1.6 0.8 copy.53
  2.4 1.0 convolution_convert_fusion.2
  3.9 0.7 iota_compare_fusion.24
  5.1 1.2 all_to_all.20
  6.3 16.5 %all-to-all-start = ((s32[128,1,1152]{2,1,0:T(1,128)}), s32[128,1,1152]{2,1,0:T(1,128)S(1)}, u32[]{:S(2)}, u32[]{:S(2)}) async-start(s32[128,1,1152]{2,1,0:T(1,128)} %all_to_all.20), calls=%async_computation | async-start | bytes 1179648 | tf_op jit(solution)/shard_map/all_to_all | solution.py:128
  26.0 2.6 %all_gather.3 = bf16[4,256,128]{2,1,0:T(8,128)(2,1)S(1)} all-gather(bf16[2,256,128]{2,1,0:T(8,128)(2,1)S(1)} %copy-done.19), channel_id=1, replica_groups=mesh['dy'=4,'dx'=4,'dz'=8,'sub'=2] {'sub'}, dimensions={0}, use_global_device_ids=true | all-gather | bytes 393216 | tf_op jit(solution)/shard_map/all_gather | solution.py:114
  29.4 1.0 copy.64
  31.8 1.9 %fusion.85 = f32[512,512]{1,0:T(8,128)S(1)} fusion(f32[512,64]{0,1:T(8,128)S(1)} %copy-done.12, f32[64,512]{1,0:T(8,128)} %param.16), kind=kOutput, calls=%fused_computation.160 | convolution fusion | flops 201326592 | bytes 1310720 | tf_op jit(solution)/shard_map/dot_general | solution.py:115
  34.7 8.7 %all-to-all-done = s32[128,1,1152]{2,1,0:T(1,128)S(1)} async-done(((s32[128,1,1152]{2,1,0:T(1,128)}), s32[128,1,1152]{2,1,0:T(1,128)S(1)}, u32[]{:S(2)}, u32[]{:S(2)}) %all-to-all-start) | async-done | bytes 589856 | tf_op jit(solution)/shard_map/all_to_all | solution.py:128
  44.3 2.2 %fusion.4 = bf16[4,1536,128]{1,2,0:T(8,128)(2,1)S(1)} fusion(bf16[4,256,128]{2,1,0:T(8,128)(2,1)S(1)} %copy-done.17, s32[1536,4]{0,1:T(4,128)S(1)} %pad_add_fusion), kind=kOutput, calls=%fused_computation.12 | convolution fusion | flops 405012480 | bytes 1859584 | tf_op jit(solution)/shard_map/feu,euq->feq/dot_general | solution.py:23
  46.4 1.6 %copy.63 = bf16[1536,512]{1,0:T(8,128)(2,1)} copy(bf16[1536,512]{0,1:T(8,128)(2,1)S(1)} %bitcast.106) | data formatting | bytes 3145728 | tf_op jit(solution)/shard_map/reshape | solution.py:26
  48.1 1.5 %pad_maximum_fusion = bf16[1792,512]{1,0:T(8,128)(2,1)S(1)} fusion(bf16[1536,512]{1,0:T(8,128)(2,1)} %copy.63, bf16[256,512]{1,0:T(8,128)(2,1)S(1)} %copy.62), kind=kLoop, calls=%fused_computation.23 | loop fusion | flops 3670016 | bytes 3670016 | tf_op jit(solution)/shard_map/concatenate | solution.py:139
  49.6 2.0 %gather_fusion.1 = bf16[16,128,512]{2,1,0:T(8,128)(2,1)} fusion(bf16[14,128,512]{2,1,0:T(8,128)(2,1)S(1)} %bitcast.99, s32[1024]{0:T(1024)S(1)} %pad_clamp_fusion), kind=kCustom, calls=%fused_computation.1 | custom fusion | bytes 4194368 | tf_op jit(solution)/shard_map/gather | solution.py:144
  51.6 2.4 %fusion.16 = bf16[2,512,128]{1,2,0:T(8,128)(2,1)S(1)} fusion(bf16[2,8,128,128]{3,2,1,0:T(8,128)(2,1)} %bitcast.112, bf16[2,8,128,512]{3,2,1,0:T(8,128)(2,1)} %bitcast.100, f32[2,8,512]{2,1,0:T(8,128)S(1)} %bitcast.114), kind=kOutput, calls=%fused_computation.28 | convolution fusion | flops 271712256 | bytes 2916352 | tf_op jit(solution)/shard_map/btij,btjd->bid/dot_general | solution.py:146
  54.1 1.1 multiply_convert_fusion
  55.8 1.3 fusion.86
  57.9 2.7 %fusion.2 = (f32[2,8,512]{2,1,0:T(8,128)S(1)}, f32[2,512,1024]{1,2,0}) fusion(bf16[2,8,128,512]{3,2,1,0:T(8,128)(2,1)S(1)} %bitcast.101, bf16[2,128,1024]{1,2,0:T(8,128)(2,1)S(1)} %bitcast.105, bf16[2,128,512]{2,1,0:T(8,128)(2,1)S(1)} %bitcast.107), kind=kOutput, calls=%fused_computation.9 | convolution fusion | flops 271572992 | bytes 7110656
  60.5 1.1 scatter_custom_fusion
  61.7 1.5 fusion.88
  63.1 1.9 %fusion.89 = f32[512,64]{1,0:T(8,128)S(1)} fusion(f32[512,512]{1,0:T(8,128)S(1)} %scatter_custom_fusion, f32[64,512]{1,0:T(8,128)} %param.16), kind=kOutput, calls=%fused_computation.164 | convolution fusion | flops 201326592 | bytes 1310720 | tf_op jit(solution)/shard_map/dot_general | solution.py:177
  65.0 2.7 %bitcast_multiply_fusion = f32[2048,512]{1,0:T(8,128)S(1)} fusion(f32[2,512,1024]{1,2,0} %get-tuple-element.94, f32[16,512]{1,0:T(8,128)S(1)} %gather_fusion), kind=kLoop, calls=%fused_computation.10 | loop fusion | flops 1048576 | bytes 8421376 | tf_op jit(solution)/shard_map/mul | solution.py:175
  67.7 2.1 %subtract_convert_fusion.3 = (bf16[2048,128]{1,0:T(8,128)(2,1)}, bf16[2048,128]{1,0:T(8,128)(2,1)}, bf16[2048,128]{1,0:T(8,128)(2,1)S(1)}, bf16[2048,128]{1,0:T(...) fusion(f32[2048,512]{1,0:T(8,128)S(1)} %bitcast_multiply_fusion), kind=kLoop, calls=%fused_computation.52 | loop fusion | flops 3145728 | bytes 10485760 | tf_op jit(solution)/shard_map/convert_element_type | solution.py:37
  70.4 2.3 %fusion.8 = f32[256,256]{1,0:T(8,128)S(1)} fusion(bf16[2048,128]{1,0:T(8,128)(2,1)} %get-tuple-element.40, bf16[2048,128]{1,0:T(8,128)(2,1)} %get-tuple-element.41, s32[2048]{0:T(1024)S(1)} %bitcast.119), kind=kOutput, calls=%fused_computation.19 | convolution fusion | flops 271056896 | bytes 1318912 | tf_op jit(solution)/shard_map/dot_general | solution.py:40
  72.8 1.0 fusion.9
  73.9 1.0 fusion.10
  75.0 1.0 fusion.11
  77.7 0.7 constant_dynamic-slice_fusion
  78.9 1.0 dynamic-slice_dynamic-update-slice_fusion.1
  80.0 1.1 dynamic-slice_dynamic-update-slice_fusion
  81.1 0.6 bitcast_dynamic-update-slice_fusion
  81.7 0.7 dynamic-slice_dynamic-update-slice_fusion.4
  82.4 0.7 constant_dynamic-update-slice_fusion.1
  83.1 2.5 %collective-permute-start = (f32[704,512]{1,0:T(8,128)}, f32[704,512]{1,0:T(8,128)S(1)}, u32[]{:S(2)}, u32[]{:S(2)}) collective-permute-start(f32[704,512]{1,0:T(8,128)} %constant_dynamic-update-slice_fusion.1), channel_id=1, source_target_pairs={{0,1},{1,0},{2,3},{3,2},{4,5},{5,4},{6,7},{7,6},{8,9},{9,8},{10,11... | collective-permute-start | bytes 4325384 | tf_op jit(solution)/shard_map/ppermute | solution.py:59
  85.6 0.7 constant_dynamic-update-slice_fusion
  86.3 2.3 %collective-permute-done = f32[704,512]{1,0:T(8,128)S(1)} collective-permute-done((f32[704,512]{1,0:T(8,128)}, f32[704,512]{1,0:T(8,128)S(1)}, u32[]{:S(2)}, u32[]{:S(2)}) %collective-permute-start) | collective-permute-done | bytes 1441824 | tf_op jit(solution)/shard_map/ppermute | solution.py:59
  88.6 1.6 %add_convert_fusion = bf16[704,512]{1,0:T(8,128)(2,1)S(1)} fusion(f32[704,512]{1,0:T(8,128)} %constant_dynamic-update-slice_fusion, f32[704,512]{1,0:T(8,128)S(1)} %collective-permute-done), kind=kLoop, calls=%fused_computation.24 | loop fusion | flops 720896 | bytes 3604480 | tf_op jit(solution)/shard_map/convert_element_type | solution.py:69
  90.4 16.7 %all_to_all.32 = bf16[16,44,512]{2,1,0:T(8,128)(2,1)S(1)} all-to-all(bf16[16,44,512]{2,1,0:T(8,128)(2,1)S(1)} %convert_element_type.192), channel_id=1, replica_groups=mesh['dy'=4,'dx'=4,'dz'=8,'sub'=2] {'dy','dx'}, dimensions={0} | all-to-all | bytes 1441792 | tf_op jit(solution)/shard_map/all_to_all | solution.py:70
  107.2 9.6 %all_to_all.33 = bf16[8,11,256]{2,1,0:T(8,128)(2,1)S(1)} all-to-all(bf16[8,11,256]{2,1,0:T(8,128)(2,1)S(1)} %convert_element_type.193), channel_id=1, replica_groups=mesh['dy'=4,'dx'=4,'dz'=8,'sub'=2] {'dz'}, dimensions={0} | all-to-all | bytes 90112 | tf_op jit(solution)/shard_map/all_to_all | solution.py:70
  116.9 9.6 %all_to_all.34 = bf16[8,11,256]{2,1,0:T(8,128)(2,1)S(1)} all-to-all(bf16[8,11,256]{2,1,0:T(8,128)(2,1)S(1)} %broadcast_in_dim.74), channel_id=1, replica_groups=mesh['dy'=4,'dx'=4,'dz'=8,'sub'=2] {'dz'}, dimensions={0} | all-to-all | bytes 90112 | tf_op jit(solution)/shard_map/all_to_all | solution.py:75
  126.6 13.9 %all_to_all.35 = bf16[16,44,512]{2,1,0:T(8,128)(2,1)S(1)} all-to-all(bf16[16,44,512]{2,1,0:T(8,128)(2,1)S(1)} %broadcast_in_dim.76), channel_id=1, replica_groups=mesh['dy'=4,'dx'=4,'dz'=8,'sub'=2] {'dy','dx'}, dimensions={0} | all-to-all | bytes 1441792 | tf_op jit(solution)/shard_map/all_to_all | solution.py:75
  140.7 4.4 %collective-permute-start.1 = (bf16[576,512]{1,0:T(8,128)(2,1)S(1)}, bf16[576,512]{1,0:T(8,128)(2,1)S(1)}, u32[]{:S(2)}, u32[]{:S(2)}) collective-permute-start(bf16[576,512]{1,0:T(8,128)(2,1)S(1)} %slice.216), channel_id=1, source_target_pairs={{0,1},{1,0},{2,3},{3,2},{4,5},{5,4},{6,7},{7,6},{8,9},{9,8},{10,11... | collective-permute-start | bytes 1769480 | tf_op jit(solution)/shard_map/ppermute | solution.py:79
  145.1 0.7 reshape.138
  145.8 0.9 collective-permute-done.1
  147.1 0.8 copy.70
  147.9 0.7 pad_maximum_fusion.4
  148.6 1.0 pad_maximum_fusion.2
  149.6 1.0 pad_maximum_fusion.1
  (118 shorter events, 9.5 us)
Async XLA Ops:
  0.6 53.4 %copy-start = (bf16[512,512]{1,0:T(8,128)(2,1)S(1)}, bf16[512,512]{1,0:T(8,128)(2,1)}, u32[]{:S(2)}) copy-start(bf16[512,512]{1,0:T(8,128)(2,1)} %param.17) | copy-start | bytes 1572868
  4.9 17.9 %copy-start.21 = (s32[2]{0:T(128)S(1)}, s32[2]{0:T(128)}, u32[]{:S(2)}) copy-start(s32[2]{0:T(128)} %param.24) | copy-start | bytes 28
  4.9 21.0 %copy-start.19 = (bf16[2,256,128]{2,1,0:T(8,128)(2,1)S(1)}, bf16[2,256,128]{2,1,0:T(8,128)(2,1)}, u32[]{:S(2)}) copy-start(bf16[2,256,128]{2,1,0:T(8,128)(2,1)} %param.14) | copy-start | bytes 393220
  4.9 23.6 %copy-start.20 = (s32[256,4]{0,1:T(4,128)S(1)}, s32[256,4]{0,1:T(4,128)}, u32[]{:S(2)}) copy-start(s32[256,4]{0,1:T(4,128)} %param.13) | copy-start | bytes 12292
  5.1 24.4 %copy-start.15 = (bf16[16,128,128]{2,1,0:T(8,128)(2,1)S(1)}, bf16[16,128,128]{2,1,0:T(8,128)(2,1)}, u32[]{:S(2)}) copy-start(bf16[16,128,128]{2,1,0:T(8,128)(2,1)} %param.19) | copy-start | bytes 1572868
  6.3 25.4 %copy-start.22 = (s32[16]{0:T(128)S(1)}, s32[16]{0:T(128)}, u32[]{:S(2)}) copy-start(s32[16]{0:T(128)} %param.20) | copy-start | bytes 196
  6.3 25.5 %copy-start.23 = (s32[16]{0:T(128)S(1)}, s32[16]{0:T(128)}, u32[]{:S(2)}) copy-start(s32[16]{0:T(128)} %param.21) | copy-start | bytes 196
  6.3 25.5 %copy-start.12 = (f32[512,64]{0,1:T(8,128)S(1)}, f32[512,64]{0,1:T(8,128)}, u32[]{:S(2)}) copy-start(f32[512,64]{0,1:T(8,128)} %param.15) | copy-start | bytes 393220
  6.3 37.0 %all-to-all-start = ((s32[128,1,1152]{2,1,0:T(1,128)}), s32[128,1,1152]{2,1,0:T(1,128)S(1)}, u32[]{:S(2)}, u32[]{:S(2)}) async-start(s32[128,1,1152]{2,1,0:T(1,128)} %all_to_all.20), calls=%async_computation | async-start | bytes 1179648 | tf_op jit(solution)/shard_map/all_to_all | solution.py:128
  28.6 0.7 copy-start.16
  28.6 5.8 %copy-start.4 = (bf16[512,512]{1,0:T(8,128)(2,1)S(1)}, bf16[512,512]{1,0:T(8,128)(2,1)}, u32[]{:S(2)}) copy-start(bf16[512,512]{1,0:T(8,128)(2,1)} %param.18) | copy-start | bytes 1572868
  34.7 9.6 %copy-start.17 = (bf16[4,256,128]{2,1,0:T(8,128)(2,1)S(1)}, bf16[4,256,128]{2,1,0:T(8,128)(2,1)}, u32[]{:S(2)}) copy-start(bf16[4,256,128]{2,1,0:T(8,128)(2,1)} %copy-done.16) | copy-start | bytes 786436
  51.6 2.4 %copy-start.18 = (bf16[256,512]{1,0:T(8,128)(2,1)S(1)}, bf16[256,512]{1,0:T(8,128)(2,1)}, u32[]{:S(2)}) copy-start(bf16[256,512]{1,0:T(8,128)(2,1)} %param.25) | copy-start | bytes 786436
  54.0 1.4 copy-start.5
  55.8 2.0 %copy-start.1 = (bf16[16,128,512]{2,1,0:T(8,128)(2,1)S(1)}, bf16[16,128,512]{2,1,0:T(8,128)(2,1)}, u32[]{:S(2)}) copy-start(bf16[16,128,512]{2,1,0:T(8,128)(2,1)} %gather_fusion.1) | copy-start | bytes 6291460
  55.8 2.0 %copy-start.3 = (bf16[2,8,128,128]{2,3,1,0:T(8,128)(2,1)S(1)}, bf16[2,8,128,128]{2,3,1,0:T(8,128)(2,1)}, u32[]{:S(2)}) copy-start(bf16[2,8,128,128]{2,3,1,0:T(8,128)(2,1)} %copy.64) | copy-start | bytes 1572868
  57.9 3.8 %copy-start.13 = (f32[512,64]{0,1:T(8,128)S(1)}, f32[512,64]{0,1:T(8,128)}, u32[]{:S(2)}) copy-start(f32[512,64]{0,1:T(8,128)} %param.15) | copy-start | bytes 393220
  70.3 2.4 %copy-start.10 = (bf16[2048,128]{1,0:T(8,128)(2,1)S(1)}, bf16[2048,128]{1,0:T(8,128)(2,1)}, u32[]{:S(2)}) copy-start(bf16[2048,128]{1,0:T(8,128)(2,1)} %get-tuple-element.52) | copy-start | bytes 1572868
  70.4 2.4 %copy-start.11 = (bf16[2048,128]{1,0:T(8,128)(2,1)S(1)}, bf16[2048,128]{1,0:T(8,128)(2,1)}, u32[]{:S(2)}) copy-start(bf16[2048,128]{1,0:T(8,128)(2,1)} %get-tuple-element.53) | copy-start | bytes 1572868
  72.7 1.2 copy-start.8
  72.7 1.2 copy-start.9
  73.8 1.2 copy-start.7
  77.6 1.3 copy-start.2
  78.9 2.1 %copy-start.14 = (f32[512,64]{0,1:T(8,128)S(1)}, f32[512,64]{0,1:T(8,128)}, u32[]{:S(2)}) copy-start(f32[512,64]{0,1:T(8,128)} %fusion.88) | copy-start | bytes 393220
  80.0 5.6 %copy-start.6 = (f32[2,256,128]{2,1,0:T(8,128)S(1)}, f32[2,256,128]{2,1,0:T(8,128)}, u32[]{:S(2)}) copy-start(f32[2,256,128]{2,1,0:T(8,128)} %get-tuple-element.69) | copy-start | bytes 786436
  83.1 5.6 %collective-permute-start = (f32[704,512]{1,0:T(8,128)}, f32[704,512]{1,0:T(8,128)S(1)}, u32[]{:S(2)}, u32[]{:S(2)}) collective-permute-start(f32[704,512]{1,0:T(8,128)} %constant_dynamic-update-slice_fusion.1), channel_id=1, source_target_pairs={{0,1},{1,0},{2,3},{3,2},{4,5},{5,4},{6,7},{7,6},{8,9},{9,8},{10,11... | collective-permute-start | bytes 4325384 | tf_op jit(solution)/shard_map/ppermute | solution.py:59
  140.7 6.0 %collective-permute-start.1 = (bf16[576,512]{1,0:T(8,128)(2,1)S(1)}, bf16[576,512]{1,0:T(8,128)(2,1)S(1)}, u32[]{:S(2)}, u32[]{:S(2)}) collective-permute-start(bf16[576,512]{1,0:T(8,128)(2,1)S(1)} %slice.216), channel_id=1, source_target_pairs={{0,1},{1,0},{2,3},{3,2},{4,5},{5,4},{6,7},{7,6},{8,9},{9,8},{10,11... | collective-permute-start | bytes 1769480 | tf_op jit(solution)/shard_map/ppermute | solution.py:79
